TPU v7x, 32 devices: a whole 2x2x4 slice. The times are simulated.
32 devices in a mesh: ctx: 8 (over z, y), tp: 4 (over x, core).
Axes of the slice: x: 2, y: 2, z: 4, core: 2. Of those that a mesh axis runs over, the one named last changes fastest.
Arguments:
- tokens: bfloat16 [1024, 4096], P('ctx'), may hold values from -6 to 6
- w_query: bfloat16 [4096, 2048], P('ctx', 'tp'), may hold values from -0.09375 to 0.09375
- w_key: bfloat16 [4096, 2048], P('ctx', 'tp'), may hold values from -0.09375 to 0.09375
- w_value: bfloat16 [4096, 2048], P('ctx', 'tp'), may hold values from -0.09375 to 0.09375
- taps_query: float32 [3, 2048], P(None, 'tp'), may hold values from -3.5 to 3.5
- taps_key: float32 [3, 2048], P(None, 'tp'), may hold values from -3.5 to 3.5
- taps_value: float32 [3, 2048], P(None, 'tp'), may hold values from -3.5 to 3.5
- decay_rate: float32 [16, 2048], P(None, 'tp'), may hold values from 1e-05 to 0.03
- residue: float32 [16, 2048], P(None, 'tp'), may hold values from -1.5 to 1.5
- skip_gain: float32 [2048], P('tp'), may hold values from -3 to 3
- w_out: bfloat16 [2048, 4096], P('ctx', 'tp'), may hold values from -0.125 to 0.125
Outputs:
- layer_out: bfloat16 [1024, 4096], P('ctx', 'tp')
All inputs are finite; a program needn't handle non-finite values.
Results may differ from a plain program's by a relative error of at most 0.015.
Values may be sent and summed in bfloat16 or wider, within the bound.
No kernel may reach another device: no remote copies, remote signals or barrier semaphores. Data moves between devices by JAX's collectives and lax.ppermute only.
A program may use at most 128 MiB of HBM per device.

v0:
```python
import math

import jax
import jax.numpy as jnp
from jax import lax
from jax.sharding import PartitionSpec as P


def exact_mul(left, right):
    return jnp.matmul(left, right, precision=lax.Precision.HIGHEST)


def dft_tables(count):
    index = jnp.arange(count, dtype=jnp.int32)
    angle = (index[:, None] * index[None, :] % count).astype(jnp.float32) * (2.0 * math.pi / count)
    return (jnp.cos(angle), jnp.sin(angle))


def long_conv(signal, rates, residues, skips, rows_a, cols_b):
    half = rows_a // 2
    total_len = rows_a * cols_b
    length = half * cols_b
    cos_a, sin_a = dft_tables(rows_a)
    cos_b, sin_b = dft_tables(cols_b)
    index_a = jnp.arange(rows_a, dtype=jnp.int32)
    index_b = jnp.arange(cols_b, dtype=jnp.int32)
    twist = (index_a[:, None] * index_b[None, :] % total_len).astype(jnp.float32) * (
        2.0 * math.pi / total_len
    )
    twist_cos = jnp.cos(twist)
    twist_sin = jnp.sin(twist)
    times = jnp.arange(length, dtype=jnp.float32)

    def one_channel(items):
        channel, rate, weight, skip = items
        channel_f = channel.astype(jnp.float32)
        coefs = weight * jnp.sqrt(2.0 * rate)
        kernel = jnp.sum(coefs[:, None] * jnp.exp(-rate[:, None] * times[None, :]), axis=0)
        stacked = jnp.stack([channel_f, kernel]).reshape(2, half, cols_b)
        first_re = exact_mul(cos_a[:, :half], stacked)
        first_im = -exact_mul(sin_a[:, :half], stacked)
        turned_re = first_re * twist_cos + first_im * twist_sin
        turned_im = first_im * twist_cos - first_re * twist_sin
        spec_re = exact_mul(turned_re, cos_b) + exact_mul(turned_im, sin_b)
        spec_im = exact_mul(turned_im, cos_b) - exact_mul(turned_re, sin_b)
        prod_re = spec_re[0] * spec_re[1] - spec_im[0] * spec_im[1]
        prod_im = spec_re[0] * spec_im[1] + spec_im[0] * spec_re[1]
        back_re = exact_mul(prod_re, cos_b) - exact_mul(prod_im, sin_b)
        back_im = exact_mul(prod_im, cos_b) + exact_mul(prod_re, sin_b)
        unturned_re = back_re * twist_cos - back_im * twist_sin
        unturned_im = back_im * twist_cos + back_re * twist_sin
        result = (
            exact_mul(cos_a[:half], unturned_re) - exact_mul(sin_a[:half], unturned_im)
        ) / total_len
        return result.reshape(length) + skip * channel_f

    return lax.map(one_channel, (signal, rates, residues, skips))


def body(
    tokens,
    w_query,
    w_key,
    w_value,
    taps_query,
    taps_key,
    taps_value,
    decay_rate,
    residue,
    skip_gain,
    w_out,
):
    tok_count = tokens.shape[0]
    width_part = w_query.shape[1]

    def add_rows(piece):
        return jnp.dot(tokens, piece, preferred_element_type=jnp.float32)

    queries = add_rows(lax.all_gather(w_query, "ctx", axis=0, tiled=True))
    keys_proj = add_rows(lax.all_gather(w_key, "ctx", axis=0, tiled=True))
    values_proj = add_rows(lax.all_gather(w_value, "ctx", axis=0, tiled=True))
    queries = queries.astype(jnp.bfloat16)
    keys_proj = keys_proj.astype(jnp.bfloat16)
    values_proj = values_proj.astype(jnp.bfloat16)
    ctx_count = lax.axis_size("ctx")
    chan_count = width_part // ctx_count
    first = lax.axis_index("ctx") * chan_count
    rates = lax.dynamic_slice_in_dim(decay_rate, first, chan_count, 1).T
    residues = lax.dynamic_slice_in_dim(residue, first, chan_count, 1).T
    skips = lax.dynamic_slice_in_dim(skip_gain, first, chan_count, 0)
    query_chan, key_chan, value_chan = (
        lax.all_to_all(queries.T, "ctx", split_axis=0, concat_axis=1, tiled=True),
        lax.all_to_all(keys_proj.T, "ctx", split_axis=0, concat_axis=1, tiled=True),
        lax.all_to_all(values_proj.T, "ctx", split_axis=0, concat_axis=1, tiled=True),
    )

    def conv_channels(signal_in, taps):
        taps_part = lax.dynamic_slice_in_dim(taps, first, chan_count, 1)
        padded = jnp.pad(signal_in.astype(jnp.float32), ((0, 0), (2, 0)))
        return (
            taps_part[0][:, None] * padded[:, 2:]
            + taps_part[1][:, None] * padded[:, 1:-1]
            + taps_part[2][:, None] * padded[:, :-2]
        )

    gate_channels = conv_channels(query_chan, taps_query).astype(jnp.bfloat16)
    signal = (conv_channels(key_chan, taps_key) * conv_channels(value_chan, taps_value)).astype(
        jnp.bfloat16
    )
    mixed_long = long_conv(signal, rates, residues, skips, tok_count, 2 * ctx_count).astype(
        jnp.bfloat16
    )
    outgoing = (gate_channels.astype(jnp.float32) * mixed_long.astype(jnp.float32)).astype(
        jnp.bfloat16
    )
    gated = lax.all_to_all(outgoing, "ctx", split_axis=1, concat_axis=0, tiled=True).T
    features = lax.all_gather(gated, "tp", axis=1, tiled=True)
    result = jnp.dot(
        features,
        lax.all_gather(w_out, "ctx", axis=0, tiled=True),
        preferred_element_type=jnp.float32,
    )
    return result.astype(jnp.bfloat16)


def solution(mesh):
    in_specs = (
        P("ctx", None),
        P("ctx", "tp"),
        P("ctx", "tp"),
        P("ctx", "tp"),
        P(None, "tp"),
        P(None, "tp"),
        P(None, "tp"),
        P(None, "tp"),
        P(None, "tp"),
        P("tp"),
        P("ctx", "tp"),
    )
    out_specs = P("ctx", "tp")
    return jax.shard_map(body, mesh=mesh, in_specs=in_specs, out_specs=out_specs, check_vma=False)
```

profile of v0, /device:TPU:0, one launch (start us, length us, event | category | flops | bytes accessed | tf_op | source)
XLA Modules:
  0.0 559.2 jit_solution(9386341728542071466)
XLA Ops:
  6.5 0.7 all-gather.9.cloned.1.call-update
  7.3 0.7 all-gather.7.cloned.1.call-update
  8.1 0.7 all-gather.5.cloned.1.call-update
  9.6 0.8 constant_dynamic-slice_fusion.4
  10.4 0.8 constant_dynamic-slice_fusion.2
  11.4 0.8 dynamic_slice.38
  12.1 0.8 constant_dynamic-slice_fusion.6
  12.9 72.7 %all-gather.9.cloned.1.call-done = bf16[4096,512]{1,0:T(8,128)(2,1)} async-done(((bf16[512,512]{1,0:T(8,128)(2,1)}), bf16[4096,512]{1,0:T(8,128)(2,1)}) %all-gather.9.cloned.1.call-update) | async-done | bytes 4194320 | tf_op jit(solution)/shard_map/all_gather | solution.py:81
  85.6 4.1 convolution_convert_fusion.1
  89.8 3.4 all-to-all-start.2
  93.1 67.3 %all-gather.7.cloned.1.call-done = bf16[4096,512]{1,0:T(8,128)(2,1)} async-done(((bf16[512,512]{1,0:T(8,128)(2,1)}), bf16[4096,512]{1,0:T(8,128)(2,1)}) %all-gather.7.cloned.1.call-update) | async-done | bytes 4194320 | tf_op jit(solution)/shard_map/all_gather | solution.py:80
  160.5 4.1 convolution_convert_fusion.2
  164.6 69.7 %all-gather.5.cloned.1.call-done = bf16[4096,512]{1,0:T(8,128)(2,1)} async-done(((bf16[512,512]{1,0:T(8,128)(2,1)}), bf16[4096,512]{1,0:T(8,128)(2,1)}) %all-gather.5.cloned.1.call-update) | async-done | bytes 4194320 | tf_op jit(solution)/shard_map/all_gather | solution.py:79
  234.3 4.1 convolution_convert_fusion.3
  238.4 3.4 all-to-all-start.1
  241.8 9.0 %all-to-all-done.1 = bf16[8,64,128]{2,1,0:T(8,128)(2,1)S(1)} async-done(((bf16[8,64,128]{2,1,0:T(8,128)(2,1)}), bf16[8,64,128]{2,1,0:T(8,128)(2,1)S(1)}, u32[]{:S(2)}, u32[]{:S(2)}) %all-to-all-start.1) | async-done | bytes 131104 | tf_op jit(solution)/shard_map/all_to_all | solution.py:93
  250.9 4.1 all-to-all-start
  255.4 273.1 %while.12 = (s32[]{:T(128)}, bf16[64,1024]{1,0:T(8,128)(2,1)S(1)}, bf16[64,1024]{1,0:T(8,128)(2,1)S(1)}, f32[64,16]{1,0:T(8,128)S(1)}, f32[64,16]{1,0:T(8,128)S(...) while((s32[]{:T(128)}, bf16[64,1024]{1,0:T(8,128)(2,1)S(1)}, ...), condition=%wide.region_2.3_spmd.clone.clone, body=%wide.region_0.2_spmd.clone.clone.sunk | while | flops 14420018 | bytes 821765 | solution.py:57
  258.5 0.6 dynamic_slice.73
  262.7 0.6 dynamic_slice.73
  267.0 0.6 dynamic_slice.73
  275.5 0.6 dynamic_slice.73
  279.8 0.6 dynamic_slice.73
  284.1 0.6 dynamic_slice.73
  288.3 0.6 dynamic_slice.73
  292.6 0.6 dynamic_slice.73
  296.9 0.6 dynamic_slice.73
  309.7 0.6 dynamic_slice.73
  322.5 0.6 dynamic_slice.73
  335.3 0.6 dynamic_slice.73
  348.1 0.6 dynamic_slice.73
  360.9 0.6 dynamic_slice.73
  373.7 0.6 dynamic_slice.73
  386.5 0.6 dynamic_slice.73
  399.3 0.6 dynamic_slice.73
  412.1 0.6 dynamic_slice.73
  424.9 0.6 dynamic_slice.73
  437.7 0.6 dynamic_slice.73
  450.5 0.6 dynamic_slice.73
  463.3 0.6 dynamic_slice.73
  476.1 0.6 dynamic_slice.73
  488.9 0.6 dynamic_slice.73
  501.7 0.6 dynamic_slice.73
  514.5 0.6 dynamic_slice.73
  527.3 0.6 dynamic_slice.73
  528.8 13.1 %all_to_all.58 = bf16[64,8,128]{2,0,1:T(8,128)(2,1)S(1)} all-to-all(bf16[64,8,128]{2,0,1:T(8,128)(2,1)S(1)} %copy_bitcast_fusion.3), channel_id=1, replica_groups=mesh['ctx'=8,'tp'=4] {'ctx'}, dimensions={1} | all-to-all | bytes 262144 | tf_op jit(solution)/shard_map/all_to_all | solution.py:116
  541.9 7.1 %all_gather.18 = bf16[128,2048]{0,1:T(8,128)(2,1)S(1)} all-gather(bf16[128,512]{0,1:T(8,128)(2,1)S(1)} %bitcast.126), channel_id=1, replica_groups=mesh['ctx'=8,'tp'=4] {'tp'}, dimensions={1}, use_global_device_ids=true | all-gather | bytes 655360 | tf_op jit(solution)/shard_map/all_gather | solution.py:117
  549.1 3.6 convolution_convert_fusion
  (1659 shorter events, 251.4 us)
Async XLA Ops:
  6.5 79.1 %copy-start = (bf16[128,4096]{1,0:T(8,128)(2,1)S(1)}, bf16[128,4096]{1,0:T(8,128)(2,1)}, u32[]{:S(2)}) copy-start(bf16[128,4096]{1,0:T(8,128)(2,1)} %param.13) | copy-start | bytes 3145732
  6.5 79.1 %all-gather.9.cloned.1.call-start = ((), (), s32[]{:S(2)}) async-start(), calls=%async_computation.6 | async-start | bytes 4718592 | tf_op jit(solution)/shard_map/all_gather | solution.py:81
  7.3 153.2 %all-gather.7.cloned.1.call-start = ((), (), s32[]{:S(2)}) async-start(), calls=%async_computation.5 | async-start | bytes 4718592 | tf_op jit(solution)/shard_map/all_gather | solution.py:80
  8.0 226.3 %all-gather.5.cloned.1.call-start = ((), (), s32[]{:S(2)}) async-start(), calls=%async_computation.4 | async-start | bytes 4718592 | tf_op jit(solution)/shard_map/all_gather | solution.py:79
  8.7 540.3 %all-gather.11.cloned.1.call-start = ((), (), s32[]{:S(2)}) async-start(), calls=%async_computation.7 | async-start | bytes 4718592 | tf_op jit(solution)/shard_map/all_gather | solution.py:120
  89.8 148.7 %all-to-all-start.2 = ((bf16[8,64,128]{2,1,0:T(8,128)(2,1)}), bf16[8,64,128]{2,1,0:T(8,128)(2,1)S(1)}, u32[]{:S(2)}, u32[]{:S(2)}) async-start(bf16[8,64,128]{2,1,0:T(8,128)(2,1)} %bitcast.11), calls=%async_computation.2 | async-start | bytes 262144 | tf_op jit(solution)/shard_map/all_to_all | solution.py:94
  238.4 12.4 %all-to-all-start.1 = ((bf16[8,64,128]{2,1,0:T(8,128)(2,1)}), bf16[8,64,128]{2,1,0:T(8,128)(2,1)S(1)}, u32[]{:S(2)}, u32[]{:S(2)}) async-start(bf16[8,64,128]{2,1,0:T(8,128)(2,1)} %bitcast.6), calls=%async_computation.1 | async-start | bytes 262144 | tf_op jit(solution)/shard_map/all_to_all | solution.py:93
  250.9 277.6 %all-to-all-start = ((bf16[8,64,128]{2,1,0:T(8,128)(2,1)}), bf16[8,64,128]{2,1,0:T(8,128)(2,1)S(1)}, u32[]{:S(2)}, u32[]{:S(2)}) async-start(bf16[8,64,128]{2,1,0:T(8,128)(2,1)} %bitcast.1), calls=%async_computation | async-start | bytes 262144 | tf_op jit(solution)/shard_map/all_to_all | solution.py:92
Sparse Core Ops, SparseCore 0:
  9.5 76.0 all-gather.8
  87.7 72.6 all-gather.6
  162.6 71.6 all-gather.4
  236.3 75.7 all-gather.10
where the time goes:
time: 561 us; the launch traced here: 559 us
  waiting for transfers between devices  221 us (39%)
  matrix products  160 us (29%)
  local copies, waits for them, and re-layouts  74.8 us (13%)
  other arithmetic  51.3 us (9%)
  blocking collectives  20.3 us (4%)
  between operations  13.2 us (2%)
  starting transfers between devices  11 us (2%)
  loops' own time  7.56 us (1%)
    dot_general x768, matrix products, exact_mul(): return jnp.matmul(left, right, precision=lax.Precision.HIGHEST)  144 us
    all_gather x1, waiting for transfers between devices, body(): values_proj = add_rows(lax.all_gather(w_value, 'ctx', axis=0, tiled=True))  72.7 us
    all_gather x1, waiting for transfers between devices, body(): queries = add_rows(lax.all_gather(w_query, 'ctx', axis=0, tiled=True))  69.7 us
    all_gather x1, waiting for transfers between devices, body(): keys_proj = add_rows(lax.all_gather(w_key, 'ctx', axis=0, tiled=True))  67.3 us
    dynamic_slice x64, local copies, waits for them, and re-layouts, long_conv(): return lax.map(one_channel, (signal, rates, residues, skips))  37.7 us
    add x64, other arithmetic, one_channel(): return result.reshape(length) + skip * channel_f  36.7 us
    another operation x256, local copies, waits for them, and re-layouts, one_channel(): stacked = jnp.stack([channel_f, kernel]).reshape(2, half, cols_b)  17.5 us
    all_to_all x1, blocking collectives, body(): lax.all_to_all(outgoing, 'ctx', split_axis=1, concat_axis=0, tiled=True)  13.1 us
  transfers between devices with their start and end apart: 7, of which 4 were waited for; matrix products, arithmetic and copies ran while one was open for 50% of the time, Pallas kernels for 0%

commit v1 on v0

v1 whole, which is shorter than its diff:
```python
import jax
import jax.numpy as jnp
from jax import lax
from jax.sharding import PartitionSpec as P


def short_conv(padded, taps):
    return taps[0] * padded[2:] + taps[1] * padded[1:-1] + taps[2] * padded[:-2]


def modal_long_conv(signal, rates, residues, skips):
    length, width = signal.shape
    order = rates.shape[0]
    ctx_count = lax.axis_size("ctx")
    me = lax.axis_index("ctx")
    coefs = residues * jnp.sqrt(2.0 * rates)
    times = jnp.arange(length, dtype=jnp.float32)[:, None, None]
    grow = jnp.exp(rates[None] * times)
    decay = jnp.exp(-rates[None] * times)
    lifted = (grow * signal[:, None, :]).reshape(length, order * width)
    rows = jnp.arange(length, dtype=jnp.int32)
    lower = (rows[:, None] >= rows[None, :]).astype(jnp.float32)
    running = jnp.matmul(lower, lifted, precision=lax.Precision.HIGHEST).reshape(
        length, order, width
    )
    end_state = running[length - 1] * jnp.exp(-rates * (length - 1))
    states = lax.all_gather(end_state, "ctx", axis=0, tiled=False)
    chunk_ids = jnp.arange(ctx_count, dtype=jnp.int32)
    gap = jnp.maximum(me - 1 - chunk_ids, 0).astype(jnp.float32)
    carry_w = jnp.where(
        (chunk_ids < me)[:, None, None],
        jnp.exp(-rates[None] * (gap[:, None, None] * length)),
        0.0,
    )
    carried = jnp.sum(carry_w * states, axis=0) * jnp.exp(-rates)
    total = running + carried[None]
    mixed = jnp.sum((coefs[None] * decay) * total, axis=1)
    return mixed + skips * signal


def body(
    tokens,
    w_query,
    w_key,
    w_value,
    taps_query,
    taps_key,
    taps_value,
    decay_rate,
    residue,
    skip_gain,
    w_out,
):
    ctx_count = lax.axis_size("ctx")
    halo = lax.ppermute(
        tokens[-2:], "ctx", perm=[(i, i + 1) for i in range(ctx_count - 1)]
    )
    rows = jnp.concatenate([halo, tokens], axis=0)

    def project(piece):
        full = lax.all_gather(piece, "ctx", axis=0, tiled=True)
        out = jnp.dot(rows, full, preferred_element_type=jnp.float32)
        return out.astype(jnp.bfloat16).astype(jnp.float32)

    queries = project(w_query)
    keys_proj = project(w_key)
    values_proj = project(w_value)
    gate = short_conv(queries, taps_query).astype(jnp.bfloat16)
    product = (short_conv(keys_proj, taps_key) * short_conv(values_proj, taps_value)).astype(
        jnp.bfloat16
    )
    mixed = modal_long_conv(product.astype(jnp.float32), decay_rate, residue, skip_gain)
    mixed = mixed.astype(jnp.bfloat16)
    gated = (gate.astype(jnp.float32) * mixed.astype(jnp.float32)).astype(jnp.bfloat16)
    features = lax.all_gather(gated, "tp", axis=1, tiled=True)
    result = jnp.dot(
        features,
        lax.all_gather(w_out, "ctx", axis=0, tiled=True),
        preferred_element_type=jnp.float32,
    )
    return result.astype(jnp.bfloat16)


def solution(mesh):
    in_specs = (
        P("ctx", None),
        P("ctx", "tp"),
        P("ctx", "tp"),
        P("ctx", "tp"),
        P(None, "tp"),
        P(None, "tp"),
        P(None, "tp"),
        P(None, "tp"),
        P(None, "tp"),
        P("tp"),
        P("ctx", "tp"),
    )
    out_specs = P("ctx", "tp")
    return jax.shard_map(body, mesh=mesh, in_specs=in_specs, out_specs=out_specs, check_vma=False)
```

time: 561 us -> 320 us (0.57)
  matrix products: 160 us -> 15.8 us
  local copies, waits for them, and re-layouts: 74.8 us -> 13.7 us
  other arithmetic: 51.3 us -> 1.94 us
  blocking collectives: 20.3 us -> 39 us
  waiting for transfers between devices: 221 us -> 231 us
  loops' own time: 7.56 us -> 0 us
  starting transfers between devices: 11 us -> 4.99 us
    dot_general x771 -> x4, matrix products: 156 us -> 12.2 us  [the longest x3 9.3 us: project(): out = jnp.dot(rows, full, preferred_element_type=jnp.float32)]
    all_gather x1, waiting for transfers between devices: 0.01 us -> 62 us  [body(): lax.all_gather(w_out, 'ctx', axis=0, tiled=True)]
    all_gather x3, waiting for transfers between devices: 210 us -> 166 us  [project(): full = lax.all_gather(piece, 'ctx', axis=0, tiled=True)]
    dynamic_slice x68 -> x0, local copies, waits for them, and re-layouts: 40.8 us -> none  [the longest x64 37.7 us: long_conv(): return lax.map(one_channel, (signal, rates, residues, skips))]
    add x64 -> x0, other arithmetic: 36.7 us -> none  [one_channel(): return result.reshape(length) + skip * channel_f]
    all_gather x0 -> x1, blocking collectives: none -> 31.8 us  [modal_long_conv(): states = lax.all_gather(end_state, 'ctx', axis=0, tiled=False)]
    another operation x256 -> x0, local copies, waits for them, and re-layouts: 17.5 us -> none  [one_channel(): stacked = jnp.stack([channel_f, kernel]).reshape(2, half, cols_b)]
    all_to_all x1 -> x0, blocking collectives: 13.1 us -> none  [body(): lax.all_to_all(outgoing, 'ctx', split_axis=1, concat_axis=0, tiled=True)]
  transfers between devices with their start and end apart: 7 -> 5, of which waited for: 4 -> 4; matrix products, arithmetic and copies ran while one was open for 50% -> 9% of each run, Pallas kernels for 0% -> 0%
where the time goes in v1:
time: 320 us; the launch traced here: 319 us
  waiting for transfers between devices  231 us (72%)
  blocking collectives  39 us (12%)
  matrix products  15.8 us (5%)
  local copies, waits for them, and re-layouts  13.7 us (4%)
  between operations  13.3 us (4%)
  starting transfers between devices  4.99 us (2%)
    all_gather x3, waiting for transfers between devices, project(): full = lax.all_gather(piece, 'ctx', axis=0, tiled=True)  166 us
    all_gather x1, waiting for transfers between devices, body(): lax.all_gather(w_out, 'ctx', axis=0, tiled=True)  62 us
    all_gather x1, blocking collectives, modal_long_conv(): states = lax.all_gather(end_state, 'ctx', axis=0, tiled=False)  31.8 us
    unnamed x13, local copies, waits for them, and re-layouts  9.79 us
    dot_general x3, matrix products, project(): out = jnp.dot(rows, full, preferred_element_type=jnp.float32)  9.3 us
    all_gather x1, blocking collectives, body(): features = lax.all_gather(gated, 'tp', axis=1, tiled=True)  7.19 us
  transfers between devices with their start and end apart: 5, of which 4 were waited for; matrix products, arithmetic and copies ran while one was open for 9% of the time, Pallas kernels for 0%

profile of v1, /device:TPU:0, one launch (start us, length us, event | category | flops | bytes accessed | tf_op | source)
XLA Modules:
  0.0 319.4 jit_solution(1594210370774384721)
XLA Ops:
  6.5 0.0 copy-start.4
  6.5 0.0 all-gather.10.cloned.1.call-start
  6.5 0.7 all-gather.10.cloned.1.call-update
  7.3 0.0 all-gather.8.cloned.1.call-start
  7.3 0.7 all-gather.8.cloned.1.call-update
  8.0 0.0 all-gather.6.cloned.1.call-start
  8.1 0.7 all-gather.6.cloned.1.call-update
  8.7 0.0 all-gather.12.cloned.1.call-start
  8.8 0.5 all-gather.12.cloned.1.call-update
  9.3 0.9 slice.62
  10.2 4.9 %collective-permute-start = (bf16[2,4096]{1,0:T(2,128)(2,1)S(1)}, bf16[2,4096]{1,0:T(2,128)(2,1)S(1)}, u32[]{:S(2)}, u32[]{:S(2)}) collective-permute-start(bf16[2,4096]{1,0:T(2,128)(2,1)S(1)} %slice.62), channel_id=1, source_target_pairs={{0,4},{4,8},{8,12},{12,16},{16,20},{20,24},{24,28},{1,5},{5,9},{9,... | collective-permute-start | bytes 49160 | tf_op jit(solution)/shard_map/ppermute | solution.py:55
  15.1 0.8 fusion.26
  15.9 0.8 fusion.25
  16.7 0.8 fusion.24
  17.5 0.8 copy.12
  18.3 0.0 collective-permute-done
  18.3 67.3 %all-gather.10.cloned.1.call-done = bf16[4096,512]{1,0:T(8,128)(2,1)} async-done(((bf16[512,512]{1,0:T(8,128)(2,1)}), bf16[4096,512]{1,0:T(8,128)(2,1)}) %all-gather.10.cloned.1.call-update) | async-done | bytes 4194320 | tf_op jit(solution)/shard_map/all_gather | solution.py:61
  85.6 3.3 %fusion.8 = f32[130,512]{1,0:T(8,128)S(1)} fusion(bf16[4096,512]{1,0:T(8,128)(2,1)} %all-gather.10.cloned.1.call-done, bf16[128,4096]{1,0:T(8,128)(2,1)} %param.11, bf16[2,4096]{1,0:T(2,128)(2,1)S(1)} %collective-permute-done), kind=kOutput, calls=%fused_computation.11 | convolution fusion | flops 547522560 | bytes 5525504 | tf_op jit(solution)/shard_map/dot_general | solution.py:62
  88.9 70.5 %all-gather.8.cloned.1.call-done = bf16[4096,512]{1,0:T(8,128)(2,1)} async-done(((bf16[512,512]{1,0:T(8,128)(2,1)}), bf16[4096,512]{1,0:T(8,128)(2,1)}) %all-gather.8.cloned.1.call-update) | async-done | bytes 4194320 | tf_op jit(solution)/shard_map/all_gather | solution.py:61
  159.4 0.0 copy-done.4
  159.4 2.9 fusion.9
  162.4 0.2 fusion.20
  162.6 0.5 mul.240
  163.1 3.4 %copy.13 = f32[16,8,16,512]{3,1,2,0:T(8,128)S(1)} copy(f32[16,8,16,512]{3,2,1,0:T(8,128)S(1)} %bitcast.28) | data formatting | bytes 8388608
  166.5 2.9 fusion.2
  169.4 0.0 copy-start.1
  169.5 0.0 copy-start.2
  169.5 5.2 %copy.14 = f32[16,8,16,512]{3,2,1,0:T(8,128)} copy(f32[16,8,16,512]{3,1,2,0:T(8,128)S(1)} %bitcast.26) | data formatting | bytes 8388608
  174.7 0.1 slice_reduce_fusion
  174.8 0.0 copy-done.1
  174.8 0.0 copy-done.2
  174.9 31.8 %all-gather = f32[128,512]{1,0:T(8,128)S(1)} all-gather(f32[16,512]{1,0:T(8,128)S(1)} %get-tuple-element.6), channel_id=2, replica_groups=mesh['ctx'=8,'tp'=4] {'ctx'}, dimensions={0}, use_global_device_ids=true | all-gather | bytes 294912 | tf_op jit(solution)/shard_map/all_gather | solution.py:27
  206.7 0.1 multiply_reduce_fusion
  206.8 0.0 copy-start.3
  206.8 28.2 %all-gather.6.cloned.1.call-done = bf16[4096,512]{1,0:T(8,128)(2,1)} async-done(((bf16[512,512]{1,0:T(8,128)(2,1)}), bf16[4096,512]{1,0:T(8,128)(2,1)}) %all-gather.6.cloned.1.call-update) | async-done | bytes 4194320 | tf_op jit(solution)/shard_map/all_gather | solution.py:61
  235.0 0.0 copy-start
  235.0 3.1 fusion.10
  238.1 0.3 copy-done
  238.4 1.5 fusion.1
  239.9 0.0 copy-done.3
  239.9 0.1 multiply_convert_fusion
  240.1 7.2 %all_gather.26 = bf16[128,2048]{1,0:T(8,128)(2,1)S(1)} all-gather(bf16[128,512]{1,0:T(8,128)(2,1)S(1)} %multiply_convert_fusion), channel_id=1, replica_groups=mesh['ctx'=8,'tp'=4] {'tp'}, dimensions={1}, use_global_device_ids=true | all-gather | bytes 655360 | tf_op jit(solution)/shard_map/all_gather | solution.py:75
  247.2 62.0 %all-gather.12.cloned.1.call-done = bf16[2048,1024]{1,0:T(8,128)(2,1)} async-done(((bf16[256,1024]{1,0:T(8,128)(2,1)}), bf16[2048,1024]{1,0:T(8,128)(2,1)}) %all-gather.12.cloned.1.call-update) | async-done | bytes 4194320 | tf_op jit(solution)/shard_map/all_gather | solution.py:78
  309.2 3.6 %convolution_convert_fusion = bf16[128,1024]{1,0:T(8,128)(2,1)} fusion(bf16[128,2048]{1,0:T(8,128)(2,1)S(1)} %all_gather.26, bf16[2048,1024]{1,0:T(8,128)(2,1)} %all-gather.12.cloned.1.call-done), kind=kOutput, calls=%fused_computation.9 | convolution fusion | flops 537001984 | bytes 4980736 | tf_op jit(solution)/shard_map/dot_general | solution.py:76
  (5 shorter events, 0.1 us)
Async XLA Ops:
  6.5 152.9 %copy-start.4 = (bf16[128,4096]{1,0:T(8,128)(2,1)S(1)}, bf16[128,4096]{1,0:T(8,128)(2,1)}, u32[]{:S(2)}) copy-start(bf16[128,4096]{1,0:T(8,128)(2,1)} %param.11) | copy-start | bytes 3145732
  6.5 79.1 %all-gather.10.cloned.1.call-start = ((), (), s32[]{:S(2)}) async-start(), calls=%async_computation.2 | async-start | bytes 4718592 | tf_op jit(solution)/shard_map/all_gather | solution.py:61
  7.3 152.2 %all-gather.8.cloned.1.call-start = ((), (), s32[]{:S(2)}) async-start(), calls=%async_computation.1 | async-start | bytes 4718592 | tf_op jit(solution)/shard_map/all_gather | solution.py:61
  8.0 227.0 %all-gather.6.cloned.1.call-start = ((), (), s32[]{:S(2)}) async-start(), calls=%async_computation | async-start | bytes 4718592 | tf_op jit(solution)/shard_map/all_gather | solution.py:61
  8.7 300.5 %all-gather.12.cloned.1.call-start = ((), (), s32[]{:S(2)}) async-start(), calls=%async_computation.3 | async-start | bytes 4718592 | tf_op jit(solution)/shard_map/all_gather | solution.py:78
  10.2 8.1 %collective-permute-start = (bf16[2,4096]{1,0:T(2,128)(2,1)S(1)}, bf16[2,4096]{1,0:T(2,128)(2,1)S(1)}, u32[]{:S(2)}, u32[]{:S(2)}) collective-permute-start(bf16[2,4096]{1,0:T(2,128)(2,1)S(1)} %slice.62), channel_id=1, source_target_pairs={{0,4},{4,8},{8,12},{12,16},{16,20},{20,24},{24,28},{1,5},{5,9},{9,... | collective-permute-start | bytes 49160 | tf_op jit(solution)/shard_map/ppermute | solution.py:55
  169.4 5.4 %copy-start.1 = (f32[16,512]{1,0:T(8,128)S(1)}, f32[16,512]{1,0:T(8,128)}, u32[]{:S(2)}) copy-start(f32[16,512]{1,0:T(8,128)} %param.18) | copy-start | bytes 98308
  169.5 5.4 %copy-start.2 = (f32[16,512]{1,0:T(8,128)S(1)}, f32[16,512]{1,0:T(8,128)}, u32[]{:S(2)}) copy-start(f32[16,512]{1,0:T(8,128)} %param.19) | copy-start | bytes 98308
  206.8 33.1 %copy-start.3 = (f32[512]{0:T(512)S(1)}, f32[512]{0:T(512)}, u32[]{:S(2)}) copy-start(f32[512]{0:T(512)} %param.20) | copy-start | bytes 6148
  235.0 3.4 %copy-start = (f32[16,8,16,512]{3,2,1,0:T(8,128)S(1)}, f32[16,8,16,512]{3,2,1,0:T(8,128)}, u32[]{:S(2)}) copy-start(f32[16,8,16,512]{3,2,1,0:T(8,128)} %copy.14) | copy-start | bytes 12582916
Sparse Core Ops, SparseCore 0:
  9.5 76.0 all-gather.9
  87.7 71.6 all-gather.7
  161.6 73.3 all-gather.5
  237.0 72.2 all-gather.11

commit v2 on v1

--- a/solution.py
+++ b/solution.py
@@ -38,6 +38,35 @@
     return mixed + skips * signal
 
 
+def ring_order(count):
+    if count % 2:
+        return list(range(count))
+    return list(range(0, count, 2)) + list(range(count - 1, 0, -2))
+
+
+def ring_contract(pieces, consume, acc):
+    count = lax.axis_size("ctx")
+    ring = ring_order(count)
+    place = [0] * count
+    for pos, dev in enumerate(ring):
+        place[dev] = pos
+    fwd = [(ring[k], ring[(k + 1) % count]) for k in range(count)]
+    bwd = [(ring[(k + 1) % count], ring[k]) for k in range(count)]
+    me = lax.axis_index("ctx")
+    my_pos = jnp.array(place, jnp.int32)[me]
+    ring_arr = jnp.array(ring, jnp.int32)
+    ups = tuple(p[0] for p in pieces)
+    lows = tuple(p[1] for p in pieces)
+    acc = consume(acc, me, ups, lows, me)
+    for step in range(1, count):
+        ups = lax.ppermute(ups, "ctx", perm=fwd)
+        lows = lax.ppermute(lows, "ctx", perm=bwd)
+        src_up = ring_arr[(my_pos - step) % count]
+        src_low = ring_arr[(my_pos + step) % count]
+        acc = consume(acc, src_up, ups, lows, src_low)
+    return acc
+
+
 def body(
     tokens,
     w_query,
@@ -56,15 +85,27 @@
         tokens[-2:], "ctx", perm=[(i, i + 1) for i in range(ctx_count - 1)]
     )
     rows = jnp.concatenate([halo, tokens], axis=0)
+    d_chunk = w_query.shape[0]
+    d_half = d_chunk // 2
+    width = w_query.shape[1]
+    weights = (w_query, w_key, w_value)
+    pieces = [(w[:d_half], w[d_half:]) for w in weights]
 
-    def project(piece):
-        full = lax.all_gather(piece, "ctx", axis=0, tiled=True)
-        out = jnp.dot(rows, full, preferred_element_type=jnp.float32)
-        return out.astype(jnp.bfloat16).astype(jnp.float32)
+    def consume_proj(acc, src_up, ups, lows, src_low):
+        cols_up = lax.dynamic_slice_in_dim(rows, src_up * d_chunk, d_half, 1)
+        cols_low = lax.dynamic_slice_in_dim(rows, src_low * d_chunk + d_half, d_half, 1)
+        return tuple(
+            a
+            + jnp.dot(cols_up, u, preferred_element_type=jnp.float32)
+            + jnp.dot(cols_low, l, preferred_element_type=jnp.float32)
+            for a, u, l in zip(acc, ups, lows)
+        )
 
-    queries = project(w_query)
-    keys_proj = project(w_key)
-    values_proj = project(w_value)
+    zero = jnp.zeros((rows.shape[0], width), jnp.float32)
+    projected = ring_contract(pieces, consume_proj, (zero, zero, zero))
+    queries, keys_proj, values_proj = (
+        p.astype(jnp.bfloat16).astype(jnp.float32) for p in projected
+    )
     gate = short_conv(queries, taps_query).astype(jnp.bfloat16)
     product = (short_conv(keys_proj, taps_key) * short_conv(values_proj, taps_value)).astype(
         jnp.bfloat16
@@ -73,11 +114,20 @@
     mixed = mixed.astype(jnp.bfloat16)
     gated = (gate.astype(jnp.float32) * mixed.astype(jnp.float32)).astype(jnp.bfloat16)
     features = lax.all_gather(gated, "tp", axis=1, tiled=True)
-    result = jnp.dot(
-        features,
-        lax.all_gather(w_out, "ctx", axis=0, tiled=True),
-        preferred_element_type=jnp.float32,
-    )
+    c_chunk = w_out.shape[0]
+    c_half = c_chunk // 2
+
+    def consume_out(acc, src_up, ups, lows, src_low):
+        cols_up = lax.dynamic_slice_in_dim(features, src_up * c_chunk, c_half, 1)
+        cols_low = lax.dynamic_slice_in_dim(features, src_low * c_chunk + c_half, c_half, 1)
+        return (
+            acc[0]
+            + jnp.dot(cols_up, ups[0], preferred_element_type=jnp.float32)
+            + jnp.dot(cols_low, lows[0], preferred_element_type=jnp.float32),
+        )
+
+    out_zero = jnp.zeros((features.shape[0], w_out.shape[1]), jnp.float32)
+    (result,) = ring_contract([(w_out[:c_half], w_out[c_half:])], consume_out, (out_zero,))
     return result.astype(jnp.bfloat16)
 
 

time: 320 us -> 271 us (0.85)
  waiting for transfers between devices: 231 us -> 85.6 us
  starting transfers between devices: 4.99 us -> 63.9 us
  between operations: 13.3 us -> 28.7 us
  matrix products: 15.8 us -> 27.2 us
  local copies, waits for them, and re-layouts: 13.7 us -> 21.7 us
    all_gather x4 -> x0, waiting for transfers between devices: 228 us -> none  [the longest x3 166 us: project(): full = lax.all_gather(piece, 'ctx', axis=0, tiled=True)]
    ppermute x0 -> x56, waiting for transfers between devices: none -> 85.6 us  [the longest x28 70.2 us: ring_contract(): lows = lax.ppermute(lows, 'ctx', perm=bwd)]
    ppermute x0 -> x56, starting transfers between devices: none -> 58.9 us  [the longest x28 42.5 us: ring_contract(): ups = lax.ppermute(ups, 'ctx', perm=fwd)]
    dot_general x4 -> x64, matrix products: 12.9 us -> 24.3 us  [the longest x24 9.45 us: consume_proj(): jnp.dot(cols_low, l, preferred_element_type=jnp.float32)]
    slice x0 -> x4, local copies, waits for them, and re-layouts: none -> 4.35 us  [the longest x3 3.53 us: body(): pieces = [(w[:d_half], w[d_half:]) for w in weights]]
    unnamed x13 -> x67, local copies, waits for them, and re-layouts: 9.79 us -> 13.9 us
  transfers between devices with their start and end apart: 5 -> 57, of which waited for: 4 -> 27; matrix products, arithmetic and copies ran while one was open for 9% -> 17% of each run, Pallas kernels for 0% -> 0%
where the time goes in v2:
time: 271 us; the launch traced here: 270 us
  waiting for transfers between devices  85.6 us (32%)
  starting transfers between devices  63.9 us (24%)
  blocking collectives  38.3 us (14%)
  between operations  28.7 us (11%)
  matrix products  27.2 us (10%)
  local copies, waits for them, and re-layouts  21.7 us (8%)
  other arithmetic  4.54 us (2%)
    ppermute x28, waiting for transfers between devices, ring_contract(): lows = lax.ppermute(lows, 'ctx', perm=bwd)  70.2 us
    ppermute x28, starting transfers between devices, ring_contract(): ups = lax.ppermute(ups, 'ctx', perm=fwd)  42.5 us
    all_gather x1, blocking collectives, modal_long_conv(): states = lax.all_gather(end_state, 'ctx', axis=0, tiled=False)  31.1 us
    ppermute x28, starting transfers between devices, ring_contract(): lows = lax.ppermute(lows, 'ctx', perm=bwd)  16.4 us
    ppermute x28, waiting for transfers between devices, ring_contract(): ups = lax.ppermute(ups, 'ctx', perm=fwd)  15.4 us
    unnamed x67, local copies, waits for them, and re-layouts  13.9 us
    dot_general x24, matrix products, consume_proj(): jnp.dot(cols_low, l, preferred_element_type=jnp.float32)  9.45 us
    all_gather x1, blocking collectives, body(): features = lax.all_gather(gated, 'tp', axis=1, tiled=True)  7.17 us
  transfers between devices with their start and end apart: 57, of which 27 were waited for; matrix products, arithmetic and copies ran while one was open for 17% of the time, Pallas kernels for 0%

profile of v2, /device:TPU:0, one launch (start us, length us, event | category | flops | bytes accessed | tf_op | source)
XLA Modules:
  0.0 270.0 jit_solution(4586388439543945145)
XLA Ops:
  0.9 5.0 %collective-permute-start = (bf16[2,4096]{1,0:T(2,128)(2,1)S(1)}, bf16[2,4096]{1,0:T(2,128)(2,1)S(1)}, u32[]{:S(2)}, u32[]{:S(2)}) collective-permute-start(bf16[2,4096]{1,0:T(2,128)(2,1)S(1)} %slice.86), channel_id=1, source_target_pairs={{0,4},{4,8},{8,12},{12,16},{16,20},{20,24},{24,28},{1,5},{5,9},{9,... | collective-permute-start | bytes 49160 | tf_op jit(solution)/shard_map/ppermute | solution.py:84
  5.9 1.9 fusion.244
  7.8 1.6 collective-permute-start.1
  10.7 1.6 collective-permute-start.15
  45.4 1.6 collective-permute-start.29
  59.9 9.1 %collective-permute-done.4 = bf16[256,512]{1,0:T(8,128)(2,1)S(1)} collective-permute-done((bf16[256,512]{1,0:T(8,128)(2,1)}, bf16[256,512]{1,0:T(8,128)(2,1)S(1)}, u32[]{:S(2)}, u32[]{:S(2)}) %collective-permute-start.4) | collective-permute-done | bytes 262176 | tf_op jit(solution)/shard_map/ppermute | solution.py:63
  68.9 1.6 collective-permute-start.17
  71.5 1.6 collective-permute-start.31
  74.6 1.6 collective-permute-start.45
  78.2 2.0 collective-permute-done.32
  80.2 1.6 collective-permute-start.5
  83.6 7.8 %collective-permute-done.6 = bf16[256,512]{1,0:T(8,128)(2,1)S(1)} collective-permute-done((bf16[256,512]{1,0:T(8,128)(2,1)S(1)}, bf16[256,512]{1,0:T(8,128)(2,1)S(1)}, u32[]{:S(2)}, u32[]{:S(2)}) %collective-permute-start.6) | collective-permute-done | bytes 262176 | tf_op jit(solution)/shard_map/ppermute | solution.py:63
  91.4 1.6 collective-permute-start.19
  94.0 1.6 collective-permute-start.33
  97.0 1.6 collective-permute-start.47
  100.6 2.0 collective-permute-done.34
  102.6 1.6 collective-permute-start.7
  106.1 7.8 %collective-permute-done.8 = bf16[256,512]{1,0:T(8,128)(2,1)S(1)} collective-permute-done((bf16[256,512]{1,0:T(8,128)(2,1)S(1)}, bf16[256,512]{1,0:T(8,128)(2,1)S(1)}, u32[]{:S(2)}, u32[]{:S(2)}) %collective-permute-start.8) | collective-permute-done | bytes 262176 | tf_op jit(solution)/shard_map/ppermute | solution.py:63
  113.9 1.6 collective-permute-start.21
  116.5 1.6 collective-permute-start.35
  119.5 1.6 collective-permute-start.49
  123.1 2.0 collective-permute-done.36
  125.1 1.6 collective-permute-start.9
  128.6 7.8 %collective-permute-done.10 = bf16[256,512]{1,0:T(8,128)(2,1)S(1)} collective-permute-done((bf16[256,512]{1,0:T(8,128)(2,1)S(1)}, bf16[256,512]{1,0:T(8,128)(2,1)S(1)}, u32[]{:S(2)}, u32[]{:S(2)}) %collective-permute-start.10) | collective-permute-done | bytes 262176 | tf_op jit(solution)/shard_map/ppermute | solution.py:63
  136.3 1.6 collective-permute-start.23
  139.0 1.6 collective-permute-start.37
  142.0 1.6 collective-permute-start.51
  145.6 2.0 collective-permute-done.38
  147.6 1.6 collective-permute-start.11
  151.1 7.9 %collective-permute-done.12 = bf16[256,512]{1,0:T(8,128)(2,1)} collective-permute-done((bf16[256,512]{1,0:T(8,128)(2,1)S(1)}, bf16[256,512]{1,0:T(8,128)(2,1)}, u32[]{:S(2)}, u32[]{:S(2)}) %collective-permute-start.12) | collective-permute-done | bytes 262176 | tf_op jit(solution)/shard_map/ppermute | solution.py:63
  158.9 1.6 collective-permute-start.25
  162.5 1.6 collective-permute-start.39
  164.6 1.6 collective-permute-start.53
  168.0 3.0 %collective-permute-done.40 = bf16[256,512]{1,0:T(8,128)(2,1)S(1)} collective-permute-done((bf16[256,512]{1,0:T(8,128)(2,1)S(1)}, bf16[256,512]{1,0:T(8,128)(2,1)S(1)}, u32[]{:S(2)}, u32[]{:S(2)}) %collective-permute-start.40) | collective-permute-done | bytes 262176 | tf_op jit(solution)/shard_map/ppermute | solution.py:63
  172.6 14.3 %collective-permute-done.28 = bf16[256,512]{1,0:T(8,128)(2,1)S(1)} collective-permute-done((bf16[256,512]{1,0:T(8,128)(2,1)S(1)}, bf16[256,512]{1,0:T(8,128)(2,1)S(1)}, u32[]{:S(2)}, u32[]{:S(2)}) %collective-permute-start.28) | collective-permute-done | bytes 262176 | tf_op jit(solution)/shard_map/ppermute | solution.py:63
  186.8 1.6 collective-permute-start.27
  189.6 1.6 collective-permute-start.41
  191.5 1.6 collective-permute-start.13
  193.6 2.5 collective-permute-done.27
  196.1 1.6 collective-permute-start.55
  197.9 3.8 %collective-permute-done.41 = bf16[256,512]{1,0:T(8,128)(2,1)S(1)} collective-permute-done((bf16[256,512]{1,0:T(8,128)(2,1)S(1)}, bf16[256,512]{1,0:T(8,128)(2,1)S(1)}, u32[]{:S(2)}, u32[]{:S(2)}) %collective-permute-start.41) | collective-permute-done | bytes 262176 | tf_op jit(solution)/shard_map/ppermute | solution.py:62
  202.7 3.4 %copy.17 = f32[16,8,16,512]{3,1,2,0:T(8,128)S(1)} copy(f32[16,8,16,512]{3,2,1,0:T(8,128)S(1)} %bitcast.135) | data formatting | bytes 8388608
  206.1 2.9 %fusion.2 = f32[128,8192]{1,0:T(8,128)S(1)} fusion(f32[128,8192]{1,0:T(8,128)S(1)} %bitcast.134, f32[8192]{0:T(1024)S(1)} %bitcast.138), kind=kOutput, calls=%fused_computation.19 | convolution fusion | flops 1612726272 | bytes 8421376 | tf_op jit(solution)/shard_map/dot_general | solution.py:23
  209.0 2.0 copy-done.1
  212.0 31.1 %all-gather = f32[128,512]{1,0:T(8,128)S(1)} all-gather(f32[16,512]{1,0:T(8,128)S(1)} %get-tuple-element.14), channel_id=2, replica_groups=mesh['ctx'=8,'tp'=4] {'ctx'}, dimensions={0}, use_global_device_ids=true | all-gather | bytes 294912 | tf_op jit(solution)/shard_map/all_gather | solution.py:27
  243.9 5.4 %copy.18 = f32[16,8,16,512]{3,2,1,0:T(8,128)S(1)} copy(f32[16,8,16,512]{3,1,2,0:T(8,128)} %bitcast.133) | data formatting | bytes 8388608
  252.9 7.2 %all_gather.11 = bf16[128,2048]{1,0:T(8,128)(2,1)S(1)} all-gather(bf16[128,512]{1,0:T(8,128)(2,1)S(1)} %multiply_convert_fusion), channel_id=1, replica_groups=mesh['ctx'=8,'tp'=4] {'tp'}, dimensions={1}, use_global_device_ids=true | all-gather | bytes 655360 | tf_op jit(solution)/shard_map/all_gather | solution.py:116
  268.1 1.9 fusion.15
  (221 shorter events, 67.3 us)
Async XLA Ops:
  0.9 44.4 %collective-permute-start = (bf16[2,4096]{1,0:T(2,128)(2,1)S(1)}, bf16[2,4096]{1,0:T(2,128)(2,1)S(1)}, u32[]{:S(2)}, u32[]{:S(2)}) collective-permute-start(bf16[2,4096]{1,0:T(2,128)(2,1)S(1)} %slice.86), channel_id=1, source_target_pairs={{0,4},{4,8},{8,12},{12,16},{16,20},{20,24},{24,28},{1,5},{5,9},{9,... | collective-permute-start | bytes 49160 | tf_op jit(solution)/shard_map/ppermute | solution.py:84
  7.8 40.0 %collective-permute-start.1 = (bf16[256,512]{1,0:T(8,128)(2,1)}, bf16[256,512]{1,0:T(8,128)(2,1)S(1)}, u32[]{:S(2)}, u32[]{:S(2)}) collective-permute-start(bf16[256,512]{1,0:T(8,128)(2,1)} %get-tuple-element.7), channel_id=1, source_target_pairs={{0,8},{8,16},{16,24},{24,28},{28,20},{20,12},{12,4},{4,0},{1,9},{9... | collective-permute-start | bytes 786440 | tf_op jit(solution)/shard_map/ppermute | solution.py:62
  9.4 42.5 %collective-permute-start.2 = (bf16[256,512]{1,0:T(8,128)(2,1)}, bf16[256,512]{1,0:T(8,128)(2,1)}, u32[]{:S(2)}, u32[]{:S(2)}) collective-permute-start(bf16[256,512]{1,0:T(8,128)(2,1)} %get-tuple-element.8), channel_id=1, source_target_pairs={{8,0},{16,8},{24,16},{28,24},{20,28},{12,20},{4,12},{0,4},{9,1},{1... | collective-permute-start | bytes 786440 | tf_op jit(solution)/shard_map/ppermute | solution.py:63
  10.7 38.4 %collective-permute-start.15 = (bf16[256,512]{1,0:T(8,128)(2,1)}, bf16[256,512]{1,0:T(8,128)(2,1)}, u32[]{:S(2)}, u32[]{:S(2)}) collective-permute-start(bf16[256,512]{1,0:T(8,128)(2,1)} %get-tuple-element.9), channel_id=1, source_target_pairs={{0,8},{8,16},{16,24},{24,28},{28,20},{20,12},{12,4},{4,0},{1,9},{9... | collective-permute-start | bytes 786440 | tf_op jit(solution)/shard_map/ppermute | solution.py:62
  12.3 41.4 %collective-permute-start.16 = (bf16[256,512]{1,0:T(8,128)(2,1)}, bf16[256,512]{1,0:T(8,128)(2,1)}, u32[]{:S(2)}, u32[]{:S(2)}) collective-permute-start(bf16[256,512]{1,0:T(8,128)(2,1)} %get-tuple-element.10), channel_id=1, source_target_pairs={{8,0},{16,8},{24,16},{28,24},{20,28},{12,20},{4,12},{0,4},{9,1},{1... | collective-permute-start | bytes 786440 | tf_op jit(solution)/shard_map/ppermute | solution.py:63
  45.4 11.4 %collective-permute-start.29 = (bf16[256,512]{1,0:T(8,128)(2,1)}, bf16[256,512]{1,0:T(8,128)(2,1)S(1)}, u32[]{:S(2)}, u32[]{:S(2)}) collective-permute-start(bf16[256,512]{1,0:T(8,128)(2,1)} %get-tuple-element.11), channel_id=1, source_target_pairs={{0,8},{8,16},{16,24},{24,28},{28,20},{20,12},{12,4},{4,0},{1,9},{9... | collective-permute-start | bytes 786440 | tf_op jit(solution)/shard_map/ppermute | solution.py:62
  49.2 22.3 %collective-permute-start.44 = (bf16[128,1024]{1,0:T(8,128)(2,1)S(1)}, bf16[128,1024]{1,0:T(8,128)(2,1)S(1)}, u32[]{:S(2)}, u32[]{:S(2)}) collective-permute-start(bf16[128,1024]{1,0:T(8,128)(2,1)S(1)} %copy-done.8), channel_id=1, source_target_pairs={{8,0},{16,8},{24,16},{28,24},{20,28},{12,20},{4,12},{0,4},{9,1},{1... | collective-permute-start | bytes 786440 | tf_op jit(solution)/shard_map/ppermute | solution.py:63
  52.0 21.2 %collective-permute-start.43 = (bf16[128,1024]{1,0:T(8,128)(2,1)S(1)}, bf16[128,1024]{1,0:T(8,128)(2,1)S(1)}, u32[]{:S(2)}, u32[]{:S(2)}) collective-permute-start(bf16[128,1024]{1,0:T(8,128)(2,1)S(1)} %copy-done.7), channel_id=1, source_target_pairs={{0,8},{8,16},{16,24},{24,28},{28,20},{20,12},{12,4},{4,0},{1,9},{9... | collective-permute-start | bytes 786440 | tf_op jit(solution)/shard_map/ppermute | solution.py:62
  53.7 15.2 %collective-permute-start.4 = (bf16[256,512]{1,0:T(8,128)(2,1)}, bf16[256,512]{1,0:T(8,128)(2,1)S(1)}, u32[]{:S(2)}, u32[]{:S(2)}) collective-permute-start(bf16[256,512]{1,0:T(8,128)(2,1)} %collective-permute-done.2), channel_id=1, source_target_pairs={{8,0},{16,8},{24,16},{28,24},{20,28},{12,20},{4,12},{0,4},{9,1},{1... | collective-permute-start | bytes 786440 | tf_op jit(solution)/shard_map/ppermute | solution.py:63
  56.7 14.0 %collective-permute-start.3 = (bf16[256,512]{1,0:T(8,128)(2,1)S(1)}, bf16[256,512]{1,0:T(8,128)(2,1)S(1)}, u32[]{:S(2)}, u32[]{:S(2)}) collective-permute-start(bf16[256,512]{1,0:T(8,128)(2,1)S(1)} %collective-permute-done.1), channel_id=1, source_target_pairs={{0,8},{8,16},{16,24},{24,28},{28,20},{20,12},{12,4},{4,0},{1,9},{9... | collective-permute-start | bytes 786440 | tf_op jit(solution)/shard_map/ppermute | solution.py:62
  57.8 16.7 %collective-permute-start.18 = (bf16[256,512]{1,0:T(8,128)(2,1)}, bf16[256,512]{1,0:T(8,128)(2,1)S(1)}, u32[]{:S(2)}, u32[]{:S(2)}) collective-permute-start(bf16[256,512]{1,0:T(8,128)(2,1)} %collective-permute-done.16), channel_id=1, source_target_pairs={{8,0},{16,8},{24,16},{28,24},{20,28},{12,20},{4,12},{0,4},{9,1},{1... | collective-permute-start | bytes 786440 | tf_op jit(solution)/shard_map/ppermute | solution.py:63
  70.8 9.4 %collective-permute-start.32 = (bf16[256,512]{1,0:T(8,128)(2,1)S(1)}, bf16[256,512]{1,0:T(8,128)(2,1)S(1)}, u32[]{:S(2)}, u32[]{:S(2)}) collective-permute-start(bf16[256,512]{1,0:T(8,128)(2,1)S(1)} %collective-permute-done.30), channel_id=1, source_target_pairs={{8,0},{16,8},{24,16},{28,24},{20,28},{12,20},{4,12},{0,4},{9,1},{1... | collective-permute-start | bytes 786440 | tf_op jit(solution)/shard_map/ppermute | solution.py:63
  71.5 11.4 %collective-permute-start.31 = (bf16[256,512]{1,0:T(8,128)(2,1)S(1)}, bf16[256,512]{1,0:T(8,128)(2,1)S(1)}, u32[]{:S(2)}, u32[]{:S(2)}) collective-permute-start(bf16[256,512]{1,0:T(8,128)(2,1)S(1)} %collective-permute-done.29), channel_id=1, source_target_pairs={{0,8},{8,16},{16,24},{24,28},{28,20},{20,12},{12,4},{4,0},{1,9},{9... | collective-permute-start | bytes 786440 | tf_op jit(solution)/shard_map/ppermute | solution.py:62
  73.2 20.8 %collective-permute-start.46 = (bf16[128,1024]{1,0:T(8,128)(2,1)S(1)}, bf16[128,1024]{1,0:T(8,128)(2,1)S(1)}, u32[]{:S(2)}, u32[]{:S(2)}) collective-permute-start(bf16[128,1024]{1,0:T(8,128)(2,1)S(1)} %collective-permute-done.44), channel_id=1, source_target_pairs={{8,0},{16,8},{24,16},{28,24},{20,28},{12,20},{4,12},{0,4},{9,1},{1... | collective-permute-start | bytes 786440 | tf_op jit(solution)/shard_map/ppermute | solution.py:63
  74.6 21.1 %collective-permute-start.45 = (bf16[128,1024]{1,0:T(8,128)(2,1)S(1)}, bf16[128,1024]{1,0:T(8,128)(2,1)S(1)}, u32[]{:S(2)}, u32[]{:S(2)}) collective-permute-start(bf16[128,1024]{1,0:T(8,128)(2,1)S(1)} %collective-permute-done.43), channel_id=1, source_target_pairs={{0,8},{8,16},{16,24},{24,28},{28,20},{20,12},{12,4},{4,0},{1,9},{9... | collective-permute-start | bytes 786440 | tf_op jit(solution)/shard_map/ppermute | solution.py:62
  77.5 13.9 %collective-permute-start.6 = (bf16[256,512]{1,0:T(8,128)(2,1)S(1)}, bf16[256,512]{1,0:T(8,128)(2,1)S(1)}, u32[]{:S(2)}, u32[]{:S(2)}) collective-permute-start(bf16[256,512]{1,0:T(8,128)(2,1)S(1)} %collective-permute-done.4), channel_id=1, source_target_pairs={{8,0},{16,8},{24,16},{28,24},{20,28},{12,20},{4,12},{0,4},{9,1},{1... | collective-permute-start | bytes 786440 | tf_op jit(solution)/shard_map/ppermute | solution.py:63
  80.2 13.1 %collective-permute-start.5 = (bf16[256,512]{1,0:T(8,128)(2,1)S(1)}, bf16[256,512]{1,0:T(8,128)(2,1)S(1)}, u32[]{:S(2)}, u32[]{:S(2)}) collective-permute-start(bf16[256,512]{1,0:T(8,128)(2,1)S(1)} %collective-permute-done.3), channel_id=1, source_target_pairs={{0,8},{8,16},{16,24},{24,28},{28,20},{20,12},{12,4},{4,0},{1,9},{9... | collective-permute-start | bytes 786440 | tf_op jit(solution)/shard_map/ppermute | solution.py:62
  82.9 14.1 %collective-permute-start.20 = (bf16[256,512]{1,0:T(8,128)(2,1)S(1)}, bf16[256,512]{1,0:T(8,128)(2,1)S(1)}, u32[]{:S(2)}, u32[]{:S(2)}) collective-permute-start(bf16[256,512]{1,0:T(8,128)(2,1)S(1)} %collective-permute-done.18), channel_id=1, source_target_pairs={{8,0},{16,8},{24,16},{28,24},{20,28},{12,20},{4,12},{0,4},{9,1},{1... | collective-permute-start | bytes 786440 | tf_op jit(solution)/shard_map/ppermute | solution.py:63
  93.2 9.4 %collective-permute-start.34 = (bf16[256,512]{1,0:T(8,128)(2,1)S(1)}, bf16[256,512]{1,0:T(8,128)(2,1)S(1)}, u32[]{:S(2)}, u32[]{:S(2)}) collective-permute-start(bf16[256,512]{1,0:T(8,128)(2,1)S(1)} %collective-permute-done.32), channel_id=1, source_target_pairs={{8,0},{16,8},{24,16},{28,24},{20,28},{12,20},{4,12},{0,4},{9,1},{1... | collective-permute-start | bytes 786440 | tf_op jit(solution)/shard_map/ppermute | solution.py:63
  94.0 11.4 %collective-permute-start.33 = (bf16[256,512]{1,0:T(8,128)(2,1)S(1)}, bf16[256,512]{1,0:T(8,128)(2,1)S(1)}, u32[]{:S(2)}, u32[]{:S(2)}) collective-permute-start(bf16[256,512]{1,0:T(8,128)(2,1)S(1)} %collective-permute-done.31), channel_id=1, source_target_pairs={{0,8},{8,16},{16,24},{24,28},{28,20},{20,12},{12,4},{4,0},{1,9},{9... | collective-permute-start | bytes 786440 | tf_op jit(solution)/shard_map/ppermute | solution.py:62
  95.6 20.8 %collective-permute-start.48 = (bf16[128,1024]{1,0:T(8,128)(2,1)S(1)}, bf16[128,1024]{1,0:T(8,128)(2,1)S(1)}, u32[]{:S(2)}, u32[]{:S(2)}) collective-permute-start(bf16[128,1024]{1,0:T(8,128)(2,1)S(1)} %collective-permute-done.46), channel_id=1, source_target_pairs={{8,0},{16,8},{24,16},{28,24},{20,28},{12,20},{4,12},{0,4},{9,1},{1... | collective-permute-start | bytes 786440 | tf_op jit(solution)/shard_map/ppermute | solution.py:63
  97.0 21.1 %collective-permute-start.47 = (bf16[128,1024]{1,0:T(8,128)(2,1)S(1)}, bf16[128,1024]{1,0:T(8,128)(2,1)S(1)}, u32[]{:S(2)}, u32[]{:S(2)}) collective-permute-start(bf16[128,1024]{1,0:T(8,128)(2,1)S(1)} %collective-permute-done.45), channel_id=1, source_target_pairs={{0,8},{8,16},{16,24},{24,28},{28,20},{20,12},{12,4},{4,0},{1,9},{9... | collective-permute-start | bytes 786440 | tf_op jit(solution)/shard_map/ppermute | solution.py:62
  99.9 13.9 %collective-permute-start.8 = (bf16[256,512]{1,0:T(8,128)(2,1)S(1)}, bf16[256,512]{1,0:T(8,128)(2,1)S(1)}, u32[]{:S(2)}, u32[]{:S(2)}) collective-permute-start(bf16[256,512]{1,0:T(8,128)(2,1)S(1)} %collective-permute-done.6), channel_id=1, source_target_pairs={{8,0},{16,8},{24,16},{28,24},{20,28},{12,20},{4,12},{0,4},{9,1},{1... | collective-permute-start | bytes 786440 | tf_op jit(solution)/shard_map/ppermute | solution.py:63
  102.6 13.1 %collective-permute-start.7 = (bf16[256,512]{1,0:T(8,128)(2,1)S(1)}, bf16[256,512]{1,0:T(8,128)(2,1)S(1)}, u32[]{:S(2)}, u32[]{:S(2)}) collective-permute-start(bf16[256,512]{1,0:T(8,128)(2,1)S(1)} %collective-permute-done.5), channel_id=1, source_target_pairs={{0,8},{8,16},{16,24},{24,28},{28,20},{20,12},{12,4},{4,0},{1,9},{9... | collective-permute-start | bytes 786440 | tf_op jit(solution)/shard_map/ppermute | solution.py:62
  105.4 14.1 %collective-permute-start.22 = (bf16[256,512]{1,0:T(8,128)(2,1)S(1)}, bf16[256,512]{1,0:T(8,128)(2,1)S(1)}, u32[]{:S(2)}, u32[]{:S(2)}) collective-permute-start(bf16[256,512]{1,0:T(8,128)(2,1)S(1)} %collective-permute-done.20), channel_id=1, source_target_pairs={{8,0},{16,8},{24,16},{28,24},{20,28},{12,20},{4,12},{0,4},{9,1},{1... | collective-permute-start | bytes 786440 | tf_op jit(solution)/shard_map/ppermute | solution.py:63
  115.7 9.4 %collective-permute-start.36 = (bf16[256,512]{1,0:T(8,128)(2,1)S(1)}, bf16[256,512]{1,0:T(8,128)(2,1)S(1)}, u32[]{:S(2)}, u32[]{:S(2)}) collective-permute-start(bf16[256,512]{1,0:T(8,128)(2,1)S(1)} %collective-permute-done.34), channel_id=1, source_target_pairs={{8,0},{16,8},{24,16},{28,24},{20,28},{12,20},{4,12},{0,4},{9,1},{1... | collective-permute-start | bytes 786440 | tf_op jit(solution)/shard_map/ppermute | solution.py:63
  116.5 11.4 %collective-permute-start.35 = (bf16[256,512]{1,0:T(8,128)(2,1)S(1)}, bf16[256,512]{1,0:T(8,128)(2,1)S(1)}, u32[]{:S(2)}, u32[]{:S(2)}) collective-permute-start(bf16[256,512]{1,0:T(8,128)(2,1)S(1)} %collective-permute-done.33), channel_id=1, source_target_pairs={{0,8},{8,16},{16,24},{24,28},{28,20},{20,12},{12,4},{4,0},{1,9},{9... | collective-permute-start | bytes 786440 | tf_op jit(solution)/shard_map/ppermute | solution.py:62
  118.1 20.8 %collective-permute-start.50 = (bf16[128,1024]{1,0:T(8,128)(2,1)S(1)}, bf16[128,1024]{1,0:T(8,128)(2,1)S(1)}, u32[]{:S(2)}, u32[]{:S(2)}) collective-permute-start(bf16[128,1024]{1,0:T(8,128)(2,1)S(1)} %collective-permute-done.48), channel_id=1, source_target_pairs={{8,0},{16,8},{24,16},{28,24},{20,28},{12,20},{4,12},{0,4},{9,1},{1... | collective-permute-start | bytes 786440 | tf_op jit(solution)/shard_map/ppermute | solution.py:63
  119.5 21.1 %collective-permute-start.49 = (bf16[128,1024]{1,0:T(8,128)(2,1)S(1)}, bf16[128,1024]{1,0:T(8,128)(2,1)S(1)}, u32[]{:S(2)}, u32[]{:S(2)}) collective-permute-start(bf16[128,1024]{1,0:T(8,128)(2,1)S(1)} %collective-permute-done.47), channel_id=1, source_target_pairs={{0,8},{8,16},{16,24},{24,28},{28,20},{20,12},{12,4},{4,0},{1,9},{9... | collective-permute-start | bytes 786440 | tf_op jit(solution)/shard_map/ppermute | solution.py:62
  122.4 13.9 %collective-permute-start.10 = (bf16[256,512]{1,0:T(8,128)(2,1)S(1)}, bf16[256,512]{1,0:T(8,128)(2,1)S(1)}, u32[]{:S(2)}, u32[]{:S(2)}) collective-permute-start(bf16[256,512]{1,0:T(8,128)(2,1)S(1)} %collective-permute-done.8), channel_id=1, source_target_pairs={{8,0},{16,8},{24,16},{28,24},{20,28},{12,20},{4,12},{0,4},{9,1},{1... | collective-permute-start | bytes 786440 | tf_op jit(solution)/shard_map/ppermute | solution.py:63
  125.1 13.1 %collective-permute-start.9 = (bf16[256,512]{1,0:T(8,128)(2,1)S(1)}, bf16[256,512]{1,0:T(8,128)(2,1)S(1)}, u32[]{:S(2)}, u32[]{:S(2)}) collective-permute-start(bf16[256,512]{1,0:T(8,128)(2,1)S(1)} %collective-permute-done.7), channel_id=1, source_target_pairs={{0,8},{8,16},{16,24},{24,28},{28,20},{20,12},{12,4},{4,0},{1,9},{9... | collective-permute-start | bytes 786440 | tf_op jit(solution)/shard_map/ppermute | solution.py:62
  127.9 14.1 %collective-permute-start.24 = (bf16[256,512]{1,0:T(8,128)(2,1)S(1)}, bf16[256,512]{1,0:T(8,128)(2,1)S(1)}, u32[]{:S(2)}, u32[]{:S(2)}) collective-permute-start(bf16[256,512]{1,0:T(8,128)(2,1)S(1)} %collective-permute-done.22), channel_id=1, source_target_pairs={{8,0},{16,8},{24,16},{28,24},{20,28},{12,20},{4,12},{0,4},{9,1},{1... | collective-permute-start | bytes 786440 | tf_op jit(solution)/shard_map/ppermute | solution.py:63
  138.2 9.4 %collective-permute-start.38 = (bf16[256,512]{1,0:T(8,128)(2,1)S(1)}, bf16[256,512]{1,0:T(8,128)(2,1)S(1)}, u32[]{:S(2)}, u32[]{:S(2)}) collective-permute-start(bf16[256,512]{1,0:T(8,128)(2,1)S(1)} %collective-permute-done.36), channel_id=1, source_target_pairs={{8,0},{16,8},{24,16},{28,24},{20,28},{12,20},{4,12},{0,4},{9,1},{1... | collective-permute-start | bytes 786440 | tf_op jit(solution)/shard_map/ppermute | solution.py:63
  139.0 11.4 %collective-permute-start.37 = (bf16[256,512]{1,0:T(8,128)(2,1)S(1)}, bf16[256,512]{1,0:T(8,128)(2,1)S(1)}, u32[]{:S(2)}, u32[]{:S(2)}) collective-permute-start(bf16[256,512]{1,0:T(8,128)(2,1)S(1)} %collective-permute-done.35), channel_id=1, source_target_pairs={{0,8},{8,16},{16,24},{24,28},{28,20},{20,12},{12,4},{4,0},{1,9},{9... | collective-permute-start | bytes 786440 | tf_op jit(solution)/shard_map/ppermute | solution.py:62
  140.6 21.9 %collective-permute-start.52 = (bf16[128,1024]{1,0:T(8,128)(2,1)S(1)}, bf16[128,1024]{1,0:T(8,128)(2,1)S(1)}, u32[]{:S(2)}, u32[]{:S(2)}) collective-permute-start(bf16[128,1024]{1,0:T(8,128)(2,1)S(1)} %collective-permute-done.50), channel_id=1, source_target_pairs={{8,0},{16,8},{24,16},{28,24},{20,28},{12,20},{4,12},{0,4},{9,1},{1... | collective-permute-start | bytes 786440 | tf_op jit(solution)/shard_map/ppermute | solution.py:63
  142.0 22.1 %collective-permute-start.51 = (bf16[128,1024]{1,0:T(8,128)(2,1)S(1)}, bf16[128,1024]{1,0:T(8,128)(2,1)S(1)}, u32[]{:S(2)}, u32[]{:S(2)}) collective-permute-start(bf16[128,1024]{1,0:T(8,128)(2,1)S(1)} %collective-permute-done.49), channel_id=1, source_target_pairs={{0,8},{8,16},{16,24},{24,28},{28,20},{20,12},{12,4},{4,0},{1,9},{9... | collective-permute-start | bytes 786440 | tf_op jit(solution)/shard_map/ppermute | solution.py:62
  144.9 14.0 %collective-permute-start.12 = (bf16[256,512]{1,0:T(8,128)(2,1)S(1)}, bf16[256,512]{1,0:T(8,128)(2,1)}, u32[]{:S(2)}, u32[]{:S(2)}) collective-permute-start(bf16[256,512]{1,0:T(8,128)(2,1)S(1)} %collective-permute-done.10), channel_id=1, source_target_pairs={{8,0},{16,8},{24,16},{28,24},{20,28},{12,20},{4,12},{0,4},{9,1},{1... | collective-permute-start | bytes 786440 | tf_op jit(solution)/shard_map/ppermute | solution.py:63
  147.6 14.1 %collective-permute-start.11 = (bf16[256,512]{1,0:T(8,128)(2,1)S(1)}, bf16[256,512]{1,0:T(8,128)(2,1)S(1)}, u32[]{:S(2)}, u32[]{:S(2)}) collective-permute-start(bf16[256,512]{1,0:T(8,128)(2,1)S(1)} %collective-permute-done.9), channel_id=1, source_target_pairs={{0,8},{8,16},{16,24},{24,28},{28,20},{20,12},{12,4},{4,0},{1,9},{9... | collective-permute-start | bytes 786440 | tf_op jit(solution)/shard_map/ppermute | solution.py:62
  150.4 14.2 %collective-permute-start.26 = (bf16[256,512]{1,0:T(8,128)(2,1)S(1)}, bf16[256,512]{1,0:T(8,128)(2,1)S(1)}, u32[]{:S(2)}, u32[]{:S(2)}) collective-permute-start(bf16[256,512]{1,0:T(8,128)(2,1)S(1)} %collective-permute-done.24), channel_id=1, source_target_pairs={{8,0},{16,8},{24,16},{28,24},{20,28},{12,20},{4,12},{0,4},{9,1},{1... | collective-permute-start | bytes 786440 | tf_op jit(solution)/shard_map/ppermute | solution.py:63
  164.1 27.4 %collective-permute-start.54 = (bf16[128,1024]{1,0:T(8,128)(2,1)S(1)}, bf16[128,1024]{1,0:T(8,128)(2,1)}, u32[]{:S(2)}, u32[]{:S(2)}) collective-permute-start(bf16[128,1024]{1,0:T(8,128)(2,1)S(1)} %collective-permute-done.52), channel_id=1, source_target_pairs={{8,0},{16,8},{24,16},{28,24},{20,28},{12,20},{4,12},{0,4},{9,1},{1... | collective-permute-start | bytes 786440 | tf_op jit(solution)/shard_map/ppermute | solution.py:63
  164.6 28.5 %collective-permute-start.53 = (bf16[128,1024]{1,0:T(8,128)(2,1)S(1)}, bf16[128,1024]{1,0:T(8,128)(2,1)}, u32[]{:S(2)}, u32[]{:S(2)}) collective-permute-start(bf16[128,1024]{1,0:T(8,128)(2,1)S(1)} %collective-permute-done.51), channel_id=1, source_target_pairs={{0,8},{8,16},{16,24},{24,28},{28,20},{20,12},{12,4},{4,0},{1,9},{9... | collective-permute-start | bytes 786440 | tf_op jit(solution)/shard_map/ppermute | solution.py:62
  167.2 83.6 %collective-permute-start.14 = (bf16[256,512]{1,0:T(8,128)(2,1)}, bf16[256,512]{1,0:T(8,128)(2,1)}, u32[]{:S(2)}, u32[]{:S(2)}) collective-permute-start(bf16[256,512]{1,0:T(8,128)(2,1)} %collective-permute-done.12), channel_id=1, source_target_pairs={{8,0},{16,8},{24,16},{28,24},{20,28},{12,20},{4,12},{0,4},{9,1},{1... | collective-permute-start | bytes 786440 | tf_op jit(solution)/shard_map/ppermute | solution.py:63
  171.0 15.8 %collective-permute-start.28 = (bf16[256,512]{1,0:T(8,128)(2,1)S(1)}, bf16[256,512]{1,0:T(8,128)(2,1)S(1)}, u32[]{:S(2)}, u32[]{:S(2)}) collective-permute-start(bf16[256,512]{1,0:T(8,128)(2,1)S(1)} %collective-permute-done.26), channel_id=1, source_target_pairs={{8,0},{16,8},{24,16},{28,24},{20,28},{12,20},{4,12},{0,4},{9,1},{1... | collective-permute-start | bytes 786440 | tf_op jit(solution)/shard_map/ppermute | solution.py:63
  171.7 17.9 %collective-permute-start.42 = (bf16[256,512]{1,0:T(8,128)(2,1)S(1)}, bf16[256,512]{1,0:T(8,128)(2,1)S(1)}, u32[]{:S(2)}, u32[]{:S(2)}) collective-permute-start(bf16[256,512]{1,0:T(8,128)(2,1)S(1)} %collective-permute-done.40), channel_id=1, source_target_pairs={{8,0},{16,8},{24,16},{28,24},{20,28},{12,20},{4,12},{0,4},{9,1},{1... | collective-permute-start | bytes 786440 | tf_op jit(solution)/shard_map/ppermute | solution.py:63
  189.6 12.1 %collective-permute-start.41 = (bf16[256,512]{1,0:T(8,128)(2,1)S(1)}, bf16[256,512]{1,0:T(8,128)(2,1)S(1)}, u32[]{:S(2)}, u32[]{:S(2)}) collective-permute-start(bf16[256,512]{1,0:T(8,128)(2,1)S(1)} %collective-permute-done.39), channel_id=1, source_target_pairs={{0,8},{8,16},{16,24},{24,28},{28,20},{20,12},{12,4},{4,0},{1,9},{9... | collective-permute-start | bytes 786440 | tf_op jit(solution)/shard_map/ppermute | solution.py:62
  191.5 60.6 %collective-permute-start.13 = (bf16[256,512]{1,0:T(8,128)(2,1)S(1)}, bf16[256,512]{1,0:T(8,128)(2,1)S(1)}, u32[]{:S(2)}, u32[]{:S(2)}) collective-permute-start(bf16[256,512]{1,0:T(8,128)(2,1)S(1)} %collective-permute-done.11), channel_id=1, source_target_pairs={{0,8},{8,16},{16,24},{24,28},{28,20},{20,12},{12,4},{4,0},{1,9},{9... | collective-permute-start | bytes 786440 | tf_op jit(solution)/shard_map/ppermute | solution.py:62
  193.1 70.0 %collective-permute-start.56 = (bf16[128,1024]{1,0:T(8,128)(2,1)}, bf16[128,1024]{1,0:T(8,128)(2,1)}, u32[]{:S(2)}, u32[]{:S(2)}) collective-permute-start(bf16[128,1024]{1,0:T(8,128)(2,1)} %collective-permute-done.54), channel_id=1, source_target_pairs={{8,0},{16,8},{24,16},{28,24},{20,28},{12,20},{4,12},{0,4},{9,1},{1... | collective-permute-start | bytes 786440 | tf_op jit(solution)/shard_map/ppermute | solution.py:63
  196.1 72.0 %collective-permute-start.55 = (bf16[128,1024]{1,0:T(8,128)(2,1)}, bf16[128,1024]{1,0:T(8,128)(2,1)}, u32[]{:S(2)}, u32[]{:S(2)}) collective-permute-start(bf16[128,1024]{1,0:T(8,128)(2,1)} %collective-permute-done.53), channel_id=1, source_target_pairs={{0,8},{8,16},{16,24},{24,28},{28,20},{20,12},{12,4},{4,0},{1,9},{9... | collective-permute-start | bytes 786440 | tf_op jit(solution)/shard_map/ppermute | solution.py:62
  (41 other events, 355.8 us)

commit v3 on v2

--- a/solution.py
+++ b/solution.py
@@ -24,7 +24,7 @@
         length, order, width
     )
     end_state = running[length - 1] * jnp.exp(-rates * (length - 1))
-    states = lax.all_gather(end_state, "ctx", axis=0, tiled=False)
+    states = lax.all_gather(end_state[None], "ctx", axis=0, tiled=True)
     chunk_ids = jnp.arange(ctx_count, dtype=jnp.int32)
     gap = jnp.maximum(me - 1 - chunk_ids, 0).astype(jnp.float32)
     carry_w = jnp.where(
@@ -67,6 +67,26 @@
     return acc
 
 
+def ring_reduce_scatter(piece, count):
+    ring = ring_order(count)
+    place = [0] * count
+    for pos, dev in enumerate(ring):
+        place[dev] = pos
+    fwd = [(ring[k], ring[(k + 1) % count]) for k in range(count)]
+    bwd = [(ring[(k + 1) % count], ring[k]) for k in range(count)]
+    me = lax.axis_index("ctx")
+    my_pos = jnp.array(place, jnp.int32)[me]
+    ring_arr = jnp.array(ring, jnp.int32)
+    up = piece(ring_arr[(my_pos - 1) % count], 0)
+    down = piece(ring_arr[(my_pos + 1) % count], 1)
+    for step in range(1, count):
+        up = lax.ppermute(up.astype(jnp.bfloat16), "ctx", perm=fwd).astype(jnp.float32)
+        down = lax.ppermute(down.astype(jnp.bfloat16), "ctx", perm=bwd).astype(jnp.float32)
+        up = up + piece(ring_arr[(my_pos - step - 1) % count], 0)
+        down = down + piece(ring_arr[(my_pos + step + 1) % count], 1)
+    return up, down
+
+
 def body(
     tokens,
     w_query,
@@ -81,31 +101,23 @@
     w_out,
 ):
     ctx_count = lax.axis_size("ctx")
-    halo = lax.ppermute(
-        tokens[-2:], "ctx", perm=[(i, i + 1) for i in range(ctx_count - 1)]
-    )
-    rows = jnp.concatenate([halo, tokens], axis=0)
-    d_chunk = w_query.shape[0]
-    d_half = d_chunk // 2
+    length = tokens.shape[0]
     width = w_query.shape[1]
-    weights = (w_query, w_key, w_value)
-    pieces = [(w[:d_half], w[d_half:]) for w in weights]
+    columns = lax.all_to_all(tokens, "ctx", split_axis=1, concat_axis=0, tiled=True)
+    columns = jnp.concatenate([jnp.zeros((2, columns.shape[1]), columns.dtype), columns], axis=0)
+    w_cat = jnp.concatenate([w_query, w_key, w_value], axis=1)
+    split = w_cat.shape[1] // 2
+    halves = (w_cat[:, :split], w_cat[:, split:])
 
-    def consume_proj(acc, src_up, ups, lows, src_low):
-        cols_up = lax.dynamic_slice_in_dim(rows, src_up * d_chunk, d_half, 1)
-        cols_low = lax.dynamic_slice_in_dim(rows, src_low * d_chunk + d_half, d_half, 1)
-        return tuple(
-            a
-            + jnp.dot(cols_up, u, preferred_element_type=jnp.float32)
-            + jnp.dot(cols_low, l, preferred_element_type=jnp.float32)
-            for a, u, l in zip(acc, ups, lows)
-        )
+    def piece(dest, side):
+        rows = lax.dynamic_slice_in_dim(columns, dest * length, length + 2, 0)
+        return jnp.dot(rows, halves[side], preferred_element_type=jnp.float32)
 
-    zero = jnp.zeros((rows.shape[0], width), jnp.float32)
-    projected = ring_contract(pieces, consume_proj, (zero, zero, zero))
-    queries, keys_proj, values_proj = (
-        p.astype(jnp.bfloat16).astype(jnp.float32) for p in projected
-    )
+    up, down = ring_reduce_scatter(piece, ctx_count)
+    projected = jnp.concatenate([up, down], axis=1).astype(jnp.bfloat16).astype(jnp.float32)
+    queries = projected[:, :width]
+    keys_proj = projected[:, width : 2 * width]
+    values_proj = projected[:, 2 * width :]
     gate = short_conv(queries, taps_query).astype(jnp.bfloat16)
     product = (short_conv(keys_proj, taps_key) * short_conv(values_proj, taps_value)).astype(
         jnp.bfloat16

time: 271 us -> 219 us (0.81)
  starting transfers between devices: 63.9 us -> 43.2 us
  waiting for transfers between devices: 85.6 us -> 65.8 us
  matrix products: 27.2 us -> 19.2 us
  local copies, waits for them, and re-layouts: 21.7 us -> 18.8 us
    ppermute x28 -> x7, waiting for transfers between devices: 70.2 us -> 32.5 us  [ring_contract(): lows = lax.ppermute(lows, 'ctx', perm=bwd)]
    ppermute x28 -> x7, starting transfers between devices: 42.5 us -> 11.6 us  [ring_contract(): ups = lax.ppermute(ups, 'ctx', perm=fwd)]
    ppermute x1 -> x14, waiting for transfers between devices: 0.01 us -> 30.6 us  [the longest x7 19 us: ring_reduce_scatter(): lax.ppermute(up.astype(jnp.bfloat16), 'ctx', perm=fwd).astype(jnp.float32)]
    ppermute x28 -> x7, waiting for transfers between devices: 15.4 us -> 2.76 us  [ring_contract(): ups = lax.ppermute(ups, 'ctx', perm=fwd)]
    dot_general x48 -> x16, matrix products: 16.3 us -> 4.49 us  [piece(): return jnp.dot(rows, halves[side], preferred_element_type=jnp.float32)]
    ppermute x1 -> x14, starting transfers between devices: 5 us -> 14.6 us  [the longest x7 7.91 us: ring_reduce_scatter(): lax.ppermute(down.astype(jnp.bfloat16), 'ctx', perm=bwd).astype(jnp.float32)]
    all_to_all x0 -> x1, starting transfers between devices: none -> 6.22 us  [body(): lax.all_to_all(tokens, 'ctx', split_axis=1, concat_axis=0, tiled=True)]
    ppermute x28 -> x7, starting transfers between devices: 16.4 us -> 10.8 us  [ring_contract(): lows = lax.ppermute(lows, 'ctx', perm=bwd)]
  transfers between devices with their start and end apart: 57 -> 29, of which waited for: 27 -> 21; matrix products, arithmetic and copies ran while one was open for 17% -> 16% of each run, Pallas kernels for 0% -> 0%
where the time goes in v3:
time: 219 us; the launch traced here: 218 us
  waiting for transfers between devices  65.8 us (30%)
  starting transfers between devices  43.2 us (20%)
  blocking collectives  38.3 us (17%)
  between operations  28.8 us (13%)
  matrix products  19.2 us (9%)
  local copies, waits for them, and re-layouts  18.8 us (9%)
  other arithmetic  3.97 us (2%)
    ppermute x7, waiting for transfers between devices, ring_contract(): lows = lax.ppermute(lows, 'ctx', perm=bwd)  32.5 us
    all_gather x1, blocking collectives, modal_long_conv(): states = lax.all_gather(end_state[None], 'ctx', axis=0, tiled=True)  31.1 us
    ppermute x7, waiting for transfers between devices, ring_reduce_scatter(): lax.ppermute(up.astype(jnp.bfloat16), 'ctx', perm=fwd).astype(jnp.float32)  19 us
    unnamed x40, local copies, waits for them, and re-layouts  14.2 us
    ppermute x7, starting transfers between devices, ring_contract(): ups = lax.ppermute(ups, 'ctx', perm=fwd)  11.6 us
    ppermute x7, waiting for transfers between devices, ring_reduce_scatter(): lax.ppermute(down.astype(jnp.bfloat16), 'ctx', perm=bwd).astype(jnp.float32)  11.6 us
    ppermute x7, starting transfers between devices, ring_contract(): lows = lax.ppermute(lows, 'ctx', perm=bwd)  10.8 us
    ppermute x7, starting transfers between devices, ring_reduce_scatter(): lax.ppermute(down.astype(jnp.bfloat16), 'ctx', perm=bwd).astype(jnp.float32)  7.91 us
  transfers between devices with their start and end apart: 29, of which 21 were waited for; matrix products, arithmetic and copies ran while one was open for 16% of the time, Pallas kernels for 0%

profile of v3, /device:TPU:0, one launch (start us, length us, event | category | flops | bytes accessed | tf_op | source)
XLA Modules:
  0.0 218.0 jit_solution(12852706001336911492)
XLA Ops:
  0.0 1.1 fusion.134
  1.2 3.0 %collective-permute-start.15 = (bf16[128,1024]{1,0:T(8,128)(2,1)S(1)}, bf16[128,1024]{1,0:T(8,128)(2,1)S(1)}, u32[]{:S(2)}, u32[]{:S(2)}) collective-permute-start(bf16[128,1024]{1,0:T(8,128)(2,1)S(1)} %get-tuple-element.6), channel_id=1, source_target_pairs={{8,0},{16,8},{24,16},{28,24},{20,28},{12,20},{4,12},{0,4},{9,1},{1... | collective-permute-start | bytes 786440 | tf_op jit(solution)/shard_map/ppermute | solution.py:63
  4.3 2.3 %copy.16 = bf16[128,4096]{0,1:T(8,128)(2,1)} copy(bf16[128,4096]{1,0:T(8,128)(2,1)} %param.15) | data formatting | bytes 2097152 | tf_op args[0]
  6.6 6.2 %all-to-all-start = ((bf16[128,8,512]{0,2,1:T(8,128)(2,1)}), bf16[128,8,512]{0,2,1:T(8,128)(2,1)S(1)}, u32[]{:S(2)}, u32[]{:S(2)}) async-start(bf16[128,8,512]{0,2,1:T(8,128)(2,1)} %bitcast.1), calls=%async_computation | async-start | bytes 2097152 | tf_op jit(solution)/shard_map/all_to_all | solution.py:106
  12.9 2.1 collective-permute-start.17
  15.0 18.2 %collective-permute-done.17 = bf16[128,1024]{1,0:T(8,128)(2,1)S(1)} collective-permute-done((bf16[128,1024]{1,0:T(8,128)(2,1)S(1)}, bf16[128,1024]{1,0:T(8,128)(2,1)S(1)}, u32[]{:S(2)}, u32[]{:S(2)}) %collective-permute-start.17) | collective-permute-done | bytes 262176 | tf_op jit(solution)/shard_map/ppermute | solution.py:63
  33.2 3.5 %collective-permute-start.19 = (bf16[128,1024]{1,0:T(8,128)(2,1)S(1)}, bf16[128,1024]{1,0:T(8,128)(2,1)}, u32[]{:S(2)}, u32[]{:S(2)}) collective-permute-start(bf16[128,1024]{1,0:T(8,128)(2,1)S(1)} %collective-permute-done.17), channel_id=1, source_target_pairs={{8,0},{16,8},{24,16},{28,24},{20,28},{12,20},{4,12},{0,4},{9,1},{1... | collective-permute-start | bytes 786440 | tf_op jit(solution)/shard_map/ppermute | solution.py:63
  36.7 7.8 %collective-permute-start.18 = (bf16[128,1024]{1,0:T(8,128)(2,1)S(1)}, bf16[128,1024]{1,0:T(8,128)(2,1)}, u32[]{:S(2)}, u32[]{:S(2)}) collective-permute-start(bf16[128,1024]{1,0:T(8,128)(2,1)S(1)} %collective-permute-done.16), channel_id=1, source_target_pairs={{0,8},{8,16},{16,24},{24,28},{28,20},{20,12},{12,4},{4,0},{1,9},{9... | collective-permute-start | bytes 786440 | tf_op jit(solution)/shard_map/ppermute | solution.py:62
  44.5 4.8 %collective-permute-done.19 = bf16[128,1024]{1,0:T(8,128)(2,1)} collective-permute-done((bf16[128,1024]{1,0:T(8,128)(2,1)S(1)}, bf16[128,1024]{1,0:T(8,128)(2,1)}, u32[]{:S(2)}, u32[]{:S(2)}) %collective-permute-start.19) | collective-permute-done | bytes 262176 | tf_op jit(solution)/shard_map/ppermute | solution.py:63
  50.1 1.4 collective-permute-start.20
  51.5 1.3 pad_maximum_fusion.1
  52.8 3.4 %collective-permute-done.21 = bf16[128,1024]{1,0:T(8,128)(2,1)} collective-permute-done((bf16[128,1024]{1,0:T(8,128)(2,1)}, bf16[128,1024]{1,0:T(8,128)(2,1)}, u32[]{:S(2)}, u32[]{:S(2)}) %collective-permute-start.21) | collective-permute-done | bytes 262176 | tf_op jit(solution)/shard_map/ppermute | solution.py:63
  57.3 1.3 collective-permute-done.20
  58.6 6.0 %collective-permute-done.23 = bf16[128,1024]{1,0:T(8,128)(2,1)} collective-permute-done((bf16[128,1024]{1,0:T(8,128)(2,1)}, bf16[128,1024]{1,0:T(8,128)(2,1)}, u32[]{:S(2)}, u32[]{:S(2)}) %collective-permute-start.23) | collective-permute-done | bytes 262176 | tf_op jit(solution)/shard_map/ppermute | solution.py:63
  97.2 1.1 collective-permute-start.26
  99.3 1.5 copy.17
  103.8 1.4 collective-permute-start.7
  107.9 1.1 collective-permute-start.1
  109.0 1.4 collective-permute-done.7
  110.7 2.5 %collective-permute-start.8 = (bf16[130,768]{1,0:T(8,128)(2,1)S(1)}, bf16[130,768]{1,0:T(8,128)(2,1)S(1)}, u32[]{:S(2)}, u32[]{:S(2)}) collective-permute-start(bf16[130,768]{1,0:T(8,128)(2,1)S(1)} %add_convert_fusion.6), channel_id=1, source_target_pairs={{8,0},{16,8},{24,16},{28,24},{20,28},{12,20},{4,12},{0,4},{9,1},{1... | collective-permute-start | bytes 599048 | tf_op jit(solution)/shard_map/ppermute | solution.py:84
  113.2 1.8 collective-permute-done.1
  116.0 2.5 %collective-permute-done.8 = bf16[130,768]{1,0:T(8,128)(2,1)S(1)} collective-permute-done((bf16[130,768]{1,0:T(8,128)(2,1)S(1)}, bf16[130,768]{1,0:T(8,128)(2,1)S(1)}, u32[]{:S(2)}, u32[]{:S(2)}) %collective-permute-start.8) | collective-permute-done | bytes 199712 | tf_op jit(solution)/shard_map/ppermute | solution.py:84
  118.5 2.1 collective-permute-start.9
  120.6 2.5 %collective-permute-done.2 = bf16[130,768]{1,0:T(8,128)(2,1)S(1)} collective-permute-done((bf16[130,768]{1,0:T(8,128)(2,1)S(1)}, bf16[130,768]{1,0:T(8,128)(2,1)S(1)}, u32[]{:S(2)}, u32[]{:S(2)}) %collective-permute-start.2) | collective-permute-done | bytes 199712 | tf_op jit(solution)/shard_map/ppermute | solution.py:83
  123.8 2.3 %collective-permute-done.9 = bf16[130,768]{1,0:T(8,128)(2,1)S(1)} collective-permute-done((bf16[130,768]{1,0:T(8,128)(2,1)S(1)}, bf16[130,768]{1,0:T(8,128)(2,1)S(1)}, u32[]{:S(2)}, u32[]{:S(2)}) %collective-permute-start.9) | collective-permute-done | bytes 199712 | tf_op jit(solution)/shard_map/ppermute | solution.py:84
  127.3 3.2 %collective-permute-done.3 = bf16[130,768]{1,0:T(8,128)(2,1)S(1)} collective-permute-done((bf16[130,768]{1,0:T(8,128)(2,1)S(1)}, bf16[130,768]{1,0:T(8,128)(2,1)S(1)}, u32[]{:S(2)}, u32[]{:S(2)}) %collective-permute-start.3) | collective-permute-done | bytes 199712 | tf_op jit(solution)/shard_map/ppermute | solution.py:83
  131.4 1.5 collective-permute-done.10
  133.3 3.7 %collective-permute-done.4 = bf16[130,768]{1,0:T(8,128)(2,1)S(1)} collective-permute-done((bf16[130,768]{1,0:T(8,128)(2,1)S(1)}, bf16[130,768]{1,0:T(8,128)(2,1)S(1)}, u32[]{:S(2)}, u32[]{:S(2)}) %collective-permute-start.4) | collective-permute-done | bytes 199712 | tf_op jit(solution)/shard_map/ppermute | solution.py:83
  137.0 1.2 collective-permute-start.5
  139.2 3.7 %collective-permute-done.5 = bf16[130,768]{1,0:T(8,128)(2,1)S(1)} collective-permute-done((bf16[130,768]{1,0:T(8,128)(2,1)S(1)}, bf16[130,768]{1,0:T(8,128)(2,1)S(1)}, u32[]{:S(2)}, u32[]{:S(2)}) %collective-permute-start.5) | collective-permute-done | bytes 199712 | tf_op jit(solution)/shard_map/ppermute | solution.py:83
  142.9 1.2 collective-permute-start.6
  145.3 3.5 %collective-permute-done.6 = bf16[130,768]{1,0:T(8,128)(2,1)S(1)} collective-permute-done((bf16[130,768]{1,0:T(8,128)(2,1)S(1)}, bf16[130,768]{1,0:T(8,128)(2,1)S(1)}, u32[]{:S(2)}, u32[]{:S(2)}) %collective-permute-start.6) | collective-permute-done | bytes 199712 | tf_op jit(solution)/shard_map/ppermute | solution.py:83
  148.8 2.2 %collective-permute-done.13 = bf16[130,768]{1,0:T(8,128)(2,1)S(1)} collective-permute-done((bf16[130,768]{1,0:T(8,128)(2,1)S(1)}, bf16[130,768]{1,0:T(8,128)(2,1)S(1)}, u32[]{:S(2)}, u32[]{:S(2)}) %collective-permute-start.13) | collective-permute-done | bytes 199712 | tf_op jit(solution)/shard_map/ppermute | solution.py:84
  151.9 3.4 %copy.19 = f32[16,8,16,512]{3,1,2,0:T(8,128)S(1)} copy(f32[16,8,16,512]{3,2,1,0:T(8,128)S(1)} %bitcast.125) | data formatting | bytes 8388608
  155.3 2.9 %fusion.2 = f32[128,8192]{1,0:T(8,128)S(1)} fusion(f32[128,8192]{1,0:T(8,128)S(1)} %bitcast.124, f32[8192]{0:T(1024)S(1)} %bitcast.129), kind=kOutput, calls=%fused_computation.3 | convolution fusion | flops 1612726272 | bytes 8421376 | tf_op jit(solution)/shard_map/dot_general | solution.py:23
  158.2 1.9 copy-done
  160.3 31.1 %all-gather = f32[128,512]{1,0:T(8,128)S(1)} all-gather(f32[16,512]{1,0:T(8,128)S(1)} %get-tuple-element.10), channel_id=2, replica_groups=mesh['ctx'=8,'tp'=4] {'ctx'}, dimensions={0}, use_global_device_ids=true | all-gather | bytes 294912 | tf_op jit(solution)/shard_map/all_gather | solution.py:27
  191.6 5.4 %copy.20 = f32[16,8,16,512]{3,2,1,0:T(8,128)S(1)} copy(f32[16,8,16,512]{3,1,2,0:T(8,128)} %bitcast.123) | data formatting | bytes 8388608
  197.1 1.5 fusion.1
  198.9 7.2 %all_gather.7 = bf16[128,2048]{1,0:T(8,128)(2,1)S(1)} all-gather(bf16[128,512]{1,0:T(8,128)(2,1)S(1)} %multiply_convert_fusion), channel_id=1, replica_groups=mesh['ctx'=8,'tp'=4] {'tp'}, dimensions={1}, use_global_device_ids=true | all-gather | bytes 655360 | tf_op jit(solution)/shard_map/all_gather | solution.py:128
  206.7 1.2 fusion.72
  207.9 1.2 fusion.69
  209.1 1.2 fusion.66
  210.3 1.2 fusion.63
  211.7 1.2 fusion.60
  213.3 1.2 fusion.10
  214.5 1.2 fusion.11
  216.2 1.9 fusion.15
  (117 shorter events, 22.7 us)
Async XLA Ops:
  0.0 66.6 %copy-start.17 = (s32[8]{0:T(128)S(1)}, s32[8]{0:T(128)}, u32[]{:S(2)}) copy-start(s32[8]{0:T(128)} %constant.305.clone) | copy-start | bytes 100
  0.0 51.5 %copy-start.3 = (bf16[512,512]{1,0:T(8,128)(2,1)S(1)}, bf16[512,512]{1,0:T(8,128)(2,1)}, u32[]{:S(2)}) copy-start(bf16[512,512]{1,0:T(8,128)(2,1)} %param.17) | copy-start | bytes 1572868
  0.0 52.8 %copy-start.13 = (f32[3,512]{1,0:T(4,128)S(1)}, f32[3,512]{1,0:T(4,128)}, u32[]{:S(2)}) copy-start(f32[3,512]{1,0:T(4,128)} %param.20) | copy-start | bytes 18436
  0.0 58.6 %copy-start.14 = (f32[3,512]{1,0:T(4,128)S(1)}, f32[3,512]{1,0:T(4,128)}, u32[]{:S(2)}) copy-start(f32[3,512]{1,0:T(4,128)} %param.21) | copy-start | bytes 18436
  1.1 75.5 %copy-start.11 = (s32[8]{0:T(128)S(1)}, s32[8]{0:T(128)}, u32[]{:S(2)}) copy-start(s32[8]{0:T(128)} %constant.306.clone) | copy-start | bytes 100
  1.1 94.8 %copy-start.4 = (f32[16,512]{1,0:T(8,128)S(1)}, f32[16,512]{1,0:T(8,128)}, u32[]{:S(2)}) copy-start(f32[16,512]{1,0:T(8,128)} %param.22) | copy-start | bytes 98308
  1.2 95.0 %copy-start.15 = (f32[3,512]{1,0:T(4,128)S(1)}, f32[3,512]{1,0:T(4,128)}, u32[]{:S(2)}) copy-start(f32[3,512]{1,0:T(4,128)} %param.19) | copy-start | bytes 18436
  1.2 11.7 %collective-permute-start.15 = (bf16[128,1024]{1,0:T(8,128)(2,1)S(1)}, bf16[128,1024]{1,0:T(8,128)(2,1)S(1)}, u32[]{:S(2)}, u32[]{:S(2)}) collective-permute-start(bf16[128,1024]{1,0:T(8,128)(2,1)S(1)} %get-tuple-element.6), channel_id=1, source_target_pairs={{8,0},{16,8},{24,16},{28,24},{20,28},{12,20},{4,12},{0,4},{9,1},{1... | collective-permute-start | bytes 786440 | tf_op jit(solution)/shard_map/ppermute | solution.py:63
  4.2 10.7 %collective-permute-start.14 = (bf16[128,1024]{1,0:T(8,128)(2,1)S(1)}, bf16[128,1024]{1,0:T(8,128)(2,1)S(1)}, u32[]{:S(2)}, u32[]{:S(2)}) collective-permute-start(bf16[128,1024]{1,0:T(8,128)(2,1)S(1)} %get-tuple-element.5), channel_id=1, source_target_pairs={{0,8},{8,16},{16,24},{24,28},{28,20},{20,12},{12,4},{4,0},{1,9},{9... | collective-permute-start | bytes 786440 | tf_op jit(solution)/shard_map/ppermute | solution.py:62
  6.6 91.7 %all-to-all-start = ((bf16[128,8,512]{0,2,1:T(8,128)(2,1)}), bf16[128,8,512]{0,2,1:T(8,128)(2,1)S(1)}, u32[]{:S(2)}, u32[]{:S(2)}) async-start(bf16[128,8,512]{0,2,1:T(8,128)(2,1)} %bitcast.1), calls=%async_computation | async-start | bytes 2097152 | tf_op jit(solution)/shard_map/all_to_all | solution.py:106
  12.8 37.2 %copy-start.7 = (bf16[128,1024]{1,0:T(8,128)(2,1)}, bf16[128,1024]{1,0:T(8,128)(2,1)S(1)}, u32[]{:S(2)}) copy-start(bf16[128,1024]{1,0:T(8,128)(2,1)S(1)} %collective-permute-done.15) | copy-start | bytes 786436
  12.9 20.4 %collective-permute-start.17 = (bf16[128,1024]{1,0:T(8,128)(2,1)S(1)}, bf16[128,1024]{1,0:T(8,128)(2,1)S(1)}, u32[]{:S(2)}, u32[]{:S(2)}) collective-permute-start(bf16[128,1024]{1,0:T(8,128)(2,1)S(1)} %collective-permute-done.15), channel_id=1, source_target_pairs={{8,0},{16,8},{24,16},{28,24},{20,28},{12,20},{4,12},{0,4},{9,1},{1... | collective-permute-start | bytes 786440 | tf_op jit(solution)/shard_map/ppermute | solution.py:63
  14.9 21.8 %collective-permute-start.16 = (bf16[128,1024]{1,0:T(8,128)(2,1)S(1)}, bf16[128,1024]{1,0:T(8,128)(2,1)S(1)}, u32[]{:S(2)}, u32[]{:S(2)}) collective-permute-start(bf16[128,1024]{1,0:T(8,128)(2,1)S(1)} %collective-permute-done.14), channel_id=1, source_target_pairs={{0,8},{8,16},{16,24},{24,28},{28,20},{20,12},{12,4},{4,0},{1,9},{9... | collective-permute-start | bytes 786440 | tf_op jit(solution)/shard_map/ppermute | solution.py:62
  33.2 16.8 %copy-start.9 = (bf16[128,1024]{1,0:T(8,128)(2,1)}, bf16[128,1024]{1,0:T(8,128)(2,1)S(1)}, u32[]{:S(2)}) copy-start(bf16[128,1024]{1,0:T(8,128)(2,1)S(1)} %collective-permute-done.17) | copy-start | bytes 786436
  33.2 16.1 %collective-permute-start.19 = (bf16[128,1024]{1,0:T(8,128)(2,1)S(1)}, bf16[128,1024]{1,0:T(8,128)(2,1)}, u32[]{:S(2)}, u32[]{:S(2)}) collective-permute-start(bf16[128,1024]{1,0:T(8,128)(2,1)S(1)} %collective-permute-done.17), channel_id=1, source_target_pairs={{8,0},{16,8},{24,16},{28,24},{20,28},{12,20},{4,12},{0,4},{9,1},{1... | collective-permute-start | bytes 786440 | tf_op jit(solution)/shard_map/ppermute | solution.py:63
  36.7 13.3 %copy-start.5 = (bf16[128,1024]{1,0:T(8,128)(2,1)}, bf16[128,1024]{1,0:T(8,128)(2,1)S(1)}, u32[]{:S(2)}) copy-start(bf16[128,1024]{1,0:T(8,128)(2,1)S(1)} %collective-permute-done.16) | copy-start | bytes 786436
  36.7 13.3 %collective-permute-start.18 = (bf16[128,1024]{1,0:T(8,128)(2,1)S(1)}, bf16[128,1024]{1,0:T(8,128)(2,1)}, u32[]{:S(2)}, u32[]{:S(2)}) collective-permute-start(bf16[128,1024]{1,0:T(8,128)(2,1)S(1)} %collective-permute-done.16), channel_id=1, source_target_pairs={{0,8},{8,16},{16,24},{24,28},{28,20},{20,12},{12,4},{4,0},{1,9},{9... | collective-permute-start | bytes 786440 | tf_op jit(solution)/shard_map/ppermute | solution.py:62
  49.4 6.8 %collective-permute-start.21 = (bf16[128,1024]{1,0:T(8,128)(2,1)}, bf16[128,1024]{1,0:T(8,128)(2,1)}, u32[]{:S(2)}, u32[]{:S(2)}) collective-permute-start(bf16[128,1024]{1,0:T(8,128)(2,1)} %collective-permute-done.19), channel_id=1, source_target_pairs={{8,0},{16,8},{24,16},{28,24},{20,28},{12,20},{4,12},{0,4},{9,1},{1... | collective-permute-start | bytes 786440 | tf_op jit(solution)/shard_map/ppermute | solution.py:63
  50.1 8.5 %collective-permute-start.20 = (bf16[128,1024]{1,0:T(8,128)(2,1)}, bf16[128,1024]{1,0:T(8,128)(2,1)}, u32[]{:S(2)}, u32[]{:S(2)}) collective-permute-start(bf16[128,1024]{1,0:T(8,128)(2,1)} %collective-permute-done.18), channel_id=1, source_target_pairs={{0,8},{8,16},{16,24},{24,28},{28,20},{20,12},{12,4},{4,0},{1,9},{9... | collective-permute-start | bytes 786440 | tf_op jit(solution)/shard_map/ppermute | solution.py:62
  56.2 8.4 %collective-permute-start.23 = (bf16[128,1024]{1,0:T(8,128)(2,1)}, bf16[128,1024]{1,0:T(8,128)(2,1)}, u32[]{:S(2)}, u32[]{:S(2)}) collective-permute-start(bf16[128,1024]{1,0:T(8,128)(2,1)} %collective-permute-done.21), channel_id=1, source_target_pairs={{8,0},{16,8},{24,16},{28,24},{20,28},{12,20},{4,12},{0,4},{9,1},{1... | collective-permute-start | bytes 786440 | tf_op jit(solution)/shard_map/ppermute | solution.py:63
  58.6 7.0 %collective-permute-start.22 = (bf16[128,1024]{1,0:T(8,128)(2,1)}, bf16[128,1024]{1,0:T(8,128)(2,1)S(1)}, u32[]{:S(2)}, u32[]{:S(2)}) collective-permute-start(bf16[128,1024]{1,0:T(8,128)(2,1)} %collective-permute-done.20), channel_id=1, source_target_pairs={{0,8},{8,16},{16,24},{24,28},{28,20},{20,12},{12,4},{4,0},{1,9},{9... | collective-permute-start | bytes 786440 | tf_op jit(solution)/shard_map/ppermute | solution.py:62
  64.6 31.6 %collective-permute-start.25 = (bf16[128,1024]{1,0:T(8,128)(2,1)}, bf16[128,1024]{1,0:T(8,128)(2,1)}, u32[]{:S(2)}, u32[]{:S(2)}) collective-permute-start(bf16[128,1024]{1,0:T(8,128)(2,1)} %collective-permute-done.23), channel_id=1, source_target_pairs={{8,0},{16,8},{24,16},{28,24},{20,28},{12,20},{4,12},{0,4},{9,1},{1... | collective-permute-start | bytes 786440 | tf_op jit(solution)/shard_map/ppermute | solution.py:63
  65.5 31.7 %collective-permute-start.24 = (bf16[128,1024]{1,0:T(8,128)(2,1)S(1)}, bf16[128,1024]{1,0:T(8,128)(2,1)S(1)}, u32[]{:S(2)}, u32[]{:S(2)}) collective-permute-start(bf16[128,1024]{1,0:T(8,128)(2,1)S(1)} %collective-permute-done.22), channel_id=1, source_target_pairs={{0,8},{8,16},{16,24},{24,28},{28,20},{20,12},{12,4},{4,0},{1,9},{9... | collective-permute-start | bytes 786440 | tf_op jit(solution)/shard_map/ppermute | solution.py:62
  96.2 115.5 %collective-permute-start.27 = (bf16[128,1024]{1,0:T(8,128)(2,1)}, bf16[128,1024]{1,0:T(8,128)(2,1)}, u32[]{:S(2)}, u32[]{:S(2)}) collective-permute-start(bf16[128,1024]{1,0:T(8,128)(2,1)} %collective-permute-done.25), channel_id=1, source_target_pairs={{8,0},{16,8},{24,16},{28,24},{20,28},{12,20},{4,12},{0,4},{9,1},{1... | collective-permute-start | bytes 786440 | tf_op jit(solution)/shard_map/ppermute | solution.py:63
  97.2 119.0 %collective-permute-start.26 = (bf16[128,1024]{1,0:T(8,128)(2,1)S(1)}, bf16[128,1024]{1,0:T(8,128)(2,1)}, u32[]{:S(2)}, u32[]{:S(2)}) collective-permute-start(bf16[128,1024]{1,0:T(8,128)(2,1)S(1)} %collective-permute-done.24), channel_id=1, source_target_pairs={{0,8},{8,16},{16,24},{24,28},{28,20},{20,12},{12,4},{4,0},{1,9},{9... | collective-permute-start | bytes 786440 | tf_op jit(solution)/shard_map/ppermute | solution.py:62
  98.3 1.0 copy-start.1
  101.1 6.5 %collective-permute-start = (bf16[130,768]{1,0:T(8,128)(2,1)S(1)}, bf16[130,768]{1,0:T(8,128)(2,1)S(1)}, u32[]{:S(2)}, u32[]{:S(2)}) collective-permute-start(bf16[130,768]{1,0:T(8,128)(2,1)S(1)} %convolution_convert_fusion.1), channel_id=1, source_target_pairs={{0,8},{8,16},{16,24},{24,28},{28,20},{20,12},{12,4},{4,0},{1,9},{9... | collective-permute-start | bytes 599048 | tf_op jit(solution)/shard_map/ppermute | solution.py:83
  103.8 6.6 %collective-permute-start.7 = (bf16[130,768]{1,0:T(8,128)(2,1)S(1)}, bf16[130,768]{1,0:T(8,128)(2,1)S(1)}, u32[]{:S(2)}, u32[]{:S(2)}) collective-permute-start(bf16[130,768]{1,0:T(8,128)(2,1)S(1)} %convolution_convert_fusion), channel_id=1, source_target_pairs={{8,0},{16,8},{24,16},{28,24},{20,28},{12,20},{4,12},{0,4},{9,1},{1... | collective-permute-start | bytes 599048 | tf_op jit(solution)/shard_map/ppermute | solution.py:84
  107.9 7.2 %collective-permute-start.1 = (bf16[130,768]{1,0:T(8,128)(2,1)S(1)}, bf16[130,768]{1,0:T(8,128)(2,1)S(1)}, u32[]{:S(2)}, u32[]{:S(2)}) collective-permute-start(bf16[130,768]{1,0:T(8,128)(2,1)S(1)} %add_convert_fusion.13), channel_id=1, source_target_pairs={{0,8},{8,16},{16,24},{24,28},{28,20},{20,12},{12,4},{4,0},{1,9},{9... | collective-permute-start | bytes 599048 | tf_op jit(solution)/shard_map/ppermute | solution.py:83
  110.7 7.8 %collective-permute-start.8 = (bf16[130,768]{1,0:T(8,128)(2,1)S(1)}, bf16[130,768]{1,0:T(8,128)(2,1)S(1)}, u32[]{:S(2)}, u32[]{:S(2)}) collective-permute-start(bf16[130,768]{1,0:T(8,128)(2,1)S(1)} %add_convert_fusion.6), channel_id=1, source_target_pairs={{8,0},{16,8},{24,16},{28,24},{20,28},{12,20},{4,12},{0,4},{9,1},{1... | collective-permute-start | bytes 599048 | tf_op jit(solution)/shard_map/ppermute | solution.py:84
  115.1 8.1 %collective-permute-start.2 = (bf16[130,768]{1,0:T(8,128)(2,1)S(1)}, bf16[130,768]{1,0:T(8,128)(2,1)S(1)}, u32[]{:S(2)}, u32[]{:S(2)}) collective-permute-start(bf16[130,768]{1,0:T(8,128)(2,1)S(1)} %add_convert_fusion.12), channel_id=1, source_target_pairs={{0,8},{8,16},{16,24},{24,28},{28,20},{20,12},{12,4},{4,0},{1,9},{9... | collective-permute-start | bytes 599048 | tf_op jit(solution)/shard_map/ppermute | solution.py:83
  118.5 7.6 %collective-permute-start.9 = (bf16[130,768]{1,0:T(8,128)(2,1)S(1)}, bf16[130,768]{1,0:T(8,128)(2,1)S(1)}, u32[]{:S(2)}, u32[]{:S(2)}) collective-permute-start(bf16[130,768]{1,0:T(8,128)(2,1)S(1)} %add_convert_fusion.5), channel_id=1, source_target_pairs={{8,0},{16,8},{24,16},{28,24},{20,28},{12,20},{4,12},{0,4},{9,1},{1... | collective-permute-start | bytes 599048 | tf_op jit(solution)/shard_map/ppermute | solution.py:84
  123.2 7.3 %collective-permute-start.3 = (bf16[130,768]{1,0:T(8,128)(2,1)S(1)}, bf16[130,768]{1,0:T(8,128)(2,1)S(1)}, u32[]{:S(2)}, u32[]{:S(2)}) collective-permute-start(bf16[130,768]{1,0:T(8,128)(2,1)S(1)} %add_convert_fusion.11), channel_id=1, source_target_pairs={{0,8},{8,16},{16,24},{24,28},{28,20},{20,12},{12,4},{4,0},{1,9},{9... | collective-permute-start | bytes 599048 | tf_op jit(solution)/shard_map/ppermute | solution.py:83
  126.1 6.8 %collective-permute-start.10 = (bf16[130,768]{1,0:T(8,128)(2,1)S(1)}, bf16[130,768]{1,0:T(8,128)(2,1)S(1)}, u32[]{:S(2)}, u32[]{:S(2)}) collective-permute-start(bf16[130,768]{1,0:T(8,128)(2,1)S(1)} %add_convert_fusion.4), channel_id=1, source_target_pairs={{8,0},{16,8},{24,16},{28,24},{20,28},{12,20},{4,12},{0,4},{9,1},{1... | collective-permute-start | bytes 599048 | tf_op jit(solution)/shard_map/ppermute | solution.py:84
  130.5 6.4 %collective-permute-start.4 = (bf16[130,768]{1,0:T(8,128)(2,1)S(1)}, bf16[130,768]{1,0:T(8,128)(2,1)S(1)}, u32[]{:S(2)}, u32[]{:S(2)}) collective-permute-start(bf16[130,768]{1,0:T(8,128)(2,1)S(1)} %add_convert_fusion.10), channel_id=1, source_target_pairs={{0,8},{8,16},{16,24},{24,28},{28,20},{20,12},{12,4},{4,0},{1,9},{9... | collective-permute-start | bytes 599048 | tf_op jit(solution)/shard_map/ppermute | solution.py:83
  133.0 6.1 %collective-permute-start.11 = (bf16[130,768]{1,0:T(8,128)(2,1)S(1)}, bf16[130,768]{1,0:T(8,128)(2,1)S(1)}, u32[]{:S(2)}, u32[]{:S(2)}) collective-permute-start(bf16[130,768]{1,0:T(8,128)(2,1)S(1)} %add_convert_fusion.3), channel_id=1, source_target_pairs={{8,0},{16,8},{24,16},{28,24},{20,28},{12,20},{4,12},{0,4},{9,1},{1... | collective-permute-start | bytes 599048 | tf_op jit(solution)/shard_map/ppermute | solution.py:84
  137.0 5.9 %collective-permute-start.5 = (bf16[130,768]{1,0:T(8,128)(2,1)S(1)}, bf16[130,768]{1,0:T(8,128)(2,1)S(1)}, u32[]{:S(2)}, u32[]{:S(2)}) collective-permute-start(bf16[130,768]{1,0:T(8,128)(2,1)S(1)} %add_convert_fusion.9), channel_id=1, source_target_pairs={{0,8},{8,16},{16,24},{24,28},{28,20},{20,12},{12,4},{4,0},{1,9},{9... | collective-permute-start | bytes 599048 | tf_op jit(solution)/shard_map/ppermute | solution.py:83
  139.1 5.9 %collective-permute-start.12 = (bf16[130,768]{1,0:T(8,128)(2,1)S(1)}, bf16[130,768]{1,0:T(8,128)(2,1)S(1)}, u32[]{:S(2)}, u32[]{:S(2)}) collective-permute-start(bf16[130,768]{1,0:T(8,128)(2,1)S(1)} %add_convert_fusion.2), channel_id=1, source_target_pairs={{8,0},{16,8},{24,16},{28,24},{20,28},{12,20},{4,12},{0,4},{9,1},{1... | collective-permute-start | bytes 599048 | tf_op jit(solution)/shard_map/ppermute | solution.py:84
  142.9 5.9 %collective-permute-start.6 = (bf16[130,768]{1,0:T(8,128)(2,1)S(1)}, bf16[130,768]{1,0:T(8,128)(2,1)S(1)}, u32[]{:S(2)}, u32[]{:S(2)}) collective-permute-start(bf16[130,768]{1,0:T(8,128)(2,1)S(1)} %add_convert_fusion.8), channel_id=1, source_target_pairs={{0,8},{8,16},{16,24},{24,28},{28,20},{20,12},{12,4},{4,0},{1,9},{9... | collective-permute-start | bytes 599048 | tf_op jit(solution)/shard_map/ppermute | solution.py:83
  145.0 6.0 %collective-permute-start.13 = (bf16[130,768]{1,0:T(8,128)(2,1)S(1)}, bf16[130,768]{1,0:T(8,128)(2,1)S(1)}, u32[]{:S(2)}, u32[]{:S(2)}) collective-permute-start(bf16[130,768]{1,0:T(8,128)(2,1)S(1)} %add_convert_fusion.1), channel_id=1, source_target_pairs={{8,0},{16,8},{24,16},{28,24},{20,28},{12,20},{4,12},{0,4},{9,1},{1... | collective-permute-start | bytes 599048 | tf_op jit(solution)/shard_map/ppermute | solution.py:84
  155.3 5.0 %copy-start.12 = (f32[16,512]{1,0:T(8,128)S(1)}, f32[16,512]{1,0:T(8,128)}, u32[]{:S(2)}) copy-start(f32[16,512]{1,0:T(8,128)} %param.23) | copy-start | bytes 98308
  158.2 2.0 copy-start
  197.0 1.5 copy-start.16
  197.1 9.0 %copy-start.2 = (bf16[256,1024]{1,0:T(8,128)(2,1)S(1)}, bf16[256,1024]{1,0:T(8,128)(2,1)}, u32[]{:S(2)}) copy-start(bf16[256,1024]{1,0:T(8,128)(2,1)} %param.25) | copy-start | bytes 1572868
  197.1 9.2 %copy-start.8 = (bf16[128,1024]{1,0:T(8,128)(2,1)S(1)}, bf16[128,1024]{1,0:T(8,128)(2,1)}, u32[]{:S(2)}) copy-start(bf16[128,1024]{1,0:T(8,128)(2,1)} %copy-done.7) | copy-start | bytes 786436
  197.1 9.4 %copy-start.10 = (bf16[128,1024]{1,0:T(8,128)(2,1)S(1)}, bf16[128,1024]{1,0:T(8,128)(2,1)}, u32[]{:S(2)}) copy-start(bf16[128,1024]{1,0:T(8,128)(2,1)} %copy-done.9) | copy-start | bytes 786436
  206.5 6.6 %copy-start.6 = (bf16[128,1024]{1,0:T(8,128)(2,1)S(1)}, bf16[128,1024]{1,0:T(8,128)(2,1)}, u32[]{:S(2)}) copy-start(bf16[128,1024]{1,0:T(8,128)(2,1)} %copy-done.5) | copy-start | bytes 786436

commit v4 on v3

--- a/solution.py
+++ b/solution.py
@@ -12,7 +12,6 @@
     length, width = signal.shape
     order = rates.shape[0]
     ctx_count = lax.axis_size("ctx")
-    me = lax.axis_index("ctx")
     coefs = residues * jnp.sqrt(2.0 * rates)
     times = jnp.arange(length, dtype=jnp.float32)[:, None, None]
     grow = jnp.exp(rates[None] * times)
@@ -24,15 +23,13 @@
         length, order, width
     )
     end_state = running[length - 1] * jnp.exp(-rates * (length - 1))
-    states = lax.all_gather(end_state[None], "ctx", axis=0, tiled=True)
-    chunk_ids = jnp.arange(ctx_count, dtype=jnp.int32)
-    gap = jnp.maximum(me - 1 - chunk_ids, 0).astype(jnp.float32)
-    carry_w = jnp.where(
-        (chunk_ids < me)[:, None, None],
-        jnp.exp(-rates[None] * (gap[:, None, None] * length)),
-        0.0,
-    )
-    carried = jnp.sum(carry_w * states, axis=0) * jnp.exp(-rates)
+    carried = jnp.zeros_like(end_state)
+    for shift in range(1, ctx_count):
+        earlier = lax.ppermute(
+            end_state, "ctx", perm=[(i, i + shift) for i in range(ctx_count - shift)]
+        )
+        carried = carried + jnp.exp(-rates * (length * (shift - 1))) * earlier
+    carried = carried * jnp.exp(-rates)
     total = running + carried[None]
     mixed = jnp.sum((coefs[None] * decay) * total, axis=1)
     return mixed + skips * signal
@@ -129,17 +126,14 @@
     c_chunk = w_out.shape[0]
     c_half = c_chunk // 2
 
-    def consume_out(acc, src_up, ups, lows, src_low):
-        cols_up = lax.dynamic_slice_in_dim(features, src_up * c_chunk, c_half, 1)
-        cols_low = lax.dynamic_slice_in_dim(features, src_low * c_chunk + c_half, c_half, 1)
-        return (
-            acc[0]
-            + jnp.dot(cols_up, ups[0], preferred_element_type=jnp.float32)
-            + jnp.dot(cols_low, lows[0], preferred_element_type=jnp.float32),
-        )
+    def place_out(acc, src_up, ups, lows, src_low):
+        acc = lax.dynamic_update_slice_in_dim(acc, ups[0][None], src_up * 2, 0)
+        return lax.dynamic_update_slice_in_dim(acc, lows[0][None], src_low * 2 + 1, 0)
 
-    out_zero = jnp.zeros((features.shape[0], w_out.shape[1]), jnp.float32)
-    (result,) = ring_contract([(w_out[:c_half], w_out[c_half:])], consume_out, (out_zero,))
+    blank = jnp.zeros((2 * ctx_count, c_half, w_out.shape[1]), w_out.dtype)
+    w_full = ring_contract([(w_out[:c_half], w_out[c_half:])], place_out, blank)
+    w_full = w_full.reshape(ctx_count * c_chunk, w_out.shape[1])
+    result = jnp.dot(features, w_full, preferred_element_type=jnp.float32)
     return result.astype(jnp.bfloat16)
 
 

time: 219 us -> 194 us (0.89)
  blocking collectives: 38.3 us -> 7.17 us
  local copies, waits for them, and re-layouts: 18.8 us -> 34.7 us
  waiting for transfers between devices: 65.8 us -> 53.8 us
  starting transfers between devices: 43.2 us -> 52 us
  matrix products: 19.2 us -> 11 us
    ppermute x7, waiting for transfers between devices: 32.5 us -> 0.02 us  [ring_contract(): lows = lax.ppermute(lows, 'ctx', perm=bwd)]
    all_gather x1 -> x0, blocking collectives: 31.1 us -> none  [modal_long_conv(): states = lax.all_gather(end_state[None], 'ctx', axis=0, tiled=True)]
    ppermute x7, waiting for transfers between devices: 2.76 us -> 20.6 us  [ring_contract(): ups = lax.ppermute(ups, 'ctx', perm=fwd)]
    ppermute x0 -> x7, starting transfers between devices: none -> 15.3 us  [modal_long_conv(): lax.ppermute(end_state, 'ctx', perm=[(i, i + shift) for i in range(ctx_co...]
    dynamic_update_slice x0 -> x16, local copies, waits for them, and re-layouts: none -> 13.6 us  [the longest x8 7.73 us: place_out(): acc = lax.dynamic_update_slice_in_dim(acc, ups[0][None], src_up * 2, 0)]
    ppermute x7, starting transfers between devices: 10.8 us -> 1.07 us  [ring_contract(): lows = lax.ppermute(lows, 'ctx', perm=bwd)]
    ppermute x7, waiting for transfers between devices: 11.6 us -> 20.6 us  [ring_reduce_scatter(): lax.ppermute(down.astype(jnp.bfloat16), 'ctx', perm=bwd).astype(jnp.float32)]
    dot_general x16 -> x1, matrix products: 11.8 us -> 3.61 us  [body(): result = jnp.dot(features, w_full, preferred_element_type=jnp.float32)]
  transfers between devices with their start and end apart: 29 -> 36, of which waited for: 21 -> 19; matrix products, arithmetic and copies ran while one was open for 16% -> 20% of each run, Pallas kernels for 0% -> 0%
where the time goes in v4:
time: 194 us
  waiting for transfers between devices  53.8 us (28%)
  starting transfers between devices  52 us (27%)
  local copies, waits for them, and re-layouts  34.7 us (18%)
  between operations  30.8 us (16%)
  matrix products  11 us (6%)
  blocking collectives  7.17 us (4%)
  other arithmetic  4.02 us (2%)
    ppermute x7, waiting for transfers between devices, ring_reduce_scatter(): lax.ppermute(down.astype(jnp.bfloat16), 'ctx', perm=bwd).astype(jnp.float32)  20.6 us
    ppermute x7, waiting for transfers between devices, ring_contract(): ups = lax.ppermute(ups, 'ctx', perm=fwd)  20.6 us
    ppermute x7, starting transfers between devices, modal_long_conv(): lax.ppermute(end_state, 'ctx', perm=[(i, i + shift) for i in range(ctx_co...  15.3 us
    unnamed x26, local copies, waits for them, and re-layouts  14.2 us
    ppermute x7, starting transfers between devices, ring_contract(): ups = lax.ppermute(ups, 'ctx', perm=fwd)  14.2 us
    ppermute x7, waiting for transfers between devices, ring_reduce_scatter(): lax.ppermute(up.astype(jnp.bfloat16), 'ctx', perm=fwd).astype(jnp.float32)  12.6 us
    ppermute x7, starting transfers between devices, ring_reduce_scatter(): lax.ppermute(down.astype(jnp.bfloat16), 'ctx', perm=bwd).astype(jnp.float32)  11.7 us
    dynamic_update_slice x8, local copies, waits for them, and re-layouts, place_out(): acc = lax.dynamic_update_slice_in_dim(acc, ups[0][None], src_up * 2, 0)  7.73 us
  transfers between devices with their start and end apart: 36, of which 19 were waited for; matrix products, arithmetic and copies ran while one was open for 20% of the time, Pallas kernels for 0%

profile of v4, /device:TPU:0, one launch (start us, length us, event | category | flops | bytes accessed | tf_op | source)
XLA Modules:
  0.0 193.5 jit_solution(5698813852823117733)
XLA Ops:
  0.0 2.3 %copy.16 = bf16[128,4096]{0,1:T(8,128)(2,1)} copy(bf16[128,4096]{1,0:T(8,128)(2,1)} %param.15) | data formatting | bytes 2097152 | tf_op args[0]
  2.4 7.3 %all-to-all-start = ((bf16[128,8,512]{0,2,1:T(8,128)(2,1)}), bf16[128,8,512]{0,2,1:T(8,128)(2,1)S(1)}, u32[]{:S(2)}, u32[]{:S(2)}) async-start(bf16[128,8,512]{0,2,1:T(8,128)(2,1)} %bitcast.1), calls=%async_computation | async-start | bytes 2097152 | tf_op jit(solution)/shard_map/all_to_all | solution.py:103
  10.5 2.0 %collective-permute-start.21 = (bf16[128,1024]{1,0:T(8,128)(2,1)}, bf16[128,1024]{1,0:T(8,128)(2,1)}, u32[]{:S(2)}, u32[]{:S(2)}) collective-permute-start(bf16[128,1024]{1,0:T(8,128)(2,1)} %get-tuple-element.6), channel_id=1, source_target_pairs={{0,8},{8,16},{16,24},{24,28},{28,20},{20,12},{12,4},{4,0},{1,9},{9... | collective-permute-start | bytes 786440 | tf_op jit(solution)/shard_map/ppermute | solution.py:59
  12.6 2.6 %broadcast_in_dim.61 = bf16[16,128,1024]{2,1,0:T(8,128)(2,1)} broadcast(bf16[]{:T(256)} %constant.274.clone.1), dimensions={} | broadcast | bytes 4194306 | tf_op jit(solution)/shard_map/broadcast_in_dim | solution.py:133
  15.9 1.5 pad_maximum_fusion.1
  49.8 2.0 %collective-permute-start.23 = (bf16[128,1024]{1,0:T(8,128)(2,1)}, bf16[128,1024]{1,0:T(8,128)(2,1)S(1)}, u32[]{:S(2)}, u32[]{:S(2)}) collective-permute-start(bf16[128,1024]{1,0:T(8,128)(2,1)} %collective-permute-done.21), channel_id=1, source_target_pairs={{0,8},{8,16},{16,24},{24,28},{28,20},{20,12},{12,4},{4,0},{1,9},{9... | collective-permute-start | bytes 786440 | tf_op jit(solution)/shard_map/ppermute | solution.py:59
  51.9 1.7 bitcast_dynamic-update-slice_fusion.13
  54.4 2.9 %collective-permute-done.23 = bf16[128,1024]{1,0:T(8,128)(2,1)S(1)} collective-permute-done((bf16[128,1024]{1,0:T(8,128)(2,1)}, bf16[128,1024]{1,0:T(8,128)(2,1)S(1)}, u32[]{:S(2)}, u32[]{:S(2)}) %collective-permute-start.23) | collective-permute-done | bytes 262176 | tf_op jit(solution)/shard_map/ppermute | solution.py:59
  57.3 1.7 collective-permute-start.25
  60.7 3.3 %collective-permute-done.25 = bf16[128,1024]{1,0:T(8,128)(2,1)S(1)} collective-permute-done((bf16[128,1024]{1,0:T(8,128)(2,1)S(1)}, bf16[128,1024]{1,0:T(8,128)(2,1)S(1)}, u32[]{:S(2)}, u32[]{:S(2)}) %collective-permute-start.25) | collective-permute-done | bytes 262176 | tf_op jit(solution)/shard_map/ppermute | solution.py:59
  64.1 2.0 %collective-permute-start.27 = (bf16[128,1024]{1,0:T(8,128)(2,1)S(1)}, bf16[128,1024]{1,0:T(8,128)(2,1)S(1)}, u32[]{:S(2)}, u32[]{:S(2)}) collective-permute-start(bf16[128,1024]{1,0:T(8,128)(2,1)S(1)} %collective-permute-done.25), channel_id=1, source_target_pairs={{0,8},{8,16},{16,24},{24,28},{28,20},{20,12},{12,4},{4,0},{1,9},{9... | collective-permute-start | bytes 786440 | tf_op jit(solution)/shard_map/ppermute | solution.py:59
  67.8 4.2 %collective-permute-done.27 = bf16[128,1024]{1,0:T(8,128)(2,1)S(1)} collective-permute-done((bf16[128,1024]{1,0:T(8,128)(2,1)S(1)}, bf16[128,1024]{1,0:T(8,128)(2,1)S(1)}, u32[]{:S(2)}, u32[]{:S(2)}) %collective-permute-start.27) | collective-permute-done | bytes 262176 | tf_op jit(solution)/shard_map/ppermute | solution.py:59
  72.0 2.3 %collective-permute-start.29 = (bf16[128,1024]{1,0:T(8,128)(2,1)S(1)}, bf16[128,1024]{1,0:T(8,128)(2,1)S(1)}, u32[]{:S(2)}, u32[]{:S(2)}) collective-permute-start(bf16[128,1024]{1,0:T(8,128)(2,1)S(1)} %collective-permute-done.27), channel_id=1, source_target_pairs={{0,8},{8,16},{16,24},{24,28},{28,20},{20,12},{12,4},{4,0},{1,9},{9... | collective-permute-start | bytes 786440 | tf_op jit(solution)/shard_map/ppermute | solution.py:59
  75.9 5.4 %collective-permute-done.29 = bf16[128,1024]{1,0:T(8,128)(2,1)S(1)} collective-permute-done((bf16[128,1024]{1,0:T(8,128)(2,1)S(1)}, bf16[128,1024]{1,0:T(8,128)(2,1)S(1)}, u32[]{:S(2)}, u32[]{:S(2)}) %collective-permute-start.29) | collective-permute-done | bytes 262176 | tf_op jit(solution)/shard_map/ppermute | solution.py:59
  81.4 2.0 %collective-permute-start.31 = (bf16[128,1024]{1,0:T(8,128)(2,1)S(1)}, bf16[128,1024]{1,0:T(8,128)(2,1)S(1)}, u32[]{:S(2)}, u32[]{:S(2)}) collective-permute-start(bf16[128,1024]{1,0:T(8,128)(2,1)S(1)} %collective-permute-done.29), channel_id=1, source_target_pairs={{0,8},{8,16},{16,24},{24,28},{28,20},{20,12},{12,4},{4,0},{1,9},{9... | collective-permute-start | bytes 786440 | tf_op jit(solution)/shard_map/ppermute | solution.py:59
  85.0 4.7 %collective-permute-done.31 = bf16[128,1024]{1,0:T(8,128)(2,1)S(1)} collective-permute-done((bf16[128,1024]{1,0:T(8,128)(2,1)S(1)}, bf16[128,1024]{1,0:T(8,128)(2,1)S(1)}, u32[]{:S(2)}, u32[]{:S(2)}) %collective-permute-start.31) | collective-permute-done | bytes 262176 | tf_op jit(solution)/shard_map/ppermute | solution.py:59
  89.8 2.0 %collective-permute-start.33 = (bf16[128,1024]{1,0:T(8,128)(2,1)S(1)}, bf16[128,1024]{1,0:T(8,128)(2,1)}, u32[]{:S(2)}, u32[]{:S(2)}) collective-permute-start(bf16[128,1024]{1,0:T(8,128)(2,1)S(1)} %collective-permute-done.31), channel_id=1, source_target_pairs={{0,8},{8,16},{16,24},{24,28},{28,20},{20,12},{12,4},{4,0},{1,9},{9... | collective-permute-start | bytes 786440 | tf_op jit(solution)/shard_map/ppermute | solution.py:59
  94.4 1.5 copy.17
  97.9 1.7 collective-permute-start.7
  102.0 2.4 %collective-permute-done.7 = bf16[130,768]{1,0:T(8,128)(2,1)S(1)} collective-permute-done((bf16[130,768]{1,0:T(8,128)(2,1)S(1)}, bf16[130,768]{1,0:T(8,128)(2,1)S(1)}, u32[]{:S(2)}, u32[]{:S(2)}) %collective-permute-start.7) | collective-permute-done | bytes 199712 | tf_op jit(solution)/shard_map/ppermute | solution.py:81
  104.6 2.4 %collective-permute-start.8 = (bf16[130,768]{1,0:T(8,128)(2,1)S(1)}, bf16[130,768]{1,0:T(8,128)(2,1)S(1)}, u32[]{:S(2)}, u32[]{:S(2)}) collective-permute-start(bf16[130,768]{1,0:T(8,128)(2,1)S(1)} %add_convert_fusion.6), channel_id=1, source_target_pairs={{8,0},{16,8},{24,16},{28,24},{20,28},{12,20},{4,12},{0,4},{9,1},{1... | collective-permute-start | bytes 599048 | tf_op jit(solution)/shard_map/ppermute | solution.py:81
  108.1 4.9 %collective-permute-done.8 = bf16[130,768]{1,0:T(8,128)(2,1)S(1)} collective-permute-done((bf16[130,768]{1,0:T(8,128)(2,1)S(1)}, bf16[130,768]{1,0:T(8,128)(2,1)S(1)}, u32[]{:S(2)}, u32[]{:S(2)}) %collective-permute-start.8) | collective-permute-done | bytes 199712 | tf_op jit(solution)/shard_map/ppermute | solution.py:81
  113.0 2.0 %collective-permute-start.9 = (bf16[130,768]{1,0:T(8,128)(2,1)S(1)}, bf16[130,768]{1,0:T(8,128)(2,1)S(1)}, u32[]{:S(2)}, u32[]{:S(2)}) collective-permute-start(bf16[130,768]{1,0:T(8,128)(2,1)S(1)} %add_convert_fusion.5), channel_id=1, source_target_pairs={{8,0},{16,8},{24,16},{28,24},{20,28},{12,20},{4,12},{0,4},{9,1},{1... | collective-permute-start | bytes 599048 | tf_op jit(solution)/shard_map/ppermute | solution.py:81
  115.8 4.5 %collective-permute-done.9 = bf16[130,768]{1,0:T(8,128)(2,1)S(1)} collective-permute-done((bf16[130,768]{1,0:T(8,128)(2,1)S(1)}, bf16[130,768]{1,0:T(8,128)(2,1)S(1)}, u32[]{:S(2)}, u32[]{:S(2)}) %collective-permute-start.9) | collective-permute-done | bytes 199712 | tf_op jit(solution)/shard_map/ppermute | solution.py:81
  120.4 1.7 collective-permute-start.10
  122.1 1.4 collective-permute-done.2
  123.6 3.3 %collective-permute-done.10 = bf16[130,768]{1,0:T(8,128)(2,1)S(1)} collective-permute-done((bf16[130,768]{1,0:T(8,128)(2,1)S(1)}, bf16[130,768]{1,0:T(8,128)(2,1)S(1)}, u32[]{:S(2)}, u32[]{:S(2)}) %collective-permute-start.10) | collective-permute-done | bytes 199712 | tf_op jit(solution)/shard_map/ppermute | solution.py:81
  127.0 1.3 collective-permute-start.11
  128.3 1.9 %collective-permute-done.3 = bf16[130,768]{1,0:T(8,128)(2,1)S(1)} collective-permute-done((bf16[130,768]{1,0:T(8,128)(2,1)S(1)}, bf16[130,768]{1,0:T(8,128)(2,1)S(1)}, u32[]{:S(2)}, u32[]{:S(2)}) %collective-permute-start.3) | collective-permute-done | bytes 199712 | tf_op jit(solution)/shard_map/ppermute | solution.py:80
  130.7 2.2 %collective-permute-done.11 = bf16[130,768]{1,0:T(8,128)(2,1)S(1)} collective-permute-done((bf16[130,768]{1,0:T(8,128)(2,1)S(1)}, bf16[130,768]{1,0:T(8,128)(2,1)S(1)}, u32[]{:S(2)}, u32[]{:S(2)}) %collective-permute-start.11) | collective-permute-done | bytes 199712 | tf_op jit(solution)/shard_map/ppermute | solution.py:81
  132.9 1.3 collective-permute-start.12
  134.2 2.1 %collective-permute-done.4 = bf16[130,768]{1,0:T(8,128)(2,1)S(1)} collective-permute-done((bf16[130,768]{1,0:T(8,128)(2,1)S(1)}, bf16[130,768]{1,0:T(8,128)(2,1)S(1)}, u32[]{:S(2)}, u32[]{:S(2)}) %collective-permute-start.4) | collective-permute-done | bytes 199712 | tf_op jit(solution)/shard_map/ppermute | solution.py:80
  137.0 1.7 collective-permute-done.12
  138.8 1.3 collective-permute-start.13
  140.1 2.1 %collective-permute-done.5 = bf16[130,768]{1,0:T(8,128)(2,1)S(1)} collective-permute-done((bf16[130,768]{1,0:T(8,128)(2,1)S(1)}, bf16[130,768]{1,0:T(8,128)(2,1)S(1)}, u32[]{:S(2)}, u32[]{:S(2)}) %collective-permute-start.5) | collective-permute-done | bytes 199712 | tf_op jit(solution)/shard_map/ppermute | solution.py:80
  143.1 1.5 collective-permute-done.13
  144.7 3.6 %collective-permute-done.6 = bf16[130,768]{1,0:T(8,128)(2,1)S(1)} collective-permute-done((bf16[130,768]{1,0:T(8,128)(2,1)S(1)}, bf16[130,768]{1,0:T(8,128)(2,1)S(1)}, u32[]{:S(2)}, u32[]{:S(2)}) %collective-permute-start.6) | collective-permute-done | bytes 199712 | tf_op jit(solution)/shard_map/ppermute | solution.py:80
  149.1 3.4 %copy.19 = f32[16,8,16,512]{3,1,2,0:T(8,128)S(1)} copy(f32[16,8,16,512]{3,2,1,0:T(8,128)S(1)} %bitcast.145) | data formatting | bytes 8388608
  152.6 2.9 %fusion.2 = f32[128,8192]{1,0:T(8,128)S(1)} fusion(f32[128,8192]{1,0:T(8,128)S(1)} %bitcast.144, f32[8192]{0:T(1024)S(1)} %bitcast.148), kind=kOutput, calls=%fused_computation.3 | convolution fusion | flops 1612726272 | bytes 8421376 | tf_op jit(solution)/shard_map/dot_general | solution.py:22
  155.5 1.9 %copy-done = f32[128,8192]{1,0:T(8,128)} copy-done((f32[128,8192]{1,0:T(8,128)}, f32[128,8192]{1,0:T(8,128)S(1)}, u32[]{:S(2)}) %copy-start) | copy-done | bytes 4194328
  157.6 4.3 %collective-permute-start.20 = (f32[16,512]{1,0:T(8,128)S(1)}, f32[16,512]{1,0:T(8,128)S(1)}, u32[]{:S(2)}, u32[]{:S(2)}) collective-permute-start(f32[16,512]{1,0:T(8,128)S(1)} %exponential_multiply_fusion.1), channel_id=1, source_target_pairs={{0,28},{1,29},{2,30},{3,31}} | collective-permute-start | bytes 98312 | tf_op jit(solution)/shard_map/ppermute | solution.py:28
  163.2 1.7 bitcast_dynamic-update-slice_fusion.1
  167.5 2.4 %collective-permute-start.16 = (f32[16,512]{1,0:T(8,128)S(1)}, f32[16,512]{1,0:T(8,128)S(1)}, u32[]{:S(2)}, u32[]{:S(2)}) collective-permute-start(f32[16,512]{1,0:T(8,128)S(1)} %exponential_multiply_fusion.1), channel_id=1, source_target_pairs={{0,12},{4,16},{8,20},{12,24},{16,28},{1,13},{5,17},{9,21},{13,25},... | collective-permute-start | bytes 98312 | tf_op jit(solution)/shard_map/ppermute | solution.py:28
  171.3 3.3 %collective-permute-start.14 = (f32[16,512]{1,0:T(8,128)S(1)}, f32[16,512]{1,0:T(8,128)S(1)}, u32[]{:S(2)}, u32[]{:S(2)}) collective-permute-start(f32[16,512]{1,0:T(8,128)S(1)} %exponential_multiply_fusion.1), channel_id=1, source_target_pairs={{0,4},{4,8},{8,12},{12,16},{16,20},{20,24},{24,28},{1,5},{5,9},{9,... | collective-permute-start | bytes 98312 | tf_op jit(solution)/shard_map/ppermute | solution.py:28
  175.4 5.4 %copy.20 = f32[16,8,16,512]{3,2,1,0:T(8,128)S(1)} copy(f32[16,8,16,512]{3,1,2,0:T(8,128)} %bitcast.143) | data formatting | bytes 8388608
  181.0 1.5 fusion.1
  182.7 7.2 %all_gather.3 = bf16[128,2048]{1,0:T(8,128)(2,1)S(1)} all-gather(bf16[128,512]{1,0:T(8,128)(2,1)S(1)} %multiply_convert_fusion), channel_id=1, replica_groups=mesh['ctx'=8,'tp'=4] {'tp'}, dimensions={1}, use_global_device_ids=true | all-gather | bytes 655360 | tf_op jit(solution)/shard_map/all_gather | solution.py:125
  189.9 3.6 %convolution_convert_fusion = bf16[128,1024]{1,0:T(8,128)(2,1)} fusion(bf16[128,2048]{1,0:T(8,128)(2,1)S(1)} %all_gather.3, bf16[2048,1024]{1,0:T(8,128)(2,1)} %bitcast.81), kind=kOutput, calls=%fused_computation.9 | convolution fusion | flops 537001984 | bytes 4980736 | tf_op jit(solution)/shard_map/dot_general | solution.py:136
  (115 shorter events, 29.9 us)
Async XLA Ops:
  0.0 9.6 %copy-start.2 = (bf16[256,1024]{1,0:T(8,128)(2,1)S(1)}, bf16[256,1024]{1,0:T(8,128)(2,1)}, u32[]{:S(2)}) copy-start(bf16[256,1024]{1,0:T(8,128)(2,1)} %param.25) | copy-start | bytes 1572868
  0.0 12.5 %copy-start.6 = (f32[3,512]{1,0:T(4,128)S(1)}, f32[3,512]{1,0:T(4,128)}, u32[]{:S(2)}) copy-start(f32[3,512]{1,0:T(4,128)} %param.21) | copy-start | bytes 18436
  0.0 12.5 %copy-start.7 = (f32[3,512]{1,0:T(4,128)S(1)}, f32[3,512]{1,0:T(4,128)}, u32[]{:S(2)}) copy-start(f32[3,512]{1,0:T(4,128)} %param.20) | copy-start | bytes 18436
  0.0 12.6 %copy-start.8 = (f32[3,512]{1,0:T(4,128)S(1)}, f32[3,512]{1,0:T(4,128)}, u32[]{:S(2)}) copy-start(f32[3,512]{1,0:T(4,128)} %param.19) | copy-start | bytes 18436
  2.4 91.0 %all-to-all-start = ((bf16[128,8,512]{0,2,1:T(8,128)(2,1)}), bf16[128,8,512]{0,2,1:T(8,128)(2,1)S(1)}, u32[]{:S(2)}, u32[]{:S(2)}) async-start(bf16[128,8,512]{0,2,1:T(8,128)(2,1)} %bitcast.1), calls=%async_computation | async-start | bytes 2097152 | tf_op jit(solution)/shard_map/all_to_all | solution.py:103
  10.5 6.9 %copy-start.10 = (s32[8]{0:T(128)S(1)}, s32[8]{0:T(128)}, u32[]{:S(2)}) copy-start(s32[8]{0:T(128)} %constant.312.clone) | copy-start | bytes 100
  10.5 39.3 %collective-permute-start.21 = (bf16[128,1024]{1,0:T(8,128)(2,1)}, bf16[128,1024]{1,0:T(8,128)(2,1)}, u32[]{:S(2)}, u32[]{:S(2)}) collective-permute-start(bf16[128,1024]{1,0:T(8,128)(2,1)} %get-tuple-element.6), channel_id=1, source_target_pairs={{0,8},{8,16},{16,24},{24,28},{28,20},{20,12},{12,4},{4,0},{1,9},{9... | collective-permute-start | bytes 786440 | tf_op jit(solution)/shard_map/ppermute | solution.py:59
  12.5 39.4 %collective-permute-start.22 = (bf16[128,1024]{1,0:T(8,128)(2,1)}, bf16[128,1024]{1,0:T(8,128)(2,1)S(1)}, u32[]{:S(2)}, u32[]{:S(2)}) collective-permute-start(bf16[128,1024]{1,0:T(8,128)(2,1)} %get-tuple-element.5), channel_id=1, source_target_pairs={{8,0},{16,8},{24,16},{28,24},{20,28},{12,20},{4,12},{0,4},{9,1},{1... | collective-permute-start | bytes 786440 | tf_op jit(solution)/shard_map/ppermute | solution.py:60
  12.6 16.7 %copy-start.4 = (s32[8]{0:T(128)S(1)}, s32[8]{0:T(128)}, u32[]{:S(2)}) copy-start(s32[8]{0:T(128)} %constant.313.clone) | copy-start | bytes 100
  12.6 36.3 %copy-start.3 = (f32[16,512]{1,0:T(8,128)S(1)}, f32[16,512]{1,0:T(8,128)}, u32[]{:S(2)}) copy-start(f32[16,512]{1,0:T(8,128)} %param.22) | copy-start | bytes 98308
  49.8 7.4 %collective-permute-start.23 = (bf16[128,1024]{1,0:T(8,128)(2,1)}, bf16[128,1024]{1,0:T(8,128)(2,1)S(1)}, u32[]{:S(2)}, u32[]{:S(2)}) collective-permute-start(bf16[128,1024]{1,0:T(8,128)(2,1)} %collective-permute-done.21), channel_id=1, source_target_pairs={{0,8},{8,16},{16,24},{24,28},{28,20},{20,12},{12,4},{4,0},{1,9},{9... | collective-permute-start | bytes 786440 | tf_op jit(solution)/shard_map/ppermute | solution.py:59
  51.9 7.1 %collective-permute-start.24 = (bf16[128,1024]{1,0:T(8,128)(2,1)S(1)}, bf16[128,1024]{1,0:T(8,128)(2,1)S(1)}, u32[]{:S(2)}, u32[]{:S(2)}) collective-permute-start(bf16[128,1024]{1,0:T(8,128)(2,1)S(1)} %collective-permute-done.22), channel_id=1, source_target_pairs={{8,0},{16,8},{24,16},{28,24},{20,28},{12,20},{4,12},{0,4},{9,1},{1... | collective-permute-start | bytes 786440 | tf_op jit(solution)/shard_map/ppermute | solution.py:60
  57.3 6.8 %collective-permute-start.25 = (bf16[128,1024]{1,0:T(8,128)(2,1)S(1)}, bf16[128,1024]{1,0:T(8,128)(2,1)S(1)}, u32[]{:S(2)}, u32[]{:S(2)}) collective-permute-start(bf16[128,1024]{1,0:T(8,128)(2,1)S(1)} %collective-permute-done.23), channel_id=1, source_target_pairs={{0,8},{8,16},{16,24},{24,28},{28,20},{20,12},{12,4},{4,0},{1,9},{9... | collective-permute-start | bytes 786440 | tf_op jit(solution)/shard_map/ppermute | solution.py:59
  59.0 7.1 %collective-permute-start.26 = (bf16[128,1024]{1,0:T(8,128)(2,1)S(1)}, bf16[128,1024]{1,0:T(8,128)(2,1)S(1)}, u32[]{:S(2)}, u32[]{:S(2)}) collective-permute-start(bf16[128,1024]{1,0:T(8,128)(2,1)S(1)} %collective-permute-done.24), channel_id=1, source_target_pairs={{8,0},{16,8},{24,16},{28,24},{20,28},{12,20},{4,12},{0,4},{9,1},{1... | collective-permute-start | bytes 786440 | tf_op jit(solution)/shard_map/ppermute | solution.py:60
  64.1 7.9 %collective-permute-start.27 = (bf16[128,1024]{1,0:T(8,128)(2,1)S(1)}, bf16[128,1024]{1,0:T(8,128)(2,1)S(1)}, u32[]{:S(2)}, u32[]{:S(2)}) collective-permute-start(bf16[128,1024]{1,0:T(8,128)(2,1)S(1)} %collective-permute-done.25), channel_id=1, source_target_pairs={{0,8},{8,16},{16,24},{24,28},{28,20},{20,12},{12,4},{4,0},{1,9},{9... | collective-permute-start | bytes 786440 | tf_op jit(solution)/shard_map/ppermute | solution.py:59
  66.1 8.2 %collective-permute-start.28 = (bf16[128,1024]{1,0:T(8,128)(2,1)S(1)}, bf16[128,1024]{1,0:T(8,128)(2,1)S(1)}, u32[]{:S(2)}, u32[]{:S(2)}) collective-permute-start(bf16[128,1024]{1,0:T(8,128)(2,1)S(1)} %collective-permute-done.26), channel_id=1, source_target_pairs={{8,0},{16,8},{24,16},{28,24},{20,28},{12,20},{4,12},{0,4},{9,1},{1... | collective-permute-start | bytes 786440 | tf_op jit(solution)/shard_map/ppermute | solution.py:60
  72.0 9.4 %collective-permute-start.29 = (bf16[128,1024]{1,0:T(8,128)(2,1)S(1)}, bf16[128,1024]{1,0:T(8,128)(2,1)S(1)}, u32[]{:S(2)}, u32[]{:S(2)}) collective-permute-start(bf16[128,1024]{1,0:T(8,128)(2,1)S(1)} %collective-permute-done.27), channel_id=1, source_target_pairs={{0,8},{8,16},{16,24},{24,28},{28,20},{20,12},{12,4},{4,0},{1,9},{9... | collective-permute-start | bytes 786440 | tf_op jit(solution)/shard_map/ppermute | solution.py:59
  74.3 9.1 %collective-permute-start.30 = (bf16[128,1024]{1,0:T(8,128)(2,1)S(1)}, bf16[128,1024]{1,0:T(8,128)(2,1)S(1)}, u32[]{:S(2)}, u32[]{:S(2)}) collective-permute-start(bf16[128,1024]{1,0:T(8,128)(2,1)S(1)} %collective-permute-done.28), channel_id=1, source_target_pairs={{8,0},{16,8},{24,16},{28,24},{20,28},{12,20},{4,12},{0,4},{9,1},{1... | collective-permute-start | bytes 786440 | tf_op jit(solution)/shard_map/ppermute | solution.py:60
  81.4 8.4 %collective-permute-start.31 = (bf16[128,1024]{1,0:T(8,128)(2,1)S(1)}, bf16[128,1024]{1,0:T(8,128)(2,1)S(1)}, u32[]{:S(2)}, u32[]{:S(2)}) collective-permute-start(bf16[128,1024]{1,0:T(8,128)(2,1)S(1)} %collective-permute-done.29), channel_id=1, source_target_pairs={{0,8},{8,16},{16,24},{24,28},{28,20},{20,12},{12,4},{4,0},{1,9},{9... | collective-permute-start | bytes 786440 | tf_op jit(solution)/shard_map/ppermute | solution.py:59
  83.4 8.4 %collective-permute-start.32 = (bf16[128,1024]{1,0:T(8,128)(2,1)S(1)}, bf16[128,1024]{1,0:T(8,128)(2,1)S(1)}, u32[]{:S(2)}, u32[]{:S(2)}) collective-permute-start(bf16[128,1024]{1,0:T(8,128)(2,1)S(1)} %collective-permute-done.30), channel_id=1, source_target_pairs={{8,0},{16,8},{24,16},{28,24},{20,28},{12,20},{4,12},{0,4},{9,1},{1... | collective-permute-start | bytes 786440 | tf_op jit(solution)/shard_map/ppermute | solution.py:60
  89.8 73.4 %collective-permute-start.33 = (bf16[128,1024]{1,0:T(8,128)(2,1)S(1)}, bf16[128,1024]{1,0:T(8,128)(2,1)}, u32[]{:S(2)}, u32[]{:S(2)}) collective-permute-start(bf16[128,1024]{1,0:T(8,128)(2,1)S(1)} %collective-permute-done.31), channel_id=1, source_target_pairs={{0,8},{8,16},{16,24},{24,28},{28,20},{20,12},{12,4},{4,0},{1,9},{9... | collective-permute-start | bytes 786440 | tf_op jit(solution)/shard_map/ppermute | solution.py:59
  91.8 75.7 %collective-permute-start.34 = (bf16[128,1024]{1,0:T(8,128)(2,1)S(1)}, bf16[128,1024]{1,0:T(8,128)(2,1)S(1)}, u32[]{:S(2)}, u32[]{:S(2)}) collective-permute-start(bf16[128,1024]{1,0:T(8,128)(2,1)S(1)} %collective-permute-done.32), channel_id=1, source_target_pairs={{8,0},{16,8},{24,16},{28,24},{20,28},{12,20},{4,12},{0,4},{9,1},{1... | collective-permute-start | bytes 786440 | tf_op jit(solution)/shard_map/ppermute | solution.py:60
  93.4 1.0 copy-start.1
  97.9 6.5 %collective-permute-start.7 = (bf16[130,768]{1,0:T(8,128)(2,1)S(1)}, bf16[130,768]{1,0:T(8,128)(2,1)S(1)}, u32[]{:S(2)}, u32[]{:S(2)}) collective-permute-start(bf16[130,768]{1,0:T(8,128)(2,1)S(1)} %convolution_convert_fusion.1), channel_id=1, source_target_pairs={{8,0},{16,8},{24,16},{28,24},{20,28},{12,20},{4,12},{0,4},{9,1},{1... | collective-permute-start | bytes 599048 | tf_op jit(solution)/shard_map/ppermute | solution.py:81
  101.3 6.4 %collective-permute-start = (bf16[130,768]{1,0:T(8,128)(2,1)S(1)}, bf16[130,768]{1,0:T(8,128)(2,1)S(1)}, u32[]{:S(2)}, u32[]{:S(2)}) collective-permute-start(bf16[130,768]{1,0:T(8,128)(2,1)S(1)} %convolution_convert_fusion.2), channel_id=1, source_target_pairs={{0,8},{8,16},{16,24},{24,28},{28,20},{20,12},{12,4},{4,0},{1,9},{9... | collective-permute-start | bytes 599048 | tf_op jit(solution)/shard_map/ppermute | solution.py:80
  104.6 8.3 %collective-permute-start.8 = (bf16[130,768]{1,0:T(8,128)(2,1)S(1)}, bf16[130,768]{1,0:T(8,128)(2,1)S(1)}, u32[]{:S(2)}, u32[]{:S(2)}) collective-permute-start(bf16[130,768]{1,0:T(8,128)(2,1)S(1)} %add_convert_fusion.6), channel_id=1, source_target_pairs={{8,0},{16,8},{24,16},{28,24},{20,28},{12,20},{4,12},{0,4},{9,1},{1... | collective-permute-start | bytes 599048 | tf_op jit(solution)/shard_map/ppermute | solution.py:81
  108.0 7.7 %collective-permute-start.1 = (bf16[130,768]{1,0:T(8,128)(2,1)S(1)}, bf16[130,768]{1,0:T(8,128)(2,1)S(1)}, u32[]{:S(2)}, u32[]{:S(2)}) collective-permute-start(bf16[130,768]{1,0:T(8,128)(2,1)S(1)} %add_convert_fusion.13), channel_id=1, source_target_pairs={{0,8},{8,16},{16,24},{24,28},{28,20},{20,12},{12,4},{4,0},{1,9},{9... | collective-permute-start | bytes 599048 | tf_op jit(solution)/shard_map/ppermute | solution.py:80
  113.0 7.4 %collective-permute-start.9 = (bf16[130,768]{1,0:T(8,128)(2,1)S(1)}, bf16[130,768]{1,0:T(8,128)(2,1)S(1)}, u32[]{:S(2)}, u32[]{:S(2)}) collective-permute-start(bf16[130,768]{1,0:T(8,128)(2,1)S(1)} %add_convert_fusion.5), channel_id=1, source_target_pairs={{8,0},{16,8},{24,16},{28,24},{20,28},{12,20},{4,12},{0,4},{9,1},{1... | collective-permute-start | bytes 599048 | tf_op jit(solution)/shard_map/ppermute | solution.py:81
  115.8 7.7 %collective-permute-start.2 = (bf16[130,768]{1,0:T(8,128)(2,1)S(1)}, bf16[130,768]{1,0:T(8,128)(2,1)S(1)}, u32[]{:S(2)}, u32[]{:S(2)}) collective-permute-start(bf16[130,768]{1,0:T(8,128)(2,1)S(1)} %add_convert_fusion.12), channel_id=1, source_target_pairs={{0,8},{8,16},{16,24},{24,28},{28,20},{20,12},{12,4},{4,0},{1,9},{9... | collective-permute-start | bytes 599048 | tf_op jit(solution)/shard_map/ppermute | solution.py:80
  120.4 6.5 %collective-permute-start.10 = (bf16[130,768]{1,0:T(8,128)(2,1)S(1)}, bf16[130,768]{1,0:T(8,128)(2,1)S(1)}, u32[]{:S(2)}, u32[]{:S(2)}) collective-permute-start(bf16[130,768]{1,0:T(8,128)(2,1)S(1)} %add_convert_fusion.4), channel_id=1, source_target_pairs={{8,0},{16,8},{24,16},{28,24},{20,28},{12,20},{4,12},{0,4},{9,1},{1... | collective-permute-start | bytes 599048 | tf_op jit(solution)/shard_map/ppermute | solution.py:81
  123.5 6.7 %collective-permute-start.3 = (bf16[130,768]{1,0:T(8,128)(2,1)S(1)}, bf16[130,768]{1,0:T(8,128)(2,1)S(1)}, u32[]{:S(2)}, u32[]{:S(2)}) collective-permute-start(bf16[130,768]{1,0:T(8,128)(2,1)S(1)} %add_convert_fusion.11), channel_id=1, source_target_pairs={{0,8},{8,16},{16,24},{24,28},{28,20},{20,12},{12,4},{4,0},{1,9},{9... | collective-permute-start | bytes 599048 | tf_op jit(solution)/shard_map/ppermute | solution.py:80
  127.0 5.9 %collective-permute-start.11 = (bf16[130,768]{1,0:T(8,128)(2,1)S(1)}, bf16[130,768]{1,0:T(8,128)(2,1)S(1)}, u32[]{:S(2)}, u32[]{:S(2)}) collective-permute-start(bf16[130,768]{1,0:T(8,128)(2,1)S(1)} %add_convert_fusion.3), channel_id=1, source_target_pairs={{8,0},{16,8},{24,16},{28,24},{20,28},{12,20},{4,12},{0,4},{9,1},{1... | collective-permute-start | bytes 599048 | tf_op jit(solution)/shard_map/ppermute | solution.py:81
  130.3 6.0 %collective-permute-start.4 = (bf16[130,768]{1,0:T(8,128)(2,1)S(1)}, bf16[130,768]{1,0:T(8,128)(2,1)S(1)}, u32[]{:S(2)}, u32[]{:S(2)}) collective-permute-start(bf16[130,768]{1,0:T(8,128)(2,1)S(1)} %add_convert_fusion.10), channel_id=1, source_target_pairs={{0,8},{8,16},{16,24},{24,28},{28,20},{20,12},{12,4},{4,0},{1,9},{9... | collective-permute-start | bytes 599048 | tf_op jit(solution)/shard_map/ppermute | solution.py:80
  132.9 5.9 %collective-permute-start.12 = (bf16[130,768]{1,0:T(8,128)(2,1)S(1)}, bf16[130,768]{1,0:T(8,128)(2,1)S(1)}, u32[]{:S(2)}, u32[]{:S(2)}) collective-permute-start(bf16[130,768]{1,0:T(8,128)(2,1)S(1)} %add_convert_fusion.2), channel_id=1, source_target_pairs={{8,0},{16,8},{24,16},{28,24},{20,28},{12,20},{4,12},{0,4},{9,1},{1... | collective-permute-start | bytes 599048 | tf_op jit(solution)/shard_map/ppermute | solution.py:81
  136.4 5.9 %collective-permute-start.5 = (bf16[130,768]{1,0:T(8,128)(2,1)S(1)}, bf16[130,768]{1,0:T(8,128)(2,1)S(1)}, u32[]{:S(2)}, u32[]{:S(2)}) collective-permute-start(bf16[130,768]{1,0:T(8,128)(2,1)S(1)} %add_convert_fusion.9), channel_id=1, source_target_pairs={{0,8},{8,16},{16,24},{24,28},{28,20},{20,12},{12,4},{4,0},{1,9},{9... | collective-permute-start | bytes 599048 | tf_op jit(solution)/shard_map/ppermute | solution.py:80
  138.8 5.9 %collective-permute-start.13 = (bf16[130,768]{1,0:T(8,128)(2,1)S(1)}, bf16[130,768]{1,0:T(8,128)(2,1)S(1)}, u32[]{:S(2)}, u32[]{:S(2)}) collective-permute-start(bf16[130,768]{1,0:T(8,128)(2,1)S(1)} %add_convert_fusion.1), channel_id=1, source_target_pairs={{8,0},{16,8},{24,16},{28,24},{20,28},{12,20},{4,12},{0,4},{9,1},{1... | collective-permute-start | bytes 599048 | tf_op jit(solution)/shard_map/ppermute | solution.py:81
  142.3 6.0 %collective-permute-start.6 = (bf16[130,768]{1,0:T(8,128)(2,1)S(1)}, bf16[130,768]{1,0:T(8,128)(2,1)S(1)}, u32[]{:S(2)}, u32[]{:S(2)}) collective-permute-start(bf16[130,768]{1,0:T(8,128)(2,1)S(1)} %add_convert_fusion.8), channel_id=1, source_target_pairs={{0,8},{8,16},{16,24},{24,28},{28,20},{20,12},{12,4},{4,0},{1,9},{9... | collective-permute-start | bytes 599048 | tf_op jit(solution)/shard_map/ppermute | solution.py:80
  155.5 2.0 %copy-start = (f32[128,8192]{1,0:T(8,128)}, f32[128,8192]{1,0:T(8,128)S(1)}, u32[]{:S(2)}) copy-start(f32[128,8192]{1,0:T(8,128)S(1)} %fusion.2) | copy-start | bytes 12582916
  157.6 12.4 %collective-permute-start.20 = (f32[16,512]{1,0:T(8,128)S(1)}, f32[16,512]{1,0:T(8,128)S(1)}, u32[]{:S(2)}, u32[]{:S(2)}) collective-permute-start(f32[16,512]{1,0:T(8,128)S(1)} %exponential_multiply_fusion.1), channel_id=1, source_target_pairs={{0,28},{1,29},{2,30},{3,31}} | collective-permute-start | bytes 98312 | tf_op jit(solution)/shard_map/ppermute | solution.py:28
  161.9 9.4 %collective-permute-start.19 = (f32[16,512]{1,0:T(8,128)S(1)}, f32[16,512]{1,0:T(8,128)S(1)}, u32[]{:S(2)}, u32[]{:S(2)}) collective-permute-start(f32[16,512]{1,0:T(8,128)S(1)} %exponential_multiply_fusion.1), channel_id=1, source_target_pairs={{0,24},{4,28},{1,25},{5,29},{2,26},{6,30},{3,27},{7,31}} | collective-permute-start | bytes 98312 | tf_op jit(solution)/shard_map/ppermute | solution.py:28
  164.9 15.9 %collective-permute-start.18 = (f32[16,512]{1,0:T(8,128)S(1)}, f32[16,512]{1,0:T(8,128)S(1)}, u32[]{:S(2)}, u32[]{:S(2)}) collective-permute-start(f32[16,512]{1,0:T(8,128)S(1)} %exponential_multiply_fusion.1), channel_id=1, source_target_pairs={{0,20},{4,24},{8,28},{1,21},{5,25},{9,29},{2,22},{6,26},{10,30},{3... | collective-permute-start | bytes 98312 | tf_op jit(solution)/shard_map/ppermute | solution.py:28
  166.2 14.6 %collective-permute-start.17 = (f32[16,512]{1,0:T(8,128)S(1)}, f32[16,512]{1,0:T(8,128)S(1)}, u32[]{:S(2)}, u32[]{:S(2)}) collective-permute-start(f32[16,512]{1,0:T(8,128)S(1)} %exponential_multiply_fusion.1), channel_id=1, source_target_pairs={{0,16},{4,20},{8,24},{12,28},{1,17},{5,21},{9,25},{13,29},{2,18},{... | collective-permute-start | bytes 98312 | tf_op jit(solution)/shard_map/ppermute | solution.py:28
  167.5 13.3 %collective-permute-start.16 = (f32[16,512]{1,0:T(8,128)S(1)}, f32[16,512]{1,0:T(8,128)S(1)}, u32[]{:S(2)}, u32[]{:S(2)}) collective-permute-start(f32[16,512]{1,0:T(8,128)S(1)} %exponential_multiply_fusion.1), channel_id=1, source_target_pairs={{0,12},{4,16},{8,20},{12,24},{16,28},{1,13},{5,17},{9,21},{13,25},... | collective-permute-start | bytes 98312 | tf_op jit(solution)/shard_map/ppermute | solution.py:28
  170.0 10.9 %collective-permute-start.15 = (f32[16,512]{1,0:T(8,128)S(1)}, f32[16,512]{1,0:T(8,128)S(1)}, u32[]{:S(2)}, u32[]{:S(2)}) collective-permute-start(f32[16,512]{1,0:T(8,128)S(1)} %exponential_multiply_fusion.1), channel_id=1, source_target_pairs={{0,8},{4,12},{8,16},{12,20},{16,24},{20,28},{1,9},{5,13},{9,17},{1... | collective-permute-start | bytes 98312 | tf_op jit(solution)/shard_map/ppermute | solution.py:28
  171.3 9.6 %collective-permute-start.14 = (f32[16,512]{1,0:T(8,128)S(1)}, f32[16,512]{1,0:T(8,128)S(1)}, u32[]{:S(2)}, u32[]{:S(2)}) collective-permute-start(f32[16,512]{1,0:T(8,128)S(1)} %exponential_multiply_fusion.1), channel_id=1, source_target_pairs={{0,4},{4,8},{8,12},{12,16},{16,20},{20,24},{24,28},{1,5},{5,9},{9,... | collective-permute-start | bytes 98312 | tf_op jit(solution)/shard_map/ppermute | solution.py:28
  175.4 5.5 %copy-start.5 = (f32[16,512]{1,0:T(8,128)S(1)}, f32[16,512]{1,0:T(8,128)}, u32[]{:S(2)}) copy-start(f32[16,512]{1,0:T(8,128)} %param.23) | copy-start | bytes 98308
  180.8 1.6 copy-start.9

commit v5 on v4

--- a/solution.py
+++ b/solution.py
@@ -41,49 +41,6 @@
     return list(range(0, count, 2)) + list(range(count - 1, 0, -2))
 
 
-def ring_contract(pieces, consume, acc):
-    count = lax.axis_size("ctx")
-    ring = ring_order(count)
-    place = [0] * count
-    for pos, dev in enumerate(ring):
-        place[dev] = pos
-    fwd = [(ring[k], ring[(k + 1) % count]) for k in range(count)]
-    bwd = [(ring[(k + 1) % count], ring[k]) for k in range(count)]
-    me = lax.axis_index("ctx")
-    my_pos = jnp.array(place, jnp.int32)[me]
-    ring_arr = jnp.array(ring, jnp.int32)
-    ups = tuple(p[0] for p in pieces)
-    lows = tuple(p[1] for p in pieces)
-    acc = consume(acc, me, ups, lows, me)
-    for step in range(1, count):
-        ups = lax.ppermute(ups, "ctx", perm=fwd)
-        lows = lax.ppermute(lows, "ctx", perm=bwd)
-        src_up = ring_arr[(my_pos - step) % count]
-        src_low = ring_arr[(my_pos + step) % count]
-        acc = consume(acc, src_up, ups, lows, src_low)
-    return acc
-
-
-def ring_reduce_scatter(piece, count):
-    ring = ring_order(count)
-    place = [0] * count
-    for pos, dev in enumerate(ring):
-        place[dev] = pos
-    fwd = [(ring[k], ring[(k + 1) % count]) for k in range(count)]
-    bwd = [(ring[(k + 1) % count], ring[k]) for k in range(count)]
-    me = lax.axis_index("ctx")
-    my_pos = jnp.array(place, jnp.int32)[me]
-    ring_arr = jnp.array(ring, jnp.int32)
-    up = piece(ring_arr[(my_pos - 1) % count], 0)
-    down = piece(ring_arr[(my_pos + 1) % count], 1)
-    for step in range(1, count):
-        up = lax.ppermute(up.astype(jnp.bfloat16), "ctx", perm=fwd).astype(jnp.float32)
-        down = lax.ppermute(down.astype(jnp.bfloat16), "ctx", perm=bwd).astype(jnp.float32)
-        up = up + piece(ring_arr[(my_pos - step - 1) % count], 0)
-        down = down + piece(ring_arr[(my_pos + step + 1) % count], 1)
-    return up, down
-
-
 def body(
     tokens,
     w_query,
@@ -110,7 +67,36 @@
         rows = lax.dynamic_slice_in_dim(columns, dest * length, length + 2, 0)
         return jnp.dot(rows, halves[side], preferred_element_type=jnp.float32)
 
-    up, down = ring_reduce_scatter(piece, ctx_count)
+    ring = ring_order(ctx_count)
+    place = [0] * ctx_count
+    for pos, dev in enumerate(ring):
+        place[dev] = pos
+    fwd = [(ring[k], ring[(k + 1) % ctx_count]) for k in range(ctx_count)]
+    bwd = [(ring[(k + 1) % ctx_count], ring[k]) for k in range(ctx_count)]
+    me = lax.axis_index("ctx")
+    my_pos = jnp.array(place, jnp.int32)[me]
+    ring_arr = jnp.array(ring, jnp.int32)
+    c_chunk = w_out.shape[0]
+    c_half = c_chunk // 2
+    w_up, w_low, columns = lax.optimization_barrier((w_out[:c_half], w_out[c_half:], columns))
+    w_rows = jnp.zeros((2 * ctx_count, c_half, w_out.shape[1]), w_out.dtype)
+    w_rows = lax.dynamic_update_slice_in_dim(w_rows, w_up[None], me * 2, 0)
+    w_rows = lax.dynamic_update_slice_in_dim(w_rows, w_low[None], me * 2 + 1, 0)
+    up = piece(ring_arr[(my_pos - 1) % ctx_count], 0)
+    down = piece(ring_arr[(my_pos + 1) % ctx_count], 1)
+    for step in range(1, ctx_count):
+        sent = lax.optimization_barrier(
+            (up.astype(jnp.bfloat16), down.astype(jnp.bfloat16), w_up, w_low)
+        )
+        up, w_up = lax.ppermute((sent[0], sent[2]), "ctx", perm=fwd)
+        down, w_low = lax.ppermute((sent[1], sent[3]), "ctx", perm=bwd)
+        src_up = ring_arr[(my_pos - step) % ctx_count]
+        src_low = ring_arr[(my_pos + step) % ctx_count]
+        w_rows = lax.dynamic_update_slice_in_dim(w_rows, w_up[None], src_up * 2, 0)
+        w_rows = lax.dynamic_update_slice_in_dim(w_rows, w_low[None], src_low * 2 + 1, 0)
+        up = up.astype(jnp.float32) + piece(ring_arr[(my_pos - step - 1) % ctx_count], 0)
+        down = down.astype(jnp.float32) + piece(ring_arr[(my_pos + step + 1) % ctx_count], 1)
+
     projected = jnp.concatenate([up, down], axis=1).astype(jnp.bfloat16).astype(jnp.float32)
     queries = projected[:, :width]
     keys_proj = projected[:, width : 2 * width]
@@ -123,16 +109,7 @@
     mixed = mixed.astype(jnp.bfloat16)
     gated = (gate.astype(jnp.float32) * mixed.astype(jnp.float32)).astype(jnp.bfloat16)
     features = lax.all_gather(gated, "tp", axis=1, tiled=True)
-    c_chunk = w_out.shape[0]
-    c_half = c_chunk // 2
-
-    def place_out(acc, src_up, ups, lows, src_low):
-        acc = lax.dynamic_update_slice_in_dim(acc, ups[0][None], src_up * 2, 0)
-        return lax.dynamic_update_slice_in_dim(acc, lows[0][None], src_low * 2 + 1, 0)
-
-    blank = jnp.zeros((2 * ctx_count, c_half, w_out.shape[1]), w_out.dtype)
-    w_full = ring_contract([(w_out[:c_half], w_out[c_half:])], place_out, blank)
-    w_full = w_full.reshape(ctx_count * c_chunk, w_out.shape[1])
+    w_full = w_rows.reshape(ctx_count * c_chunk, w_out.shape[1])
     result = jnp.dot(features, w_full, preferred_element_type=jnp.float32)
     return result.astype(jnp.bfloat16)
 

time: 194 us -> 172 us (0.89)
  local copies, waits for them, and re-layouts: 34.7 us -> 21.3 us
  starting transfers between devices: 52 us -> 48.7 us
  waiting for transfers between devices: 53.8 us -> 50.8 us
  matrix products: 11 us -> 8.84 us
    dynamic_update_slice x16, local copies, waits for them, and re-layouts: 13.6 us -> 1.8 us  [the longest x7 0.89 us: body(): lax.dynamic_update_slice_in_dim(w_rows, w_low[None], src_low * 2 + 1, 0)]
    ppermute x28, waiting for transfers between devices: 53.8 us -> 50.7 us  [the longest x14 30.6 us: body(): up, w_up = lax.ppermute((sent[0], sent[2]), 'ctx', perm=fwd)]
    ppermute x7, starting transfers between devices: 15.3 us -> 12.6 us  [modal_long_conv(): lax.ppermute(end_state, 'ctx', perm=[(i, i + shift) for i in range(ctx_co...]
    dot_general x1, matrix products: 3.61 us -> 1.45 us  [body(): result = jnp.dot(features, w_full, preferred_element_type=jnp.float32)]
    broadcast_in_dim x1, local copies, waits for them, and re-layouts: 2.55 us -> 0.52 us  [body(): w_rows = jnp.zeros((2 * ctx_count, c_half, w_out.shape[1]), w_out.dtype)]
    unnamed x26 -> x30, local copies, waits for them, and re-layouts: 14.2 us -> 14.2 us
  transfers between devices with their start and end apart: 36 -> 36, of which waited for: 19 -> 25; matrix products, arithmetic and copies ran while one was open for 20% -> 9% of each run, Pallas kernels for 0% -> 0%
where the time goes in v5:
time: 172 us; the launch traced here: 171 us
  waiting for transfers between devices  50.8 us (30%)
  starting transfers between devices  48.7 us (28%)
  between operations  30.4 us (18%)
  local copies, waits for them, and re-layouts  21.3 us (12%)
  matrix products  8.84 us (5%)
  blocking collectives  7.17 us (4%)
  other arithmetic  3.96 us (2%)
    ppermute x14, waiting for transfers between devices, body(): up, w_up = lax.ppermute((sent[0], sent[2]), 'ctx', perm=fwd)  30.6 us
    ppermute x14, waiting for transfers between devices, body(): down, w_low = lax.ppermute((sent[1], sent[3]), 'ctx', perm=bwd)  20.2 us
    ppermute x14, starting transfers between devices, body(): up, w_up = lax.ppermute((sent[0], sent[2]), 'ctx', perm=fwd)  17.7 us
    unnamed x30, local copies, waits for them, and re-layouts  14.2 us
    ppermute x7, starting transfers between devices, modal_long_conv(): lax.ppermute(end_state, 'ctx', perm=[(i, i + shift) for i in range(ctx_co...  12.6 us
    ppermute x14, starting transfers between devices, body(): down, w_low = lax.ppermute((sent[1], sent[3]), 'ctx', perm=bwd)  11.1 us
    all_to_all x1, starting transfers between devices, body(): lax.all_to_all(tokens, 'ctx', split_axis=1, concat_axis=0, tiled=True)  7.3 us
    all_gather x1, blocking collectives, body(): features = lax.all_gather(gated, 'tp', axis=1, tiled=True)  7.17 us
  transfers between devices with their start and end apart: 36, of which 25 were waited for; matrix products, arithmetic and copies ran while one was open for 9% of the time, Pallas kernels for 0%

profile of v5, /device:TPU:0, one launch (start us, length us, event | category | flops | bytes accessed | tf_op | source)
XLA Modules:
  0.0 171.1 jit_solution(9566032040427729120)
XLA Ops:
  0.0 2.3 %copy.14 = bf16[128,4096]{0,1:T(8,128)(2,1)} copy(bf16[128,4096]{1,0:T(8,128)(2,1)} %param.13) | data formatting | bytes 2097152 | tf_op args[0]
  2.4 7.3 %all-to-all-start = ((bf16[128,8,512]{0,2,1:T(8,128)(2,1)}), bf16[128,8,512]{0,2,1:T(8,128)(2,1)S(1)}, u32[]{:S(2)}, u32[]{:S(2)}) async-start(bf16[128,8,512]{0,2,1:T(8,128)(2,1)} %bitcast.1), calls=%async_computation | async-start | bytes 2097152 | tf_op jit(solution)/shard_map/all_to_all | solution.py:60
  40.9 1.3 pad_maximum_fusion.1
  44.3 1.5 copy.15
  48.3 2.1 %collective-permute-start = (bf16[130,768]{1,0:T(8,128)(2,1)S(1)}, bf16[130,768]{1,0:T(8,128)(2,1)S(1)}, u32[]{:S(2)}, u32[]{:S(2)}) collective-permute-start(bf16[130,768]{1,0:T(8,128)(2,1)S(1)} %convolution_convert_fusion.2), channel_id=1, source_target_pairs={{0,8},{8,16},{16,24},{24,28},{28,20},{20,12},{12,4},{4,0},{1,9},{9... | collective-permute-start | bytes 599048 | tf_op jit(solution)/shard_map/ppermute | solution.py:91
  50.5 2.0 %collective-permute-start.2 = (bf16[128,1024]{1,0:T(8,128)(2,1)S(1)}, bf16[128,1024]{1,0:T(8,128)(2,1)S(1)}, u32[]{:S(2)}, u32[]{:S(2)}) collective-permute-start(bf16[128,1024]{1,0:T(8,128)(2,1)S(1)} %get-tuple-element.41), channel_id=1, source_target_pairs={{0,8},{8,16},{16,24},{24,28},{28,20},{20,12},{12,4},{4,0},{1,9},{9... | collective-permute-start | bytes 786440 | tf_op jit(solution)/shard_map/ppermute | solution.py:91
  54.8 1.7 collective-permute-done
  56.8 1.7 %collective-permute-done.1 = bf16[130,768]{1,0:T(8,128)(2,1)S(1)} collective-permute-done((bf16[130,768]{1,0:T(8,128)(2,1)S(1)}, bf16[130,768]{1,0:T(8,128)(2,1)S(1)}, u32[]{:S(2)}, u32[]{:S(2)}) %collective-permute-start.1) | collective-permute-done | bytes 199712 | tf_op jit(solution)/shard_map/ppermute | solution.py:92
  58.8 1.8 %collective-permute-done.2 = bf16[128,1024]{1,0:T(8,128)(2,1)S(1)} collective-permute-done((bf16[128,1024]{1,0:T(8,128)(2,1)S(1)}, bf16[128,1024]{1,0:T(8,128)(2,1)S(1)}, u32[]{:S(2)}, u32[]{:S(2)}) %collective-permute-start.2) | collective-permute-done | bytes 262176 | tf_op jit(solution)/shard_map/ppermute | solution.py:91
  60.6 1.5 collective-permute-done.3
  62.1 1.5 collective-permute-start.4
  64.1 1.5 collective-permute-start.6
  66.2 3.8 %collective-permute-done.4 = bf16[130,768]{1,0:T(8,128)(2,1)S(1)} collective-permute-done((bf16[130,768]{1,0:T(8,128)(2,1)S(1)}, bf16[130,768]{1,0:T(8,128)(2,1)S(1)}, u32[]{:S(2)}, u32[]{:S(2)}) %collective-permute-start.4) | collective-permute-done | bytes 199712 | tf_op jit(solution)/shard_map/ppermute | solution.py:91
  71.3 1.6 collective-permute-done.6
  74.0 1.5 collective-permute-start.8
  76.1 1.5 collective-permute-start.10
  78.2 2.6 %collective-permute-done.8 = bf16[130,768]{1,0:T(8,128)(2,1)S(1)} collective-permute-done((bf16[130,768]{1,0:T(8,128)(2,1)S(1)}, bf16[130,768]{1,0:T(8,128)(2,1)S(1)}, u32[]{:S(2)}, u32[]{:S(2)}) %collective-permute-start.8) | collective-permute-done | bytes 199712 | tf_op jit(solution)/shard_map/ppermute | solution.py:91
  82.0 2.0 %collective-permute-done.10 = bf16[128,1024]{1,0:T(8,128)(2,1)S(1)} collective-permute-done((bf16[128,1024]{1,0:T(8,128)(2,1)S(1)}, bf16[128,1024]{1,0:T(8,128)(2,1)S(1)}, u32[]{:S(2)}, u32[]{:S(2)}) %collective-permute-start.10) | collective-permute-done | bytes 262176 | tf_op jit(solution)/shard_map/ppermute | solution.py:91
  84.1 1.4 collective-permute-done.11
  85.5 1.8 %collective-permute-start.12 = (bf16[130,768]{1,0:T(8,128)(2,1)S(1)}, bf16[130,768]{1,0:T(8,128)(2,1)S(1)}, u32[]{:S(2)}, u32[]{:S(2)}) collective-permute-start(bf16[130,768]{1,0:T(8,128)(2,1)S(1)} %add_convert_fusion.9), channel_id=1, source_target_pairs={{0,8},{8,16},{16,24},{24,28},{28,20},{20,12},{12,4},{4,0},{1,9},{9... | collective-permute-start | bytes 599048 | tf_op jit(solution)/shard_map/ppermute | solution.py:91
  87.5 1.8 %collective-permute-start.14 = (bf16[128,1024]{1,0:T(8,128)(2,1)S(1)}, bf16[128,1024]{1,0:T(8,128)(2,1)S(1)}, u32[]{:S(2)}, u32[]{:S(2)}) collective-permute-start(bf16[128,1024]{1,0:T(8,128)(2,1)S(1)} %collective-permute-done.10), channel_id=1, source_target_pairs={{0,8},{8,16},{16,24},{24,28},{28,20},{20,12},{12,4},{4,0},{1,9},{9... | collective-permute-start | bytes 786440 | tf_op jit(solution)/shard_map/ppermute | solution.py:91
  89.6 1.7 collective-permute-done.12
  91.3 1.8 %collective-permute-done.13 = bf16[130,768]{1,0:T(8,128)(2,1)S(1)} collective-permute-done((bf16[130,768]{1,0:T(8,128)(2,1)S(1)}, bf16[130,768]{1,0:T(8,128)(2,1)S(1)}, u32[]{:S(2)}, u32[]{:S(2)}) %collective-permute-start.13) | collective-permute-done | bytes 199712 | tf_op jit(solution)/shard_map/ppermute | solution.py:92
  93.2 2.4 %collective-permute-done.14 = bf16[128,1024]{1,0:T(8,128)(2,1)S(1)} collective-permute-done((bf16[128,1024]{1,0:T(8,128)(2,1)S(1)}, bf16[128,1024]{1,0:T(8,128)(2,1)S(1)}, u32[]{:S(2)}, u32[]{:S(2)}) %collective-permute-start.14) | collective-permute-done | bytes 262176 | tf_op jit(solution)/shard_map/ppermute | solution.py:91
  95.5 2.5 %collective-permute-done.15 = bf16[128,1024]{1,0:T(8,128)(2,1)S(1)} collective-permute-done((bf16[128,1024]{1,0:T(8,128)(2,1)S(1)}, bf16[128,1024]{1,0:T(8,128)(2,1)S(1)}, u32[]{:S(2)}, u32[]{:S(2)}) %collective-permute-start.15) | collective-permute-done | bytes 262176 | tf_op jit(solution)/shard_map/ppermute | solution.py:92
  98.1 1.3 collective-permute-start.16
  100.1 1.3 collective-permute-start.18
  102.2 2.1 %collective-permute-done.16 = bf16[130,768]{1,0:T(8,128)(2,1)S(1)} collective-permute-done((bf16[130,768]{1,0:T(8,128)(2,1)S(1)}, bf16[130,768]{1,0:T(8,128)(2,1)S(1)}, u32[]{:S(2)}, u32[]{:S(2)}) %collective-permute-start.16) | collective-permute-done | bytes 199712 | tf_op jit(solution)/shard_map/ppermute | solution.py:91
  104.3 1.8 %collective-permute-done.17 = bf16[130,768]{1,0:T(8,128)(2,1)S(1)} collective-permute-done((bf16[130,768]{1,0:T(8,128)(2,1)S(1)}, bf16[130,768]{1,0:T(8,128)(2,1)S(1)}, u32[]{:S(2)}, u32[]{:S(2)}) %collective-permute-start.17) | collective-permute-done | bytes 199712 | tf_op jit(solution)/shard_map/ppermute | solution.py:92
  106.2 3.7 %collective-permute-done.18 = bf16[128,1024]{1,0:T(8,128)(2,1)S(1)} collective-permute-done((bf16[128,1024]{1,0:T(8,128)(2,1)S(1)}, bf16[128,1024]{1,0:T(8,128)(2,1)S(1)}, u32[]{:S(2)}, u32[]{:S(2)}) %collective-permute-start.18) | collective-permute-done | bytes 262176 | tf_op jit(solution)/shard_map/ppermute | solution.py:91
  109.9 1.9 %collective-permute-done.19 = bf16[128,1024]{1,0:T(8,128)(2,1)S(1)} collective-permute-done((bf16[128,1024]{1,0:T(8,128)(2,1)S(1)}, bf16[128,1024]{1,0:T(8,128)(2,1)S(1)}, u32[]{:S(2)}, u32[]{:S(2)}) %collective-permute-start.19) | collective-permute-done | bytes 262176 | tf_op jit(solution)/shard_map/ppermute | solution.py:92
  111.7 2.0 %collective-permute-start.21 = (bf16[130,768]{1,0:T(8,128)(2,1)S(1)}, bf16[130,768]{1,0:T(8,128)(2,1)S(1)}, u32[]{:S(2)}, u32[]{:S(2)}) collective-permute-start(bf16[130,768]{1,0:T(8,128)(2,1)S(1)} %add_convert_fusion.4), channel_id=1, source_target_pairs={{8,0},{16,8},{24,16},{28,24},{20,28},{12,20},{4,12},{0,4},{9,1},{1... | collective-permute-start | bytes 599048 | tf_op jit(solution)/shard_map/ppermute | solution.py:92
  113.8 2.0 %collective-permute-start.23 = (bf16[128,1024]{1,0:T(8,128)(2,1)S(1)}, bf16[128,1024]{1,0:T(8,128)(2,1)S(1)}, u32[]{:S(2)}, u32[]{:S(2)}) collective-permute-start(bf16[128,1024]{1,0:T(8,128)(2,1)S(1)} %collective-permute-done.19), channel_id=1, source_target_pairs={{8,0},{16,8},{24,16},{28,24},{20,28},{12,20},{4,12},{0,4},{9,1},{1... | collective-permute-start | bytes 786440 | tf_op jit(solution)/shard_map/ppermute | solution.py:92
  115.8 3.1 %collective-permute-done.20 = bf16[130,768]{1,0:T(8,128)(2,1)S(1)} collective-permute-done((bf16[130,768]{1,0:T(8,128)(2,1)S(1)}, bf16[130,768]{1,0:T(8,128)(2,1)S(1)}, u32[]{:S(2)}, u32[]{:S(2)}) %collective-permute-start.20) | collective-permute-done | bytes 199712 | tf_op jit(solution)/shard_map/ppermute | solution.py:91
  119.7 2.9 %collective-permute-done.22 = bf16[128,1024]{1,0:T(8,128)(2,1)S(1)} collective-permute-done((bf16[128,1024]{1,0:T(8,128)(2,1)S(1)}, bf16[128,1024]{1,0:T(8,128)(2,1)S(1)}, u32[]{:S(2)}, u32[]{:S(2)}) %collective-permute-start.22) | collective-permute-done | bytes 262176 | tf_op jit(solution)/shard_map/ppermute | solution.py:91
  123.5 1.4 collective-permute-start.24
  124.9 3.5 %collective-permute-done.25 = bf16[130,768]{1,0:T(8,128)(2,1)S(1)} collective-permute-done((bf16[130,768]{1,0:T(8,128)(2,1)S(1)}, bf16[130,768]{1,0:T(8,128)(2,1)S(1)}, u32[]{:S(2)}, u32[]{:S(2)}) %collective-permute-start.25) | collective-permute-done | bytes 199712 | tf_op jit(solution)/shard_map/ppermute | solution.py:92
  130.4 3.4 %copy.17 = f32[16,8,16,512]{3,1,2,0:T(8,128)S(1)} copy(f32[16,8,16,512]{3,2,1,0:T(8,128)S(1)} %bitcast.130) | data formatting | bytes 8388608
  133.8 2.9 %fusion.2 = f32[128,8192]{1,0:T(8,128)S(1)} fusion(f32[128,8192]{1,0:T(8,128)S(1)} %bitcast.129, f32[8192]{0:T(1024)S(1)} %bitcast.134), kind=kOutput, calls=%fused_computation.3 | convolution fusion | flops 1612726272 | bytes 8421376 | tf_op jit(solution)/shard_map/dot_general | solution.py:22
  136.7 2.0 %copy-done = f32[128,8192]{1,0:T(8,128)} copy-done((f32[128,8192]{1,0:T(8,128)}, f32[128,8192]{1,0:T(8,128)S(1)}, u32[]{:S(2)}) %copy-start) | copy-done | bytes 4194328
  138.8 1.8 %collective-permute-start.32 = (f32[16,512]{1,0:T(8,128)S(1)}, f32[16,512]{1,0:T(8,128)S(1)}, u32[]{:S(2)}, u32[]{:S(2)}) collective-permute-start(f32[16,512]{1,0:T(8,128)S(1)} %exponential_multiply_fusion.1), channel_id=1, source_target_pairs={{0,28},{1,29},{2,30},{3,31}} | collective-permute-start | bytes 98312 | tf_op jit(solution)/shard_map/ppermute | solution.py:28
  145.3 2.5 %collective-permute-start.28 = (f32[16,512]{1,0:T(8,128)S(1)}, f32[16,512]{1,0:T(8,128)S(1)}, u32[]{:S(2)}, u32[]{:S(2)}) collective-permute-start(f32[16,512]{1,0:T(8,128)S(1)} %exponential_multiply_fusion.1), channel_id=1, source_target_pairs={{0,12},{4,16},{8,20},{12,24},{16,28},{1,13},{5,17},{9,21},{13,25},... | collective-permute-start | bytes 98312 | tf_op jit(solution)/shard_map/ppermute | solution.py:28
  149.0 3.2 %collective-permute-start.26 = (f32[16,512]{1,0:T(8,128)S(1)}, f32[16,512]{1,0:T(8,128)S(1)}, u32[]{:S(2)}, u32[]{:S(2)}) collective-permute-start(f32[16,512]{1,0:T(8,128)S(1)} %exponential_multiply_fusion.1), channel_id=1, source_target_pairs={{0,4},{4,8},{8,12},{12,16},{16,20},{20,24},{24,28},{1,5},{5,9},{9,... | collective-permute-start | bytes 98312 | tf_op jit(solution)/shard_map/ppermute | solution.py:28
  153.0 5.4 %copy.18 = f32[16,8,16,512]{3,2,1,0:T(8,128)S(1)} copy(f32[16,8,16,512]{3,1,2,0:T(8,128)} %bitcast.127) | data formatting | bytes 8388608
  158.5 2.0 %collective-permute-start.34 = (bf16[128,1024]{1,0:T(8,128)(2,1)S(1)}, bf16[128,1024]{1,0:T(8,128)(2,1)S(1)}, u32[]{:S(2)}, u32[]{:S(2)}) collective-permute-start(bf16[128,1024]{1,0:T(8,128)(2,1)S(1)} %collective-permute-done.23), channel_id=1, source_target_pairs={{8,0},{16,8},{24,16},{28,24},{20,28},{12,20},{4,12},{0,4},{9,1},{1... | collective-permute-start | bytes 786440 | tf_op jit(solution)/shard_map/ppermute | solution.py:92
  160.6 1.5 fusion.1
  162.4 7.2 %all_gather.3 = bf16[128,2048]{1,0:T(8,128)(2,1)S(1)} all-gather(bf16[128,512]{1,0:T(8,128)(2,1)S(1)} %multiply_convert_fusion), channel_id=1, replica_groups=mesh['ctx'=8,'tp'=4] {'tp'}, dimensions={1}, use_global_device_ids=true | all-gather | bytes 655360 | tf_op jit(solution)/shard_map/all_gather | solution.py:111
  169.7 1.4 convolution_convert_fusion
  (120 shorter events, 27.8 us)
Async XLA Ops:
  0.0 9.7 %copy-start.12 = (s32[8]{0:T(128)S(1)}, s32[8]{0:T(128)}, u32[]{:S(2)}) copy-start(s32[8]{0:T(128)} %constant.275.clone) | copy-start | bytes 100
  0.0 20.9 %copy-start.6 = (s32[8]{0:T(128)S(1)}, s32[8]{0:T(128)}, u32[]{:S(2)}) copy-start(s32[8]{0:T(128)} %constant.276.clone) | copy-start | bytes 100
  0.0 40.6 %copy-start.5 = (f32[16,512]{1,0:T(8,128)S(1)}, f32[16,512]{1,0:T(8,128)}, u32[]{:S(2)}) copy-start(f32[16,512]{1,0:T(8,128)} %param.20) | copy-start | bytes 98308
  0.0 40.8 %copy-start.4 = (bf16[512,512]{1,0:T(8,128)(2,1)S(1)}, bf16[512,512]{1,0:T(8,128)(2,1)}, u32[]{:S(2)}) copy-start(bf16[512,512]{1,0:T(8,128)(2,1)} %param.15) | copy-start | bytes 1572868
  0.0 42.2 %copy-start.8 = (f32[3,512]{1,0:T(4,128)S(1)}, f32[3,512]{1,0:T(4,128)}, u32[]{:S(2)}) copy-start(f32[3,512]{1,0:T(4,128)} %param.19) | copy-start | bytes 18436
  0.0 42.2 %copy-start.9 = (f32[3,512]{1,0:T(4,128)S(1)}, f32[3,512]{1,0:T(4,128)}, u32[]{:S(2)}) copy-start(f32[3,512]{1,0:T(4,128)} %param.18) | copy-start | bytes 18436
  0.0 42.2 %copy-start.10 = (f32[3,512]{1,0:T(4,128)S(1)}, f32[3,512]{1,0:T(4,128)}, u32[]{:S(2)}) copy-start(f32[3,512]{1,0:T(4,128)} %param.17) | copy-start | bytes 18436
  2.4 40.9 %all-to-all-start = ((bf16[128,8,512]{0,2,1:T(8,128)(2,1)}), bf16[128,8,512]{0,2,1:T(8,128)(2,1)S(1)}, u32[]{:S(2)}, u32[]{:S(2)}) async-start(bf16[128,8,512]{0,2,1:T(8,128)(2,1)} %bitcast.1), calls=%async_computation | async-start | bytes 2097152 | tf_op jit(solution)/shard_map/all_to_all | solution.py:60
  48.3 8.1 %collective-permute-start = (bf16[130,768]{1,0:T(8,128)(2,1)S(1)}, bf16[130,768]{1,0:T(8,128)(2,1)S(1)}, u32[]{:S(2)}, u32[]{:S(2)}) collective-permute-start(bf16[130,768]{1,0:T(8,128)(2,1)S(1)} %convolution_convert_fusion.2), channel_id=1, source_target_pairs={{0,8},{8,16},{16,24},{24,28},{28,20},{20,12},{12,4},{4,0},{1,9},{9... | collective-permute-start | bytes 599048 | tf_op jit(solution)/shard_map/ppermute | solution.py:91
  50.4 8.1 %collective-permute-start.1 = (bf16[130,768]{1,0:T(8,128)(2,1)S(1)}, bf16[130,768]{1,0:T(8,128)(2,1)S(1)}, u32[]{:S(2)}, u32[]{:S(2)}) collective-permute-start(bf16[130,768]{1,0:T(8,128)(2,1)S(1)} %convolution_convert_fusion.1), channel_id=1, source_target_pairs={{8,0},{16,8},{24,16},{28,24},{20,28},{12,20},{4,12},{0,4},{9,1},{1... | collective-permute-start | bytes 599048 | tf_op jit(solution)/shard_map/ppermute | solution.py:92
  50.5 10.2 %collective-permute-start.2 = (bf16[128,1024]{1,0:T(8,128)(2,1)S(1)}, bf16[128,1024]{1,0:T(8,128)(2,1)S(1)}, u32[]{:S(2)}, u32[]{:S(2)}) collective-permute-start(bf16[128,1024]{1,0:T(8,128)(2,1)S(1)} %get-tuple-element.41), channel_id=1, source_target_pairs={{0,8},{8,16},{16,24},{24,28},{28,20},{20,12},{12,4},{4,0},{1,9},{9... | collective-permute-start | bytes 786440 | tf_op jit(solution)/shard_map/ppermute | solution.py:91
  52.4 9.7 %collective-permute-start.3 = (bf16[128,1024]{1,0:T(8,128)(2,1)S(1)}, bf16[128,1024]{1,0:T(8,128)(2,1)S(1)}, u32[]{:S(2)}, u32[]{:S(2)}) collective-permute-start(bf16[128,1024]{1,0:T(8,128)(2,1)S(1)} %get-tuple-element.42), channel_id=1, source_target_pairs={{8,0},{16,8},{24,16},{28,24},{20,28},{12,20},{4,12},{0,4},{9,1},{1... | collective-permute-start | bytes 786440 | tf_op jit(solution)/shard_map/ppermute | solution.py:92
  62.1 8.0 %collective-permute-start.4 = (bf16[130,768]{1,0:T(8,128)(2,1)S(1)}, bf16[130,768]{1,0:T(8,128)(2,1)S(1)}, u32[]{:S(2)}, u32[]{:S(2)}) collective-permute-start(bf16[130,768]{1,0:T(8,128)(2,1)S(1)} %add_convert_fusion.13), channel_id=1, source_target_pairs={{0,8},{8,16},{16,24},{24,28},{28,20},{20,12},{12,4},{4,0},{1,9},{9... | collective-permute-start | bytes 599048 | tf_op jit(solution)/shard_map/ppermute | solution.py:91
  63.6 7.7 %collective-permute-start.5 = (bf16[130,768]{1,0:T(8,128)(2,1)S(1)}, bf16[130,768]{1,0:T(8,128)(2,1)S(1)}, u32[]{:S(2)}, u32[]{:S(2)}) collective-permute-start(bf16[130,768]{1,0:T(8,128)(2,1)S(1)} %add_convert_fusion.12), channel_id=1, source_target_pairs={{8,0},{16,8},{24,16},{28,24},{20,28},{12,20},{4,12},{0,4},{9,1},{1... | collective-permute-start | bytes 599048 | tf_op jit(solution)/shard_map/ppermute | solution.py:92
  64.1 8.7 %collective-permute-start.6 = (bf16[128,1024]{1,0:T(8,128)(2,1)S(1)}, bf16[128,1024]{1,0:T(8,128)(2,1)S(1)}, u32[]{:S(2)}, u32[]{:S(2)}) collective-permute-start(bf16[128,1024]{1,0:T(8,128)(2,1)S(1)} %collective-permute-done.2), channel_id=1, source_target_pairs={{0,8},{8,16},{16,24},{24,28},{28,20},{20,12},{12,4},{4,0},{1,9},{9... | collective-permute-start | bytes 786440 | tf_op jit(solution)/shard_map/ppermute | solution.py:91
  65.6 8.4 %collective-permute-start.7 = (bf16[128,1024]{1,0:T(8,128)(2,1)S(1)}, bf16[128,1024]{1,0:T(8,128)(2,1)S(1)}, u32[]{:S(2)}, u32[]{:S(2)}) collective-permute-start(bf16[128,1024]{1,0:T(8,128)(2,1)S(1)} %collective-permute-done.3), channel_id=1, source_target_pairs={{8,0},{16,8},{24,16},{28,24},{20,28},{12,20},{4,12},{0,4},{9,1},{1... | collective-permute-start | bytes 786440 | tf_op jit(solution)/shard_map/ppermute | solution.py:92
  74.0 6.7 %collective-permute-start.8 = (bf16[130,768]{1,0:T(8,128)(2,1)S(1)}, bf16[130,768]{1,0:T(8,128)(2,1)S(1)}, u32[]{:S(2)}, u32[]{:S(2)}) collective-permute-start(bf16[130,768]{1,0:T(8,128)(2,1)S(1)} %add_convert_fusion.11), channel_id=1, source_target_pairs={{0,8},{8,16},{16,24},{24,28},{28,20},{20,12},{12,4},{4,0},{1,9},{9... | collective-permute-start | bytes 599048 | tf_op jit(solution)/shard_map/ppermute | solution.py:91
  75.5 6.5 %collective-permute-start.9 = (bf16[130,768]{1,0:T(8,128)(2,1)S(1)}, bf16[130,768]{1,0:T(8,128)(2,1)S(1)}, u32[]{:S(2)}, u32[]{:S(2)}) collective-permute-start(bf16[130,768]{1,0:T(8,128)(2,1)S(1)} %add_convert_fusion.10), channel_id=1, source_target_pairs={{8,0},{16,8},{24,16},{28,24},{20,28},{12,20},{4,12},{0,4},{9,1},{1... | collective-permute-start | bytes 599048 | tf_op jit(solution)/shard_map/ppermute | solution.py:92
  76.1 8.0 %collective-permute-start.10 = (bf16[128,1024]{1,0:T(8,128)(2,1)S(1)}, bf16[128,1024]{1,0:T(8,128)(2,1)S(1)}, u32[]{:S(2)}, u32[]{:S(2)}) collective-permute-start(bf16[128,1024]{1,0:T(8,128)(2,1)S(1)} %collective-permute-done.6), channel_id=1, source_target_pairs={{0,8},{8,16},{16,24},{24,28},{28,20},{20,12},{12,4},{4,0},{1,9},{9... | collective-permute-start | bytes 786440 | tf_op jit(solution)/shard_map/ppermute | solution.py:91
  77.5 7.9 %collective-permute-start.11 = (bf16[128,1024]{1,0:T(8,128)(2,1)S(1)}, bf16[128,1024]{1,0:T(8,128)(2,1)S(1)}, u32[]{:S(2)}, u32[]{:S(2)}) collective-permute-start(bf16[128,1024]{1,0:T(8,128)(2,1)S(1)} %collective-permute-done.7), channel_id=1, source_target_pairs={{8,0},{16,8},{24,16},{28,24},{20,28},{12,20},{4,12},{0,4},{9,1},{1... | collective-permute-start | bytes 786440 | tf_op jit(solution)/shard_map/ppermute | solution.py:92
  85.5 5.8 %collective-permute-start.12 = (bf16[130,768]{1,0:T(8,128)(2,1)S(1)}, bf16[130,768]{1,0:T(8,128)(2,1)S(1)}, u32[]{:S(2)}, u32[]{:S(2)}) collective-permute-start(bf16[130,768]{1,0:T(8,128)(2,1)S(1)} %add_convert_fusion.9), channel_id=1, source_target_pairs={{0,8},{8,16},{16,24},{24,28},{28,20},{20,12},{12,4},{4,0},{1,9},{9... | collective-permute-start | bytes 599048 | tf_op jit(solution)/shard_map/ppermute | solution.py:91
  87.3 5.8 %collective-permute-start.13 = (bf16[130,768]{1,0:T(8,128)(2,1)S(1)}, bf16[130,768]{1,0:T(8,128)(2,1)S(1)}, u32[]{:S(2)}, u32[]{:S(2)}) collective-permute-start(bf16[130,768]{1,0:T(8,128)(2,1)S(1)} %add_convert_fusion.8), channel_id=1, source_target_pairs={{8,0},{16,8},{24,16},{28,24},{20,28},{12,20},{4,12},{0,4},{9,1},{1... | collective-permute-start | bytes 599048 | tf_op jit(solution)/shard_map/ppermute | solution.py:92
  87.5 8.0 %collective-permute-start.14 = (bf16[128,1024]{1,0:T(8,128)(2,1)S(1)}, bf16[128,1024]{1,0:T(8,128)(2,1)S(1)}, u32[]{:S(2)}, u32[]{:S(2)}) collective-permute-start(bf16[128,1024]{1,0:T(8,128)(2,1)S(1)} %collective-permute-done.10), channel_id=1, source_target_pairs={{0,8},{8,16},{16,24},{24,28},{28,20},{20,12},{12,4},{4,0},{1,9},{9... | collective-permute-start | bytes 786440 | tf_op jit(solution)/shard_map/ppermute | solution.py:91
  89.3 8.7 %collective-permute-start.15 = (bf16[128,1024]{1,0:T(8,128)(2,1)S(1)}, bf16[128,1024]{1,0:T(8,128)(2,1)S(1)}, u32[]{:S(2)}, u32[]{:S(2)}) collective-permute-start(bf16[128,1024]{1,0:T(8,128)(2,1)S(1)} %collective-permute-done.11), channel_id=1, source_target_pairs={{8,0},{16,8},{24,16},{28,24},{20,28},{12,20},{4,12},{0,4},{9,1},{1... | collective-permute-start | bytes 786440 | tf_op jit(solution)/shard_map/ppermute | solution.py:92
  98.1 6.2 %collective-permute-start.16 = (bf16[130,768]{1,0:T(8,128)(2,1)S(1)}, bf16[130,768]{1,0:T(8,128)(2,1)S(1)}, u32[]{:S(2)}, u32[]{:S(2)}) collective-permute-start(bf16[130,768]{1,0:T(8,128)(2,1)S(1)} %add_convert_fusion.7), channel_id=1, source_target_pairs={{0,8},{8,16},{16,24},{24,28},{28,20},{20,12},{12,4},{4,0},{1,9},{9... | collective-permute-start | bytes 599048 | tf_op jit(solution)/shard_map/ppermute | solution.py:91
  99.4 6.8 %collective-permute-start.17 = (bf16[130,768]{1,0:T(8,128)(2,1)S(1)}, bf16[130,768]{1,0:T(8,128)(2,1)S(1)}, u32[]{:S(2)}, u32[]{:S(2)}) collective-permute-start(bf16[130,768]{1,0:T(8,128)(2,1)S(1)} %add_convert_fusion.6), channel_id=1, source_target_pairs={{8,0},{16,8},{24,16},{28,24},{20,28},{12,20},{4,12},{0,4},{9,1},{1... | collective-permute-start | bytes 599048 | tf_op jit(solution)/shard_map/ppermute | solution.py:92
  100.1 9.8 %collective-permute-start.18 = (bf16[128,1024]{1,0:T(8,128)(2,1)S(1)}, bf16[128,1024]{1,0:T(8,128)(2,1)S(1)}, u32[]{:S(2)}, u32[]{:S(2)}) collective-permute-start(bf16[128,1024]{1,0:T(8,128)(2,1)S(1)} %collective-permute-done.14), channel_id=1, source_target_pairs={{0,8},{8,16},{16,24},{24,28},{28,20},{20,12},{12,4},{4,0},{1,9},{9... | collective-permute-start | bytes 786440 | tf_op jit(solution)/shard_map/ppermute | solution.py:91
  101.4 10.4 %collective-permute-start.19 = (bf16[128,1024]{1,0:T(8,128)(2,1)S(1)}, bf16[128,1024]{1,0:T(8,128)(2,1)S(1)}, u32[]{:S(2)}, u32[]{:S(2)}) collective-permute-start(bf16[128,1024]{1,0:T(8,128)(2,1)S(1)} %collective-permute-done.15), channel_id=1, source_target_pairs={{8,0},{16,8},{24,16},{28,24},{20,28},{12,20},{4,12},{0,4},{9,1},{1... | collective-permute-start | bytes 786440 | tf_op jit(solution)/shard_map/ppermute | solution.py:92
  111.7 7.2 %collective-permute-start.20 = (bf16[130,768]{1,0:T(8,128)(2,1)S(1)}, bf16[130,768]{1,0:T(8,128)(2,1)S(1)}, u32[]{:S(2)}, u32[]{:S(2)}) collective-permute-start(bf16[130,768]{1,0:T(8,128)(2,1)S(1)} %add_convert_fusion.5), channel_id=1, source_target_pairs={{0,8},{8,16},{16,24},{24,28},{28,20},{20,12},{12,4},{4,0},{1,9},{9... | collective-permute-start | bytes 599048 | tf_op jit(solution)/shard_map/ppermute | solution.py:91
  111.7 7.9 %collective-permute-start.21 = (bf16[130,768]{1,0:T(8,128)(2,1)S(1)}, bf16[130,768]{1,0:T(8,128)(2,1)S(1)}, u32[]{:S(2)}, u32[]{:S(2)}) collective-permute-start(bf16[130,768]{1,0:T(8,128)(2,1)S(1)} %add_convert_fusion.4), channel_id=1, source_target_pairs={{8,0},{16,8},{24,16},{28,24},{20,28},{12,20},{4,12},{0,4},{9,1},{1... | collective-permute-start | bytes 599048 | tf_op jit(solution)/shard_map/ppermute | solution.py:92
  113.8 8.8 %collective-permute-start.22 = (bf16[128,1024]{1,0:T(8,128)(2,1)S(1)}, bf16[128,1024]{1,0:T(8,128)(2,1)S(1)}, u32[]{:S(2)}, u32[]{:S(2)}) collective-permute-start(bf16[128,1024]{1,0:T(8,128)(2,1)S(1)} %collective-permute-done.18), channel_id=1, source_target_pairs={{0,8},{8,16},{16,24},{24,28},{28,20},{20,12},{12,4},{4,0},{1,9},{9... | collective-permute-start | bytes 786440 | tf_op jit(solution)/shard_map/ppermute | solution.py:91
  113.8 8.8 %collective-permute-start.23 = (bf16[128,1024]{1,0:T(8,128)(2,1)S(1)}, bf16[128,1024]{1,0:T(8,128)(2,1)S(1)}, u32[]{:S(2)}, u32[]{:S(2)}) collective-permute-start(bf16[128,1024]{1,0:T(8,128)(2,1)S(1)} %collective-permute-done.19), channel_id=1, source_target_pairs={{8,0},{16,8},{24,16},{28,24},{20,28},{12,20},{4,12},{0,4},{9,1},{1... | collective-permute-start | bytes 786440 | tf_op jit(solution)/shard_map/ppermute | solution.py:92
  122.6 5.8 %collective-permute-start.25 = (bf16[130,768]{1,0:T(8,128)(2,1)S(1)}, bf16[130,768]{1,0:T(8,128)(2,1)S(1)}, u32[]{:S(2)}, u32[]{:S(2)}) collective-permute-start(bf16[130,768]{1,0:T(8,128)(2,1)S(1)} %add_convert_fusion.2), channel_id=1, source_target_pairs={{8,0},{16,8},{24,16},{28,24},{20,28},{12,20},{4,12},{0,4},{9,1},{1... | collective-permute-start | bytes 599048 | tf_op jit(solution)/shard_map/ppermute | solution.py:92
  123.5 6.9 %copy-start.1 = (bf16[16,128,1024]{2,1,0:T(8,128)(2,1)}, bf16[16,128,1024]{2,1,0:T(8,128)(2,1)S(1)}, u32[]{:S(2)}) copy-start(bf16[16,128,1024]{2,1,0:T(8,128)(2,1)S(1)} %bitcast_dynamic-update-slice_fusion.4) | copy-start | bytes 12582916
  123.5 6.0 %collective-permute-start.24 = (bf16[130,768]{1,0:T(8,128)(2,1)S(1)}, bf16[130,768]{1,0:T(8,128)(2,1)S(1)}, u32[]{:S(2)}, u32[]{:S(2)}) collective-permute-start(bf16[130,768]{1,0:T(8,128)(2,1)S(1)} %add_convert_fusion.3), channel_id=1, source_target_pairs={{0,8},{8,16},{16,24},{24,28},{28,20},{20,12},{12,4},{4,0},{1,9},{9... | collective-permute-start | bytes 599048 | tf_op jit(solution)/shard_map/ppermute | solution.py:91
  136.7 2.0 %copy-start = (f32[128,8192]{1,0:T(8,128)}, f32[128,8192]{1,0:T(8,128)S(1)}, u32[]{:S(2)}) copy-start(f32[128,8192]{1,0:T(8,128)S(1)} %fusion.2) | copy-start | bytes 12582916
  138.8 8.9 %collective-permute-start.32 = (f32[16,512]{1,0:T(8,128)S(1)}, f32[16,512]{1,0:T(8,128)S(1)}, u32[]{:S(2)}, u32[]{:S(2)}) collective-permute-start(f32[16,512]{1,0:T(8,128)S(1)} %exponential_multiply_fusion.1), channel_id=1, source_target_pairs={{0,28},{1,29},{2,30},{3,31}} | collective-permute-start | bytes 98312 | tf_op jit(solution)/shard_map/ppermute | solution.py:28
  140.6 8.4 %collective-permute-start.31 = (f32[16,512]{1,0:T(8,128)S(1)}, f32[16,512]{1,0:T(8,128)S(1)}, u32[]{:S(2)}, u32[]{:S(2)}) collective-permute-start(f32[16,512]{1,0:T(8,128)S(1)} %exponential_multiply_fusion.1), channel_id=1, source_target_pairs={{0,24},{4,28},{1,25},{5,29},{2,26},{6,30},{3,27},{7,31}} | collective-permute-start | bytes 98312 | tf_op jit(solution)/shard_map/ppermute | solution.py:28
  142.7 15.8 %collective-permute-start.30 = (f32[16,512]{1,0:T(8,128)S(1)}, f32[16,512]{1,0:T(8,128)S(1)}, u32[]{:S(2)}, u32[]{:S(2)}) collective-permute-start(f32[16,512]{1,0:T(8,128)S(1)} %exponential_multiply_fusion.1), channel_id=1, source_target_pairs={{0,20},{4,24},{8,28},{1,21},{5,25},{9,29},{2,22},{6,26},{10,30},{3... | collective-permute-start | bytes 98312 | tf_op jit(solution)/shard_map/ppermute | solution.py:28
  144.0 14.6 %collective-permute-start.29 = (f32[16,512]{1,0:T(8,128)S(1)}, f32[16,512]{1,0:T(8,128)S(1)}, u32[]{:S(2)}, u32[]{:S(2)}) collective-permute-start(f32[16,512]{1,0:T(8,128)S(1)} %exponential_multiply_fusion.1), channel_id=1, source_target_pairs={{0,16},{4,20},{8,24},{12,28},{1,17},{5,21},{9,25},{13,29},{2,18},{... | collective-permute-start | bytes 98312 | tf_op jit(solution)/shard_map/ppermute | solution.py:28
  145.3 15.3 %collective-permute-start.28 = (f32[16,512]{1,0:T(8,128)S(1)}, f32[16,512]{1,0:T(8,128)S(1)}, u32[]{:S(2)}, u32[]{:S(2)}) collective-permute-start(f32[16,512]{1,0:T(8,128)S(1)} %exponential_multiply_fusion.1), channel_id=1, source_target_pairs={{0,12},{4,16},{8,20},{12,24},{16,28},{1,13},{5,17},{9,21},{13,25},... | collective-permute-start | bytes 98312 | tf_op jit(solution)/shard_map/ppermute | solution.py:28
  147.7 12.8 %collective-permute-start.27 = (f32[16,512]{1,0:T(8,128)S(1)}, f32[16,512]{1,0:T(8,128)S(1)}, u32[]{:S(2)}, u32[]{:S(2)}) collective-permute-start(f32[16,512]{1,0:T(8,128)S(1)} %exponential_multiply_fusion.1), channel_id=1, source_target_pairs={{0,8},{4,12},{8,16},{12,20},{16,24},{20,28},{1,9},{5,13},{9,17},{1... | collective-permute-start | bytes 98312 | tf_op jit(solution)/shard_map/ppermute | solution.py:28
  149.0 11.5 %collective-permute-start.26 = (f32[16,512]{1,0:T(8,128)S(1)}, f32[16,512]{1,0:T(8,128)S(1)}, u32[]{:S(2)}, u32[]{:S(2)}) collective-permute-start(f32[16,512]{1,0:T(8,128)S(1)} %exponential_multiply_fusion.1), channel_id=1, source_target_pairs={{0,4},{4,8},{8,12},{12,16},{16,20},{20,24},{24,28},{1,5},{5,9},{9,... | collective-permute-start | bytes 98312 | tf_op jit(solution)/shard_map/ppermute | solution.py:28
  153.0 7.6 %copy-start.7 = (f32[16,512]{1,0:T(8,128)S(1)}, f32[16,512]{1,0:T(8,128)}, u32[]{:S(2)}) copy-start(f32[16,512]{1,0:T(8,128)} %param.21) | copy-start | bytes 98308
  158.4 3.7 %copy-start.11 = (f32[512]{0:T(512)S(1)}, f32[512]{0:T(512)}, u32[]{:S(2)}) copy-start(f32[512]{0:T(512)} %param.22) | copy-start | bytes 6148
  158.4 11.2 %copy-start.2 = (bf16[16,128,1024]{2,1,0:T(8,128)(2,1)S(1)}, bf16[16,128,1024]{2,1,0:T(8,128)(2,1)}, u32[]{:S(2)}) copy-start(bf16[16,128,1024]{2,1,0:T(8,128)(2,1)} %bitcast_dynamic-update-slice_fusion.2) | copy-start | bytes 12582916
  158.5 11.1 %collective-permute-start.33 = (bf16[128,1024]{1,0:T(8,128)(2,1)S(1)}, bf16[128,1024]{1,0:T(8,128)(2,1)S(1)}, u32[]{:S(2)}, u32[]{:S(2)}) collective-permute-start(bf16[128,1024]{1,0:T(8,128)(2,1)S(1)} %collective-permute-done.22), channel_id=1, source_target_pairs={{0,8},{8,16},{16,24},{24,28},{28,20},{20,12},{12,4},{4,0},{1,9},{9... | collective-permute-start | bytes 786440 | tf_op jit(solution)/shard_map/ppermute | solution.py:91
  158.5 11.1 %collective-permute-start.34 = (bf16[128,1024]{1,0:T(8,128)(2,1)S(1)}, bf16[128,1024]{1,0:T(8,128)(2,1)S(1)}, u32[]{:S(2)}, u32[]{:S(2)}) collective-permute-start(bf16[128,1024]{1,0:T(8,128)(2,1)S(1)} %collective-permute-done.23), channel_id=1, source_target_pairs={{8,0},{16,8},{24,16},{28,24},{20,28},{12,20},{4,12},{0,4},{9,1},{1... | collective-permute-start | bytes 786440 | tf_op jit(solution)/shard_map/ppermute | solution.py:92
  (1 other events, 1.0 us)

commit v6 on v5

--- a/solution.py
+++ b/solution.py
@@ -13,16 +13,21 @@
     order = rates.shape[0]
     ctx_count = lax.axis_size("ctx")
     coefs = residues * jnp.sqrt(2.0 * rates)
-    times = jnp.arange(length, dtype=jnp.float32)[:, None, None]
-    grow = jnp.exp(rates[None] * times)
-    decay = jnp.exp(-rates[None] * times)
-    lifted = (grow * signal[:, None, :]).reshape(length, order * width)
+    times = jnp.arange(length, dtype=jnp.float32)[None, :, None]
+    grow = jnp.exp(rates[:, None, :] * times)
+    decay = jnp.exp(-rates[:, None, :] * times)
+    lifted = grow * signal[None]
     rows = jnp.arange(length, dtype=jnp.int32)
     lower = (rows[:, None] >= rows[None, :]).astype(jnp.float32)
-    running = jnp.matmul(lower, lifted, precision=lax.Precision.HIGHEST).reshape(
-        length, order, width
+    lower = jnp.broadcast_to(lower[None], (order, length, length))
+    running = lax.dot_general(
+        lower,
+        lifted,
+        (((2,), (1,)), ((0,), (0,))),
+        precision=lax.Precision.HIGHEST,
+        preferred_element_type=jnp.float32,
     )
-    end_state = running[length - 1] * jnp.exp(-rates * (length - 1))
+    end_state = running[:, length - 1] * jnp.exp(-rates * (length - 1))
     carried = jnp.zeros_like(end_state)
     for shift in range(1, ctx_count):
         earlier = lax.ppermute(
@@ -30,8 +35,8 @@
         )
         carried = carried + jnp.exp(-rates * (length * (shift - 1))) * earlier
     carried = carried * jnp.exp(-rates)
-    total = running + carried[None]
-    mixed = jnp.sum((coefs[None] * decay) * total, axis=1)
+    total = running + carried[:, None, :]
+    mixed = jnp.sum((coefs[:, None, :] * decay) * total, axis=0)
     return mixed + skips * signal
 
 
@@ -78,24 +83,26 @@
     ring_arr = jnp.array(ring, jnp.int32)
     c_chunk = w_out.shape[0]
     c_half = c_chunk // 2
-    w_up, w_low, columns = lax.optimization_barrier((w_out[:c_half], w_out[c_half:], columns))
+    up = piece(ring_arr[(my_pos - 1) % ctx_count], 0)
+    down = piece(ring_arr[(my_pos + 1) % ctx_count], 1)
+    for step in range(1, ctx_count):
+        up = lax.ppermute(up.astype(jnp.bfloat16), "ctx", perm=fwd).astype(jnp.float32)
+        down = lax.ppermute(down.astype(jnp.bfloat16), "ctx", perm=bwd).astype(jnp.float32)
+        up = up + piece(ring_arr[(my_pos - step - 1) % ctx_count], 0)
+        down = down + piece(ring_arr[(my_pos + step + 1) % ctx_count], 1)
+    w_up, w_low, up, down = lax.optimization_barrier(
+        (w_out[:c_half], w_out[c_half:], up, down)
+    )
     w_rows = jnp.zeros((2 * ctx_count, c_half, w_out.shape[1]), w_out.dtype)
     w_rows = lax.dynamic_update_slice_in_dim(w_rows, w_up[None], me * 2, 0)
     w_rows = lax.dynamic_update_slice_in_dim(w_rows, w_low[None], me * 2 + 1, 0)
-    up = piece(ring_arr[(my_pos - 1) % ctx_count], 0)
-    down = piece(ring_arr[(my_pos + 1) % ctx_count], 1)
     for step in range(1, ctx_count):
-        sent = lax.optimization_barrier(
-            (up.astype(jnp.bfloat16), down.astype(jnp.bfloat16), w_up, w_low)
-        )
-        up, w_up = lax.ppermute((sent[0], sent[2]), "ctx", perm=fwd)
-        down, w_low = lax.ppermute((sent[1], sent[3]), "ctx", perm=bwd)
+        w_up = lax.ppermute(w_up, "ctx", perm=fwd)
+        w_low = lax.ppermute(w_low, "ctx", perm=bwd)
         src_up = ring_arr[(my_pos - step) % ctx_count]
         src_low = ring_arr[(my_pos + step) % ctx_count]
         w_rows = lax.dynamic_update_slice_in_dim(w_rows, w_up[None], src_up * 2, 0)
         w_rows = lax.dynamic_update_slice_in_dim(w_rows, w_low[None], src_low * 2 + 1, 0)
-        up = up.astype(jnp.float32) + piece(ring_arr[(my_pos - step - 1) % ctx_count], 0)
-        down = down.astype(jnp.float32) + piece(ring_arr[(my_pos + step + 1) % ctx_count], 1)
 
     projected = jnp.concatenate([up, down], axis=1).astype(jnp.bfloat16).astype(jnp.float32)
     queries = projected[:, :width]

time: 172 us -> 179 us (1.041)
  waiting for transfers between devices: 50.8 us -> 68.5 us
  local copies, waits for them, and re-layouts: 21.3 us -> 8.23 us
  starting transfers between devices: 48.7 us -> 50.7 us
    ppermute x28, waiting for transfers between devices: 50.7 us -> 68.4 us  [the longest x7 31.9 us: body(): w_up = lax.ppermute(w_up, 'ctx', perm=fwd)]
    unnamed x30 -> x21, local copies, waits for them, and re-layouts: 14.2 us -> 3.37 us
    ppermute x7, starting transfers between devices: 12.6 us -> 14.9 us  [modal_long_conv(): lax.ppermute(end_state, 'ctx', perm=[(i, i + shift) for i in range(ctx_co...]
  transfers between devices with their start and end apart: 36 -> 36, of which waited for: 25 -> 21; matrix products, arithmetic and copies ran while one was open for 9% -> 5% of each run, Pallas kernels for 0% -> 0%
where the time goes in v6:
time: 179 us
  waiting for transfers between devices  68.5 us (38%)
  starting transfers between devices  50.7 us (28%)
  between operations  30.5 us (17%)
  matrix products  10.1 us (6%)
  local copies, waits for them, and re-layouts  8.23 us (5%)
  blocking collectives  7.21 us (4%)
  other arithmetic  3.44 us (2%)
    ppermute x7, waiting for transfers between devices, body(): w_up = lax.ppermute(w_up, 'ctx', perm=fwd)  31.9 us
    ppermute x7, waiting for transfers between devices, body(): lax.ppermute(up.astype(jnp.bfloat16), 'ctx', perm=fwd).astype(jnp.float32)  20.4 us
    ppermute x7, starting transfers between devices, modal_long_conv(): lax.ppermute(end_state, 'ctx', perm=[(i, i + shift) for i in range(ctx_co...  14.9 us
    ppermute x7, waiting for transfers between devices, body(): lax.ppermute(down.astype(jnp.bfloat16), 'ctx', perm=bwd).astype(jnp.float32)  13.9 us
    ppermute x7, starting transfers between devices, body(): w_up = lax.ppermute(w_up, 'ctx', perm=fwd)  12.5 us
    ppermute x7, starting transfers between devices, body(): lax.ppermute(up.astype(jnp.bfloat16), 'ctx', perm=fwd).astype(jnp.float32)  12.4 us
    all_to_all x1, starting transfers between devices, body(): lax.all_to_all(tokens, 'ctx', split_axis=1, concat_axis=0, tiled=True)  7.29 us
    all_gather x1, blocking collectives, body(): features = lax.all_gather(gated, 'tp', axis=1, tiled=True)  7.21 us
  transfers between devices with their start and end apart: 36, of which 21 were waited for; matrix products, arithmetic and copies ran while one was open for 5% of the time, Pallas kernels for 0%

profile of v6, /device:TPU:0, one launch (start us, length us, event | category | flops | bytes accessed | tf_op | source)
XLA Modules:
  0.0 178.7 jit_solution(18026841008272018344)
XLA Ops:
  0.0 2.3 %copy.14 = bf16[128,4096]{0,1:T(8,128)(2,1)} copy(bf16[128,4096]{1,0:T(8,128)(2,1)} %param.13) | data formatting | bytes 2097152 | tf_op args[0]
  2.4 7.3 %all-to-all-start = ((bf16[128,8,512]{0,2,1:T(8,128)(2,1)}), bf16[128,8,512]{0,2,1:T(8,128)(2,1)S(1)}, u32[]{:S(2)}, u32[]{:S(2)}) async-start(bf16[128,8,512]{0,2,1:T(8,128)(2,1)} %bitcast.1), calls=%async_computation | async-start | bytes 2097152 | tf_op jit(solution)/shard_map/all_to_all | solution.py:65
  41.0 1.3 pad_maximum_fusion
  44.4 1.5 copy.15
  47.9 2.1 %collective-permute-start = (bf16[130,768]{1,0:T(8,128)(2,1)S(1)}, bf16[130,768]{1,0:T(8,128)(2,1)S(1)}, u32[]{:S(2)}, u32[]{:S(2)}) collective-permute-start(bf16[130,768]{1,0:T(8,128)(2,1)S(1)} %convolution_convert_fusion.2), channel_id=1, source_target_pairs={{0,8},{8,16},{16,24},{24,28},{28,20},{20,12},{12,4},{4,0},{1,9},{9... | collective-permute-start | bytes 599048 | tf_op jit(solution)/shard_map/ppermute | solution.py:89
  52.1 2.5 %collective-permute-done = bf16[130,768]{1,0:T(8,128)(2,1)S(1)} collective-permute-done((bf16[130,768]{1,0:T(8,128)(2,1)S(1)}, bf16[130,768]{1,0:T(8,128)(2,1)S(1)}, u32[]{:S(2)}, u32[]{:S(2)}) %collective-permute-start) | collective-permute-done | bytes 199712 | tf_op jit(solution)/shard_map/ppermute | solution.py:89
  54.9 1.8 %collective-permute-start.1 = (bf16[130,768]{1,0:T(8,128)(2,1)S(1)}, bf16[130,768]{1,0:T(8,128)(2,1)S(1)}, u32[]{:S(2)}, u32[]{:S(2)}) collective-permute-start(bf16[130,768]{1,0:T(8,128)(2,1)S(1)} %add_convert_fusion.11), channel_id=1, source_target_pairs={{0,8},{8,16},{16,24},{24,28},{28,20},{20,12},{12,4},{4,0},{1,9},{9... | collective-permute-start | bytes 599048 | tf_op jit(solution)/shard_map/ppermute | solution.py:89
  58.5 2.3 %collective-permute-done.1 = bf16[130,768]{1,0:T(8,128)(2,1)S(1)} collective-permute-done((bf16[130,768]{1,0:T(8,128)(2,1)S(1)}, bf16[130,768]{1,0:T(8,128)(2,1)S(1)}, u32[]{:S(2)}, u32[]{:S(2)}) %collective-permute-start.1) | collective-permute-done | bytes 199712 | tf_op jit(solution)/shard_map/ppermute | solution.py:89
  60.8 1.8 %collective-permute-start.2 = (bf16[130,768]{1,0:T(8,128)(2,1)S(1)}, bf16[130,768]{1,0:T(8,128)(2,1)S(1)}, u32[]{:S(2)}, u32[]{:S(2)}) collective-permute-start(bf16[130,768]{1,0:T(8,128)(2,1)S(1)} %add_convert_fusion.10), channel_id=1, source_target_pairs={{0,8},{8,16},{16,24},{24,28},{28,20},{20,12},{12,4},{4,0},{1,9},{9... | collective-permute-start | bytes 599048 | tf_op jit(solution)/shard_map/ppermute | solution.py:89
  62.6 1.7 collective-permute-done.8
  64.4 2.8 %collective-permute-done.2 = bf16[130,768]{1,0:T(8,128)(2,1)S(1)} collective-permute-done((bf16[130,768]{1,0:T(8,128)(2,1)S(1)}, bf16[130,768]{1,0:T(8,128)(2,1)S(1)}, u32[]{:S(2)}, u32[]{:S(2)}) %collective-permute-start.2) | collective-permute-done | bytes 199712 | tf_op jit(solution)/shard_map/ppermute | solution.py:89
  67.3 2.1 %collective-permute-start.3 = (bf16[130,768]{1,0:T(8,128)(2,1)S(1)}, bf16[130,768]{1,0:T(8,128)(2,1)S(1)}, u32[]{:S(2)}, u32[]{:S(2)}) collective-permute-start(bf16[130,768]{1,0:T(8,128)(2,1)S(1)} %add_convert_fusion.9), channel_id=1, source_target_pairs={{0,8},{8,16},{16,24},{24,28},{28,20},{20,12},{12,4},{4,0},{1,9},{9... | collective-permute-start | bytes 599048 | tf_op jit(solution)/shard_map/ppermute | solution.py:89
  69.4 2.0 %collective-permute-done.9 = bf16[130,768]{1,0:T(8,128)(2,1)S(1)} collective-permute-done((bf16[130,768]{1,0:T(8,128)(2,1)S(1)}, bf16[130,768]{1,0:T(8,128)(2,1)S(1)}, u32[]{:S(2)}, u32[]{:S(2)}) %collective-permute-start.9) | collective-permute-done | bytes 199712 | tf_op jit(solution)/shard_map/ppermute | solution.py:90
  71.5 3.8 %collective-permute-done.3 = bf16[130,768]{1,0:T(8,128)(2,1)S(1)} collective-permute-done((bf16[130,768]{1,0:T(8,128)(2,1)S(1)}, bf16[130,768]{1,0:T(8,128)(2,1)S(1)}, u32[]{:S(2)}, u32[]{:S(2)}) %collective-permute-start.3) | collective-permute-done | bytes 199712 | tf_op jit(solution)/shard_map/ppermute | solution.py:89
  75.3 1.7 collective-permute-start.4
  77.0 2.2 %collective-permute-done.10 = bf16[130,768]{1,0:T(8,128)(2,1)S(1)} collective-permute-done((bf16[130,768]{1,0:T(8,128)(2,1)S(1)}, bf16[130,768]{1,0:T(8,128)(2,1)S(1)}, u32[]{:S(2)}, u32[]{:S(2)}) %collective-permute-start.10) | collective-permute-done | bytes 199712 | tf_op jit(solution)/shard_map/ppermute | solution.py:90
  79.4 3.8 %collective-permute-done.4 = bf16[130,768]{1,0:T(8,128)(2,1)S(1)} collective-permute-done((bf16[130,768]{1,0:T(8,128)(2,1)S(1)}, bf16[130,768]{1,0:T(8,128)(2,1)S(1)}, u32[]{:S(2)}, u32[]{:S(2)}) %collective-permute-start.4) | collective-permute-done | bytes 199712 | tf_op jit(solution)/shard_map/ppermute | solution.py:89
  83.3 1.5 collective-permute-start.5
  84.8 2.0 %collective-permute-done.11 = bf16[130,768]{1,0:T(8,128)(2,1)S(1)} collective-permute-done((bf16[130,768]{1,0:T(8,128)(2,1)S(1)}, bf16[130,768]{1,0:T(8,128)(2,1)S(1)}, u32[]{:S(2)}, u32[]{:S(2)}) %collective-permute-start.11) | collective-permute-done | bytes 199712 | tf_op jit(solution)/shard_map/ppermute | solution.py:90
  87.2 3.1 %collective-permute-done.5 = bf16[130,768]{1,0:T(8,128)(2,1)S(1)} collective-permute-done((bf16[130,768]{1,0:T(8,128)(2,1)S(1)}, bf16[130,768]{1,0:T(8,128)(2,1)S(1)}, u32[]{:S(2)}, u32[]{:S(2)}) %collective-permute-start.5) | collective-permute-done | bytes 199712 | tf_op jit(solution)/shard_map/ppermute | solution.py:89
  90.3 1.5 collective-permute-start.6
  91.8 1.7 collective-permute-done.12
  94.2 2.0 %collective-permute-done.6 = bf16[130,768]{1,0:T(8,128)(2,1)S(1)} collective-permute-done((bf16[130,768]{1,0:T(8,128)(2,1)S(1)}, bf16[130,768]{1,0:T(8,128)(2,1)S(1)}, u32[]{:S(2)}, u32[]{:S(2)}) %collective-permute-start.6) | collective-permute-done | bytes 199712 | tf_op jit(solution)/shard_map/ppermute | solution.py:89
  96.2 3.2 %collective-permute-done.13 = bf16[130,768]{1,0:T(8,128)(2,1)S(1)} collective-permute-done((bf16[130,768]{1,0:T(8,128)(2,1)S(1)}, bf16[130,768]{1,0:T(8,128)(2,1)S(1)}, u32[]{:S(2)}, u32[]{:S(2)}) %collective-permute-start.13) | collective-permute-done | bytes 199712 | tf_op jit(solution)/shard_map/ppermute | solution.py:90
  99.7 4.1 %fusion = f32[16,128,512]{2,1,0:T(8,128)S(1)} fusion(f32[128,512]{1,0:T(8,128)S(1)} %fusion.51, f32[16,512]{1,0:T(8,128)S(1)} %copy-done.2, f32[128,128]{1,0:T(8,128)S(1)} %fusion.52), kind=kOutput, calls=%fused_computation.1 | convolution fusion | flops 1612709888 | bytes 4554752 | tf_op jit(solution)/shard_map/dot_general | solution.py:23
  103.9 4.0 %collective-permute-start.20 = (f32[16,512]{1,0:T(8,128)S(1)}, f32[16,512]{1,0:T(8,128)S(1)}, u32[]{:S(2)}, u32[]{:S(2)}) collective-permute-start(f32[16,512]{1,0:T(8,128)S(1)} %bitcast_multiply_fusion), channel_id=1, source_target_pairs={{0,28},{1,29},{2,30},{3,31}} | collective-permute-start | bytes 98312 | tf_op jit(solution)/shard_map/ppermute | solution.py:33
  107.9 1.3 collective-permute-start.19
  109.2 1.3 collective-permute-start.18
  110.5 1.3 collective-permute-start.17
  111.8 2.5 %collective-permute-start.16 = (f32[16,512]{1,0:T(8,128)S(1)}, f32[16,512]{1,0:T(8,128)S(1)}, u32[]{:S(2)}, u32[]{:S(2)}) collective-permute-start(f32[16,512]{1,0:T(8,128)S(1)} %bitcast_multiply_fusion), channel_id=1, source_target_pairs={{0,12},{4,16},{8,20},{12,24},{16,28},{1,13},{5,17},{9,21},{13,25},... | collective-permute-start | bytes 98312 | tf_op jit(solution)/shard_map/ppermute | solution.py:33
  114.8 1.5 collective-permute-start.15
  116.3 3.1 %collective-permute-start.14 = (f32[16,512]{1,0:T(8,128)S(1)}, f32[16,512]{1,0:T(8,128)S(1)}, u32[]{:S(2)}, u32[]{:S(2)}) collective-permute-start(f32[16,512]{1,0:T(8,128)S(1)} %bitcast_multiply_fusion), channel_id=1, source_target_pairs={{0,4},{4,8},{8,12},{12,16},{16,20},{20,24},{24,28},{1,5},{5,9},{9,... | collective-permute-start | bytes 98312 | tf_op jit(solution)/shard_map/ppermute | solution.py:33
  119.5 2.0 %collective-permute-start.22 = (bf16[128,1024]{1,0:T(8,128)(2,1)S(1)}, bf16[128,1024]{1,0:T(8,128)(2,1)S(1)}, u32[]{:S(2)}, u32[]{:S(2)}) collective-permute-start(bf16[128,1024]{1,0:T(8,128)(2,1)S(1)} %get-tuple-element.12), channel_id=1, source_target_pairs={{8,0},{16,8},{24,16},{28,24},{20,28},{12,20},{4,12},{0,4},{9,1},{1... | collective-permute-start | bytes 786440 | tf_op jit(solution)/shard_map/ppermute | solution.py:101
  123.0 7.2 %all_gather.3 = bf16[128,2048]{1,0:T(8,128)(2,1)S(1)} all-gather(bf16[128,512]{1,0:T(8,128)(2,1)S(1)} %multiply_convert_fusion), channel_id=1, replica_groups=mesh['ctx'=8,'tp'=4] {'tp'}, dimensions={1}, use_global_device_ids=true | all-gather | bytes 655360 | tf_op jit(solution)/shard_map/all_gather | solution.py:118
  130.2 2.0 %collective-permute-start.23 = (bf16[128,1024]{1,0:T(8,128)(2,1)S(1)}, bf16[128,1024]{1,0:T(8,128)(2,1)S(1)}, u32[]{:S(2)}, u32[]{:S(2)}) collective-permute-start(bf16[128,1024]{1,0:T(8,128)(2,1)S(1)} %collective-permute-done.21), channel_id=1, source_target_pairs={{0,8},{8,16},{16,24},{24,28},{28,20},{20,12},{12,4},{4,0},{1,9},{9... | collective-permute-start | bytes 786440 | tf_op jit(solution)/shard_map/ppermute | solution.py:100
  132.3 6.5 %collective-permute-done.23 = bf16[128,1024]{1,0:T(8,128)(2,1)S(1)} collective-permute-done((bf16[128,1024]{1,0:T(8,128)(2,1)S(1)}, bf16[128,1024]{1,0:T(8,128)(2,1)S(1)}, u32[]{:S(2)}, u32[]{:S(2)}) %collective-permute-start.23) | collective-permute-done | bytes 262176 | tf_op jit(solution)/shard_map/ppermute | solution.py:100
  138.7 2.0 %collective-permute-start.25 = (bf16[128,1024]{1,0:T(8,128)(2,1)S(1)}, bf16[128,1024]{1,0:T(8,128)(2,1)S(1)}, u32[]{:S(2)}, u32[]{:S(2)}) collective-permute-start(bf16[128,1024]{1,0:T(8,128)(2,1)S(1)} %collective-permute-done.23), channel_id=1, source_target_pairs={{0,8},{8,16},{16,24},{24,28},{28,20},{20,12},{12,4},{4,0},{1,9},{9... | collective-permute-start | bytes 786440 | tf_op jit(solution)/shard_map/ppermute | solution.py:100
  140.8 5.7 %collective-permute-done.25 = bf16[128,1024]{1,0:T(8,128)(2,1)S(1)} collective-permute-done((bf16[128,1024]{1,0:T(8,128)(2,1)S(1)}, bf16[128,1024]{1,0:T(8,128)(2,1)S(1)}, u32[]{:S(2)}, u32[]{:S(2)}) %collective-permute-start.25) | collective-permute-done | bytes 262176 | tf_op jit(solution)/shard_map/ppermute | solution.py:100
  146.5 2.0 %collective-permute-start.27 = (bf16[128,1024]{1,0:T(8,128)(2,1)S(1)}, bf16[128,1024]{1,0:T(8,128)(2,1)S(1)}, u32[]{:S(2)}, u32[]{:S(2)}) collective-permute-start(bf16[128,1024]{1,0:T(8,128)(2,1)S(1)} %collective-permute-done.25), channel_id=1, source_target_pairs={{0,8},{8,16},{16,24},{24,28},{28,20},{20,12},{12,4},{4,0},{1,9},{9... | collective-permute-start | bytes 786440 | tf_op jit(solution)/shard_map/ppermute | solution.py:100
  148.6 4.8 %collective-permute-done.27 = bf16[128,1024]{1,0:T(8,128)(2,1)S(1)} collective-permute-done((bf16[128,1024]{1,0:T(8,128)(2,1)S(1)}, bf16[128,1024]{1,0:T(8,128)(2,1)S(1)}, u32[]{:S(2)}, u32[]{:S(2)}) %collective-permute-start.27) | collective-permute-done | bytes 262176 | tf_op jit(solution)/shard_map/ppermute | solution.py:100
  153.3 2.0 %collective-permute-start.29 = (bf16[128,1024]{1,0:T(8,128)(2,1)S(1)}, bf16[128,1024]{1,0:T(8,128)(2,1)S(1)}, u32[]{:S(2)}, u32[]{:S(2)}) collective-permute-start(bf16[128,1024]{1,0:T(8,128)(2,1)S(1)} %collective-permute-done.27), channel_id=1, source_target_pairs={{0,8},{8,16},{16,24},{24,28},{28,20},{20,12},{12,4},{4,0},{1,9},{9... | collective-permute-start | bytes 786440 | tf_op jit(solution)/shard_map/ppermute | solution.py:100
  155.4 5.1 %collective-permute-done.29 = bf16[128,1024]{1,0:T(8,128)(2,1)S(1)} collective-permute-done((bf16[128,1024]{1,0:T(8,128)(2,1)S(1)}, bf16[128,1024]{1,0:T(8,128)(2,1)S(1)}, u32[]{:S(2)}, u32[]{:S(2)}) %collective-permute-start.29) | collective-permute-done | bytes 262176 | tf_op jit(solution)/shard_map/ppermute | solution.py:100
  160.5 2.0 %collective-permute-start.31 = (bf16[128,1024]{1,0:T(8,128)(2,1)S(1)}, bf16[128,1024]{1,0:T(8,128)(2,1)S(1)}, u32[]{:S(2)}, u32[]{:S(2)}) collective-permute-start(bf16[128,1024]{1,0:T(8,128)(2,1)S(1)} %collective-permute-done.29), channel_id=1, source_target_pairs={{0,8},{8,16},{16,24},{24,28},{28,20},{20,12},{12,4},{4,0},{1,9},{9... | collective-permute-start | bytes 786440 | tf_op jit(solution)/shard_map/ppermute | solution.py:100
  162.6 5.9 %collective-permute-done.31 = bf16[128,1024]{1,0:T(8,128)(2,1)S(1)} collective-permute-done((bf16[128,1024]{1,0:T(8,128)(2,1)S(1)}, bf16[128,1024]{1,0:T(8,128)(2,1)S(1)}, u32[]{:S(2)}, u32[]{:S(2)}) %collective-permute-start.31) | collective-permute-done | bytes 262176 | tf_op jit(solution)/shard_map/ppermute | solution.py:100
  168.5 2.3 %collective-permute-start.33 = (bf16[128,1024]{1,0:T(8,128)(2,1)S(1)}, bf16[128,1024]{1,0:T(8,128)(2,1)S(1)}, u32[]{:S(2)}, u32[]{:S(2)}) collective-permute-start(bf16[128,1024]{1,0:T(8,128)(2,1)S(1)} %collective-permute-done.31), channel_id=1, source_target_pairs={{0,8},{8,16},{16,24},{24,28},{28,20},{20,12},{12,4},{4,0},{1,9},{9... | collective-permute-start | bytes 786440 | tf_op jit(solution)/shard_map/ppermute | solution.py:100
  170.9 4.0 %collective-permute-done.33 = bf16[128,1024]{1,0:T(8,128)(2,1)S(1)} collective-permute-done((bf16[128,1024]{1,0:T(8,128)(2,1)S(1)}, bf16[128,1024]{1,0:T(8,128)(2,1)S(1)}, u32[]{:S(2)}, u32[]{:S(2)}) %collective-permute-start.33) | collective-permute-done | bytes 262176 | tf_op jit(solution)/shard_map/ppermute | solution.py:100
  174.9 2.3 %collective-permute-done.34 = bf16[128,1024]{1,0:T(8,128)(2,1)S(1)} collective-permute-done((bf16[128,1024]{1,0:T(8,128)(2,1)S(1)}, bf16[128,1024]{1,0:T(8,128)(2,1)S(1)}, u32[]{:S(2)}, u32[]{:S(2)}) %collective-permute-start.34) | collective-permute-done | bytes 262176 | tf_op jit(solution)/shard_map/ppermute | solution.py:101
  177.2 1.4 convolution_convert_fusion
  (109 shorter events, 13.9 us)
Async XLA Ops:
  0.0 9.7 %copy-start.9 = (s32[8]{0:T(128)S(1)}, s32[8]{0:T(128)}, u32[]{:S(2)}) copy-start(s32[8]{0:T(128)} %constant.275.clone) | copy-start | bytes 100
  0.0 20.9 %copy-start.3 = (s32[8]{0:T(128)S(1)}, s32[8]{0:T(128)}, u32[]{:S(2)}) copy-start(s32[8]{0:T(128)} %constant.276.clone) | copy-start | bytes 100
  0.0 41.0 %copy-start.1 = (bf16[512,512]{1,0:T(8,128)(2,1)S(1)}, bf16[512,512]{1,0:T(8,128)(2,1)}, u32[]{:S(2)}) copy-start(bf16[512,512]{1,0:T(8,128)(2,1)} %param.16) | copy-start | bytes 1572868
  0.0 42.3 %copy-start.5 = (f32[3,512]{1,0:T(4,128)S(1)}, f32[3,512]{1,0:T(4,128)}, u32[]{:S(2)}) copy-start(f32[3,512]{1,0:T(4,128)} %param.19) | copy-start | bytes 18436
  0.0 42.3 %copy-start.6 = (f32[3,512]{1,0:T(4,128)S(1)}, f32[3,512]{1,0:T(4,128)}, u32[]{:S(2)}) copy-start(f32[3,512]{1,0:T(4,128)} %param.18) | copy-start | bytes 18436
  0.0 42.3 %copy-start.7 = (f32[3,512]{1,0:T(4,128)S(1)}, f32[3,512]{1,0:T(4,128)}, u32[]{:S(2)}) copy-start(f32[3,512]{1,0:T(4,128)} %param.17) | copy-start | bytes 18436
  2.4 41.1 %all-to-all-start = ((bf16[128,8,512]{0,2,1:T(8,128)(2,1)}), bf16[128,8,512]{0,2,1:T(8,128)(2,1)S(1)}, u32[]{:S(2)}, u32[]{:S(2)}) async-start(bf16[128,8,512]{0,2,1:T(8,128)(2,1)} %bitcast.1), calls=%async_computation | async-start | bytes 2097152 | tf_op jit(solution)/shard_map/all_to_all | solution.py:65
  43.4 1.0 copy-start
  47.9 6.7 %collective-permute-start = (bf16[130,768]{1,0:T(8,128)(2,1)S(1)}, bf16[130,768]{1,0:T(8,128)(2,1)S(1)}, u32[]{:S(2)}, u32[]{:S(2)}) collective-permute-start(bf16[130,768]{1,0:T(8,128)(2,1)S(1)} %convolution_convert_fusion.2), channel_id=1, source_target_pairs={{0,8},{8,16},{16,24},{24,28},{28,20},{20,12},{12,4},{4,0},{1,9},{9... | collective-permute-start | bytes 599048 | tf_op jit(solution)/shard_map/ppermute | solution.py:89
  51.7 6.1 %collective-permute-start.7 = (bf16[130,768]{1,0:T(8,128)(2,1)S(1)}, bf16[130,768]{1,0:T(8,128)(2,1)S(1)}, u32[]{:S(2)}, u32[]{:S(2)}) collective-permute-start(bf16[130,768]{1,0:T(8,128)(2,1)S(1)} %convolution_convert_fusion.1), channel_id=1, source_target_pairs={{8,0},{16,8},{24,16},{28,24},{20,28},{12,20},{4,12},{0,4},{9,1},{1... | collective-permute-start | bytes 599048 | tf_op jit(solution)/shard_map/ppermute | solution.py:90
  54.9 5.9 %collective-permute-start.1 = (bf16[130,768]{1,0:T(8,128)(2,1)S(1)}, bf16[130,768]{1,0:T(8,128)(2,1)S(1)}, u32[]{:S(2)}, u32[]{:S(2)}) collective-permute-start(bf16[130,768]{1,0:T(8,128)(2,1)S(1)} %add_convert_fusion.11), channel_id=1, source_target_pairs={{0,8},{8,16},{16,24},{24,28},{28,20},{20,12},{12,4},{4,0},{1,9},{9... | collective-permute-start | bytes 599048 | tf_op jit(solution)/shard_map/ppermute | solution.py:89
  58.1 6.2 %collective-permute-start.8 = (bf16[130,768]{1,0:T(8,128)(2,1)S(1)}, bf16[130,768]{1,0:T(8,128)(2,1)S(1)}, u32[]{:S(2)}, u32[]{:S(2)}) collective-permute-start(bf16[130,768]{1,0:T(8,128)(2,1)S(1)} %add_convert_fusion.5), channel_id=1, source_target_pairs={{8,0},{16,8},{24,16},{28,24},{20,28},{12,20},{4,12},{0,4},{9,1},{1... | collective-permute-start | bytes 599048 | tf_op jit(solution)/shard_map/ppermute | solution.py:90
  60.8 6.5 %collective-permute-start.2 = (bf16[130,768]{1,0:T(8,128)(2,1)S(1)}, bf16[130,768]{1,0:T(8,128)(2,1)S(1)}, u32[]{:S(2)}, u32[]{:S(2)}) collective-permute-start(bf16[130,768]{1,0:T(8,128)(2,1)S(1)} %add_convert_fusion.10), channel_id=1, source_target_pairs={{0,8},{8,16},{16,24},{24,28},{28,20},{20,12},{12,4},{4,0},{1,9},{9... | collective-permute-start | bytes 599048 | tf_op jit(solution)/shard_map/ppermute | solution.py:89
  64.4 7.0 %collective-permute-start.9 = (bf16[130,768]{1,0:T(8,128)(2,1)S(1)}, bf16[130,768]{1,0:T(8,128)(2,1)S(1)}, u32[]{:S(2)}, u32[]{:S(2)}) collective-permute-start(bf16[130,768]{1,0:T(8,128)(2,1)S(1)} %add_convert_fusion.4), channel_id=1, source_target_pairs={{8,0},{16,8},{24,16},{28,24},{20,28},{12,20},{4,12},{0,4},{9,1},{1... | collective-permute-start | bytes 599048 | tf_op jit(solution)/shard_map/ppermute | solution.py:90
  67.3 8.0 %collective-permute-start.3 = (bf16[130,768]{1,0:T(8,128)(2,1)S(1)}, bf16[130,768]{1,0:T(8,128)(2,1)S(1)}, u32[]{:S(2)}, u32[]{:S(2)}) collective-permute-start(bf16[130,768]{1,0:T(8,128)(2,1)S(1)} %add_convert_fusion.9), channel_id=1, source_target_pairs={{0,8},{8,16},{16,24},{24,28},{28,20},{20,12},{12,4},{4,0},{1,9},{9... | collective-permute-start | bytes 599048 | tf_op jit(solution)/shard_map/ppermute | solution.py:89
  71.4 7.9 %collective-permute-start.10 = (bf16[130,768]{1,0:T(8,128)(2,1)S(1)}, bf16[130,768]{1,0:T(8,128)(2,1)S(1)}, u32[]{:S(2)}, u32[]{:S(2)}) collective-permute-start(bf16[130,768]{1,0:T(8,128)(2,1)S(1)} %add_convert_fusion.3), channel_id=1, source_target_pairs={{8,0},{16,8},{24,16},{28,24},{20,28},{12,20},{4,12},{0,4},{9,1},{1... | collective-permute-start | bytes 599048 | tf_op jit(solution)/shard_map/ppermute | solution.py:90
  75.3 7.9 %collective-permute-start.4 = (bf16[130,768]{1,0:T(8,128)(2,1)S(1)}, bf16[130,768]{1,0:T(8,128)(2,1)S(1)}, u32[]{:S(2)}, u32[]{:S(2)}) collective-permute-start(bf16[130,768]{1,0:T(8,128)(2,1)S(1)} %add_convert_fusion.8), channel_id=1, source_target_pairs={{0,8},{8,16},{16,24},{24,28},{28,20},{20,12},{12,4},{4,0},{1,9},{9... | collective-permute-start | bytes 599048 | tf_op jit(solution)/shard_map/ppermute | solution.py:89
  79.3 20.3 %copy-start.2 = (f32[16,512]{1,0:T(8,128)S(1)}, f32[16,512]{1,0:T(8,128)}, u32[]{:S(2)}) copy-start(f32[16,512]{1,0:T(8,128)} %param.20) | copy-start | bytes 98308
  79.4 7.4 %collective-permute-start.11 = (bf16[130,768]{1,0:T(8,128)(2,1)S(1)}, bf16[130,768]{1,0:T(8,128)(2,1)S(1)}, u32[]{:S(2)}, u32[]{:S(2)}) collective-permute-start(bf16[130,768]{1,0:T(8,128)(2,1)S(1)} %add_convert_fusion.2), channel_id=1, source_target_pairs={{8,0},{16,8},{24,16},{28,24},{20,28},{12,20},{4,12},{0,4},{9,1},{1... | collective-permute-start | bytes 599048 | tf_op jit(solution)/shard_map/ppermute | solution.py:90
  83.3 7.0 %collective-permute-start.5 = (bf16[130,768]{1,0:T(8,128)(2,1)S(1)}, bf16[130,768]{1,0:T(8,128)(2,1)S(1)}, u32[]{:S(2)}, u32[]{:S(2)}) collective-permute-start(bf16[130,768]{1,0:T(8,128)(2,1)S(1)} %add_convert_fusion.7), channel_id=1, source_target_pairs={{0,8},{8,16},{16,24},{24,28},{28,20},{20,12},{12,4},{4,0},{1,9},{9... | collective-permute-start | bytes 599048 | tf_op jit(solution)/shard_map/ppermute | solution.py:89
  86.8 6.6 %collective-permute-start.12 = (bf16[130,768]{1,0:T(8,128)(2,1)S(1)}, bf16[130,768]{1,0:T(8,128)(2,1)S(1)}, u32[]{:S(2)}, u32[]{:S(2)}) collective-permute-start(bf16[130,768]{1,0:T(8,128)(2,1)S(1)} %add_convert_fusion.1), channel_id=1, source_target_pairs={{8,0},{16,8},{24,16},{28,24},{20,28},{12,20},{4,12},{0,4},{9,1},{1... | collective-permute-start | bytes 599048 | tf_op jit(solution)/shard_map/ppermute | solution.py:90
  90.3 5.9 %collective-permute-start.6 = (bf16[130,768]{1,0:T(8,128)(2,1)S(1)}, bf16[130,768]{1,0:T(8,128)(2,1)S(1)}, u32[]{:S(2)}, u32[]{:S(2)}) collective-permute-start(bf16[130,768]{1,0:T(8,128)(2,1)S(1)} %add_convert_fusion.6), channel_id=1, source_target_pairs={{0,8},{8,16},{16,24},{24,28},{28,20},{20,12},{12,4},{4,0},{1,9},{9... | collective-permute-start | bytes 599048 | tf_op jit(solution)/shard_map/ppermute | solution.py:89
  93.5 5.9 %collective-permute-start.13 = (bf16[130,768]{1,0:T(8,128)(2,1)S(1)}, bf16[130,768]{1,0:T(8,128)(2,1)S(1)}, u32[]{:S(2)}, u32[]{:S(2)}) collective-permute-start(bf16[130,768]{1,0:T(8,128)(2,1)S(1)} %add_convert_fusion), channel_id=1, source_target_pairs={{8,0},{16,8},{24,16},{28,24},{20,28},{12,20},{4,12},{0,4},{9,1},{1... | collective-permute-start | bytes 599048 | tf_op jit(solution)/shard_map/ppermute | solution.py:90
  99.7 21.9 %copy-start.4 = (f32[16,512]{1,0:T(8,128)S(1)}, f32[16,512]{1,0:T(8,128)}, u32[]{:S(2)}) copy-start(f32[16,512]{1,0:T(8,128)} %param.21) | copy-start | bytes 98308
  103.9 18.8 %copy-start.8 = (f32[512]{0:T(512)S(1)}, f32[512]{0:T(512)}, u32[]{:S(2)}) copy-start(f32[512]{0:T(512)} %param.22) | copy-start | bytes 6148
  103.9 10.9 %collective-permute-start.20 = (f32[16,512]{1,0:T(8,128)S(1)}, f32[16,512]{1,0:T(8,128)S(1)}, u32[]{:S(2)}, u32[]{:S(2)}) collective-permute-start(f32[16,512]{1,0:T(8,128)S(1)} %bitcast_multiply_fusion), channel_id=1, source_target_pairs={{0,28},{1,29},{2,30},{3,31}} | collective-permute-start | bytes 98312 | tf_op jit(solution)/shard_map/ppermute | solution.py:33
  107.9 8.4 %collective-permute-start.19 = (f32[16,512]{1,0:T(8,128)S(1)}, f32[16,512]{1,0:T(8,128)S(1)}, u32[]{:S(2)}, u32[]{:S(2)}) collective-permute-start(f32[16,512]{1,0:T(8,128)S(1)} %bitcast_multiply_fusion), channel_id=1, source_target_pairs={{0,24},{4,28},{1,25},{5,29},{2,26},{6,30},{3,27},{7,31}} | collective-permute-start | bytes 98312 | tf_op jit(solution)/shard_map/ppermute | solution.py:33
  109.2 10.3 %collective-permute-start.18 = (f32[16,512]{1,0:T(8,128)S(1)}, f32[16,512]{1,0:T(8,128)S(1)}, u32[]{:S(2)}, u32[]{:S(2)}) collective-permute-start(f32[16,512]{1,0:T(8,128)S(1)} %bitcast_multiply_fusion), channel_id=1, source_target_pairs={{0,20},{4,24},{8,28},{1,21},{5,25},{9,29},{2,22},{6,26},{10,30},{3... | collective-permute-start | bytes 98312 | tf_op jit(solution)/shard_map/ppermute | solution.py:33
  110.5 9.1 %collective-permute-start.17 = (f32[16,512]{1,0:T(8,128)S(1)}, f32[16,512]{1,0:T(8,128)S(1)}, u32[]{:S(2)}, u32[]{:S(2)}) collective-permute-start(f32[16,512]{1,0:T(8,128)S(1)} %bitcast_multiply_fusion), channel_id=1, source_target_pairs={{0,16},{4,20},{8,24},{12,28},{1,17},{5,21},{9,25},{13,29},{2,18},{... | collective-permute-start | bytes 98312 | tf_op jit(solution)/shard_map/ppermute | solution.py:33
  111.8 9.8 %collective-permute-start.16 = (f32[16,512]{1,0:T(8,128)S(1)}, f32[16,512]{1,0:T(8,128)S(1)}, u32[]{:S(2)}, u32[]{:S(2)}) collective-permute-start(f32[16,512]{1,0:T(8,128)S(1)} %bitcast_multiply_fusion), channel_id=1, source_target_pairs={{0,12},{4,16},{8,20},{12,24},{16,28},{1,13},{5,17},{9,21},{13,25},... | collective-permute-start | bytes 98312 | tf_op jit(solution)/shard_map/ppermute | solution.py:33
  114.8 6.7 %collective-permute-start.15 = (f32[16,512]{1,0:T(8,128)S(1)}, f32[16,512]{1,0:T(8,128)S(1)}, u32[]{:S(2)}, u32[]{:S(2)}) collective-permute-start(f32[16,512]{1,0:T(8,128)S(1)} %bitcast_multiply_fusion), channel_id=1, source_target_pairs={{0,8},{4,12},{8,16},{12,20},{16,24},{20,28},{1,9},{5,13},{9,17},{1... | collective-permute-start | bytes 98312 | tf_op jit(solution)/shard_map/ppermute | solution.py:33
  116.3 5.2 %collective-permute-start.14 = (f32[16,512]{1,0:T(8,128)S(1)}, f32[16,512]{1,0:T(8,128)S(1)}, u32[]{:S(2)}, u32[]{:S(2)}) collective-permute-start(f32[16,512]{1,0:T(8,128)S(1)} %bitcast_multiply_fusion), channel_id=1, source_target_pairs={{0,4},{4,8},{8,12},{12,16},{16,20},{20,24},{24,28},{1,5},{5,9},{9,... | collective-permute-start | bytes 98312 | tf_op jit(solution)/shard_map/ppermute | solution.py:33
  119.5 10.7 %collective-permute-start.21 = (bf16[128,1024]{1,0:T(8,128)(2,1)S(1)}, bf16[128,1024]{1,0:T(8,128)(2,1)S(1)}, u32[]{:S(2)}, u32[]{:S(2)}) collective-permute-start(bf16[128,1024]{1,0:T(8,128)(2,1)S(1)} %get-tuple-element.11), channel_id=1, source_target_pairs={{0,8},{8,16},{16,24},{24,28},{28,20},{20,12},{12,4},{4,0},{1,9},{9... | collective-permute-start | bytes 786440 | tf_op jit(solution)/shard_map/ppermute | solution.py:100
  119.5 12.7 %collective-permute-start.22 = (bf16[128,1024]{1,0:T(8,128)(2,1)S(1)}, bf16[128,1024]{1,0:T(8,128)(2,1)S(1)}, u32[]{:S(2)}, u32[]{:S(2)}) collective-permute-start(bf16[128,1024]{1,0:T(8,128)(2,1)S(1)} %get-tuple-element.12), channel_id=1, source_target_pairs={{8,0},{16,8},{24,16},{28,24},{20,28},{12,20},{4,12},{0,4},{9,1},{1... | collective-permute-start | bytes 786440 | tf_op jit(solution)/shard_map/ppermute | solution.py:101
  130.2 8.6 %collective-permute-start.23 = (bf16[128,1024]{1,0:T(8,128)(2,1)S(1)}, bf16[128,1024]{1,0:T(8,128)(2,1)S(1)}, u32[]{:S(2)}, u32[]{:S(2)}) collective-permute-start(bf16[128,1024]{1,0:T(8,128)(2,1)S(1)} %collective-permute-done.21), channel_id=1, source_target_pairs={{0,8},{8,16},{16,24},{24,28},{28,20},{20,12},{12,4},{4,0},{1,9},{9... | collective-permute-start | bytes 786440 | tf_op jit(solution)/shard_map/ppermute | solution.py:100
  132.2 8.6 %collective-permute-start.24 = (bf16[128,1024]{1,0:T(8,128)(2,1)S(1)}, bf16[128,1024]{1,0:T(8,128)(2,1)S(1)}, u32[]{:S(2)}, u32[]{:S(2)}) collective-permute-start(bf16[128,1024]{1,0:T(8,128)(2,1)S(1)} %collective-permute-done.22), channel_id=1, source_target_pairs={{8,0},{16,8},{24,16},{28,24},{20,28},{12,20},{4,12},{0,4},{9,1},{1... | collective-permute-start | bytes 786440 | tf_op jit(solution)/shard_map/ppermute | solution.py:101
  138.7 7.8 %collective-permute-start.25 = (bf16[128,1024]{1,0:T(8,128)(2,1)S(1)}, bf16[128,1024]{1,0:T(8,128)(2,1)S(1)}, u32[]{:S(2)}, u32[]{:S(2)}) collective-permute-start(bf16[128,1024]{1,0:T(8,128)(2,1)S(1)} %collective-permute-done.23), channel_id=1, source_target_pairs={{0,8},{8,16},{16,24},{24,28},{28,20},{20,12},{12,4},{4,0},{1,9},{9... | collective-permute-start | bytes 786440 | tf_op jit(solution)/shard_map/ppermute | solution.py:100
  140.8 7.8 %collective-permute-start.26 = (bf16[128,1024]{1,0:T(8,128)(2,1)S(1)}, bf16[128,1024]{1,0:T(8,128)(2,1)S(1)}, u32[]{:S(2)}, u32[]{:S(2)}) collective-permute-start(bf16[128,1024]{1,0:T(8,128)(2,1)S(1)} %collective-permute-done.24), channel_id=1, source_target_pairs={{8,0},{16,8},{24,16},{28,24},{20,28},{12,20},{4,12},{0,4},{9,1},{1... | collective-permute-start | bytes 786440 | tf_op jit(solution)/shard_map/ppermute | solution.py:101
  146.5 6.8 %collective-permute-start.27 = (bf16[128,1024]{1,0:T(8,128)(2,1)S(1)}, bf16[128,1024]{1,0:T(8,128)(2,1)S(1)}, u32[]{:S(2)}, u32[]{:S(2)}) collective-permute-start(bf16[128,1024]{1,0:T(8,128)(2,1)S(1)} %collective-permute-done.25), channel_id=1, source_target_pairs={{0,8},{8,16},{16,24},{24,28},{28,20},{20,12},{12,4},{4,0},{1,9},{9... | collective-permute-start | bytes 786440 | tf_op jit(solution)/shard_map/ppermute | solution.py:100
  148.5 6.8 %collective-permute-start.28 = (bf16[128,1024]{1,0:T(8,128)(2,1)S(1)}, bf16[128,1024]{1,0:T(8,128)(2,1)S(1)}, u32[]{:S(2)}, u32[]{:S(2)}) collective-permute-start(bf16[128,1024]{1,0:T(8,128)(2,1)S(1)} %collective-permute-done.26), channel_id=1, source_target_pairs={{8,0},{16,8},{24,16},{28,24},{20,28},{12,20},{4,12},{0,4},{9,1},{1... | collective-permute-start | bytes 786440 | tf_op jit(solution)/shard_map/ppermute | solution.py:101
  153.3 7.1 %collective-permute-start.29 = (bf16[128,1024]{1,0:T(8,128)(2,1)S(1)}, bf16[128,1024]{1,0:T(8,128)(2,1)S(1)}, u32[]{:S(2)}, u32[]{:S(2)}) collective-permute-start(bf16[128,1024]{1,0:T(8,128)(2,1)S(1)} %collective-permute-done.27), channel_id=1, source_target_pairs={{0,8},{8,16},{16,24},{24,28},{28,20},{20,12},{12,4},{4,0},{1,9},{9... | collective-permute-start | bytes 786440 | tf_op jit(solution)/shard_map/ppermute | solution.py:100
  155.4 7.1 %collective-permute-start.30 = (bf16[128,1024]{1,0:T(8,128)(2,1)S(1)}, bf16[128,1024]{1,0:T(8,128)(2,1)S(1)}, u32[]{:S(2)}, u32[]{:S(2)}) collective-permute-start(bf16[128,1024]{1,0:T(8,128)(2,1)S(1)} %collective-permute-done.28), channel_id=1, source_target_pairs={{8,0},{16,8},{24,16},{28,24},{20,28},{12,20},{4,12},{0,4},{9,1},{1... | collective-permute-start | bytes 786440 | tf_op jit(solution)/shard_map/ppermute | solution.py:101
  160.5 8.0 %collective-permute-start.31 = (bf16[128,1024]{1,0:T(8,128)(2,1)S(1)}, bf16[128,1024]{1,0:T(8,128)(2,1)S(1)}, u32[]{:S(2)}, u32[]{:S(2)}) collective-permute-start(bf16[128,1024]{1,0:T(8,128)(2,1)S(1)} %collective-permute-done.29), channel_id=1, source_target_pairs={{0,8},{8,16},{16,24},{24,28},{28,20},{20,12},{12,4},{4,0},{1,9},{9... | collective-permute-start | bytes 786440 | tf_op jit(solution)/shard_map/ppermute | solution.py:100
  162.5 8.3 %collective-permute-start.32 = (bf16[128,1024]{1,0:T(8,128)(2,1)S(1)}, bf16[128,1024]{1,0:T(8,128)(2,1)S(1)}, u32[]{:S(2)}, u32[]{:S(2)}) collective-permute-start(bf16[128,1024]{1,0:T(8,128)(2,1)S(1)} %collective-permute-done.30), channel_id=1, source_target_pairs={{8,0},{16,8},{24,16},{28,24},{20,28},{12,20},{4,12},{0,4},{9,1},{1... | collective-permute-start | bytes 786440 | tf_op jit(solution)/shard_map/ppermute | solution.py:101
  168.5 6.4 %collective-permute-start.33 = (bf16[128,1024]{1,0:T(8,128)(2,1)S(1)}, bf16[128,1024]{1,0:T(8,128)(2,1)S(1)}, u32[]{:S(2)}, u32[]{:S(2)}) collective-permute-start(bf16[128,1024]{1,0:T(8,128)(2,1)S(1)} %collective-permute-done.31), channel_id=1, source_target_pairs={{0,8},{8,16},{16,24},{24,28},{28,20},{20,12},{12,4},{4,0},{1,9},{9... | collective-permute-start | bytes 786440 | tf_op jit(solution)/shard_map/ppermute | solution.py:100
  170.8 6.4 %collective-permute-start.34 = (bf16[128,1024]{1,0:T(8,128)(2,1)S(1)}, bf16[128,1024]{1,0:T(8,128)(2,1)S(1)}, u32[]{:S(2)}, u32[]{:S(2)}) collective-permute-start(bf16[128,1024]{1,0:T(8,128)(2,1)S(1)} %collective-permute-done.32), channel_id=1, source_target_pairs={{8,0},{16,8},{24,16},{28,24},{20,28},{12,20},{4,12},{0,4},{9,1},{1... | collective-permute-start | bytes 786440 | tf_op jit(solution)/shard_map/ppermute | solution.py:101

commit v7 on v5

--- a/solution.py
+++ b/solution.py
@@ -13,16 +13,21 @@
     order = rates.shape[0]
     ctx_count = lax.axis_size("ctx")
     coefs = residues * jnp.sqrt(2.0 * rates)
-    times = jnp.arange(length, dtype=jnp.float32)[:, None, None]
-    grow = jnp.exp(rates[None] * times)
-    decay = jnp.exp(-rates[None] * times)
-    lifted = (grow * signal[:, None, :]).reshape(length, order * width)
+    times = jnp.arange(length, dtype=jnp.float32)[None, :, None]
+    grow = jnp.exp(rates[:, None, :] * times)
+    decay = jnp.exp(-rates[:, None, :] * times)
+    lifted = grow * signal[None]
     rows = jnp.arange(length, dtype=jnp.int32)
     lower = (rows[:, None] >= rows[None, :]).astype(jnp.float32)
-    running = jnp.matmul(lower, lifted, precision=lax.Precision.HIGHEST).reshape(
-        length, order, width
+    lower = jnp.broadcast_to(lower[None], (order, length, length))
+    running = lax.dot_general(
+        lower,
+        lifted,
+        (((2,), (1,)), ((0,), (0,))),
+        precision=lax.Precision.HIGHEST,
+        preferred_element_type=jnp.float32,
     )
-    end_state = running[length - 1] * jnp.exp(-rates * (length - 1))
+    end_state = running[:, length - 1] * jnp.exp(-rates * (length - 1))
     carried = jnp.zeros_like(end_state)
     for shift in range(1, ctx_count):
         earlier = lax.ppermute(
@@ -30,8 +35,8 @@
         )
         carried = carried + jnp.exp(-rates * (length * (shift - 1))) * earlier
     carried = carried * jnp.exp(-rates)
-    total = running + carried[None]
-    mixed = jnp.sum((coefs[None] * decay) * total, axis=1)
+    total = running + carried[:, None, :]
+    mixed = jnp.sum((coefs[:, None, :] * decay) * total, axis=0)
     return mixed + skips * signal
 
 
@@ -57,7 +62,19 @@
     ctx_count = lax.axis_size("ctx")
     length = tokens.shape[0]
     width = w_query.shape[1]
-    columns = lax.all_to_all(tokens, "ctx", split_axis=1, concat_axis=0, tiled=True)
+    tp_count = lax.axis_size("tp")
+    if tp_count % 2 == 0 and length % 2 == 0:
+        half = length // 2
+        core = lax.axis_index("tp") % 2
+        mine = lax.dynamic_slice_in_dim(tokens, core * half, half, 0)
+        mine = lax.all_to_all(mine, "ctx", split_axis=1, concat_axis=0, tiled=True)
+        pairs = [(k, k ^ 1) for k in range(tp_count)]
+        other = lax.ppermute(mine, "tp", perm=pairs)
+        first = jnp.where(core == 0, mine, other).reshape(ctx_count, half, -1)
+        second = jnp.where(core == 0, other, mine).reshape(ctx_count, half, -1)
+        columns = jnp.concatenate([first, second], axis=1).reshape(ctx_count * length, -1)
+    else:
+        columns = lax.all_to_all(tokens, "ctx", split_axis=1, concat_axis=0, tiled=True)
     columns = jnp.concatenate([jnp.zeros((2, columns.shape[1]), columns.dtype), columns], axis=0)
     w_cat = jnp.concatenate([w_query, w_key, w_value], axis=1)
     split = w_cat.shape[1] // 2

time: 172 us -> 172 us (level)
  local copies, waits for them, and re-layouts: 21.3 us -> 5.74 us
  waiting for transfers between devices: 50.8 us -> 62.4 us
  starting transfers between devices: 48.7 us -> 50.6 us
    ppermute x14, waiting for transfers between devices: 30.6 us -> 3.55 us  [body(): up, w_up = lax.ppermute((sent[0], sent[2]), 'ctx', perm=fwd)]
    ppermute x14, waiting for transfers between devices: 20.2 us -> 45.9 us  [body(): down, w_low = lax.ppermute((sent[1], sent[3]), 'ctx', perm=bwd)]
    all_to_all x1, waiting for transfers between devices: 0.01 us -> 13 us  [body(): mine = lax.all_to_all(mine, 'ctx', split_axis=1, concat_axis=0, tiled=True)]
    unnamed x30 -> x18, local copies, waits for them, and re-layouts: 14.2 us -> 1.25 us
    ppermute x14, starting transfers between devices: 11.1 us -> 15.6 us  [body(): down, w_low = lax.ppermute((sent[1], sent[3]), 'ctx', perm=bwd)]
    ppermute x14, starting transfers between devices: 17.7 us -> 14.1 us  [body(): up, w_up = lax.ppermute((sent[0], sent[2]), 'ctx', perm=fwd)]
  transfers between devices with their start and end apart: 36 -> 37, of which waited for: 25 -> 9; matrix products, arithmetic and copies ran while one was open for 9% -> 6% of each run, Pallas kernels for 0% -> 0%
where the time goes in v7:
time: 172 us; the launch traced here: 171 us
  waiting for transfers between devices  62.4 us (36%)
  starting transfers between devices  50.6 us (29%)
  between operations  30.3 us (18%)
  matrix products  10.1 us (6%)
  blocking collectives  7.17 us (4%)
  local copies, waits for them, and re-layouts  5.74 us (3%)
  other arithmetic  4.85 us (3%)
    ppermute x14, waiting for transfers between devices, body(): down, w_low = lax.ppermute((sent[1], sent[3]), 'ctx', perm=bwd)  45.9 us
    ppermute x14, starting transfers between devices, body(): down, w_low = lax.ppermute((sent[1], sent[3]), 'ctx', perm=bwd)  15.6 us
    ppermute x14, starting transfers between devices, body(): up, w_up = lax.ppermute((sent[0], sent[2]), 'ctx', perm=fwd)  14.1 us
    ppermute x7, starting transfers between devices, modal_long_conv(): lax.ppermute(end_state, 'ctx', perm=[(i, i + shift) for i in range(ctx_co...  13.7 us
    all_to_all x1, waiting for transfers between devices, body(): mine = lax.all_to_all(mine, 'ctx', split_axis=1, concat_axis=0, tiled=True)  13 us
    all_to_all x1, starting transfers between devices, body(): mine = lax.all_to_all(mine, 'ctx', split_axis=1, concat_axis=0, tiled=True)  7.28 us
    all_gather x1, blocking collectives, body(): features = lax.all_gather(gated, 'tp', axis=1, tiled=True)  7.17 us
    dot_general x16, matrix products, piece(): return jnp.dot(rows, halves[side], preferred_element_type=jnp.float32)  4.48 us
  transfers between devices with their start and end apart: 37, of which 9 were waited for; matrix products, arithmetic and copies ran while one was open for 6% of the time, Pallas kernels for 0%

profile of v7, /device:TPU:0, one launch (start us, length us, event | category | flops | bytes accessed | tf_op | source)
XLA Modules:
  0.0 171.2 jit_solution(3207838984545006794)
XLA Ops:
  0.0 1.2 copy-done
  1.3 0.8 copy.20
  2.1 7.3 %all-to-all-start = ((bf16[64,8,512]{2,0,1:T(8,128)(2,1)}), bf16[64,8,512]{2,0,1:T(8,128)(2,1)S(1)}, u32[]{:S(2)}, u32[]{:S(2)}) async-start(bf16[64,8,512]{2,0,1:T(8,128)(2,1)} %bitcast.126), calls=%async_computation | async-start | bytes 1048576 | tf_op jit(solution)/shard_map/all_to_all | solution.py:70
  9.4 1.5 pad_maximum_fusion.2
  10.9 13.0 %all-to-all-done = bf16[64,8,512]{2,0,1:T(8,128)(2,1)S(1)} async-done(((bf16[64,8,512]{2,0,1:T(8,128)(2,1)}), bf16[64,8,512]{2,0,1:T(8,128)(2,1)S(1)}, u32[]{:S(2)}, u32[]{:S(2)}) %all-to-all-start) | async-done | bytes 524320 | tf_op jit(solution)/shard_map/all_to_all | solution.py:70
  35.2 0.8 fusion.73
  54.9 1.1 fusion.69
  56.0 1.1 broadcast_select_fusion.1
  58.0 0.8 collective-permute-start.3
  58.8 1.3 collective-permute-start.4
  60.1 1.5 collective-permute-start.2
  66.1 5.6 %collective-permute-done.2 = bf16[130,768]{1,0:T(8,128)(2,1)S(1)} collective-permute-done((bf16[130,768]{1,0:T(8,128)(2,1)S(1)}, bf16[130,768]{1,0:T(8,128)(2,1)S(1)}, u32[]{:S(2)}, u32[]{:S(2)}) %collective-permute-start.2) | collective-permute-done | bytes 199712 | tf_op jit(solution)/shard_map/ppermute | solution.py:109
  72.7 1.7 collective-permute-start.8
  74.4 1.3 collective-permute-start.6
  75.7 0.8 collective-permute-start.5
  76.5 8.4 %collective-permute-done.6 = bf16[130,768]{1,0:T(8,128)(2,1)S(1)} collective-permute-done((bf16[130,768]{1,0:T(8,128)(2,1)S(1)}, bf16[130,768]{1,0:T(8,128)(2,1)S(1)}, u32[]{:S(2)}, u32[]{:S(2)}) %collective-permute-start.6) | collective-permute-done | bytes 199712 | tf_op jit(solution)/shard_map/ppermute | solution.py:109
  85.0 0.9 collective-permute-start.11
  85.9 1.1 collective-permute-start.12
  87.1 1.4 collective-permute-start.10
  89.1 7.4 %collective-permute-done.10 = bf16[130,768]{1,0:T(8,128)(2,1)S(1)} collective-permute-done((bf16[130,768]{1,0:T(8,128)(2,1)S(1)}, bf16[130,768]{1,0:T(8,128)(2,1)S(1)}, u32[]{:S(2)}, u32[]{:S(2)}) %collective-permute-start.10) | collective-permute-done | bytes 199712 | tf_op jit(solution)/shard_map/ppermute | solution.py:109
  96.7 1.8 %collective-permute-start.15 = (bf16[128,1024]{1,0:T(8,128)(2,1)S(1)}, bf16[128,1024]{1,0:T(8,128)(2,1)S(1)}, u32[]{:S(2)}, u32[]{:S(2)}) collective-permute-start(bf16[128,1024]{1,0:T(8,128)(2,1)S(1)} %collective-permute-done.11), channel_id=1, source_target_pairs={{0,8},{8,16},{16,24},{24,28},{28,20},{20,12},{12,4},{4,0},{1,9},{9... | collective-permute-start | bytes 786440 | tf_op jit(solution)/shard_map/ppermute | solution.py:108
  98.7 1.5 collective-permute-start.14
  100.8 7.0 %collective-permute-done.14 = bf16[130,768]{1,0:T(8,128)(2,1)S(1)} collective-permute-done((bf16[130,768]{1,0:T(8,128)(2,1)S(1)}, bf16[130,768]{1,0:T(8,128)(2,1)S(1)}, u32[]{:S(2)}, u32[]{:S(2)}) %collective-permute-start.14) | collective-permute-done | bytes 199712 | tf_op jit(solution)/shard_map/ppermute | solution.py:109
  108.0 1.3 collective-permute-start.19
  109.3 0.8 collective-permute-start.20
  110.1 1.1 collective-permute-start.18
  111.1 0.9 collective-permute-start.17
  112.2 7.2 %collective-permute-done.18 = bf16[130,768]{1,0:T(8,128)(2,1)S(1)} collective-permute-done((bf16[130,768]{1,0:T(8,128)(2,1)S(1)}, bf16[130,768]{1,0:T(8,128)(2,1)S(1)}, u32[]{:S(2)}, u32[]{:S(2)}) %collective-permute-start.18) | collective-permute-done | bytes 199712 | tf_op jit(solution)/shard_map/ppermute | solution.py:109
  119.5 2.7 %collective-permute-start.23 = (bf16[128,1024]{1,0:T(8,128)(2,1)S(1)}, bf16[128,1024]{1,0:T(8,128)(2,1)S(1)}, u32[]{:S(2)}, u32[]{:S(2)}) collective-permute-start(bf16[128,1024]{1,0:T(8,128)(2,1)S(1)} %collective-permute-done.19), channel_id=1, source_target_pairs={{0,8},{8,16},{16,24},{24,28},{28,20},{20,12},{12,4},{4,0},{1,9},{9... | collective-permute-start | bytes 786440 | tf_op jit(solution)/shard_map/ppermute | solution.py:108
  122.2 0.9 collective-permute-start.22
  123.1 1.2 collective-permute-start.21
  124.3 8.8 %collective-permute-done.22 = bf16[130,768]{1,0:T(8,128)(2,1)S(1)} collective-permute-done((bf16[130,768]{1,0:T(8,128)(2,1)S(1)}, bf16[130,768]{1,0:T(8,128)(2,1)S(1)}, u32[]{:S(2)}, u32[]{:S(2)}) %collective-permute-start.22) | collective-permute-done | bytes 199712 | tf_op jit(solution)/shard_map/ppermute | solution.py:109
  133.2 1.4 collective-permute-start.25
  134.6 0.9 collective-permute-start.26
  135.6 3.5 %collective-permute-done.25 = bf16[130,768]{1,0:T(8,128)(2,1)S(1)} collective-permute-done((bf16[130,768]{1,0:T(8,128)(2,1)S(1)}, bf16[130,768]{1,0:T(8,128)(2,1)S(1)}, u32[]{:S(2)}, u32[]{:S(2)}) %collective-permute-start.25) | collective-permute-done | bytes 199712 | tf_op jit(solution)/shard_map/ppermute | solution.py:108
  139.1 1.5 collective-permute-done.26
  141.0 4.1 %fusion = f32[16,128,512]{2,1,0:T(8,128)S(1)} fusion(f32[128,512]{1,0:T(8,128)S(1)} %fusion.51, f32[16,512]{1,0:T(8,128)S(1)} %copy-done.1, f32[128,128]{1,0:T(8,128)S(1)} %fusion.52), kind=kOutput, calls=%fused_computation.1 | convolution fusion | flops 1612709888 | bytes 4554752 | tf_op jit(solution)/shard_map/dot_general | solution.py:23
  145.2 2.6 %collective-permute-start.27 = (f32[16,512]{1,0:T(8,128)S(1)}, f32[16,512]{1,0:T(8,128)S(1)}, u32[]{:S(2)}, u32[]{:S(2)}) collective-permute-start(f32[16,512]{1,0:T(8,128)S(1)} %bitcast_multiply_fusion), channel_id=1, source_target_pairs={{0,4},{4,8},{8,12},{12,16},{16,20},{20,24},{24,28},{1,5},{5,9},{9,... | collective-permute-start | bytes 98312 | tf_op jit(solution)/shard_map/ppermute | solution.py:33
  147.8 1.9 %collective-permute-start.28 = (f32[16,512]{1,0:T(8,128)S(1)}, f32[16,512]{1,0:T(8,128)S(1)}, u32[]{:S(2)}, u32[]{:S(2)}) collective-permute-start(f32[16,512]{1,0:T(8,128)S(1)} %bitcast_multiply_fusion), channel_id=1, source_target_pairs={{0,8},{4,12},{8,16},{12,20},{16,24},{20,28},{1,9},{5,13},{9,17},{1... | collective-permute-start | bytes 98312 | tf_op jit(solution)/shard_map/ppermute | solution.py:33
  149.8 4.0 %collective-permute-start.29 = (f32[16,512]{1,0:T(8,128)S(1)}, f32[16,512]{1,0:T(8,128)S(1)}, u32[]{:S(2)}, u32[]{:S(2)}) collective-permute-start(f32[16,512]{1,0:T(8,128)S(1)} %bitcast_multiply_fusion), channel_id=1, source_target_pairs={{0,12},{4,16},{8,20},{12,24},{16,28},{1,13},{5,17},{9,21},{13,25},... | collective-permute-start | bytes 98312 | tf_op jit(solution)/shard_map/ppermute | solution.py:33
  153.8 1.3 collective-permute-start.30
  155.1 1.3 collective-permute-start.31
  156.4 1.3 collective-permute-start.32
  157.7 1.3 collective-permute-start.33
  159.1 2.0 %collective-permute-start.35 = (bf16[128,1024]{1,0:T(8,128)(2,1)S(1)}, bf16[128,1024]{1,0:T(8,128)(2,1)S(1)}, u32[]{:S(2)}, u32[]{:S(2)}) collective-permute-start(bf16[128,1024]{1,0:T(8,128)(2,1)S(1)} %collective-permute-done.24), channel_id=1, source_target_pairs={{8,0},{16,8},{24,16},{28,24},{20,28},{12,20},{4,12},{0,4},{9,1},{1... | collective-permute-start | bytes 786440 | tf_op jit(solution)/shard_map/ppermute | solution.py:109
  161.2 1.0 multiply_reduce_fusion
  162.5 7.2 %all_gather.3 = bf16[128,2048]{1,0:T(8,128)(2,1)S(1)} all-gather(bf16[128,512]{1,0:T(8,128)(2,1)S(1)} %multiply_convert_fusion), channel_id=1, replica_groups=mesh['ctx'=8,'tp'=4] {'tp'}, dimensions={1}, use_global_device_ids=true | all-gather | bytes 655360 | tf_op jit(solution)/shard_map/all_gather | solution.py:128
  169.8 1.4 convolution_convert_fusion
  (112 shorter events, 10.2 us)
Async XLA Ops:
  0.0 1.3 copy-start
  0.0 23.9 %copy-start.8 = (s32[8]{0:T(128)S(1)}, s32[8]{0:T(128)}, u32[]{:S(2)}) copy-start(s32[8]{0:T(128)} %constant.288.clone) | copy-start | bytes 100
  0.0 35.2 %copy-start.2 = (s32[8]{0:T(128)S(1)}, s32[8]{0:T(128)}, u32[]{:S(2)}) copy-start(s32[8]{0:T(128)} %constant.289.clone) | copy-start | bytes 100
  0.0 10.9 %copy-start.4 = (f32[3,512]{1,0:T(4,128)S(1)}, f32[3,512]{1,0:T(4,128)}, u32[]{:S(2)}) copy-start(f32[3,512]{1,0:T(4,128)} %param.18) | copy-start | bytes 18436
  0.0 10.9 %copy-start.5 = (f32[3,512]{1,0:T(4,128)S(1)}, f32[3,512]{1,0:T(4,128)}, u32[]{:S(2)}) copy-start(f32[3,512]{1,0:T(4,128)} %param.19) | copy-start | bytes 18436
  0.0 54.8 %copy-start.6 = (f32[3,512]{1,0:T(4,128)S(1)}, f32[3,512]{1,0:T(4,128)}, u32[]{:S(2)}) copy-start(f32[3,512]{1,0:T(4,128)} %param.17) | copy-start | bytes 18436
  2.1 21.8 %all-to-all-start = ((bf16[64,8,512]{2,0,1:T(8,128)(2,1)}), bf16[64,8,512]{2,0,1:T(8,128)(2,1)S(1)}, u32[]{:S(2)}, u32[]{:S(2)}) async-start(bf16[64,8,512]{2,0,1:T(8,128)(2,1)} %bitcast.126), calls=%async_computation | async-start | bytes 1048576 | tf_op jit(solution)/shard_map/all_to_all | solution.py:70
  23.9 32.0 %collective-permute-start = (bf16[512,512]{1,0:T(8,128)(2,1)S(1)}, bf16[512,512]{1,0:T(8,128)(2,1)}, u32[]{:S(2)}, u32[]{:S(2)}) collective-permute-start(bf16[512,512]{1,0:T(8,128)(2,1)S(1)} %bitcast.129), channel_id=1, source_target_pairs={{0,1},{1,0},{2,3},{3,2},{4,5},{5,4},{6,7},{7,6},{8,9},{9,8},{10,11... | collective-permute-start | bytes 1572872 | tf_op jit(solution)/shard_map/ppermute | solution.py:72
  58.0 14.3 %collective-permute-start.3 = (bf16[128,1024]{1,0:T(8,128)(2,1)S(1)}, bf16[128,1024]{1,0:T(8,128)(2,1)S(1)}, u32[]{:S(2)}, u32[]{:S(2)}) collective-permute-start(bf16[128,1024]{1,0:T(8,128)(2,1)S(1)} %get-tuple-element.41), channel_id=1, source_target_pairs={{0,8},{8,16},{16,24},{24,28},{28,20},{20,12},{12,4},{4,0},{1,9},{9... | collective-permute-start | bytes 786440 | tf_op jit(solution)/shard_map/ppermute | solution.py:108
  58.8 13.5 %collective-permute-start.4 = (bf16[128,1024]{1,0:T(8,128)(2,1)S(1)}, bf16[128,1024]{1,0:T(8,128)(2,1)S(1)}, u32[]{:S(2)}, u32[]{:S(2)}) collective-permute-start(bf16[128,1024]{1,0:T(8,128)(2,1)S(1)} %get-tuple-element.42), channel_id=1, source_target_pairs={{8,0},{16,8},{24,16},{28,24},{20,28},{12,20},{4,12},{0,4},{9,1},{1... | collective-permute-start | bytes 786440 | tf_op jit(solution)/shard_map/ppermute | solution.py:109
  60.1 11.6 %collective-permute-start.2 = (bf16[130,768]{1,0:T(8,128)(2,1)S(1)}, bf16[130,768]{1,0:T(8,128)(2,1)S(1)}, u32[]{:S(2)}, u32[]{:S(2)}) collective-permute-start(bf16[130,768]{1,0:T(8,128)(2,1)S(1)} %convolution_convert_fusion.1), channel_id=1, source_target_pairs={{8,0},{16,8},{24,16},{28,24},{20,28},{12,20},{4,12},{0,4},{9,1},{1... | collective-permute-start | bytes 599048 | tf_op jit(solution)/shard_map/ppermute | solution.py:109
  61.5 10.5 %collective-permute-start.1 = (bf16[130,768]{1,0:T(8,128)(2,1)S(1)}, bf16[130,768]{1,0:T(8,128)(2,1)S(1)}, u32[]{:S(2)}, u32[]{:S(2)}) collective-permute-start(bf16[130,768]{1,0:T(8,128)(2,1)S(1)} %convolution_convert_fusion.2), channel_id=1, source_target_pairs={{0,8},{8,16},{16,24},{24,28},{28,20},{20,12},{12,4},{4,0},{1,9},{9... | collective-permute-start | bytes 599048 | tf_op jit(solution)/shard_map/ppermute | solution.py:108
  72.3 12.6 %collective-permute-start.7 = (bf16[128,1024]{1,0:T(8,128)(2,1)S(1)}, bf16[128,1024]{1,0:T(8,128)(2,1)S(1)}, u32[]{:S(2)}, u32[]{:S(2)}) collective-permute-start(bf16[128,1024]{1,0:T(8,128)(2,1)S(1)} %collective-permute-done.3), channel_id=1, source_target_pairs={{0,8},{8,16},{16,24},{24,28},{28,20},{20,12},{12,4},{4,0},{1,9},{9... | collective-permute-start | bytes 786440 | tf_op jit(solution)/shard_map/ppermute | solution.py:108
  72.7 12.3 %collective-permute-start.8 = (bf16[128,1024]{1,0:T(8,128)(2,1)S(1)}, bf16[128,1024]{1,0:T(8,128)(2,1)S(1)}, u32[]{:S(2)}, u32[]{:S(2)}) collective-permute-start(bf16[128,1024]{1,0:T(8,128)(2,1)S(1)} %collective-permute-done.4), channel_id=1, source_target_pairs={{8,0},{16,8},{24,16},{28,24},{20,28},{12,20},{4,12},{0,4},{9,1},{1... | collective-permute-start | bytes 786440 | tf_op jit(solution)/shard_map/ppermute | solution.py:109
  74.4 10.4 %collective-permute-start.6 = (bf16[130,768]{1,0:T(8,128)(2,1)S(1)}, bf16[130,768]{1,0:T(8,128)(2,1)S(1)}, u32[]{:S(2)}, u32[]{:S(2)}) collective-permute-start(bf16[130,768]{1,0:T(8,128)(2,1)S(1)} %add_convert_fusion.12), channel_id=1, source_target_pairs={{8,0},{16,8},{24,16},{28,24},{20,28},{12,20},{4,12},{0,4},{9,1},{1... | collective-permute-start | bytes 599048 | tf_op jit(solution)/shard_map/ppermute | solution.py:109
  75.7 9.2 %collective-permute-start.5 = (bf16[130,768]{1,0:T(8,128)(2,1)S(1)}, bf16[130,768]{1,0:T(8,128)(2,1)S(1)}, u32[]{:S(2)}, u32[]{:S(2)}) collective-permute-start(bf16[130,768]{1,0:T(8,128)(2,1)S(1)} %add_convert_fusion.13), channel_id=1, source_target_pairs={{0,8},{8,16},{16,24},{24,28},{28,20},{20,12},{12,4},{4,0},{1,9},{9... | collective-permute-start | bytes 599048 | tf_op jit(solution)/shard_map/ppermute | solution.py:108
  85.0 11.7 %collective-permute-start.11 = (bf16[128,1024]{1,0:T(8,128)(2,1)S(1)}, bf16[128,1024]{1,0:T(8,128)(2,1)S(1)}, u32[]{:S(2)}, u32[]{:S(2)}) collective-permute-start(bf16[128,1024]{1,0:T(8,128)(2,1)S(1)} %collective-permute-done.7), channel_id=1, source_target_pairs={{0,8},{8,16},{16,24},{24,28},{28,20},{20,12},{12,4},{4,0},{1,9},{9... | collective-permute-start | bytes 786440 | tf_op jit(solution)/shard_map/ppermute | solution.py:108
  85.9 10.7 %collective-permute-start.12 = (bf16[128,1024]{1,0:T(8,128)(2,1)S(1)}, bf16[128,1024]{1,0:T(8,128)(2,1)S(1)}, u32[]{:S(2)}, u32[]{:S(2)}) collective-permute-start(bf16[128,1024]{1,0:T(8,128)(2,1)S(1)} %collective-permute-done.8), channel_id=1, source_target_pairs={{8,0},{16,8},{24,16},{28,24},{20,28},{12,20},{4,12},{0,4},{9,1},{1... | collective-permute-start | bytes 786440 | tf_op jit(solution)/shard_map/ppermute | solution.py:109
  87.1 9.5 %collective-permute-start.10 = (bf16[130,768]{1,0:T(8,128)(2,1)S(1)}, bf16[130,768]{1,0:T(8,128)(2,1)S(1)}, u32[]{:S(2)}, u32[]{:S(2)}) collective-permute-start(bf16[130,768]{1,0:T(8,128)(2,1)S(1)} %add_convert_fusion.10), channel_id=1, source_target_pairs={{8,0},{16,8},{24,16},{28,24},{20,28},{12,20},{4,12},{0,4},{9,1},{1... | collective-permute-start | bytes 599048 | tf_op jit(solution)/shard_map/ppermute | solution.py:109
  88.4 8.2 %collective-permute-start.9 = (bf16[130,768]{1,0:T(8,128)(2,1)S(1)}, bf16[130,768]{1,0:T(8,128)(2,1)S(1)}, u32[]{:S(2)}, u32[]{:S(2)}) collective-permute-start(bf16[130,768]{1,0:T(8,128)(2,1)S(1)} %add_convert_fusion.11), channel_id=1, source_target_pairs={{0,8},{8,16},{16,24},{24,28},{28,20},{20,12},{12,4},{4,0},{1,9},{9... | collective-permute-start | bytes 599048 | tf_op jit(solution)/shard_map/ppermute | solution.py:108
  96.7 11.3 %collective-permute-start.15 = (bf16[128,1024]{1,0:T(8,128)(2,1)S(1)}, bf16[128,1024]{1,0:T(8,128)(2,1)S(1)}, u32[]{:S(2)}, u32[]{:S(2)}) collective-permute-start(bf16[128,1024]{1,0:T(8,128)(2,1)S(1)} %collective-permute-done.11), channel_id=1, source_target_pairs={{0,8},{8,16},{16,24},{24,28},{28,20},{20,12},{12,4},{4,0},{1,9},{9... | collective-permute-start | bytes 786440 | tf_op jit(solution)/shard_map/ppermute | solution.py:108
  98.4 9.5 %collective-permute-start.16 = (bf16[128,1024]{1,0:T(8,128)(2,1)S(1)}, bf16[128,1024]{1,0:T(8,128)(2,1)S(1)}, u32[]{:S(2)}, u32[]{:S(2)}) collective-permute-start(bf16[128,1024]{1,0:T(8,128)(2,1)S(1)} %collective-permute-done.12), channel_id=1, source_target_pairs={{8,0},{16,8},{24,16},{28,24},{20,28},{12,20},{4,12},{0,4},{9,1},{1... | collective-permute-start | bytes 786440 | tf_op jit(solution)/shard_map/ppermute | solution.py:109
  98.7 9.1 %collective-permute-start.14 = (bf16[130,768]{1,0:T(8,128)(2,1)S(1)}, bf16[130,768]{1,0:T(8,128)(2,1)S(1)}, u32[]{:S(2)}, u32[]{:S(2)}) collective-permute-start(bf16[130,768]{1,0:T(8,128)(2,1)S(1)} %add_convert_fusion.8), channel_id=1, source_target_pairs={{8,0},{16,8},{24,16},{28,24},{20,28},{12,20},{4,12},{0,4},{9,1},{1... | collective-permute-start | bytes 599048 | tf_op jit(solution)/shard_map/ppermute | solution.py:109
  100.2 7.7 %collective-permute-start.13 = (bf16[130,768]{1,0:T(8,128)(2,1)S(1)}, bf16[130,768]{1,0:T(8,128)(2,1)S(1)}, u32[]{:S(2)}, u32[]{:S(2)}) collective-permute-start(bf16[130,768]{1,0:T(8,128)(2,1)S(1)} %add_convert_fusion.9), channel_id=1, source_target_pairs={{0,8},{8,16},{16,24},{24,28},{28,20},{20,12},{12,4},{4,0},{1,9},{9... | collective-permute-start | bytes 599048 | tf_op jit(solution)/shard_map/ppermute | solution.py:108
  108.0 11.5 %collective-permute-start.19 = (bf16[128,1024]{1,0:T(8,128)(2,1)S(1)}, bf16[128,1024]{1,0:T(8,128)(2,1)S(1)}, u32[]{:S(2)}, u32[]{:S(2)}) collective-permute-start(bf16[128,1024]{1,0:T(8,128)(2,1)S(1)} %collective-permute-done.15), channel_id=1, source_target_pairs={{0,8},{8,16},{16,24},{24,28},{28,20},{20,12},{12,4},{4,0},{1,9},{9... | collective-permute-start | bytes 786440 | tf_op jit(solution)/shard_map/ppermute | solution.py:108
  109.3 10.2 %collective-permute-start.20 = (bf16[128,1024]{1,0:T(8,128)(2,1)S(1)}, bf16[128,1024]{1,0:T(8,128)(2,1)S(1)}, u32[]{:S(2)}, u32[]{:S(2)}) collective-permute-start(bf16[128,1024]{1,0:T(8,128)(2,1)S(1)} %collective-permute-done.16), channel_id=1, source_target_pairs={{8,0},{16,8},{24,16},{28,24},{20,28},{12,20},{4,12},{0,4},{9,1},{1... | collective-permute-start | bytes 786440 | tf_op jit(solution)/shard_map/ppermute | solution.py:109
  110.1 9.3 %collective-permute-start.18 = (bf16[130,768]{1,0:T(8,128)(2,1)S(1)}, bf16[130,768]{1,0:T(8,128)(2,1)S(1)}, u32[]{:S(2)}, u32[]{:S(2)}) collective-permute-start(bf16[130,768]{1,0:T(8,128)(2,1)S(1)} %add_convert_fusion.6), channel_id=1, source_target_pairs={{8,0},{16,8},{24,16},{28,24},{20,28},{12,20},{4,12},{0,4},{9,1},{1... | collective-permute-start | bytes 599048 | tf_op jit(solution)/shard_map/ppermute | solution.py:109
  111.1 8.3 %collective-permute-start.17 = (bf16[130,768]{1,0:T(8,128)(2,1)S(1)}, bf16[130,768]{1,0:T(8,128)(2,1)S(1)}, u32[]{:S(2)}, u32[]{:S(2)}) collective-permute-start(bf16[130,768]{1,0:T(8,128)(2,1)S(1)} %add_convert_fusion.7), channel_id=1, source_target_pairs={{0,8},{8,16},{16,24},{24,28},{28,20},{20,12},{12,4},{4,0},{1,9},{9... | collective-permute-start | bytes 599048 | tf_op jit(solution)/shard_map/ppermute | solution.py:108
  119.4 21.5 %copy-start.1 = (f32[16,512]{1,0:T(8,128)S(1)}, f32[16,512]{1,0:T(8,128)}, u32[]{:S(2)}) copy-start(f32[16,512]{1,0:T(8,128)} %param.20) | copy-start | bytes 98308
  119.5 13.7 %collective-permute-start.23 = (bf16[128,1024]{1,0:T(8,128)(2,1)S(1)}, bf16[128,1024]{1,0:T(8,128)(2,1)S(1)}, u32[]{:S(2)}, u32[]{:S(2)}) collective-permute-start(bf16[128,1024]{1,0:T(8,128)(2,1)S(1)} %collective-permute-done.19), channel_id=1, source_target_pairs={{0,8},{8,16},{16,24},{24,28},{28,20},{20,12},{12,4},{4,0},{1,9},{9... | collective-permute-start | bytes 786440 | tf_op jit(solution)/shard_map/ppermute | solution.py:108
  122.2 11.0 %collective-permute-start.24 = (bf16[128,1024]{1,0:T(8,128)(2,1)S(1)}, bf16[128,1024]{1,0:T(8,128)(2,1)S(1)}, u32[]{:S(2)}, u32[]{:S(2)}) collective-permute-start(bf16[128,1024]{1,0:T(8,128)(2,1)S(1)} %collective-permute-done.20), channel_id=1, source_target_pairs={{8,0},{16,8},{24,16},{28,24},{20,28},{12,20},{4,12},{0,4},{9,1},{1... | collective-permute-start | bytes 786440 | tf_op jit(solution)/shard_map/ppermute | solution.py:109
  122.2 10.8 %collective-permute-start.22 = (bf16[130,768]{1,0:T(8,128)(2,1)S(1)}, bf16[130,768]{1,0:T(8,128)(2,1)S(1)}, u32[]{:S(2)}, u32[]{:S(2)}) collective-permute-start(bf16[130,768]{1,0:T(8,128)(2,1)S(1)} %add_convert_fusion.4), channel_id=1, source_target_pairs={{8,0},{16,8},{24,16},{28,24},{20,28},{12,20},{4,12},{0,4},{9,1},{1... | collective-permute-start | bytes 599048 | tf_op jit(solution)/shard_map/ppermute | solution.py:109
  123.1 10.0 %collective-permute-start.21 = (bf16[130,768]{1,0:T(8,128)(2,1)S(1)}, bf16[130,768]{1,0:T(8,128)(2,1)S(1)}, u32[]{:S(2)}, u32[]{:S(2)}) collective-permute-start(bf16[130,768]{1,0:T(8,128)(2,1)S(1)} %add_convert_fusion.5), channel_id=1, source_target_pairs={{0,8},{8,16},{16,24},{24,28},{28,20},{20,12},{12,4},{4,0},{1,9},{9... | collective-permute-start | bytes 599048 | tf_op jit(solution)/shard_map/ppermute | solution.py:108
  133.2 5.9 %collective-permute-start.25 = (bf16[130,768]{1,0:T(8,128)(2,1)S(1)}, bf16[130,768]{1,0:T(8,128)(2,1)S(1)}, u32[]{:S(2)}, u32[]{:S(2)}) collective-permute-start(bf16[130,768]{1,0:T(8,128)(2,1)S(1)} %add_convert_fusion.3), channel_id=1, source_target_pairs={{0,8},{8,16},{16,24},{24,28},{28,20},{20,12},{12,4},{4,0},{1,9},{9... | collective-permute-start | bytes 599048 | tf_op jit(solution)/shard_map/ppermute | solution.py:108
  134.6 6.0 %collective-permute-start.26 = (bf16[130,768]{1,0:T(8,128)(2,1)S(1)}, bf16[130,768]{1,0:T(8,128)(2,1)S(1)}, u32[]{:S(2)}, u32[]{:S(2)}) collective-permute-start(bf16[130,768]{1,0:T(8,128)(2,1)S(1)} %add_convert_fusion.2), channel_id=1, source_target_pairs={{8,0},{16,8},{24,16},{28,24},{20,28},{12,20},{4,12},{0,4},{9,1},{1... | collective-permute-start | bytes 599048 | tf_op jit(solution)/shard_map/ppermute | solution.py:109
  140.7 20.4 %copy-start.3 = (f32[16,512]{1,0:T(8,128)S(1)}, f32[16,512]{1,0:T(8,128)}, u32[]{:S(2)}) copy-start(f32[16,512]{1,0:T(8,128)} %param.21) | copy-start | bytes 98308
  145.1 17.1 %copy-start.7 = (f32[512]{0:T(512)S(1)}, f32[512]{0:T(512)}, u32[]{:S(2)}) copy-start(f32[512]{0:T(512)} %param.22) | copy-start | bytes 6148
  145.2 11.2 %collective-permute-start.27 = (f32[16,512]{1,0:T(8,128)S(1)}, f32[16,512]{1,0:T(8,128)S(1)}, u32[]{:S(2)}, u32[]{:S(2)}) collective-permute-start(f32[16,512]{1,0:T(8,128)S(1)} %bitcast_multiply_fusion), channel_id=1, source_target_pairs={{0,4},{4,8},{8,12},{12,16},{16,20},{20,24},{24,28},{1,5},{5,9},{9,... | collective-permute-start | bytes 98312 | tf_op jit(solution)/shard_map/ppermute | solution.py:33
  147.8 9.9 %collective-permute-start.28 = (f32[16,512]{1,0:T(8,128)S(1)}, f32[16,512]{1,0:T(8,128)S(1)}, u32[]{:S(2)}, u32[]{:S(2)}) collective-permute-start(f32[16,512]{1,0:T(8,128)S(1)} %bitcast_multiply_fusion), channel_id=1, source_target_pairs={{0,8},{4,12},{8,16},{12,20},{16,24},{20,28},{1,9},{5,13},{9,17},{1... | collective-permute-start | bytes 98312 | tf_op jit(solution)/shard_map/ppermute | solution.py:33
  149.8 9.3 %collective-permute-start.29 = (f32[16,512]{1,0:T(8,128)S(1)}, f32[16,512]{1,0:T(8,128)S(1)}, u32[]{:S(2)}, u32[]{:S(2)}) collective-permute-start(f32[16,512]{1,0:T(8,128)S(1)} %bitcast_multiply_fusion), channel_id=1, source_target_pairs={{0,12},{4,16},{8,20},{12,24},{16,28},{1,13},{5,17},{9,21},{13,25},... | collective-permute-start | bytes 98312 | tf_op jit(solution)/shard_map/ppermute | solution.py:33
  153.8 5.3 %collective-permute-start.30 = (f32[16,512]{1,0:T(8,128)S(1)}, f32[16,512]{1,0:T(8,128)S(1)}, u32[]{:S(2)}, u32[]{:S(2)}) collective-permute-start(f32[16,512]{1,0:T(8,128)S(1)} %bitcast_multiply_fusion), channel_id=1, source_target_pairs={{0,16},{4,20},{8,24},{12,28},{1,17},{5,21},{9,25},{13,29},{2,18},{... | collective-permute-start | bytes 98312 | tf_op jit(solution)/shard_map/ppermute | solution.py:33
  155.1 6.0 %collective-permute-start.31 = (f32[16,512]{1,0:T(8,128)S(1)}, f32[16,512]{1,0:T(8,128)S(1)}, u32[]{:S(2)}, u32[]{:S(2)}) collective-permute-start(f32[16,512]{1,0:T(8,128)S(1)} %bitcast_multiply_fusion), channel_id=1, source_target_pairs={{0,20},{4,24},{8,28},{1,21},{5,25},{9,29},{2,22},{6,26},{10,30},{3... | collective-permute-start | bytes 98312 | tf_op jit(solution)/shard_map/ppermute | solution.py:33
  156.4 4.7 %collective-permute-start.32 = (f32[16,512]{1,0:T(8,128)S(1)}, f32[16,512]{1,0:T(8,128)S(1)}, u32[]{:S(2)}, u32[]{:S(2)}) collective-permute-start(f32[16,512]{1,0:T(8,128)S(1)} %bitcast_multiply_fusion), channel_id=1, source_target_pairs={{0,24},{4,28},{1,25},{5,29},{2,26},{6,30},{3,27},{7,31}} | collective-permute-start | bytes 98312 | tf_op jit(solution)/shard_map/ppermute | solution.py:33
  157.7 3.4 %collective-permute-start.33 = (f32[16,512]{1,0:T(8,128)S(1)}, f32[16,512]{1,0:T(8,128)S(1)}, u32[]{:S(2)}, u32[]{:S(2)}) collective-permute-start(f32[16,512]{1,0:T(8,128)S(1)} %bitcast_multiply_fusion), channel_id=1, source_target_pairs={{0,28},{1,29},{2,30},{3,31}} | collective-permute-start | bytes 98312 | tf_op jit(solution)/shard_map/ppermute | solution.py:33
  159.0 10.7 %collective-permute-start.34 = (bf16[128,1024]{1,0:T(8,128)(2,1)S(1)}, bf16[128,1024]{1,0:T(8,128)(2,1)S(1)}, u32[]{:S(2)}, u32[]{:S(2)}) collective-permute-start(bf16[128,1024]{1,0:T(8,128)(2,1)S(1)} %collective-permute-done.23), channel_id=1, source_target_pairs={{0,8},{8,16},{16,24},{24,28},{28,20},{20,12},{12,4},{4,0},{1,9},{9... | collective-permute-start | bytes 786440 | tf_op jit(solution)/shard_map/ppermute | solution.py:108
  159.1 10.6 %collective-permute-start.35 = (bf16[128,1024]{1,0:T(8,128)(2,1)S(1)}, bf16[128,1024]{1,0:T(8,128)(2,1)S(1)}, u32[]{:S(2)}, u32[]{:S(2)}) collective-permute-start(bf16[128,1024]{1,0:T(8,128)(2,1)S(1)} %collective-permute-done.24), channel_id=1, source_target_pairs={{8,0},{16,8},{24,16},{28,24},{20,28},{12,20},{4,12},{0,4},{9,1},{1... | collective-permute-start | bytes 786440 | tf_op jit(solution)/shard_map/ppermute | solution.py:109

commit v8 on v7

--- a/solution.py
+++ b/solution.py
@@ -62,19 +62,7 @@
     ctx_count = lax.axis_size("ctx")
     length = tokens.shape[0]
     width = w_query.shape[1]
-    tp_count = lax.axis_size("tp")
-    if tp_count % 2 == 0 and length % 2 == 0:
-        half = length // 2
-        core = lax.axis_index("tp") % 2
-        mine = lax.dynamic_slice_in_dim(tokens, core * half, half, 0)
-        mine = lax.all_to_all(mine, "ctx", split_axis=1, concat_axis=0, tiled=True)
-        pairs = [(k, k ^ 1) for k in range(tp_count)]
-        other = lax.ppermute(mine, "tp", perm=pairs)
-        first = jnp.where(core == 0, mine, other).reshape(ctx_count, half, -1)
-        second = jnp.where(core == 0, other, mine).reshape(ctx_count, half, -1)
-        columns = jnp.concatenate([first, second], axis=1).reshape(ctx_count * length, -1)
-    else:
-        columns = lax.all_to_all(tokens, "ctx", split_axis=1, concat_axis=0, tiled=True)
+    columns = lax.all_to_all(tokens, "ctx", split_axis=1, concat_axis=0, tiled=True)
     columns = jnp.concatenate([jnp.zeros((2, columns.shape[1]), columns.dtype), columns], axis=0)
     w_cat = jnp.concatenate([w_query, w_key, w_value], axis=1)
     split = w_cat.shape[1] // 2

time: 172 us -> 162 us (0.942)
  waiting for transfers between devices: 62.4 us -> 49.7 us
  local copies, waits for them, and re-layouts: 5.74 us -> 8.46 us
    all_to_all x1, waiting for transfers between devices: 13 us -> 0.01 us  [body(): lax.all_to_all(tokens, 'ctx', split_axis=1, concat_axis=0, tiled=True)]
    ppermute x14, starting transfers between devices: 15.6 us -> 11.9 us  [body(): down, w_low = lax.ppermute((sent[1], sent[3]), 'ctx', perm=bwd)]
    ppermute x14, starting transfers between devices: 14.1 us -> 17.4 us  [body(): up, w_up = lax.ppermute((sent[0], sent[2]), 'ctx', perm=fwd)]
    unnamed x18 -> x21, local copies, waits for them, and re-layouts: 1.25 us -> 3.37 us
  transfers between devices with their start and end apart: 37 -> 36, of which waited for: 9 -> 8; matrix products, arithmetic and copies ran while one was open for 6% -> 6% of each run, Pallas kernels for 0% -> 0%
where the time goes in v8:
time: 162 us; the launch traced here: 161 us
  starting transfers between devices  51.9 us (32%)
  waiting for transfers between devices  49.7 us (31%)
  between operations  30.1 us (19%)
  matrix products  10 us (6%)
  local copies, waits for them, and re-layouts  8.46 us (5%)
  blocking collectives  7.13 us (4%)
  other arithmetic  3.49 us (2%)
    ppermute x14, waiting for transfers between devices, body(): down, w_low = lax.ppermute((sent[1], sent[3]), 'ctx', perm=bwd)  46.1 us
    ppermute x14, starting transfers between devices, body(): up, w_up = lax.ppermute((sent[0], sent[2]), 'ctx', perm=fwd)  17.4 us
    ppermute x7, starting transfers between devices, modal_long_conv(): lax.ppermute(end_state, 'ctx', perm=[(i, i + shift) for i in range(ctx_co...  15.3 us
    ppermute x14, starting transfers between devices, body(): down, w_low = lax.ppermute((sent[1], sent[3]), 'ctx', perm=bwd)  11.9 us
    all_to_all x1, starting transfers between devices, body(): lax.all_to_all(tokens, 'ctx', split_axis=1, concat_axis=0, tiled=True)  7.29 us
    all_gather x1, blocking collectives, body(): features = lax.all_gather(gated, 'tp', axis=1, tiled=True)  7.13 us
    dot_general x16, matrix products, piece(): return jnp.dot(rows, halves[side], preferred_element_type=jnp.float32)  4.48 us
    dot_general x1, matrix products, modal_long_conv(): lax.dot_general(lower, lifted, (((2,), (1,)), ((0,), (0,))), precision=la...  4.13 us
  transfers between devices with their start and end apart: 36, of which 8 were waited for; matrix products, arithmetic and copies ran while one was open for 6% of the time, Pallas kernels for 0%

profile of v8, /device:TPU:0, one launch (start us, length us, event | category | flops | bytes accessed | tf_op | source)
XLA Modules:
  0.0 160.8 jit_solution(9993611439080769053)
XLA Ops:
  0.0 2.3 %copy.14 = bf16[128,4096]{0,1:T(8,128)(2,1)} copy(bf16[128,4096]{1,0:T(8,128)(2,1)} %param.13) | data formatting | bytes 2097152 | tf_op args[0]
  2.4 7.3 %all-to-all-start = ((bf16[128,8,512]{0,2,1:T(8,128)(2,1)}), bf16[128,8,512]{0,2,1:T(8,128)(2,1)S(1)}, u32[]{:S(2)}, u32[]{:S(2)}) async-start(bf16[128,8,512]{0,2,1:T(8,128)(2,1)} %bitcast.1), calls=%async_computation | async-start | bytes 2097152 | tf_op jit(solution)/shard_map/all_to_all | solution.py:65
  9.7 0.6 dynamic_slice.113
  20.9 0.8 fusion.73
  40.4 1.3 pad_maximum_fusion.1
  41.8 1.1 fusion.69
  42.9 1.0 copy-done
  43.9 1.5 copy.15
  46.2 2.1 %collective-permute-start.2 = (bf16[128,1024]{1,0:T(8,128)(2,1)S(1)}, bf16[128,1024]{1,0:T(8,128)(2,1)S(1)}, u32[]{:S(2)}, u32[]{:S(2)}) collective-permute-start(bf16[128,1024]{1,0:T(8,128)(2,1)S(1)} %get-tuple-element.41), channel_id=1, source_target_pairs={{0,8},{8,16},{16,24},{24,28},{28,20},{20,12},{12,4},{4,0},{1,9},{9... | collective-permute-start | bytes 786440 | tf_op jit(solution)/shard_map/ppermute | solution.py:96
  48.3 2.0 %collective-permute-start.1 = (bf16[130,768]{1,0:T(8,128)(2,1)S(1)}, bf16[130,768]{1,0:T(8,128)(2,1)S(1)}, u32[]{:S(2)}, u32[]{:S(2)}) collective-permute-start(bf16[130,768]{1,0:T(8,128)(2,1)S(1)} %convolution_convert_fusion.1), channel_id=1, source_target_pairs={{8,0},{16,8},{24,16},{28,24},{20,28},{12,20},{4,12},{0,4},{9,1},{1... | collective-permute-start | bytes 599048 | tf_op jit(solution)/shard_map/ppermute | solution.py:97
  54.4 5.6 %collective-permute-done.1 = bf16[130,768]{1,0:T(8,128)(2,1)S(1)} collective-permute-done((bf16[130,768]{1,0:T(8,128)(2,1)S(1)}, bf16[130,768]{1,0:T(8,128)(2,1)S(1)}, u32[]{:S(2)}, u32[]{:S(2)}) %collective-permute-start.1) | collective-permute-done | bytes 199712 | tf_op jit(solution)/shard_map/ppermute | solution.py:97
  60.6 1.5 collective-permute-start.6
  62.1 0.6 collective-permute-start.7
  63.0 1.7 %collective-permute-start.4 = (bf16[130,768]{1,0:T(8,128)(2,1)S(1)}, bf16[130,768]{1,0:T(8,128)(2,1)S(1)}, u32[]{:S(2)}, u32[]{:S(2)}) collective-permute-start(bf16[130,768]{1,0:T(8,128)(2,1)S(1)} %add_convert_fusion.13), channel_id=1, source_target_pairs={{0,8},{8,16},{16,24},{24,28},{28,20},{20,12},{12,4},{4,0},{1,9},{9... | collective-permute-start | bytes 599048 | tf_op jit(solution)/shard_map/ppermute | solution.py:96
  64.7 7.8 %collective-permute-done.5 = bf16[130,768]{1,0:T(8,128)(2,1)S(1)} collective-permute-done((bf16[130,768]{1,0:T(8,128)(2,1)S(1)}, bf16[130,768]{1,0:T(8,128)(2,1)S(1)}, u32[]{:S(2)}, u32[]{:S(2)}) %collective-permute-start.5) | collective-permute-done | bytes 199712 | tf_op jit(solution)/shard_map/ppermute | solution.py:97
  72.7 1.5 collective-permute-start.10
  74.2 0.6 collective-permute-start.11
  74.8 0.6 collective-permute-start.9
  75.3 1.5 collective-permute-start.8
  76.8 6.9 %collective-permute-done.9 = bf16[130,768]{1,0:T(8,128)(2,1)S(1)} collective-permute-done((bf16[130,768]{1,0:T(8,128)(2,1)S(1)}, bf16[130,768]{1,0:T(8,128)(2,1)S(1)}, u32[]{:S(2)}, u32[]{:S(2)}) %collective-permute-start.9) | collective-permute-done | bytes 199712 | tf_op jit(solution)/shard_map/ppermute | solution.py:97
  83.9 2.3 %collective-permute-start.14 = (bf16[128,1024]{1,0:T(8,128)(2,1)S(1)}, bf16[128,1024]{1,0:T(8,128)(2,1)S(1)}, u32[]{:S(2)}, u32[]{:S(2)}) collective-permute-start(bf16[128,1024]{1,0:T(8,128)(2,1)S(1)} %collective-permute-done.10), channel_id=1, source_target_pairs={{0,8},{8,16},{16,24},{24,28},{28,20},{20,12},{12,4},{4,0},{1,9},{9... | collective-permute-start | bytes 786440 | tf_op jit(solution)/shard_map/ppermute | solution.py:96
  86.5 1.7 %collective-permute-start.12 = (bf16[130,768]{1,0:T(8,128)(2,1)S(1)}, bf16[130,768]{1,0:T(8,128)(2,1)S(1)}, u32[]{:S(2)}, u32[]{:S(2)}) collective-permute-start(bf16[130,768]{1,0:T(8,128)(2,1)S(1)} %add_convert_fusion.9), channel_id=1, source_target_pairs={{0,8},{8,16},{16,24},{24,28},{28,20},{20,12},{12,4},{4,0},{1,9},{9... | collective-permute-start | bytes 599048 | tf_op jit(solution)/shard_map/ppermute | solution.py:96
  88.3 8.6 %collective-permute-done.13 = bf16[130,768]{1,0:T(8,128)(2,1)S(1)} collective-permute-done((bf16[130,768]{1,0:T(8,128)(2,1)S(1)}, bf16[130,768]{1,0:T(8,128)(2,1)S(1)}, u32[]{:S(2)}, u32[]{:S(2)}) %collective-permute-start.13) | collective-permute-done | bytes 199712 | tf_op jit(solution)/shard_map/ppermute | solution.py:97
  97.1 0.7 collective-permute-start.18
  97.9 1.3 collective-permute-start.19
  99.2 2.0 %collective-permute-start.16 = (bf16[130,768]{1,0:T(8,128)(2,1)S(1)}, bf16[130,768]{1,0:T(8,128)(2,1)S(1)}, u32[]{:S(2)}, u32[]{:S(2)}) collective-permute-start(bf16[130,768]{1,0:T(8,128)(2,1)S(1)} %add_convert_fusion.7), channel_id=1, source_target_pairs={{0,8},{8,16},{16,24},{24,28},{28,20},{20,12},{12,4},{4,0},{1,9},{9... | collective-permute-start | bytes 599048 | tf_op jit(solution)/shard_map/ppermute | solution.py:96
  101.3 8.7 %collective-permute-done.17 = bf16[130,768]{1,0:T(8,128)(2,1)S(1)} collective-permute-done((bf16[130,768]{1,0:T(8,128)(2,1)S(1)}, bf16[130,768]{1,0:T(8,128)(2,1)S(1)}, u32[]{:S(2)}, u32[]{:S(2)}) %collective-permute-start.17) | collective-permute-done | bytes 199712 | tf_op jit(solution)/shard_map/ppermute | solution.py:97
  110.1 0.7 collective-permute-start.22
  110.9 1.4 collective-permute-start.23
  112.2 1.3 collective-permute-start.21
  113.5 0.7 collective-permute-start.20
  114.3 7.4 %collective-permute-done.21 = bf16[130,768]{1,0:T(8,128)(2,1)S(1)} collective-permute-done((bf16[130,768]{1,0:T(8,128)(2,1)S(1)}, bf16[130,768]{1,0:T(8,128)(2,1)S(1)}, u32[]{:S(2)}, u32[]{:S(2)}) %collective-permute-start.21) | collective-permute-done | bytes 199712 | tf_op jit(solution)/shard_map/ppermute | solution.py:97
  121.8 0.8 collective-permute-start.24
  122.6 1.5 collective-permute-start.25
  124.2 3.5 %collective-permute-done.24 = bf16[130,768]{1,0:T(8,128)(2,1)S(1)} collective-permute-done((bf16[130,768]{1,0:T(8,128)(2,1)S(1)}, bf16[130,768]{1,0:T(8,128)(2,1)S(1)}, u32[]{:S(2)}, u32[]{:S(2)}) %collective-permute-start.24) | collective-permute-done | bytes 199712 | tf_op jit(solution)/shard_map/ppermute | solution.py:96
  127.8 0.9 collective-permute-done.25
  129.0 4.1 %fusion = f32[16,128,512]{2,1,0:T(8,128)S(1)} fusion(f32[128,512]{1,0:T(8,128)S(1)} %fusion.51, f32[16,512]{1,0:T(8,128)S(1)} %copy-done.2, f32[128,128]{1,0:T(8,128)S(1)} %fusion.52), kind=kOutput, calls=%fused_computation.1 | convolution fusion | flops 1612709888 | bytes 4554752 | tf_op jit(solution)/shard_map/dot_general | solution.py:23
  133.2 3.4 %collective-permute-start.26 = (f32[16,512]{1,0:T(8,128)S(1)}, f32[16,512]{1,0:T(8,128)S(1)}, u32[]{:S(2)}, u32[]{:S(2)}) collective-permute-start(f32[16,512]{1,0:T(8,128)S(1)} %bitcast_multiply_fusion), channel_id=1, source_target_pairs={{0,4},{4,8},{8,12},{12,16},{16,20},{20,24},{24,28},{1,5},{5,9},{9,... | collective-permute-start | bytes 98312 | tf_op jit(solution)/shard_map/ppermute | solution.py:33
  136.6 3.4 %collective-permute-start.27 = (f32[16,512]{1,0:T(8,128)S(1)}, f32[16,512]{1,0:T(8,128)S(1)}, u32[]{:S(2)}, u32[]{:S(2)}) collective-permute-start(f32[16,512]{1,0:T(8,128)S(1)} %bitcast_multiply_fusion), channel_id=1, source_target_pairs={{0,8},{4,12},{8,16},{12,20},{16,24},{20,28},{1,9},{5,13},{9,17},{1... | collective-permute-start | bytes 98312 | tf_op jit(solution)/shard_map/ppermute | solution.py:33
  140.1 2.6 %collective-permute-start.28 = (f32[16,512]{1,0:T(8,128)S(1)}, f32[16,512]{1,0:T(8,128)S(1)}, u32[]{:S(2)}, u32[]{:S(2)}) collective-permute-start(f32[16,512]{1,0:T(8,128)S(1)} %bitcast_multiply_fusion), channel_id=1, source_target_pairs={{0,12},{4,16},{8,20},{12,24},{16,28},{1,13},{5,17},{9,21},{13,25},... | collective-permute-start | bytes 98312 | tf_op jit(solution)/shard_map/ppermute | solution.py:33
  142.8 1.9 %collective-permute-start.29 = (f32[16,512]{1,0:T(8,128)S(1)}, f32[16,512]{1,0:T(8,128)S(1)}, u32[]{:S(2)}, u32[]{:S(2)}) collective-permute-start(f32[16,512]{1,0:T(8,128)S(1)} %bitcast_multiply_fusion), channel_id=1, source_target_pairs={{0,16},{4,20},{8,24},{12,28},{1,17},{5,21},{9,25},{13,29},{2,18},{... | collective-permute-start | bytes 98312 | tf_op jit(solution)/shard_map/ppermute | solution.py:33
  144.7 1.3 collective-permute-start.30
  146.0 1.3 collective-permute-start.31
  147.3 1.3 collective-permute-start.32
  148.7 2.0 %collective-permute-start.34 = (bf16[128,1024]{1,0:T(8,128)(2,1)S(1)}, bf16[128,1024]{1,0:T(8,128)(2,1)S(1)}, u32[]{:S(2)}, u32[]{:S(2)}) collective-permute-start(bf16[128,1024]{1,0:T(8,128)(2,1)S(1)} %collective-permute-done.23), channel_id=1, source_target_pairs={{8,0},{16,8},{24,16},{28,24},{20,28},{12,20},{4,12},{0,4},{9,1},{1... | collective-permute-start | bytes 786440 | tf_op jit(solution)/shard_map/ppermute | solution.py:97
  150.8 1.0 multiply_reduce_fusion
  152.1 7.1 %all_gather.3 = bf16[128,2048]{1,0:T(8,128)(2,1)S(1)} all-gather(bf16[128,512]{1,0:T(8,128)(2,1)S(1)} %multiply_convert_fusion), channel_id=1, replica_groups=mesh['ctx'=8,'tp'=4] {'tp'}, dimensions={1}, use_global_device_ids=true | all-gather | bytes 655360 | tf_op jit(solution)/shard_map/all_gather | solution.py:116
  159.4 1.4 convolution_convert_fusion
  (110 shorter events, 7.8 us)
Async XLA Ops:
  0.0 9.7 %copy-start.9 = (s32[8]{0:T(128)S(1)}, s32[8]{0:T(128)}, u32[]{:S(2)}) copy-start(s32[8]{0:T(128)} %constant.275.clone) | copy-start | bytes 100
  0.0 20.9 %copy-start.3 = (s32[8]{0:T(128)S(1)}, s32[8]{0:T(128)}, u32[]{:S(2)}) copy-start(s32[8]{0:T(128)} %constant.276.clone) | copy-start | bytes 100
  0.0 40.4 %copy-start.1 = (bf16[512,512]{1,0:T(8,128)(2,1)S(1)}, bf16[512,512]{1,0:T(8,128)(2,1)}, u32[]{:S(2)}) copy-start(bf16[512,512]{1,0:T(8,128)(2,1)} %param.15) | copy-start | bytes 1572868
  0.0 41.7 %copy-start.5 = (f32[3,512]{1,0:T(4,128)S(1)}, f32[3,512]{1,0:T(4,128)}, u32[]{:S(2)}) copy-start(f32[3,512]{1,0:T(4,128)} %param.18) | copy-start | bytes 18436
  0.0 41.8 %copy-start.6 = (f32[3,512]{1,0:T(4,128)S(1)}, f32[3,512]{1,0:T(4,128)}, u32[]{:S(2)}) copy-start(f32[3,512]{1,0:T(4,128)} %param.19) | copy-start | bytes 18436
  0.0 41.8 %copy-start.7 = (f32[3,512]{1,0:T(4,128)S(1)}, f32[3,512]{1,0:T(4,128)}, u32[]{:S(2)}) copy-start(f32[3,512]{1,0:T(4,128)} %param.17) | copy-start | bytes 18436
  2.4 40.5 %all-to-all-start = ((bf16[128,8,512]{0,2,1:T(8,128)(2,1)}), bf16[128,8,512]{0,2,1:T(8,128)(2,1)S(1)}, u32[]{:S(2)}, u32[]{:S(2)}) async-start(bf16[128,8,512]{0,2,1:T(8,128)(2,1)} %bitcast.1), calls=%async_computation | async-start | bytes 2097152 | tf_op jit(solution)/shard_map/all_to_all | solution.py:65
  42.9 1.0 copy-start
  46.2 14.3 %collective-permute-start.2 = (bf16[128,1024]{1,0:T(8,128)(2,1)S(1)}, bf16[128,1024]{1,0:T(8,128)(2,1)S(1)}, u32[]{:S(2)}, u32[]{:S(2)}) collective-permute-start(bf16[128,1024]{1,0:T(8,128)(2,1)S(1)} %get-tuple-element.41), channel_id=1, source_target_pairs={{0,8},{8,16},{16,24},{24,28},{28,20},{20,12},{12,4},{4,0},{1,9},{9... | collective-permute-start | bytes 786440 | tf_op jit(solution)/shard_map/ppermute | solution.py:96
  48.3 12.3 %collective-permute-start.3 = (bf16[128,1024]{1,0:T(8,128)(2,1)S(1)}, bf16[128,1024]{1,0:T(8,128)(2,1)S(1)}, u32[]{:S(2)}, u32[]{:S(2)}) collective-permute-start(bf16[128,1024]{1,0:T(8,128)(2,1)S(1)} %get-tuple-element.42), channel_id=1, source_target_pairs={{8,0},{16,8},{24,16},{28,24},{20,28},{12,20},{4,12},{0,4},{9,1},{1... | collective-permute-start | bytes 786440 | tf_op jit(solution)/shard_map/ppermute | solution.py:97
  48.3 11.6 %collective-permute-start.1 = (bf16[130,768]{1,0:T(8,128)(2,1)S(1)}, bf16[130,768]{1,0:T(8,128)(2,1)S(1)}, u32[]{:S(2)}, u32[]{:S(2)}) collective-permute-start(bf16[130,768]{1,0:T(8,128)(2,1)S(1)} %convolution_convert_fusion.1), channel_id=1, source_target_pairs={{8,0},{16,8},{24,16},{28,24},{20,28},{12,20},{4,12},{0,4},{9,1},{1... | collective-permute-start | bytes 599048 | tf_op jit(solution)/shard_map/ppermute | solution.py:97
  50.3 9.9 %collective-permute-start = (bf16[130,768]{1,0:T(8,128)(2,1)S(1)}, bf16[130,768]{1,0:T(8,128)(2,1)S(1)}, u32[]{:S(2)}, u32[]{:S(2)}) collective-permute-start(bf16[130,768]{1,0:T(8,128)(2,1)S(1)} %convolution_convert_fusion.2), channel_id=1, source_target_pairs={{0,8},{8,16},{16,24},{24,28},{28,20},{20,12},{12,4},{4,0},{1,9},{9... | collective-permute-start | bytes 599048 | tf_op jit(solution)/shard_map/ppermute | solution.py:96
  60.6 12.1 %collective-permute-start.6 = (bf16[128,1024]{1,0:T(8,128)(2,1)S(1)}, bf16[128,1024]{1,0:T(8,128)(2,1)S(1)}, u32[]{:S(2)}, u32[]{:S(2)}) collective-permute-start(bf16[128,1024]{1,0:T(8,128)(2,1)S(1)} %collective-permute-done.2), channel_id=1, source_target_pairs={{0,8},{8,16},{16,24},{24,28},{28,20},{20,12},{12,4},{4,0},{1,9},{9... | collective-permute-start | bytes 786440 | tf_op jit(solution)/shard_map/ppermute | solution.py:96
  62.1 10.6 %collective-permute-start.7 = (bf16[128,1024]{1,0:T(8,128)(2,1)S(1)}, bf16[128,1024]{1,0:T(8,128)(2,1)S(1)}, u32[]{:S(2)}, u32[]{:S(2)}) collective-permute-start(bf16[128,1024]{1,0:T(8,128)(2,1)S(1)} %collective-permute-done.3), channel_id=1, source_target_pairs={{8,0},{16,8},{24,16},{28,24},{20,28},{12,20},{4,12},{0,4},{9,1},{1... | collective-permute-start | bytes 786440 | tf_op jit(solution)/shard_map/ppermute | solution.py:97
  62.6 9.9 %collective-permute-start.5 = (bf16[130,768]{1,0:T(8,128)(2,1)S(1)}, bf16[130,768]{1,0:T(8,128)(2,1)S(1)}, u32[]{:S(2)}, u32[]{:S(2)}) collective-permute-start(bf16[130,768]{1,0:T(8,128)(2,1)S(1)} %add_convert_fusion.12), channel_id=1, source_target_pairs={{8,0},{16,8},{24,16},{28,24},{20,28},{12,20},{4,12},{0,4},{9,1},{1... | collective-permute-start | bytes 599048 | tf_op jit(solution)/shard_map/ppermute | solution.py:97
  63.0 9.6 %collective-permute-start.4 = (bf16[130,768]{1,0:T(8,128)(2,1)S(1)}, bf16[130,768]{1,0:T(8,128)(2,1)S(1)}, u32[]{:S(2)}, u32[]{:S(2)}) collective-permute-start(bf16[130,768]{1,0:T(8,128)(2,1)S(1)} %add_convert_fusion.13), channel_id=1, source_target_pairs={{0,8},{8,16},{16,24},{24,28},{28,20},{20,12},{12,4},{4,0},{1,9},{9... | collective-permute-start | bytes 599048 | tf_op jit(solution)/shard_map/ppermute | solution.py:96
  72.7 11.2 %collective-permute-start.10 = (bf16[128,1024]{1,0:T(8,128)(2,1)S(1)}, bf16[128,1024]{1,0:T(8,128)(2,1)S(1)}, u32[]{:S(2)}, u32[]{:S(2)}) collective-permute-start(bf16[128,1024]{1,0:T(8,128)(2,1)S(1)} %collective-permute-done.6), channel_id=1, source_target_pairs={{0,8},{8,16},{16,24},{24,28},{28,20},{20,12},{12,4},{4,0},{1,9},{9... | collective-permute-start | bytes 786440 | tf_op jit(solution)/shard_map/ppermute | solution.py:96
  74.2 9.7 %collective-permute-start.11 = (bf16[128,1024]{1,0:T(8,128)(2,1)S(1)}, bf16[128,1024]{1,0:T(8,128)(2,1)S(1)}, u32[]{:S(2)}, u32[]{:S(2)}) collective-permute-start(bf16[128,1024]{1,0:T(8,128)(2,1)S(1)} %collective-permute-done.7), channel_id=1, source_target_pairs={{8,0},{16,8},{24,16},{28,24},{20,28},{12,20},{4,12},{0,4},{9,1},{1... | collective-permute-start | bytes 786440 | tf_op jit(solution)/shard_map/ppermute | solution.py:97
  74.8 9.0 %collective-permute-start.9 = (bf16[130,768]{1,0:T(8,128)(2,1)S(1)}, bf16[130,768]{1,0:T(8,128)(2,1)S(1)}, u32[]{:S(2)}, u32[]{:S(2)}) collective-permute-start(bf16[130,768]{1,0:T(8,128)(2,1)S(1)} %add_convert_fusion.10), channel_id=1, source_target_pairs={{8,0},{16,8},{24,16},{28,24},{20,28},{12,20},{4,12},{0,4},{9,1},{1... | collective-permute-start | bytes 599048 | tf_op jit(solution)/shard_map/ppermute | solution.py:97
  75.3 8.5 %collective-permute-start.8 = (bf16[130,768]{1,0:T(8,128)(2,1)S(1)}, bf16[130,768]{1,0:T(8,128)(2,1)S(1)}, u32[]{:S(2)}, u32[]{:S(2)}) collective-permute-start(bf16[130,768]{1,0:T(8,128)(2,1)S(1)} %add_convert_fusion.11), channel_id=1, source_target_pairs={{0,8},{8,16},{16,24},{24,28},{28,20},{20,12},{12,4},{4,0},{1,9},{9... | collective-permute-start | bytes 599048 | tf_op jit(solution)/shard_map/ppermute | solution.py:96
  83.9 13.2 %collective-permute-start.14 = (bf16[128,1024]{1,0:T(8,128)(2,1)S(1)}, bf16[128,1024]{1,0:T(8,128)(2,1)S(1)}, u32[]{:S(2)}, u32[]{:S(2)}) collective-permute-start(bf16[128,1024]{1,0:T(8,128)(2,1)S(1)} %collective-permute-done.10), channel_id=1, source_target_pairs={{0,8},{8,16},{16,24},{24,28},{28,20},{20,12},{12,4},{4,0},{1,9},{9... | collective-permute-start | bytes 786440 | tf_op jit(solution)/shard_map/ppermute | solution.py:96
  86.2 10.9 %collective-permute-start.15 = (bf16[128,1024]{1,0:T(8,128)(2,1)S(1)}, bf16[128,1024]{1,0:T(8,128)(2,1)S(1)}, u32[]{:S(2)}, u32[]{:S(2)}) collective-permute-start(bf16[128,1024]{1,0:T(8,128)(2,1)S(1)} %collective-permute-done.11), channel_id=1, source_target_pairs={{8,0},{16,8},{24,16},{28,24},{20,28},{12,20},{4,12},{0,4},{9,1},{1... | collective-permute-start | bytes 786440 | tf_op jit(solution)/shard_map/ppermute | solution.py:97
  86.2 10.8 %collective-permute-start.13 = (bf16[130,768]{1,0:T(8,128)(2,1)S(1)}, bf16[130,768]{1,0:T(8,128)(2,1)S(1)}, u32[]{:S(2)}, u32[]{:S(2)}) collective-permute-start(bf16[130,768]{1,0:T(8,128)(2,1)S(1)} %add_convert_fusion.8), channel_id=1, source_target_pairs={{8,0},{16,8},{24,16},{28,24},{20,28},{12,20},{4,12},{0,4},{9,1},{1... | collective-permute-start | bytes 599048 | tf_op jit(solution)/shard_map/ppermute | solution.py:97
  86.5 10.5 %collective-permute-start.12 = (bf16[130,768]{1,0:T(8,128)(2,1)S(1)}, bf16[130,768]{1,0:T(8,128)(2,1)S(1)}, u32[]{:S(2)}, u32[]{:S(2)}) collective-permute-start(bf16[130,768]{1,0:T(8,128)(2,1)S(1)} %add_convert_fusion.9), channel_id=1, source_target_pairs={{0,8},{8,16},{16,24},{24,28},{28,20},{20,12},{12,4},{4,0},{1,9},{9... | collective-permute-start | bytes 599048 | tf_op jit(solution)/shard_map/ppermute | solution.py:96
  97.1 13.0 %collective-permute-start.18 = (bf16[128,1024]{1,0:T(8,128)(2,1)S(1)}, bf16[128,1024]{1,0:T(8,128)(2,1)S(1)}, u32[]{:S(2)}, u32[]{:S(2)}) collective-permute-start(bf16[128,1024]{1,0:T(8,128)(2,1)S(1)} %collective-permute-done.14), channel_id=1, source_target_pairs={{0,8},{8,16},{16,24},{24,28},{28,20},{20,12},{12,4},{4,0},{1,9},{9... | collective-permute-start | bytes 786440 | tf_op jit(solution)/shard_map/ppermute | solution.py:96
  97.9 12.3 %collective-permute-start.19 = (bf16[128,1024]{1,0:T(8,128)(2,1)S(1)}, bf16[128,1024]{1,0:T(8,128)(2,1)S(1)}, u32[]{:S(2)}, u32[]{:S(2)}) collective-permute-start(bf16[128,1024]{1,0:T(8,128)(2,1)S(1)} %collective-permute-done.15), channel_id=1, source_target_pairs={{8,0},{16,8},{24,16},{28,24},{20,28},{12,20},{4,12},{0,4},{9,1},{1... | collective-permute-start | bytes 786440 | tf_op jit(solution)/shard_map/ppermute | solution.py:97
  99.2 10.8 %collective-permute-start.17 = (bf16[130,768]{1,0:T(8,128)(2,1)S(1)}, bf16[130,768]{1,0:T(8,128)(2,1)S(1)}, u32[]{:S(2)}, u32[]{:S(2)}) collective-permute-start(bf16[130,768]{1,0:T(8,128)(2,1)S(1)} %add_convert_fusion.6), channel_id=1, source_target_pairs={{8,0},{16,8},{24,16},{28,24},{20,28},{12,20},{4,12},{0,4},{9,1},{1... | collective-permute-start | bytes 599048 | tf_op jit(solution)/shard_map/ppermute | solution.py:97
  99.2 10.9 %collective-permute-start.16 = (bf16[130,768]{1,0:T(8,128)(2,1)S(1)}, bf16[130,768]{1,0:T(8,128)(2,1)S(1)}, u32[]{:S(2)}, u32[]{:S(2)}) collective-permute-start(bf16[130,768]{1,0:T(8,128)(2,1)S(1)} %add_convert_fusion.7), channel_id=1, source_target_pairs={{0,8},{8,16},{16,24},{24,28},{28,20},{20,12},{12,4},{4,0},{1,9},{9... | collective-permute-start | bytes 599048 | tf_op jit(solution)/shard_map/ppermute | solution.py:96
  110.1 18.9 %copy-start.2 = (f32[16,512]{1,0:T(8,128)S(1)}, f32[16,512]{1,0:T(8,128)}, u32[]{:S(2)}) copy-start(f32[16,512]{1,0:T(8,128)} %param.20) | copy-start | bytes 98308
  110.1 11.7 %collective-permute-start.22 = (bf16[128,1024]{1,0:T(8,128)(2,1)S(1)}, bf16[128,1024]{1,0:T(8,128)(2,1)S(1)}, u32[]{:S(2)}, u32[]{:S(2)}) collective-permute-start(bf16[128,1024]{1,0:T(8,128)(2,1)S(1)} %collective-permute-done.18), channel_id=1, source_target_pairs={{0,8},{8,16},{16,24},{24,28},{28,20},{20,12},{12,4},{4,0},{1,9},{9... | collective-permute-start | bytes 786440 | tf_op jit(solution)/shard_map/ppermute | solution.py:96
  110.9 11.0 %collective-permute-start.23 = (bf16[128,1024]{1,0:T(8,128)(2,1)S(1)}, bf16[128,1024]{1,0:T(8,128)(2,1)S(1)}, u32[]{:S(2)}, u32[]{:S(2)}) collective-permute-start(bf16[128,1024]{1,0:T(8,128)(2,1)S(1)} %collective-permute-done.19), channel_id=1, source_target_pairs={{8,0},{16,8},{24,16},{28,24},{20,28},{12,20},{4,12},{0,4},{9,1},{1... | collective-permute-start | bytes 786440 | tf_op jit(solution)/shard_map/ppermute | solution.py:97
  112.2 9.5 %collective-permute-start.21 = (bf16[130,768]{1,0:T(8,128)(2,1)S(1)}, bf16[130,768]{1,0:T(8,128)(2,1)S(1)}, u32[]{:S(2)}, u32[]{:S(2)}) collective-permute-start(bf16[130,768]{1,0:T(8,128)(2,1)S(1)} %add_convert_fusion.4), channel_id=1, source_target_pairs={{8,0},{16,8},{24,16},{28,24},{20,28},{12,20},{4,12},{0,4},{9,1},{1... | collective-permute-start | bytes 599048 | tf_op jit(solution)/shard_map/ppermute | solution.py:97
  113.5 8.3 %collective-permute-start.20 = (bf16[130,768]{1,0:T(8,128)(2,1)S(1)}, bf16[130,768]{1,0:T(8,128)(2,1)S(1)}, u32[]{:S(2)}, u32[]{:S(2)}) collective-permute-start(bf16[130,768]{1,0:T(8,128)(2,1)S(1)} %add_convert_fusion.5), channel_id=1, source_target_pairs={{0,8},{8,16},{16,24},{24,28},{28,20},{20,12},{12,4},{4,0},{1,9},{9... | collective-permute-start | bytes 599048 | tf_op jit(solution)/shard_map/ppermute | solution.py:96
  121.8 5.9 %collective-permute-start.24 = (bf16[130,768]{1,0:T(8,128)(2,1)S(1)}, bf16[130,768]{1,0:T(8,128)(2,1)S(1)}, u32[]{:S(2)}, u32[]{:S(2)}) collective-permute-start(bf16[130,768]{1,0:T(8,128)(2,1)S(1)} %add_convert_fusion.3), channel_id=1, source_target_pairs={{0,8},{8,16},{16,24},{24,28},{28,20},{20,12},{12,4},{4,0},{1,9},{9... | collective-permute-start | bytes 599048 | tf_op jit(solution)/shard_map/ppermute | solution.py:96
  122.6 6.0 %collective-permute-start.25 = (bf16[130,768]{1,0:T(8,128)(2,1)S(1)}, bf16[130,768]{1,0:T(8,128)(2,1)S(1)}, u32[]{:S(2)}, u32[]{:S(2)}) collective-permute-start(bf16[130,768]{1,0:T(8,128)(2,1)S(1)} %add_convert_fusion.2), channel_id=1, source_target_pairs={{8,0},{16,8},{24,16},{28,24},{20,28},{12,20},{4,12},{0,4},{9,1},{1... | collective-permute-start | bytes 599048 | tf_op jit(solution)/shard_map/ppermute | solution.py:97
  128.7 22.0 %copy-start.4 = (f32[16,512]{1,0:T(8,128)S(1)}, f32[16,512]{1,0:T(8,128)}, u32[]{:S(2)}) copy-start(f32[16,512]{1,0:T(8,128)} %param.21) | copy-start | bytes 98308
  133.1 18.7 %copy-start.8 = (f32[512]{0:T(512)S(1)}, f32[512]{0:T(512)}, u32[]{:S(2)}) copy-start(f32[512]{0:T(512)} %param.22) | copy-start | bytes 6148
  133.2 12.8 %collective-permute-start.26 = (f32[16,512]{1,0:T(8,128)S(1)}, f32[16,512]{1,0:T(8,128)S(1)}, u32[]{:S(2)}, u32[]{:S(2)}) collective-permute-start(f32[16,512]{1,0:T(8,128)S(1)} %bitcast_multiply_fusion), channel_id=1, source_target_pairs={{0,4},{4,8},{8,12},{12,16},{16,20},{20,24},{24,28},{1,5},{5,9},{9,... | collective-permute-start | bytes 98312 | tf_op jit(solution)/shard_map/ppermute | solution.py:33
  136.6 10.7 %collective-permute-start.27 = (f32[16,512]{1,0:T(8,128)S(1)}, f32[16,512]{1,0:T(8,128)S(1)}, u32[]{:S(2)}, u32[]{:S(2)}) collective-permute-start(f32[16,512]{1,0:T(8,128)S(1)} %bitcast_multiply_fusion), channel_id=1, source_target_pairs={{0,8},{4,12},{8,16},{12,20},{16,24},{20,28},{1,9},{5,13},{9,17},{1... | collective-permute-start | bytes 98312 | tf_op jit(solution)/shard_map/ppermute | solution.py:33
  140.1 8.5 %collective-permute-start.28 = (f32[16,512]{1,0:T(8,128)S(1)}, f32[16,512]{1,0:T(8,128)S(1)}, u32[]{:S(2)}, u32[]{:S(2)}) collective-permute-start(f32[16,512]{1,0:T(8,128)S(1)} %bitcast_multiply_fusion), channel_id=1, source_target_pairs={{0,12},{4,16},{8,20},{12,24},{16,28},{1,13},{5,17},{9,21},{13,25},... | collective-permute-start | bytes 98312 | tf_op jit(solution)/shard_map/ppermute | solution.py:33
  142.8 6.0 %collective-permute-start.29 = (f32[16,512]{1,0:T(8,128)S(1)}, f32[16,512]{1,0:T(8,128)S(1)}, u32[]{:S(2)}, u32[]{:S(2)}) collective-permute-start(f32[16,512]{1,0:T(8,128)S(1)} %bitcast_multiply_fusion), channel_id=1, source_target_pairs={{0,16},{4,20},{8,24},{12,28},{1,17},{5,21},{9,25},{13,29},{2,18},{... | collective-permute-start | bytes 98312 | tf_op jit(solution)/shard_map/ppermute | solution.py:33
  144.7 6.0 %collective-permute-start.30 = (f32[16,512]{1,0:T(8,128)S(1)}, f32[16,512]{1,0:T(8,128)S(1)}, u32[]{:S(2)}, u32[]{:S(2)}) collective-permute-start(f32[16,512]{1,0:T(8,128)S(1)} %bitcast_multiply_fusion), channel_id=1, source_target_pairs={{0,20},{4,24},{8,28},{1,21},{5,25},{9,29},{2,22},{6,26},{10,30},{3... | collective-permute-start | bytes 98312 | tf_op jit(solution)/shard_map/ppermute | solution.py:33
  146.0 4.7 %collective-permute-start.31 = (f32[16,512]{1,0:T(8,128)S(1)}, f32[16,512]{1,0:T(8,128)S(1)}, u32[]{:S(2)}, u32[]{:S(2)}) collective-permute-start(f32[16,512]{1,0:T(8,128)S(1)} %bitcast_multiply_fusion), channel_id=1, source_target_pairs={{0,24},{4,28},{1,25},{5,29},{2,26},{6,30},{3,27},{7,31}} | collective-permute-start | bytes 98312 | tf_op jit(solution)/shard_map/ppermute | solution.py:33
  147.3 3.4 %collective-permute-start.32 = (f32[16,512]{1,0:T(8,128)S(1)}, f32[16,512]{1,0:T(8,128)S(1)}, u32[]{:S(2)}, u32[]{:S(2)}) collective-permute-start(f32[16,512]{1,0:T(8,128)S(1)} %bitcast_multiply_fusion), channel_id=1, source_target_pairs={{0,28},{1,29},{2,30},{3,31}} | collective-permute-start | bytes 98312 | tf_op jit(solution)/shard_map/ppermute | solution.py:33
  148.6 10.6 %collective-permute-start.33 = (bf16[128,1024]{1,0:T(8,128)(2,1)S(1)}, bf16[128,1024]{1,0:T(8,128)(2,1)S(1)}, u32[]{:S(2)}, u32[]{:S(2)}) collective-permute-start(bf16[128,1024]{1,0:T(8,128)(2,1)S(1)} %collective-permute-done.22), channel_id=1, source_target_pairs={{0,8},{8,16},{16,24},{24,28},{28,20},{20,12},{12,4},{4,0},{1,9},{9... | collective-permute-start | bytes 786440 | tf_op jit(solution)/shard_map/ppermute | solution.py:96
  148.7 10.6 %collective-permute-start.34 = (bf16[128,1024]{1,0:T(8,128)(2,1)S(1)}, bf16[128,1024]{1,0:T(8,128)(2,1)S(1)}, u32[]{:S(2)}, u32[]{:S(2)}) collective-permute-start(bf16[128,1024]{1,0:T(8,128)(2,1)S(1)} %collective-permute-done.23), channel_id=1, source_target_pairs={{8,0},{16,8},{24,16},{28,24},{20,28},{12,20},{4,12},{0,4},{9,1},{1... | collective-permute-start | bytes 786440 | tf_op jit(solution)/shard_map/ppermute | solution.py:97

commit v9 on v8

--- a/solution.py
+++ b/solution.py
@@ -83,22 +83,37 @@
     ring_arr = jnp.array(ring, jnp.int32)
     c_chunk = w_out.shape[0]
     c_half = c_chunk // 2
-    w_up, w_low, columns = lax.optimization_barrier((w_out[:c_half], w_out[c_half:], columns))
+    w_up, w_low = w_out[:c_half], w_out[c_half:]
     w_rows = jnp.zeros((2 * ctx_count, c_half, w_out.shape[1]), w_out.dtype)
     w_rows = lax.dynamic_update_slice_in_dim(w_rows, w_up[None], me * 2, 0)
     w_rows = lax.dynamic_update_slice_in_dim(w_rows, w_low[None], me * 2 + 1, 0)
+
+    def w_step(step, w_up, w_low, w_rows):
+        src_up = ring_arr[(my_pos - step) % ctx_count]
+        src_low = ring_arr[(my_pos + step) % ctx_count]
+        w_rows = lax.dynamic_update_slice_in_dim(w_rows, w_up[None], src_up * 2, 0)
+        return lax.dynamic_update_slice_in_dim(w_rows, w_low[None], src_low * 2 + 1, 0)
+
+    early = min(3, ctx_count - 1)
+    for step in range(1, early + 1):
+        w_up = lax.ppermute(w_up, "ctx", perm=fwd)
+        w_low = lax.ppermute(w_low, "ctx", perm=bwd)
+        w_rows = w_step(step, w_up, w_low, w_rows)
+    w_up, w_low, columns = lax.optimization_barrier((w_up, w_low, columns))
     up = piece(ring_arr[(my_pos - 1) % ctx_count], 0)
     down = piece(ring_arr[(my_pos + 1) % ctx_count], 1)
     for step in range(1, ctx_count):
-        sent = lax.optimization_barrier(
-            (up.astype(jnp.bfloat16), down.astype(jnp.bfloat16), w_up, w_low)
-        )
-        up, w_up = lax.ppermute((sent[0], sent[2]), "ctx", perm=fwd)
-        down, w_low = lax.ppermute((sent[1], sent[3]), "ctx", perm=bwd)
-        src_up = ring_arr[(my_pos - step) % ctx_count]
-        src_low = ring_arr[(my_pos + step) % ctx_count]
-        w_rows = lax.dynamic_update_slice_in_dim(w_rows, w_up[None], src_up * 2, 0)
-        w_rows = lax.dynamic_update_slice_in_dim(w_rows, w_low[None], src_low * 2 + 1, 0)
+        w_more = early + step < ctx_count
+        if w_more:
+            sent = lax.optimization_barrier(
+                (up.astype(jnp.bfloat16), down.astype(jnp.bfloat16), w_up, w_low)
+            )
+            up, w_up = lax.ppermute((sent[0], sent[2]), "ctx", perm=fwd)
+            down, w_low = lax.ppermute((sent[1], sent[3]), "ctx", perm=bwd)
+            w_rows = w_step(early + step, w_up, w_low, w_rows)
+        else:
+            up = lax.ppermute(up.astype(jnp.bfloat16), "ctx", perm=fwd)
+            down = lax.ppermute(down.astype(jnp.bfloat16), "ctx", perm=bwd)
         up = up.astype(jnp.float32) + piece(ring_arr[(my_pos - step - 1) % ctx_count], 0)
         down = down.astype(jnp.float32) + piece(ring_arr[(my_pos + step + 1) % ctx_count], 1)
 

time: 162 us -> 178 us (1.099)
  local copies, waits for them, and re-layouts: 8.46 us -> 24.4 us
  waiting for transfers between devices: 49.7 us -> 46.4 us
  matrix products: 10 us -> 12.5 us
  starting transfers between devices: 51.9 us -> 53.7 us
    ppermute x14 -> x8, waiting for transfers between devices: 46.1 us -> 17.5 us  [body(): down, w_low = lax.ppermute((sent[1], sent[3]), 'ctx', perm=bwd)]
    ppermute x0 -> x12, waiting for transfers between devices: none -> 18 us  [the longest x3 10.4 us: body(): up = lax.ppermute(up.astype(jnp.bfloat16), 'ctx', perm=fwd)]
    ppermute x0 -> x12, starting transfers between devices: none -> 15.4 us  [the longest x3 7.48 us: body(): up = lax.ppermute(up.astype(jnp.bfloat16), 'ctx', perm=fwd)]
    dynamic_update_slice x14, local copies, waits for them, and re-layouts: 0.33 us -> 12 us  [the longest x7 6.05 us: w_step(): w_rows = lax.dynamic_update_slice_in_dim(w_rows, w_up[None], src_up * 2, 0)]
    ppermute x14 -> x8, starting transfers between devices: 17.4 us -> 6.71 us  [body(): up, w_up = lax.ppermute((sent[0], sent[2]), 'ctx', perm=fwd)]
    ppermute x14 -> x8, waiting for transfers between devices: 3.55 us -> 10.1 us  [body(): up, w_up = lax.ppermute((sent[0], sent[2]), 'ctx', perm=fwd)]
    ppermute x14 -> x8, starting transfers between devices: 11.9 us -> 9.73 us  [body(): down, w_low = lax.ppermute((sent[1], sent[3]), 'ctx', perm=bwd)]
    dot_general x1, matrix products: 1.42 us -> 3.61 us  [body(): result = jnp.dot(features, w_full, preferred_element_type=jnp.float32)]
  transfers between devices with their start and end apart: 36 -> 36, of which waited for: 8 -> 12; matrix products, arithmetic and copies ran while one was open for 6% -> 18% of each run, Pallas kernels for 0% -> 0%
where the time goes in v9:
time: 178 us; the launch traced here: 177 us
  starting transfers between devices  53.7 us (30%)
  waiting for transfers between devices  46.4 us (26%)
  between operations  30 us (17%)
  local copies, waits for them, and re-layouts  24.4 us (14%)
  matrix products  12.5 us (7%)
  blocking collectives  7.18 us (4%)
  other arithmetic  3.18 us (2%)
    ppermute x8, waiting for transfers between devices, body(): down, w_low = lax.ppermute((sent[1], sent[3]), 'ctx', perm=bwd)  17.5 us
    ppermute x7, starting transfers between devices, modal_long_conv(): lax.ppermute(end_state, 'ctx', perm=[(i, i + shift) for i in range(ctx_co...  15.6 us
    ppermute x3, waiting for transfers between devices, body(): up = lax.ppermute(up.astype(jnp.bfloat16), 'ctx', perm=fwd)  10.4 us
    ppermute x8, waiting for transfers between devices, body(): up, w_up = lax.ppermute((sent[0], sent[2]), 'ctx', perm=fwd)  10.1 us
    ppermute x8, starting transfers between devices, body(): down, w_low = lax.ppermute((sent[1], sent[3]), 'ctx', perm=bwd)  9.73 us
    ppermute x3, starting transfers between devices, body(): up = lax.ppermute(up.astype(jnp.bfloat16), 'ctx', perm=fwd)  7.48 us
    all_gather x1, blocking collectives, body(): features = lax.all_gather(gated, 'tp', axis=1, tiled=True)  7.18 us
    ppermute x3, starting transfers between devices, body(): w_up = lax.ppermute(w_up, 'ctx', perm=fwd)  6.79 us
  transfers between devices with their start and end apart: 36, of which 12 were waited for; matrix products, arithmetic and copies ran while one was open for 18% of the time, Pallas kernels for 0%

profile of v9, /device:TPU:0, one launch (start us, length us, event | category | flops | bytes accessed | tf_op | source)
XLA Modules:
  0.0 177.4 jit_solution(18181866193438691716)
XLA Ops:
  0.0 1.9 %fusion.65 = (bf16[128,1024]{1,0:T(8,128)(2,1)}, bf16[128,1024]{1,0:T(8,128)(2,1)}) fusion(bf16[256,1024]{1,0:T(8,128)(2,1)} %param.23), kind=kLoop, calls=%fused_computation.117 | loop fusion | bytes 1048576 | tf_op jit(solution)/shard_map/slice | solution.py:86
  1.9 3.0 %collective-permute-start = (bf16[128,1024]{1,0:T(8,128)(2,1)}, bf16[128,1024]{1,0:T(8,128)(2,1)}, u32[]{:S(2)}, u32[]{:S(2)}) collective-permute-start(bf16[128,1024]{1,0:T(8,128)(2,1)} %get-tuple-element.44), channel_id=1, source_target_pairs={{0,8},{8,16},{16,24},{24,28},{28,20},{20,12},{12,4},{4,0},{1,9},{9... | collective-permute-start | bytes 786440 | tf_op jit(solution)/shard_map/ppermute | solution.py:99
  4.9 2.3 %copy.14 = bf16[128,4096]{0,1:T(8,128)(2,1)} copy(bf16[128,4096]{1,0:T(8,128)(2,1)} %param.13) | data formatting | bytes 2097152 | tf_op args[0]
  7.2 6.3 %all-to-all-start = ((bf16[128,8,512]{0,2,1:T(8,128)(2,1)}), bf16[128,8,512]{0,2,1:T(8,128)(2,1)S(1)}, u32[]{:S(2)}, u32[]{:S(2)}) async-start(bf16[128,8,512]{0,2,1:T(8,128)(2,1)} %bitcast.1), calls=%async_computation | async-start | bytes 2097152 | tf_op jit(solution)/shard_map/all_to_all | solution.py:65
  13.6 1.5 pad_maximum_fusion.1
  15.1 2.5 %broadcast_in_dim.68 = bf16[16,128,1024]{2,1,0:T(8,128)(2,1)} broadcast(bf16[]{:T(256)} %constant.237.clone.1), dimensions={} | broadcast | bytes 4194306 | tf_op jit(solution)/shard_map/broadcast_in_dim | solution.py:87
  29.3 0.8 fusion.69
  50.0 2.0 %collective-permute-start.1 = (bf16[128,1024]{1,0:T(8,128)(2,1)}, bf16[128,1024]{1,0:T(8,128)(2,1)S(1)}, u32[]{:S(2)}, u32[]{:S(2)}) collective-permute-start(bf16[128,1024]{1,0:T(8,128)(2,1)} %collective-permute-done), channel_id=1, source_target_pairs={{0,8},{8,16},{16,24},{24,28},{28,20},{20,12},{12,4},{4,0},{1,9},{9... | collective-permute-start | bytes 786440 | tf_op jit(solution)/shard_map/ppermute | solution.py:99
  52.1 1.7 bitcast_dynamic-update-slice_fusion.13
  54.6 2.9 %collective-permute-done.1 = bf16[128,1024]{1,0:T(8,128)(2,1)S(1)} collective-permute-done((bf16[128,1024]{1,0:T(8,128)(2,1)}, bf16[128,1024]{1,0:T(8,128)(2,1)S(1)}, u32[]{:S(2)}, u32[]{:S(2)}) %collective-permute-start.1) | collective-permute-done | bytes 262176 | tf_op jit(solution)/shard_map/ppermute | solution.py:99
  57.5 1.7 collective-permute-start.2
  60.2 1.7 bitcast_dynamic-update-slice_fusion.10
  61.9 2.0 %collective-permute-done.2 = bf16[128,1024]{1,0:T(8,128)(2,1)S(1)} collective-permute-done((bf16[128,1024]{1,0:T(8,128)(2,1)S(1)}, bf16[128,1024]{1,0:T(8,128)(2,1)S(1)}, u32[]{:S(2)}, u32[]{:S(2)}) %collective-permute-start.2) | collective-permute-done | bytes 262176 | tf_op jit(solution)/shard_map/ppermute | solution.py:99
  64.6 1.0 copy-done
  65.6 1.5 copy.15
  67.9 1.8 %collective-permute-start.7 = (bf16[130,768]{1,0:T(8,128)(2,1)S(1)}, bf16[130,768]{1,0:T(8,128)(2,1)S(1)}, u32[]{:S(2)}, u32[]{:S(2)}) collective-permute-start(bf16[130,768]{1,0:T(8,128)(2,1)S(1)} %convolution_convert_fusion.1), channel_id=1, source_target_pairs={{8,0},{16,8},{24,16},{28,24},{20,28},{12,20},{4,12},{0,4},{9,1},{1... | collective-permute-start | bytes 599048 | tf_op jit(solution)/shard_map/ppermute | solution.py:112
  70.7 1.7 collective-permute-start.9
  72.7 2.0 %collective-permute-done.7 = bf16[130,768]{1,0:T(8,128)(2,1)S(1)} collective-permute-done((bf16[130,768]{1,0:T(8,128)(2,1)S(1)}, bf16[130,768]{1,0:T(8,128)(2,1)S(1)}, u32[]{:S(2)}, u32[]{:S(2)}) %collective-permute-start.7) | collective-permute-done | bytes 199712 | tf_op jit(solution)/shard_map/ppermute | solution.py:112
  75.0 6.0 %collective-permute-done.6 = bf16[130,768]{1,0:T(8,128)(2,1)S(1)} collective-permute-done((bf16[130,768]{1,0:T(8,128)(2,1)S(1)}, bf16[130,768]{1,0:T(8,128)(2,1)S(1)}, u32[]{:S(2)}, u32[]{:S(2)}) %collective-permute-start.6) | collective-permute-done | bytes 199712 | tf_op jit(solution)/shard_map/ppermute | solution.py:111
  81.6 1.7 collective-permute-start.13
  83.4 1.4 collective-permute-start.11
  86.9 6.0 %collective-permute-done.11 = bf16[130,768]{1,0:T(8,128)(2,1)S(1)} collective-permute-done((bf16[130,768]{1,0:T(8,128)(2,1)S(1)}, bf16[130,768]{1,0:T(8,128)(2,1)S(1)}, u32[]{:S(2)}, u32[]{:S(2)}) %collective-permute-start.11) | collective-permute-done | bytes 199712 | tf_op jit(solution)/shard_map/ppermute | solution.py:112
  93.5 2.1 %collective-permute-start.16 = (bf16[128,1024]{1,0:T(8,128)(2,1)S(1)}, bf16[128,1024]{1,0:T(8,128)(2,1)S(1)}, u32[]{:S(2)}, u32[]{:S(2)}) collective-permute-start(bf16[128,1024]{1,0:T(8,128)(2,1)S(1)} %collective-permute-done.12), channel_id=1, source_target_pairs={{0,8},{8,16},{16,24},{24,28},{28,20},{20,12},{12,4},{4,0},{1,9},{9... | collective-permute-start | bytes 786440 | tf_op jit(solution)/shard_map/ppermute | solution.py:111
  95.6 1.9 %collective-permute-start.15 = (bf16[130,768]{1,0:T(8,128)(2,1)S(1)}, bf16[130,768]{1,0:T(8,128)(2,1)S(1)}, u32[]{:S(2)}, u32[]{:S(2)}) collective-permute-start(bf16[130,768]{1,0:T(8,128)(2,1)S(1)} %fusion.10), channel_id=1, source_target_pairs={{8,0},{16,8},{24,16},{28,24},{20,28},{12,20},{4,12},{0,4},{9,1},{1... | collective-permute-start | bytes 599048 | tf_op jit(solution)/shard_map/ppermute | solution.py:112
  99.0 9.5 %collective-permute-done.15 = bf16[130,768]{1,0:T(8,128)(2,1)S(1)} collective-permute-done((bf16[130,768]{1,0:T(8,128)(2,1)S(1)}, bf16[130,768]{1,0:T(8,128)(2,1)S(1)}, u32[]{:S(2)}, u32[]{:S(2)}) %collective-permute-start.15) | collective-permute-done | bytes 199712 | tf_op jit(solution)/shard_map/ppermute | solution.py:112
  109.1 1.5 collective-permute-start.33
  111.2 1.5 collective-permute-start.18
  113.2 0.7 bitcast_dynamic-update-slice_fusion.3
  114.7 4.1 %collective-permute-done.18 = bf16[130,768]{1,0:T(8,128)(2,1)S(1)} collective-permute-done((bf16[130,768]{1,0:T(8,128)(2,1)S(1)}, bf16[130,768]{1,0:T(8,128)(2,1)S(1)}, u32[]{:S(2)}, u32[]{:S(2)}) %collective-permute-start.18) | collective-permute-done | bytes 199712 | tf_op jit(solution)/shard_map/ppermute | solution.py:111
  119.1 2.5 %collective-permute-start.19 = (bf16[130,768]{1,0:T(8,128)(2,1)S(1)}, bf16[130,768]{1,0:T(8,128)(2,1)S(1)}, u32[]{:S(2)}, u32[]{:S(2)}) collective-permute-start(bf16[130,768]{1,0:T(8,128)(2,1)S(1)} %fusion.13), channel_id=1, source_target_pairs={{0,8},{8,16},{16,24},{24,28},{28,20},{20,12},{12,4},{4,0},{1,9},{9... | collective-permute-start | bytes 599048 | tf_op jit(solution)/shard_map/ppermute | solution.py:115
  122.0 4.9 %collective-permute-done.19 = bf16[130,768]{1,0:T(8,128)(2,1)S(1)} collective-permute-done((bf16[130,768]{1,0:T(8,128)(2,1)S(1)}, bf16[130,768]{1,0:T(8,128)(2,1)S(1)}, u32[]{:S(2)}, u32[]{:S(2)}) %collective-permute-start.19) | collective-permute-done | bytes 199712 | tf_op jit(solution)/shard_map/ppermute | solution.py:115
  127.2 2.5 %collective-permute-start.20 = (bf16[130,768]{1,0:T(8,128)(2,1)S(1)}, bf16[130,768]{1,0:T(8,128)(2,1)S(1)}, u32[]{:S(2)}, u32[]{:S(2)}) collective-permute-start(bf16[130,768]{1,0:T(8,128)(2,1)S(1)} %fusion.14), channel_id=1, source_target_pairs={{0,8},{8,16},{16,24},{24,28},{28,20},{20,12},{12,4},{4,0},{1,9},{9... | collective-permute-start | bytes 599048 | tf_op jit(solution)/shard_map/ppermute | solution.py:115
  130.2 2.8 %collective-permute-done.20 = bf16[130,768]{1,0:T(8,128)(2,1)S(1)} collective-permute-done((bf16[130,768]{1,0:T(8,128)(2,1)S(1)}, bf16[130,768]{1,0:T(8,128)(2,1)S(1)}, u32[]{:S(2)}, u32[]{:S(2)}) %collective-permute-start.20) | collective-permute-done | bytes 199712 | tf_op jit(solution)/shard_map/ppermute | solution.py:115
  133.3 2.5 %collective-permute-start.21 = (bf16[130,768]{1,0:T(8,128)(2,1)S(1)}, bf16[130,768]{1,0:T(8,128)(2,1)S(1)}, u32[]{:S(2)}, u32[]{:S(2)}) collective-permute-start(bf16[130,768]{1,0:T(8,128)(2,1)S(1)} %fusion.15), channel_id=1, source_target_pairs={{0,8},{8,16},{16,24},{24,28},{28,20},{20,12},{12,4},{4,0},{1,9},{9... | collective-permute-start | bytes 599048 | tf_op jit(solution)/shard_map/ppermute | solution.py:115
  136.5 2.6 %collective-permute-done.21 = bf16[130,768]{1,0:T(8,128)(2,1)S(1)} collective-permute-done((bf16[130,768]{1,0:T(8,128)(2,1)S(1)}, bf16[130,768]{1,0:T(8,128)(2,1)S(1)}, u32[]{:S(2)}, u32[]{:S(2)}) %collective-permute-start.21) | collective-permute-done | bytes 199712 | tf_op jit(solution)/shard_map/ppermute | solution.py:115
  139.4 2.7 %collective-permute-done.25 = bf16[130,768]{1,0:T(8,128)(2,1)S(1)} collective-permute-done((bf16[130,768]{1,0:T(8,128)(2,1)S(1)}, bf16[130,768]{1,0:T(8,128)(2,1)S(1)}, u32[]{:S(2)}, u32[]{:S(2)}) %collective-permute-start.25) | collective-permute-done | bytes 199712 | tf_op jit(solution)/shard_map/ppermute | solution.py:116
  142.7 4.4 %fusion = f32[16,128,512]{2,1,0:T(8,128)S(1)} fusion(f32[128,512]{1,0:T(8,128)S(1)} %fusion.47, f32[16,512]{1,0:T(8,128)S(1)} %copy-done.2, f32[128,128]{1,0:T(8,128)S(1)} %fusion.48), kind=kOutput, calls=%fused_computation.1 | convolution fusion | flops 1612709888 | bytes 4554752 | tf_op jit(solution)/shard_map/dot_general | solution.py:23
  147.1 2.1 %collective-permute-start.26 = (f32[16,512]{1,0:T(8,128)S(1)}, f32[16,512]{1,0:T(8,128)S(1)}, u32[]{:S(2)}, u32[]{:S(2)}) collective-permute-start(f32[16,512]{1,0:T(8,128)S(1)} %bitcast_multiply_fusion), channel_id=1, source_target_pairs={{0,4},{4,8},{8,12},{12,16},{16,20},{20,24},{24,28},{1,5},{5,9},{9,... | collective-permute-start | bytes 98312 | tf_op jit(solution)/shard_map/ppermute | solution.py:33
  149.3 3.2 %collective-permute-start.27 = (f32[16,512]{1,0:T(8,128)S(1)}, f32[16,512]{1,0:T(8,128)S(1)}, u32[]{:S(2)}, u32[]{:S(2)}) collective-permute-start(f32[16,512]{1,0:T(8,128)S(1)} %bitcast_multiply_fusion), channel_id=1, source_target_pairs={{0,8},{4,12},{8,16},{12,20},{16,24},{20,28},{1,9},{5,13},{9,17},{1... | collective-permute-start | bytes 98312 | tf_op jit(solution)/shard_map/ppermute | solution.py:33
  153.2 5.2 %collective-permute-start.28 = (f32[16,512]{1,0:T(8,128)S(1)}, f32[16,512]{1,0:T(8,128)S(1)}, u32[]{:S(2)}, u32[]{:S(2)}) collective-permute-start(f32[16,512]{1,0:T(8,128)S(1)} %bitcast_multiply_fusion), channel_id=1, source_target_pairs={{0,12},{4,16},{8,20},{12,24},{16,28},{1,13},{5,17},{9,21},{13,25},... | collective-permute-start | bytes 98312 | tf_op jit(solution)/shard_map/ppermute | solution.py:33
  158.4 1.3 collective-permute-start.29
  159.7 1.3 collective-permute-start.30
  161.0 1.3 collective-permute-start.31
  162.3 1.3 collective-permute-start.32
  164.4 0.8 collective-permute-done.32
  165.2 1.0 multiply_reduce_fusion
  166.6 7.2 %all_gather.3 = bf16[128,2048]{1,0:T(8,128)(2,1)S(1)} all-gather(bf16[128,512]{1,0:T(8,128)(2,1)S(1)} %multiply_convert_fusion), channel_id=1, replica_groups=mesh['ctx'=8,'tp'=4] {'tp'}, dimensions={1}, use_global_device_ids=true | all-gather | bytes 655360 | tf_op jit(solution)/shard_map/all_gather | solution.py:131
  173.8 3.6 %convolution_convert_fusion = bf16[128,1024]{1,0:T(8,128)(2,1)} fusion(bf16[128,2048]{1,0:T(8,128)(2,1)S(1)} %all_gather.3, bf16[2048,1024]{1,0:T(8,128)(2,1)} %bitcast.81), kind=kOutput, calls=%fused_computation.22 | convolution fusion | flops 537001984 | bytes 4980736 | tf_op jit(solution)/shard_map/dot_general | solution.py:133
  (98 shorter events, 19.4 us)
Async XLA Ops:
  0.0 13.5 %copy-start.5 = (f32[3,512]{1,0:T(4,128)S(1)}, f32[3,512]{1,0:T(4,128)}, u32[]{:S(2)}) copy-start(f32[3,512]{1,0:T(4,128)} %param.18) | copy-start | bytes 18436
  0.0 13.6 %copy-start.6 = (f32[3,512]{1,0:T(4,128)S(1)}, f32[3,512]{1,0:T(4,128)}, u32[]{:S(2)}) copy-start(f32[3,512]{1,0:T(4,128)} %param.19) | copy-start | bytes 18436
  0.0 13.6 %copy-start.7 = (f32[3,512]{1,0:T(4,128)S(1)}, f32[3,512]{1,0:T(4,128)}, u32[]{:S(2)}) copy-start(f32[3,512]{1,0:T(4,128)} %param.17) | copy-start | bytes 18436
  1.9 48.1 %collective-permute-start = (bf16[128,1024]{1,0:T(8,128)(2,1)}, bf16[128,1024]{1,0:T(8,128)(2,1)}, u32[]{:S(2)}, u32[]{:S(2)}) collective-permute-start(bf16[128,1024]{1,0:T(8,128)(2,1)} %get-tuple-element.44), channel_id=1, source_target_pairs={{0,8},{8,16},{16,24},{24,28},{28,20},{20,12},{12,4},{4,0},{1,9},{9... | collective-permute-start | bytes 786440 | tf_op jit(solution)/shard_map/ppermute | solution.py:99
  4.9 47.1 %collective-permute-start.3 = (bf16[128,1024]{1,0:T(8,128)(2,1)}, bf16[128,1024]{1,0:T(8,128)(2,1)S(1)}, u32[]{:S(2)}, u32[]{:S(2)}) collective-permute-start(bf16[128,1024]{1,0:T(8,128)(2,1)} %get-tuple-element.43), channel_id=1, source_target_pairs={{8,0},{16,8},{24,16},{28,24},{20,28},{12,20},{4,12},{0,4},{9,1},{1... | collective-permute-start | bytes 786440 | tf_op jit(solution)/shard_map/ppermute | solution.py:100
  7.2 57.3 %all-to-all-start = ((bf16[128,8,512]{0,2,1:T(8,128)(2,1)}), bf16[128,8,512]{0,2,1:T(8,128)(2,1)S(1)}, u32[]{:S(2)}, u32[]{:S(2)}) async-start(bf16[128,8,512]{0,2,1:T(8,128)(2,1)} %bitcast.1), calls=%async_computation | async-start | bytes 2097152 | tf_op jit(solution)/shard_map/all_to_all | solution.py:65
  13.5 4.1 %copy-start.1 = (bf16[256,1024]{1,0:T(8,128)(2,1)S(1)}, bf16[256,1024]{1,0:T(8,128)(2,1)}, u32[]{:S(2)}) copy-start(bf16[256,1024]{1,0:T(8,128)(2,1)} %param.23) | copy-start | bytes 1572868
  13.5 4.8 %copy-start.9 = (s32[8]{0:T(128)S(1)}, s32[8]{0:T(128)}, u32[]{:S(2)}) copy-start(s32[8]{0:T(128)} %constant.275.clone) | copy-start | bytes 100
  13.6 15.7 %copy-start.3 = (s32[8]{0:T(128)S(1)}, s32[8]{0:T(128)}, u32[]{:S(2)}) copy-start(s32[8]{0:T(128)} %constant.276.clone) | copy-start | bytes 100
  50.0 7.4 %collective-permute-start.1 = (bf16[128,1024]{1,0:T(8,128)(2,1)}, bf16[128,1024]{1,0:T(8,128)(2,1)S(1)}, u32[]{:S(2)}, u32[]{:S(2)}) collective-permute-start(bf16[128,1024]{1,0:T(8,128)(2,1)} %collective-permute-done), channel_id=1, source_target_pairs={{0,8},{8,16},{16,24},{24,28},{28,20},{20,12},{12,4},{4,0},{1,9},{9... | collective-permute-start | bytes 786440 | tf_op jit(solution)/shard_map/ppermute | solution.py:99
  52.1 7.1 %collective-permute-start.4 = (bf16[128,1024]{1,0:T(8,128)(2,1)S(1)}, bf16[128,1024]{1,0:T(8,128)(2,1)}, u32[]{:S(2)}, u32[]{:S(2)}) collective-permute-start(bf16[128,1024]{1,0:T(8,128)(2,1)S(1)} %collective-permute-done.3), channel_id=1, source_target_pairs={{8,0},{16,8},{24,16},{28,24},{20,28},{12,20},{4,12},{0,4},{9,1},{1... | collective-permute-start | bytes 786440 | tf_op jit(solution)/shard_map/ppermute | solution.py:100
  57.5 6.4 %collective-permute-start.2 = (bf16[128,1024]{1,0:T(8,128)(2,1)S(1)}, bf16[128,1024]{1,0:T(8,128)(2,1)S(1)}, u32[]{:S(2)}, u32[]{:S(2)}) collective-permute-start(bf16[128,1024]{1,0:T(8,128)(2,1)S(1)} %collective-permute-done.1), channel_id=1, source_target_pairs={{0,8},{8,16},{16,24},{24,28},{28,20},{20,12},{12,4},{4,0},{1,9},{9... | collective-permute-start | bytes 786440 | tf_op jit(solution)/shard_map/ppermute | solution.py:99
  59.2 8.1 %collective-permute-start.5 = (bf16[128,1024]{1,0:T(8,128)(2,1)}, bf16[128,1024]{1,0:T(8,128)(2,1)S(1)}, u32[]{:S(2)}, u32[]{:S(2)}) collective-permute-start(bf16[128,1024]{1,0:T(8,128)(2,1)} %collective-permute-done.4), channel_id=1, source_target_pairs={{8,0},{16,8},{24,16},{28,24},{20,28},{12,20},{4,12},{0,4},{9,1},{1... | collective-permute-start | bytes 786440 | tf_op jit(solution)/shard_map/ppermute | solution.py:100
  64.5 1.0 copy-start
  67.9 6.9 %collective-permute-start.7 = (bf16[130,768]{1,0:T(8,128)(2,1)S(1)}, bf16[130,768]{1,0:T(8,128)(2,1)S(1)}, u32[]{:S(2)}, u32[]{:S(2)}) collective-permute-start(bf16[130,768]{1,0:T(8,128)(2,1)S(1)} %convolution_convert_fusion.1), channel_id=1, source_target_pairs={{8,0},{16,8},{24,16},{28,24},{20,28},{12,20},{4,12},{0,4},{9,1},{1... | collective-permute-start | bytes 599048 | tf_op jit(solution)/shard_map/ppermute | solution.py:112
  70.4 10.9 %collective-permute-start.8 = (bf16[128,1024]{1,0:T(8,128)(2,1)S(1)}, bf16[128,1024]{1,0:T(8,128)(2,1)S(1)}, u32[]{:S(2)}, u32[]{:S(2)}) collective-permute-start(bf16[128,1024]{1,0:T(8,128)(2,1)S(1)} %collective-permute-done.2), channel_id=1, source_target_pairs={{0,8},{8,16},{16,24},{24,28},{28,20},{20,12},{12,4},{4,0},{1,9},{9... | collective-permute-start | bytes 786440 | tf_op jit(solution)/shard_map/ppermute | solution.py:111
  70.7 10.6 %collective-permute-start.9 = (bf16[128,1024]{1,0:T(8,128)(2,1)S(1)}, bf16[128,1024]{1,0:T(8,128)(2,1)S(1)}, u32[]{:S(2)}, u32[]{:S(2)}) collective-permute-start(bf16[128,1024]{1,0:T(8,128)(2,1)S(1)} %collective-permute-done.5), channel_id=1, source_target_pairs={{8,0},{16,8},{24,16},{28,24},{20,28},{12,20},{4,12},{0,4},{9,1},{1... | collective-permute-start | bytes 786440 | tf_op jit(solution)/shard_map/ppermute | solution.py:112
  72.4 8.6 %collective-permute-start.6 = (bf16[130,768]{1,0:T(8,128)(2,1)S(1)}, bf16[130,768]{1,0:T(8,128)(2,1)S(1)}, u32[]{:S(2)}, u32[]{:S(2)}) collective-permute-start(bf16[130,768]{1,0:T(8,128)(2,1)S(1)} %convolution_convert_fusion.2), channel_id=1, source_target_pairs={{0,8},{8,16},{16,24},{24,28},{28,20},{20,12},{12,4},{4,0},{1,9},{9... | collective-permute-start | bytes 599048 | tf_op jit(solution)/shard_map/ppermute | solution.py:111
  81.3 12.2 %collective-permute-start.12 = (bf16[128,1024]{1,0:T(8,128)(2,1)S(1)}, bf16[128,1024]{1,0:T(8,128)(2,1)S(1)}, u32[]{:S(2)}, u32[]{:S(2)}) collective-permute-start(bf16[128,1024]{1,0:T(8,128)(2,1)S(1)} %collective-permute-done.8), channel_id=1, source_target_pairs={{0,8},{8,16},{16,24},{24,28},{28,20},{20,12},{12,4},{4,0},{1,9},{9... | collective-permute-start | bytes 786440 | tf_op jit(solution)/shard_map/ppermute | solution.py:111
  81.6 11.8 %collective-permute-start.13 = (bf16[128,1024]{1,0:T(8,128)(2,1)S(1)}, bf16[128,1024]{1,0:T(8,128)(2,1)S(1)}, u32[]{:S(2)}, u32[]{:S(2)}) collective-permute-start(bf16[128,1024]{1,0:T(8,128)(2,1)S(1)} %collective-permute-done.9), channel_id=1, source_target_pairs={{8,0},{16,8},{24,16},{28,24},{20,28},{12,20},{4,12},{0,4},{9,1},{1... | collective-permute-start | bytes 786440 | tf_op jit(solution)/shard_map/ppermute | solution.py:112
  83.4 9.5 %collective-permute-start.11 = (bf16[130,768]{1,0:T(8,128)(2,1)S(1)}, bf16[130,768]{1,0:T(8,128)(2,1)S(1)}, u32[]{:S(2)}, u32[]{:S(2)}) collective-permute-start(bf16[130,768]{1,0:T(8,128)(2,1)S(1)} %fusion.8), channel_id=1, source_target_pairs={{8,0},{16,8},{24,16},{28,24},{20,28},{12,20},{4,12},{0,4},{9,1},{1... | collective-permute-start | bytes 599048 | tf_op jit(solution)/shard_map/ppermute | solution.py:112
  84.8 8.4 %collective-permute-start.10 = (bf16[130,768]{1,0:T(8,128)(2,1)S(1)}, bf16[130,768]{1,0:T(8,128)(2,1)S(1)}, u32[]{:S(2)}, u32[]{:S(2)}) collective-permute-start(bf16[130,768]{1,0:T(8,128)(2,1)S(1)} %fusion.7), channel_id=1, source_target_pairs={{0,8},{8,16},{16,24},{24,28},{28,20},{20,12},{12,4},{4,0},{1,9},{9... | collective-permute-start | bytes 599048 | tf_op jit(solution)/shard_map/ppermute | solution.py:111
  93.5 15.6 %collective-permute-start.16 = (bf16[128,1024]{1,0:T(8,128)(2,1)S(1)}, bf16[128,1024]{1,0:T(8,128)(2,1)S(1)}, u32[]{:S(2)}, u32[]{:S(2)}) collective-permute-start(bf16[128,1024]{1,0:T(8,128)(2,1)S(1)} %collective-permute-done.12), channel_id=1, source_target_pairs={{0,8},{8,16},{16,24},{24,28},{28,20},{20,12},{12,4},{4,0},{1,9},{9... | collective-permute-start | bytes 786440 | tf_op jit(solution)/shard_map/ppermute | solution.py:111
  95.5 13.6 %collective-permute-start.17 = (bf16[128,1024]{1,0:T(8,128)(2,1)S(1)}, bf16[128,1024]{1,0:T(8,128)(2,1)S(1)}, u32[]{:S(2)}, u32[]{:S(2)}) collective-permute-start(bf16[128,1024]{1,0:T(8,128)(2,1)S(1)} %collective-permute-done.13), channel_id=1, source_target_pairs={{8,0},{16,8},{24,16},{28,24},{20,28},{12,20},{4,12},{0,4},{9,1},{1... | collective-permute-start | bytes 786440 | tf_op jit(solution)/shard_map/ppermute | solution.py:112
  95.6 13.0 %collective-permute-start.15 = (bf16[130,768]{1,0:T(8,128)(2,1)S(1)}, bf16[130,768]{1,0:T(8,128)(2,1)S(1)}, u32[]{:S(2)}, u32[]{:S(2)}) collective-permute-start(bf16[130,768]{1,0:T(8,128)(2,1)S(1)} %fusion.10), channel_id=1, source_target_pairs={{8,0},{16,8},{24,16},{28,24},{20,28},{12,20},{4,12},{0,4},{9,1},{1... | collective-permute-start | bytes 599048 | tf_op jit(solution)/shard_map/ppermute | solution.py:112
  97.5 11.3 %collective-permute-start.14 = (bf16[130,768]{1,0:T(8,128)(2,1)S(1)}, bf16[130,768]{1,0:T(8,128)(2,1)S(1)}, u32[]{:S(2)}, u32[]{:S(2)}) collective-permute-start(bf16[130,768]{1,0:T(8,128)(2,1)S(1)} %fusion.9), channel_id=1, source_target_pairs={{0,8},{8,16},{16,24},{24,28},{28,20},{20,12},{12,4},{4,0},{1,9},{9... | collective-permute-start | bytes 599048 | tf_op jit(solution)/shard_map/ppermute | solution.py:111
  109.1 43.4 %collective-permute-start.33 = (bf16[128,1024]{1,0:T(8,128)(2,1)S(1)}, bf16[128,1024]{1,0:T(8,128)(2,1)S(1)}, u32[]{:S(2)}, u32[]{:S(2)}) collective-permute-start(bf16[128,1024]{1,0:T(8,128)(2,1)S(1)} %collective-permute-done.16), channel_id=1, source_target_pairs={{0,8},{8,16},{16,24},{24,28},{28,20},{20,12},{12,4},{4,0},{1,9},{9... | collective-permute-start | bytes 786440 | tf_op jit(solution)/shard_map/ppermute | solution.py:111
  110.7 49.0 %collective-permute-start.34 = (bf16[128,1024]{1,0:T(8,128)(2,1)S(1)}, bf16[128,1024]{1,0:T(8,128)(2,1)S(1)}, u32[]{:S(2)}, u32[]{:S(2)}) collective-permute-start(bf16[128,1024]{1,0:T(8,128)(2,1)S(1)} %collective-permute-done.17), channel_id=1, source_target_pairs={{8,0},{16,8},{24,16},{28,24},{20,28},{12,20},{4,12},{0,4},{9,1},{1... | collective-permute-start | bytes 786440 | tf_op jit(solution)/shard_map/ppermute | solution.py:112
  111.2 7.6 %collective-permute-start.18 = (bf16[130,768]{1,0:T(8,128)(2,1)S(1)}, bf16[130,768]{1,0:T(8,128)(2,1)S(1)}, u32[]{:S(2)}, u32[]{:S(2)}) collective-permute-start(bf16[130,768]{1,0:T(8,128)(2,1)S(1)} %fusion.11), channel_id=1, source_target_pairs={{0,8},{8,16},{16,24},{24,28},{28,20},{20,12},{12,4},{4,0},{1,9},{9... | collective-permute-start | bytes 599048 | tf_op jit(solution)/shard_map/ppermute | solution.py:111
  112.7 8.9 %collective-permute-start.22 = (bf16[130,768]{1,0:T(8,128)(2,1)S(1)}, bf16[130,768]{1,0:T(8,128)(2,1)S(1)}, u32[]{:S(2)}, u32[]{:S(2)}) collective-permute-start(bf16[130,768]{1,0:T(8,128)(2,1)S(1)} %fusion.12), channel_id=1, source_target_pairs={{8,0},{16,8},{24,16},{28,24},{20,28},{12,20},{4,12},{0,4},{9,1},{1... | collective-permute-start | bytes 599048 | tf_op jit(solution)/shard_map/ppermute | solution.py:112
  119.1 7.8 %collective-permute-start.19 = (bf16[130,768]{1,0:T(8,128)(2,1)S(1)}, bf16[130,768]{1,0:T(8,128)(2,1)S(1)}, u32[]{:S(2)}, u32[]{:S(2)}) collective-permute-start(bf16[130,768]{1,0:T(8,128)(2,1)S(1)} %fusion.13), channel_id=1, source_target_pairs={{0,8},{8,16},{16,24},{24,28},{28,20},{20,12},{12,4},{4,0},{1,9},{9... | collective-permute-start | bytes 599048 | tf_op jit(solution)/shard_map/ppermute | solution.py:115
  121.9 7.7 %collective-permute-start.23 = (bf16[130,768]{1,0:T(8,128)(2,1)S(1)}, bf16[130,768]{1,0:T(8,128)(2,1)S(1)}, u32[]{:S(2)}, u32[]{:S(2)}) collective-permute-start(bf16[130,768]{1,0:T(8,128)(2,1)S(1)} %fusion.17), channel_id=1, source_target_pairs={{8,0},{16,8},{24,16},{28,24},{20,28},{12,20},{4,12},{0,4},{9,1},{1... | collective-permute-start | bytes 599048 | tf_op jit(solution)/shard_map/ppermute | solution.py:116
  127.2 5.9 %collective-permute-start.20 = (bf16[130,768]{1,0:T(8,128)(2,1)S(1)}, bf16[130,768]{1,0:T(8,128)(2,1)S(1)}, u32[]{:S(2)}, u32[]{:S(2)}) collective-permute-start(bf16[130,768]{1,0:T(8,128)(2,1)S(1)} %fusion.14), channel_id=1, source_target_pairs={{0,8},{8,16},{16,24},{24,28},{28,20},{20,12},{12,4},{4,0},{1,9},{9... | collective-permute-start | bytes 599048 | tf_op jit(solution)/shard_map/ppermute | solution.py:115
  129.9 12.8 %copy-start.2 = (f32[16,512]{1,0:T(8,128)S(1)}, f32[16,512]{1,0:T(8,128)}, u32[]{:S(2)}) copy-start(f32[16,512]{1,0:T(8,128)} %param.20) | copy-start | bytes 98308
  129.9 5.9 %collective-permute-start.24 = (bf16[130,768]{1,0:T(8,128)(2,1)S(1)}, bf16[130,768]{1,0:T(8,128)(2,1)S(1)}, u32[]{:S(2)}, u32[]{:S(2)}) collective-permute-start(bf16[130,768]{1,0:T(8,128)(2,1)S(1)} %fusion.18), channel_id=1, source_target_pairs={{8,0},{16,8},{24,16},{28,24},{20,28},{12,20},{4,12},{0,4},{9,1},{1... | collective-permute-start | bytes 599048 | tf_op jit(solution)/shard_map/ppermute | solution.py:116
  133.3 5.9 %collective-permute-start.21 = (bf16[130,768]{1,0:T(8,128)(2,1)S(1)}, bf16[130,768]{1,0:T(8,128)(2,1)S(1)}, u32[]{:S(2)}, u32[]{:S(2)}) collective-permute-start(bf16[130,768]{1,0:T(8,128)(2,1)S(1)} %fusion.15), channel_id=1, source_target_pairs={{0,8},{8,16},{16,24},{24,28},{28,20},{20,12},{12,4},{4,0},{1,9},{9... | collective-permute-start | bytes 599048 | tf_op jit(solution)/shard_map/ppermute | solution.py:115
  136.1 6.0 %collective-permute-start.25 = (bf16[130,768]{1,0:T(8,128)(2,1)S(1)}, bf16[130,768]{1,0:T(8,128)(2,1)S(1)}, u32[]{:S(2)}, u32[]{:S(2)}) collective-permute-start(bf16[130,768]{1,0:T(8,128)(2,1)S(1)} %fusion.19), channel_id=1, source_target_pairs={{8,0},{16,8},{24,16},{28,24},{20,28},{12,20},{4,12},{0,4},{9,1},{1... | collective-permute-start | bytes 599048 | tf_op jit(solution)/shard_map/ppermute | solution.py:116
  142.4 22.8 %copy-start.4 = (f32[16,512]{1,0:T(8,128)S(1)}, f32[16,512]{1,0:T(8,128)}, u32[]{:S(2)}) copy-start(f32[16,512]{1,0:T(8,128)} %param.21) | copy-start | bytes 98308
  147.1 19.2 %copy-start.8 = (f32[512]{0:T(512)S(1)}, f32[512]{0:T(512)}, u32[]{:S(2)}) copy-start(f32[512]{0:T(512)} %param.22) | copy-start | bytes 6148
  147.1 13.8 %collective-permute-start.26 = (f32[16,512]{1,0:T(8,128)S(1)}, f32[16,512]{1,0:T(8,128)S(1)}, u32[]{:S(2)}, u32[]{:S(2)}) collective-permute-start(f32[16,512]{1,0:T(8,128)S(1)} %bitcast_multiply_fusion), channel_id=1, source_target_pairs={{0,4},{4,8},{8,12},{12,16},{16,20},{20,24},{24,28},{1,5},{5,9},{9,... | collective-permute-start | bytes 98312 | tf_op jit(solution)/shard_map/ppermute | solution.py:33
  149.3 13.0 %collective-permute-start.27 = (f32[16,512]{1,0:T(8,128)S(1)}, f32[16,512]{1,0:T(8,128)S(1)}, u32[]{:S(2)}, u32[]{:S(2)}) collective-permute-start(f32[16,512]{1,0:T(8,128)S(1)} %bitcast_multiply_fusion), channel_id=1, source_target_pairs={{0,8},{4,12},{8,16},{12,20},{16,24},{20,28},{1,9},{5,13},{9,17},{1... | collective-permute-start | bytes 98312 | tf_op jit(solution)/shard_map/ppermute | solution.py:33
  153.2 11.1 %collective-permute-start.28 = (f32[16,512]{1,0:T(8,128)S(1)}, f32[16,512]{1,0:T(8,128)S(1)}, u32[]{:S(2)}, u32[]{:S(2)}) collective-permute-start(f32[16,512]{1,0:T(8,128)S(1)} %bitcast_multiply_fusion), channel_id=1, source_target_pairs={{0,12},{4,16},{8,20},{12,24},{16,28},{1,13},{5,17},{9,21},{13,25},... | collective-permute-start | bytes 98312 | tf_op jit(solution)/shard_map/ppermute | solution.py:33
  158.4 6.0 %collective-permute-start.29 = (f32[16,512]{1,0:T(8,128)S(1)}, f32[16,512]{1,0:T(8,128)S(1)}, u32[]{:S(2)}, u32[]{:S(2)}) collective-permute-start(f32[16,512]{1,0:T(8,128)S(1)} %bitcast_multiply_fusion), channel_id=1, source_target_pairs={{0,16},{4,20},{8,24},{12,28},{1,17},{5,21},{9,25},{13,29},{2,18},{... | collective-permute-start | bytes 98312 | tf_op jit(solution)/shard_map/ppermute | solution.py:33
  159.7 4.7 %collective-permute-start.30 = (f32[16,512]{1,0:T(8,128)S(1)}, f32[16,512]{1,0:T(8,128)S(1)}, u32[]{:S(2)}, u32[]{:S(2)}) collective-permute-start(f32[16,512]{1,0:T(8,128)S(1)} %bitcast_multiply_fusion), channel_id=1, source_target_pairs={{0,20},{4,24},{8,28},{1,21},{5,25},{9,29},{2,22},{6,26},{10,30},{3... | collective-permute-start | bytes 98312 | tf_op jit(solution)/shard_map/ppermute | solution.py:33
  161.0 3.4 %collective-permute-start.31 = (f32[16,512]{1,0:T(8,128)S(1)}, f32[16,512]{1,0:T(8,128)S(1)}, u32[]{:S(2)}, u32[]{:S(2)}) collective-permute-start(f32[16,512]{1,0:T(8,128)S(1)} %bitcast_multiply_fusion), channel_id=1, source_target_pairs={{0,24},{4,28},{1,25},{5,29},{2,26},{6,30},{3,27},{7,31}} | collective-permute-start | bytes 98312 | tf_op jit(solution)/shard_map/ppermute | solution.py:33
  162.3 2.9 %collective-permute-start.32 = (f32[16,512]{1,0:T(8,128)S(1)}, f32[16,512]{1,0:T(8,128)S(1)}, u32[]{:S(2)}, u32[]{:S(2)}) collective-permute-start(f32[16,512]{1,0:T(8,128)S(1)} %bitcast_multiply_fusion), channel_id=1, source_target_pairs={{0,28},{1,29},{2,30},{3,31}} | collective-permute-start | bytes 98312 | tf_op jit(solution)/shard_map/ppermute | solution.py:33

commit v10 on v8

--- a/solution.py
+++ b/solution.py
@@ -62,8 +62,6 @@
     ctx_count = lax.axis_size("ctx")
     length = tokens.shape[0]
     width = w_query.shape[1]
-    columns = lax.all_to_all(tokens, "ctx", split_axis=1, concat_axis=0, tiled=True)
-    columns = jnp.concatenate([jnp.zeros((2, columns.shape[1]), columns.dtype), columns], axis=0)
     w_cat = jnp.concatenate([w_query, w_key, w_value], axis=1)
     split = w_cat.shape[1] // 2
     halves = (w_cat[:, :split], w_cat[:, split:])
@@ -81,6 +79,20 @@
     me = lax.axis_index("ctx")
     my_pos = jnp.array(place, jnp.int32)[me]
     ring_arr = jnp.array(ring, jnp.int32)
+    d_chunk = tokens.shape[1] // ctx_count
+    blocks = jnp.zeros((ctx_count, length, d_chunk), tokens.dtype)
+    blocks = lax.dynamic_update_slice_in_dim(
+        blocks, lax.dynamic_slice_in_dim(tokens, me * d_chunk, d_chunk, 1)[None], me, 0
+    )
+    for offset in range(1, ctx_count):
+        dest = ring_arr[(my_pos + offset) % ctx_count]
+        src_dev = ring_arr[(my_pos - offset) % ctx_count]
+        shift = [(ring[k], ring[(k + offset) % ctx_count]) for k in range(ctx_count)]
+        outgoing = lax.dynamic_slice_in_dim(tokens, dest * d_chunk, d_chunk, 1)
+        incoming = lax.ppermute(outgoing, "ctx", perm=shift)
+        blocks = lax.dynamic_update_slice_in_dim(blocks, incoming[None], src_dev, 0)
+    columns = blocks.reshape(ctx_count * length, d_chunk)
+    columns = jnp.concatenate([jnp.zeros((2, d_chunk), columns.dtype), columns], axis=0)
     c_chunk = w_out.shape[0]
     c_half = c_chunk // 2
     w_up, w_low, columns = lax.optimization_barrier((w_out[:c_half], w_out[c_half:], columns))

time: 162 us -> 193 us (1.19)
  between operations: 30.1 us -> 48.1 us
  starting transfers between devices: 51.9 us -> 58.1 us
  local copies, waits for them, and re-layouts: 8.46 us -> 12.2 us
  waiting for transfers between devices: 49.7 us -> 51.9 us
    ppermute x0 -> x7, starting transfers between devices: none -> 13.4 us  [body(): incoming = lax.ppermute(outgoing, 'ctx', perm=shift)]
    all_to_all x1 -> x0, starting transfers between devices: 7.29 us -> none  [body(): lax.all_to_all(tokens, 'ctx', split_axis=1, concat_axis=0, tiled=True)]
    ppermute x0 -> x7, waiting for transfers between devices: none -> 5.02 us  [body(): incoming = lax.ppermute(outgoing, 'ctx', perm=shift)]
    ppermute x14, starting transfers between devices: 17.4 us -> 13.1 us  [body(): up, w_up = lax.ppermute((sent[0], sent[2]), 'ctx', perm=fwd)]
    ppermute x14, starting transfers between devices: 11.9 us -> 15.9 us  [body(): down, w_low = lax.ppermute((sent[1], sent[3]), 'ctx', perm=bwd)]
    ppermute x14, waiting for transfers between devices: 46.1 us -> 42.2 us  [body(): down, w_low = lax.ppermute((sent[1], sent[3]), 'ctx', perm=bwd)]
    unnamed x21 -> x6, local copies, waits for them, and re-layouts: 3.37 us -> 0.02 us
    dynamic_update_slice x0 -> x8, local copies, waits for them, and re-layouts: none -> 2.83 us  [the longest x7 1.9 us: body(): blocks = lax.dynamic_update_slice_in_dim(blocks, incoming[None], src_dev, 0)]
  transfers between devices with their start and end apart: 36 -> 42, of which waited for: 8 -> 13; matrix products, arithmetic and copies ran while one was open for 6% -> 8% of each run, Pallas kernels for 0% -> 0%
where the time goes in v10:
time: 193 us; the launch traced here: 191 us
  starting transfers between devices  58.1 us (30%)
  waiting for transfers between devices  51.9 us (27%)
  between operations  48.1 us (25%)
  local copies, waits for them, and re-layouts  12.2 us (6%)
  matrix products  10.3 us (5%)
  blocking collectives  7.19 us (4%)
  other arithmetic  3.68 us (2%)
    ppermute x14, waiting for transfers between devices, body(): down, w_low = lax.ppermute((sent[1], sent[3]), 'ctx', perm=bwd)  42.2 us
    ppermute x14, starting transfers between devices, body(): down, w_low = lax.ppermute((sent[1], sent[3]), 'ctx', perm=bwd)  15.9 us
    ppermute x7, starting transfers between devices, modal_long_conv(): lax.ppermute(end_state, 'ctx', perm=[(i, i + shift) for i in range(ctx_co...  15.7 us
    ppermute x7, starting transfers between devices, body(): incoming = lax.ppermute(outgoing, 'ctx', perm=shift)  13.4 us
    ppermute x14, starting transfers between devices, body(): up, w_up = lax.ppermute((sent[0], sent[2]), 'ctx', perm=fwd)  13.1 us
    all_gather x1, blocking collectives, body(): features = lax.all_gather(gated, 'tp', axis=1, tiled=True)  7.19 us
    ppermute x7, waiting for transfers between devices, body(): incoming = lax.ppermute(outgoing, 'ctx', perm=shift)  5.02 us
    ppermute x14, waiting for transfers between devices, body(): up, w_up = lax.ppermute((sent[0], sent[2]), 'ctx', perm=fwd)  4.69 us
  transfers between devices with their start and end apart: 42, of which 13 were waited for; matrix products, arithmetic and copies ran while one was open for 8% of the time, Pallas kernels for 0%

profile of v10, /device:TPU:0, one launch (start us, length us, event | category | flops | bytes accessed | tf_op | source)
XLA Modules:
  0.0 191.5 jit_solution(14790830582066322400)
XLA Ops:
  0.0 1.2 dynamic_slice.152
  11.9 2.0 %fusion.73 = (s32[1]{0:T(128)}, s32[1]{0:T(128)}, s32[1]{0:T(128)}, s32[1]{0:T(128)}, s32[1]{0:T(128)}, /*index=5*/s32[1]{0:T(128)}, s32[1]{0:T(128)}, s32[1]{0:...) fusion(s32[8]{0:T(128)} %constant.304.clone, ...), kind=kLoop, calls=%fused_computation.136 | loop fusion | bytes 192 | tf_op jit(solution)/shard_map/dynamic_slice | solution.py:114
  18.4 1.3 constant_dynamic-slice_fusion
  19.7 3.1 %collective-permute-start = (bf16[128,512]{1,0:T(8,128)(2,1)S(1)}, bf16[128,512]{1,0:T(8,128)(2,1)}, u32[]{:S(2)}, u32[]{:S(2)}) collective-permute-start(bf16[128,512]{1,0:T(8,128)(2,1)S(1)} %get-tuple-element.72), channel_id=1, source_target_pairs={{0,8},{8,16},{16,24},{24,28},{28,20},{20,12},{12,4},{4,0},{1,9},{9... | collective-permute-start | bytes 393224 | tf_op jit(solution)/shard_map/ppermute | solution.py:92
  22.8 2.6 %collective-permute-start.1 = (bf16[128,512]{1,0:T(8,128)(2,1)S(1)}, bf16[128,512]{1,0:T(8,128)(2,1)}, u32[]{:S(2)}, u32[]{:S(2)}) collective-permute-start(bf16[128,512]{1,0:T(8,128)(2,1)S(1)} %get-tuple-element.71), channel_id=1, source_target_pairs={{0,16},{8,24},{16,28},{24,20},{28,12},{20,4},{12,0},{4,8},{1,17},{... | collective-permute-start | bytes 393224 | tf_op jit(solution)/shard_map/ppermute | solution.py:92
  25.4 1.3 collective-permute-start.2
  26.7 2.4 %collective-permute-start.3 = (bf16[128,512]{1,0:T(8,128)(2,1)S(1)}, bf16[128,512]{1,0:T(8,128)(2,1)S(1)}, u32[]{:S(2)}, u32[]{:S(2)}) collective-permute-start(bf16[128,512]{1,0:T(8,128)(2,1)S(1)} %get-tuple-element.69), channel_id=1, source_target_pairs={{0,28},{8,20},{16,12},{24,4},{28,0},{20,8},{12,16},{4,24},{1,29},{... | collective-permute-start | bytes 393224 | tf_op jit(solution)/shard_map/ppermute | solution.py:92
  29.5 1.1 fusion.69
  33.0 1.5 pad_maximum_fusion.1
  66.9 0.9 bitcast_dynamic-update-slice_fusion.23
  67.8 3.5 %collective-permute-start.5 = (bf16[128,512]{1,0:T(8,128)(2,1)S(1)}, bf16[128,512]{1,0:T(8,128)(2,1)S(1)}, u32[]{:S(2)}, u32[]{:S(2)}) collective-permute-start(bf16[128,512]{1,0:T(8,128)(2,1)S(1)} %get-tuple-element.73), channel_id=1, source_target_pairs={{0,12},{8,4},{16,0},{24,8},{28,16},{20,24},{12,28},{4,20},{1,13},{... | collective-permute-start | bytes 393224 | tf_op jit(solution)/shard_map/ppermute | solution.py:92
  73.3 3.2 %collective-permute-done.5 = bf16[128,512]{1,0:T(8,128)(2,1)S(1)} collective-permute-done((bf16[128,512]{1,0:T(8,128)(2,1)S(1)}, bf16[128,512]{1,0:T(8,128)(2,1)S(1)}, u32[]{:S(2)}, u32[]{:S(2)}) %collective-permute-start.5) | collective-permute-done | bytes 131104 | tf_op jit(solution)/shard_map/ppermute | solution.py:92
  76.6 1.8 collective-permute-done.6
  79.7 1.6 collective-permute-start.10
  81.4 1.9 %collective-permute-start.7 = (bf16[130,768]{1,0:T(8,128)(2,1)S(1)}, bf16[130,768]{1,0:T(8,128)(2,1)S(1)}, u32[]{:S(2)}, u32[]{:S(2)}) collective-permute-start(bf16[130,768]{1,0:T(8,128)(2,1)S(1)} %convolution_convert_fusion.2), channel_id=1, source_target_pairs={{0,8},{8,16},{16,24},{24,28},{28,20},{20,12},{12,4},{4,0},{1,9},{9... | collective-permute-start | bytes 599048 | tf_op jit(solution)/shard_map/ppermute | solution.py:108
  87.4 3.7 %collective-permute-done.8 = bf16[130,768]{1,0:T(8,128)(2,1)S(1)} collective-permute-done((bf16[130,768]{1,0:T(8,128)(2,1)S(1)}, bf16[130,768]{1,0:T(8,128)(2,1)S(1)}, u32[]{:S(2)}, u32[]{:S(2)}) %collective-permute-start.8) | collective-permute-done | bytes 199712 | tf_op jit(solution)/shard_map/ppermute | solution.py:109
  92.1 1.7 collective-permute-start.14
  94.7 1.1 collective-permute-start.11
  95.9 6.6 %collective-permute-done.12 = bf16[130,768]{1,0:T(8,128)(2,1)S(1)} collective-permute-done((bf16[130,768]{1,0:T(8,128)(2,1)S(1)}, bf16[130,768]{1,0:T(8,128)(2,1)S(1)}, u32[]{:S(2)}, u32[]{:S(2)}) %collective-permute-start.12) | collective-permute-done | bytes 199712 | tf_op jit(solution)/shard_map/ppermute | solution.py:109
  102.7 0.9 collective-permute-start.17
  103.6 1.1 collective-permute-start.18
  104.7 1.8 collective-permute-start.16
  106.8 6.0 %collective-permute-done.16 = bf16[130,768]{1,0:T(8,128)(2,1)S(1)} collective-permute-done((bf16[130,768]{1,0:T(8,128)(2,1)S(1)}, bf16[130,768]{1,0:T(8,128)(2,1)S(1)}, u32[]{:S(2)}, u32[]{:S(2)}) %collective-permute-start.16) | collective-permute-done | bytes 199712 | tf_op jit(solution)/shard_map/ppermute | solution.py:109
  114.6 1.2 collective-permute-start.22
  115.8 1.7 collective-permute-start.20
  117.9 7.2 %collective-permute-done.20 = bf16[130,768]{1,0:T(8,128)(2,1)S(1)} collective-permute-done((bf16[130,768]{1,0:T(8,128)(2,1)S(1)}, bf16[130,768]{1,0:T(8,128)(2,1)S(1)}, u32[]{:S(2)}, u32[]{:S(2)}) %collective-permute-start.20) | collective-permute-done | bytes 199712 | tf_op jit(solution)/shard_map/ppermute | solution.py:109
  125.6 2.1 %collective-permute-start.25 = (bf16[128,1024]{1,0:T(8,128)(2,1)S(1)}, bf16[128,1024]{1,0:T(8,128)(2,1)S(1)}, u32[]{:S(2)}, u32[]{:S(2)}) collective-permute-start(bf16[128,1024]{1,0:T(8,128)(2,1)S(1)} %collective-permute-done.21), channel_id=1, source_target_pairs={{0,8},{8,16},{16,24},{24,28},{28,20},{20,12},{12,4},{4,0},{1,9},{9... | collective-permute-start | bytes 786440 | tf_op jit(solution)/shard_map/ppermute | solution.py:108
  127.6 1.2 collective-permute-start.24
  129.8 9.8 %collective-permute-done.24 = bf16[130,768]{1,0:T(8,128)(2,1)S(1)} collective-permute-done((bf16[130,768]{1,0:T(8,128)(2,1)S(1)}, bf16[130,768]{1,0:T(8,128)(2,1)S(1)}, u32[]{:S(2)}, u32[]{:S(2)}) %collective-permute-start.24) | collective-permute-done | bytes 199712 | tf_op jit(solution)/shard_map/ppermute | solution.py:109
  140.6 1.2 collective-permute-start.30
  141.8 2.0 %collective-permute-start.27 = (bf16[130,768]{1,0:T(8,128)(2,1)S(1)}, bf16[130,768]{1,0:T(8,128)(2,1)S(1)}, u32[]{:S(2)}, u32[]{:S(2)}) collective-permute-start(bf16[130,768]{1,0:T(8,128)(2,1)S(1)} %add_convert_fusion.5), channel_id=1, source_target_pairs={{0,8},{8,16},{16,24},{24,28},{28,20},{20,12},{12,4},{4,0},{1,9},{9... | collective-permute-start | bytes 599048 | tf_op jit(solution)/shard_map/ppermute | solution.py:108
  143.8 7.6 %collective-permute-done.28 = bf16[130,768]{1,0:T(8,128)(2,1)S(1)} collective-permute-done((bf16[130,768]{1,0:T(8,128)(2,1)S(1)}, bf16[130,768]{1,0:T(8,128)(2,1)S(1)}, u32[]{:S(2)}, u32[]{:S(2)}) %collective-permute-start.28) | collective-permute-done | bytes 199712 | tf_op jit(solution)/shard_map/ppermute | solution.py:109
  151.6 1.0 collective-permute-start.31
  152.6 1.3 collective-permute-start.32
  153.9 3.5 %collective-permute-done.31 = bf16[130,768]{1,0:T(8,128)(2,1)S(1)} collective-permute-done((bf16[130,768]{1,0:T(8,128)(2,1)S(1)}, bf16[130,768]{1,0:T(8,128)(2,1)S(1)}, u32[]{:S(2)}, u32[]{:S(2)}) %collective-permute-start.31) | collective-permute-done | bytes 199712 | tf_op jit(solution)/shard_map/ppermute | solution.py:108
  157.5 1.1 collective-permute-done.32
  159.0 4.4 %fusion = f32[16,128,512]{2,1,0:T(8,128)S(1)} fusion(f32[128,512]{1,0:T(8,128)S(1)} %fusion.51, f32[16,512]{1,0:T(8,128)S(1)} %copy-done, f32[128,128]{1,0:T(8,128)S(1)} %fusion.52), kind=kOutput, calls=%fused_computation.1 | convolution fusion | flops 1612709888 | bytes 4554752 | tf_op jit(solution)/shard_map/dot_general | solution.py:23
  163.4 3.0 %collective-permute-start.33 = (f32[16,512]{1,0:T(8,128)S(1)}, f32[16,512]{1,0:T(8,128)S(1)}, u32[]{:S(2)}, u32[]{:S(2)}) collective-permute-start(f32[16,512]{1,0:T(8,128)S(1)} %bitcast_multiply_fusion), channel_id=1, source_target_pairs={{0,4},{4,8},{8,12},{12,16},{16,20},{20,24},{24,28},{1,5},{5,9},{9,... | collective-permute-start | bytes 98312 | tf_op jit(solution)/shard_map/ppermute | solution.py:33
  166.4 3.1 %collective-permute-start.34 = (f32[16,512]{1,0:T(8,128)S(1)}, f32[16,512]{1,0:T(8,128)S(1)}, u32[]{:S(2)}, u32[]{:S(2)}) collective-permute-start(f32[16,512]{1,0:T(8,128)S(1)} %bitcast_multiply_fusion), channel_id=1, source_target_pairs={{0,8},{4,12},{8,16},{12,20},{16,24},{20,28},{1,9},{5,13},{9,17},{1... | collective-permute-start | bytes 98312 | tf_op jit(solution)/shard_map/ppermute | solution.py:33
  169.6 4.4 %collective-permute-start.35 = (f32[16,512]{1,0:T(8,128)S(1)}, f32[16,512]{1,0:T(8,128)S(1)}, u32[]{:S(2)}, u32[]{:S(2)}) collective-permute-start(f32[16,512]{1,0:T(8,128)S(1)} %bitcast_multiply_fusion), channel_id=1, source_target_pairs={{0,12},{4,16},{8,20},{12,24},{16,28},{1,13},{5,17},{9,21},{13,25},... | collective-permute-start | bytes 98312 | tf_op jit(solution)/shard_map/ppermute | solution.py:33
  174.0 1.3 collective-permute-start.36
  175.3 1.3 collective-permute-start.37
  176.6 1.3 collective-permute-start.38
  177.9 1.3 collective-permute-start.39
  179.3 2.0 %collective-permute-start.41 = (bf16[128,1024]{1,0:T(8,128)(2,1)S(1)}, bf16[128,1024]{1,0:T(8,128)(2,1)S(1)}, u32[]{:S(2)}, u32[]{:S(2)}) collective-permute-start(bf16[128,1024]{1,0:T(8,128)(2,1)S(1)} %collective-permute-done.30), channel_id=1, source_target_pairs={{8,0},{16,8},{24,16},{28,24},{20,28},{12,20},{4,12},{0,4},{9,1},{1... | collective-permute-start | bytes 786440 | tf_op jit(solution)/shard_map/ppermute | solution.py:109
  181.4 1.0 multiply_reduce_fusion
  182.8 7.2 %all_gather.3 = bf16[128,2048]{1,0:T(8,128)(2,1)S(1)} all-gather(bf16[128,512]{1,0:T(8,128)(2,1)S(1)} %multiply_convert_fusion), channel_id=1, replica_groups=mesh['ctx'=8,'tp'=4] {'tp'}, dimensions={1}, use_global_device_ids=true | all-gather | bytes 655360 | tf_op jit(solution)/shard_map/all_gather | solution.py:128
  190.0 1.4 convolution_convert_fusion
  (116 shorter events, 18.1 us)
Async XLA Ops:
  19.7 48.1 %collective-permute-start = (bf16[128,512]{1,0:T(8,128)(2,1)S(1)}, bf16[128,512]{1,0:T(8,128)(2,1)}, u32[]{:S(2)}, u32[]{:S(2)}) collective-permute-start(bf16[128,512]{1,0:T(8,128)(2,1)S(1)} %get-tuple-element.72), channel_id=1, source_target_pairs={{0,8},{8,16},{16,24},{24,28},{28,20},{20,12},{12,4},{4,0},{1,9},{9... | collective-permute-start | bytes 393224 | tf_op jit(solution)/shard_map/ppermute | solution.py:92
  22.8 49.4 %collective-permute-start.1 = (bf16[128,512]{1,0:T(8,128)(2,1)S(1)}, bf16[128,512]{1,0:T(8,128)(2,1)}, u32[]{:S(2)}, u32[]{:S(2)}) collective-permute-start(bf16[128,512]{1,0:T(8,128)(2,1)S(1)} %get-tuple-element.71), channel_id=1, source_target_pairs={{0,16},{8,24},{16,28},{24,20},{28,12},{20,4},{12,0},{4,8},{1,17},{... | collective-permute-start | bytes 393224 | tf_op jit(solution)/shard_map/ppermute | solution.py:92
  25.4 47.9 %collective-permute-start.2 = (bf16[128,512]{1,0:T(8,128)(2,1)S(1)}, bf16[128,512]{1,0:T(8,128)(2,1)S(1)}, u32[]{:S(2)}, u32[]{:S(2)}) collective-permute-start(bf16[128,512]{1,0:T(8,128)(2,1)S(1)} %get-tuple-element.70), channel_id=1, source_target_pairs={{0,24},{8,28},{16,20},{24,12},{28,4},{20,0},{12,8},{4,16},{1,25},{... | collective-permute-start | bytes 393224 | tf_op jit(solution)/shard_map/ppermute | solution.py:92
  26.7 46.6 %collective-permute-start.3 = (bf16[128,512]{1,0:T(8,128)(2,1)S(1)}, bf16[128,512]{1,0:T(8,128)(2,1)S(1)}, u32[]{:S(2)}, u32[]{:S(2)}) collective-permute-start(bf16[128,512]{1,0:T(8,128)(2,1)S(1)} %get-tuple-element.69), channel_id=1, source_target_pairs={{0,28},{8,20},{16,12},{24,4},{28,0},{20,8},{12,16},{4,24},{1,29},{... | collective-permute-start | bytes 393224 | tf_op jit(solution)/shard_map/ppermute | solution.py:92
  29.1 44.2 %collective-permute-start.4 = (bf16[128,512]{1,0:T(8,128)(2,1)S(1)}, bf16[128,512]{1,0:T(8,128)(2,1)S(1)}, u32[]{:S(2)}, u32[]{:S(2)}) collective-permute-start(bf16[128,512]{1,0:T(8,128)(2,1)S(1)} %get-tuple-element.68), channel_id=1, source_target_pairs={{0,20},{8,12},{16,4},{24,0},{28,8},{20,16},{12,24},{4,28},{1,21},{... | collective-permute-start | bytes 393224 | tf_op jit(solution)/shard_map/ppermute | solution.py:92
  67.8 8.8 %collective-permute-start.5 = (bf16[128,512]{1,0:T(8,128)(2,1)S(1)}, bf16[128,512]{1,0:T(8,128)(2,1)S(1)}, u32[]{:S(2)}, u32[]{:S(2)}) collective-permute-start(bf16[128,512]{1,0:T(8,128)(2,1)S(1)} %get-tuple-element.73), channel_id=1, source_target_pairs={{0,12},{8,4},{16,0},{24,8},{28,16},{20,24},{12,28},{4,20},{1,13},{... | collective-permute-start | bytes 393224 | tf_op jit(solution)/shard_map/ppermute | solution.py:92
  72.3 6.1 %collective-permute-start.6 = (bf16[128,512]{1,0:T(8,128)(2,1)S(1)}, bf16[128,512]{1,0:T(8,128)(2,1)S(1)}, u32[]{:S(2)}, u32[]{:S(2)}) collective-permute-start(bf16[128,512]{1,0:T(8,128)(2,1)S(1)} %get-tuple-element.67), channel_id=1, source_target_pairs={{0,4},{8,0},{16,8},{24,16},{28,24},{20,28},{12,20},{4,12},{1,5},{9... | collective-permute-start | bytes 393224 | tf_op jit(solution)/shard_map/ppermute | solution.py:92
  79.2 12.5 %collective-permute-start.9 = (bf16[128,1024]{1,0:T(8,128)(2,1)S(1)}, bf16[128,1024]{1,0:T(8,128)(2,1)S(1)}, u32[]{:S(2)}, u32[]{:S(2)}) collective-permute-start(bf16[128,1024]{1,0:T(8,128)(2,1)S(1)} %get-tuple-element.41), channel_id=1, source_target_pairs={{0,8},{8,16},{16,24},{24,28},{28,20},{20,12},{12,4},{4,0},{1,9},{9... | collective-permute-start | bytes 786440 | tf_op jit(solution)/shard_map/ppermute | solution.py:108
  79.7 12.0 %collective-permute-start.10 = (bf16[128,1024]{1,0:T(8,128)(2,1)S(1)}, bf16[128,1024]{1,0:T(8,128)(2,1)S(1)}, u32[]{:S(2)}, u32[]{:S(2)}) collective-permute-start(bf16[128,1024]{1,0:T(8,128)(2,1)S(1)} %get-tuple-element.42), channel_id=1, source_target_pairs={{8,0},{16,8},{24,16},{28,24},{20,28},{12,20},{4,12},{0,4},{9,1},{1... | collective-permute-start | bytes 786440 | tf_op jit(solution)/shard_map/ppermute | solution.py:109
  81.3 9.8 %collective-permute-start.8 = (bf16[130,768]{1,0:T(8,128)(2,1)S(1)}, bf16[130,768]{1,0:T(8,128)(2,1)S(1)}, u32[]{:S(2)}, u32[]{:S(2)}) collective-permute-start(bf16[130,768]{1,0:T(8,128)(2,1)S(1)} %convolution_convert_fusion.1), channel_id=1, source_target_pairs={{8,0},{16,8},{24,16},{28,24},{20,28},{12,20},{4,12},{0,4},{9,1},{1... | collective-permute-start | bytes 599048 | tf_op jit(solution)/shard_map/ppermute | solution.py:109
  81.4 10.0 %collective-permute-start.7 = (bf16[130,768]{1,0:T(8,128)(2,1)S(1)}, bf16[130,768]{1,0:T(8,128)(2,1)S(1)}, u32[]{:S(2)}, u32[]{:S(2)}) collective-permute-start(bf16[130,768]{1,0:T(8,128)(2,1)S(1)} %convolution_convert_fusion.2), channel_id=1, source_target_pairs={{0,8},{8,16},{16,24},{24,28},{28,20},{20,12},{12,4},{4,0},{1,9},{9... | collective-permute-start | bytes 599048 | tf_op jit(solution)/shard_map/ppermute | solution.py:108
  91.7 10.9 %collective-permute-start.13 = (bf16[128,1024]{1,0:T(8,128)(2,1)S(1)}, bf16[128,1024]{1,0:T(8,128)(2,1)S(1)}, u32[]{:S(2)}, u32[]{:S(2)}) collective-permute-start(bf16[128,1024]{1,0:T(8,128)(2,1)S(1)} %collective-permute-done.9), channel_id=1, source_target_pairs={{0,8},{8,16},{16,24},{24,28},{28,20},{20,12},{12,4},{4,0},{1,9},{9... | collective-permute-start | bytes 786440 | tf_op jit(solution)/shard_map/ppermute | solution.py:108
  92.1 10.5 %collective-permute-start.14 = (bf16[128,1024]{1,0:T(8,128)(2,1)S(1)}, bf16[128,1024]{1,0:T(8,128)(2,1)S(1)}, u32[]{:S(2)}, u32[]{:S(2)}) collective-permute-start(bf16[128,1024]{1,0:T(8,128)(2,1)S(1)} %collective-permute-done.10), channel_id=1, source_target_pairs={{8,0},{16,8},{24,16},{28,24},{20,28},{12,20},{4,12},{0,4},{9,1},{1... | collective-permute-start | bytes 786440 | tf_op jit(solution)/shard_map/ppermute | solution.py:109
  93.8 8.7 %collective-permute-start.12 = (bf16[130,768]{1,0:T(8,128)(2,1)S(1)}, bf16[130,768]{1,0:T(8,128)(2,1)S(1)}, u32[]{:S(2)}, u32[]{:S(2)}) collective-permute-start(bf16[130,768]{1,0:T(8,128)(2,1)S(1)} %add_convert_fusion.12), channel_id=1, source_target_pairs={{8,0},{16,8},{24,16},{28,24},{20,28},{12,20},{4,12},{0,4},{9,1},{1... | collective-permute-start | bytes 599048 | tf_op jit(solution)/shard_map/ppermute | solution.py:109
  94.7 7.9 %collective-permute-start.11 = (bf16[130,768]{1,0:T(8,128)(2,1)S(1)}, bf16[130,768]{1,0:T(8,128)(2,1)S(1)}, u32[]{:S(2)}, u32[]{:S(2)}) collective-permute-start(bf16[130,768]{1,0:T(8,128)(2,1)S(1)} %add_convert_fusion.13), channel_id=1, source_target_pairs={{0,8},{8,16},{16,24},{24,28},{28,20},{20,12},{12,4},{4,0},{1,9},{9... | collective-permute-start | bytes 599048 | tf_op jit(solution)/shard_map/ppermute | solution.py:108
  102.7 11.0 %collective-permute-start.17 = (bf16[128,1024]{1,0:T(8,128)(2,1)S(1)}, bf16[128,1024]{1,0:T(8,128)(2,1)S(1)}, u32[]{:S(2)}, u32[]{:S(2)}) collective-permute-start(bf16[128,1024]{1,0:T(8,128)(2,1)S(1)} %collective-permute-done.13), channel_id=1, source_target_pairs={{0,8},{8,16},{16,24},{24,28},{28,20},{20,12},{12,4},{4,0},{1,9},{9... | collective-permute-start | bytes 786440 | tf_op jit(solution)/shard_map/ppermute | solution.py:108
  103.6 10.1 %collective-permute-start.18 = (bf16[128,1024]{1,0:T(8,128)(2,1)S(1)}, bf16[128,1024]{1,0:T(8,128)(2,1)S(1)}, u32[]{:S(2)}, u32[]{:S(2)}) collective-permute-start(bf16[128,1024]{1,0:T(8,128)(2,1)S(1)} %collective-permute-done.14), channel_id=1, source_target_pairs={{8,0},{16,8},{24,16},{28,24},{20,28},{12,20},{4,12},{0,4},{9,1},{1... | collective-permute-start | bytes 786440 | tf_op jit(solution)/shard_map/ppermute | solution.py:109
  104.7 8.1 %collective-permute-start.16 = (bf16[130,768]{1,0:T(8,128)(2,1)S(1)}, bf16[130,768]{1,0:T(8,128)(2,1)S(1)}, u32[]{:S(2)}, u32[]{:S(2)}) collective-permute-start(bf16[130,768]{1,0:T(8,128)(2,1)S(1)} %add_convert_fusion.10), channel_id=1, source_target_pairs={{8,0},{16,8},{24,16},{28,24},{20,28},{12,20},{4,12},{0,4},{9,1},{1... | collective-permute-start | bytes 599048 | tf_op jit(solution)/shard_map/ppermute | solution.py:109
  106.5 7.1 %collective-permute-start.15 = (bf16[130,768]{1,0:T(8,128)(2,1)S(1)}, bf16[130,768]{1,0:T(8,128)(2,1)S(1)}, u32[]{:S(2)}, u32[]{:S(2)}) collective-permute-start(bf16[130,768]{1,0:T(8,128)(2,1)S(1)} %add_convert_fusion.11), channel_id=1, source_target_pairs={{0,8},{8,16},{16,24},{24,28},{28,20},{20,12},{12,4},{4,0},{1,9},{9... | collective-permute-start | bytes 599048 | tf_op jit(solution)/shard_map/ppermute | solution.py:108
  113.7 11.8 %collective-permute-start.21 = (bf16[128,1024]{1,0:T(8,128)(2,1)S(1)}, bf16[128,1024]{1,0:T(8,128)(2,1)S(1)}, u32[]{:S(2)}, u32[]{:S(2)}) collective-permute-start(bf16[128,1024]{1,0:T(8,128)(2,1)S(1)} %collective-permute-done.17), channel_id=1, source_target_pairs={{0,8},{8,16},{16,24},{24,28},{28,20},{20,12},{12,4},{4,0},{1,9},{9... | collective-permute-start | bytes 786440 | tf_op jit(solution)/shard_map/ppermute | solution.py:108
  114.6 11.0 %collective-permute-start.22 = (bf16[128,1024]{1,0:T(8,128)(2,1)S(1)}, bf16[128,1024]{1,0:T(8,128)(2,1)S(1)}, u32[]{:S(2)}, u32[]{:S(2)}) collective-permute-start(bf16[128,1024]{1,0:T(8,128)(2,1)S(1)} %collective-permute-done.18), channel_id=1, source_target_pairs={{8,0},{16,8},{24,16},{28,24},{20,28},{12,20},{4,12},{0,4},{9,1},{1... | collective-permute-start | bytes 786440 | tf_op jit(solution)/shard_map/ppermute | solution.py:109
  115.8 9.3 %collective-permute-start.20 = (bf16[130,768]{1,0:T(8,128)(2,1)S(1)}, bf16[130,768]{1,0:T(8,128)(2,1)S(1)}, u32[]{:S(2)}, u32[]{:S(2)}) collective-permute-start(bf16[130,768]{1,0:T(8,128)(2,1)S(1)} %add_convert_fusion.8), channel_id=1, source_target_pairs={{8,0},{16,8},{24,16},{28,24},{20,28},{12,20},{4,12},{0,4},{9,1},{1... | collective-permute-start | bytes 599048 | tf_op jit(solution)/shard_map/ppermute | solution.py:109
  117.5 8.0 %collective-permute-start.19 = (bf16[130,768]{1,0:T(8,128)(2,1)S(1)}, bf16[130,768]{1,0:T(8,128)(2,1)S(1)}, u32[]{:S(2)}, u32[]{:S(2)}) collective-permute-start(bf16[130,768]{1,0:T(8,128)(2,1)S(1)} %add_convert_fusion.9), channel_id=1, source_target_pairs={{0,8},{8,16},{16,24},{24,28},{28,20},{20,12},{12,4},{4,0},{1,9},{9... | collective-permute-start | bytes 599048 | tf_op jit(solution)/shard_map/ppermute | solution.py:108
  125.6 14.1 %collective-permute-start.25 = (bf16[128,1024]{1,0:T(8,128)(2,1)S(1)}, bf16[128,1024]{1,0:T(8,128)(2,1)S(1)}, u32[]{:S(2)}, u32[]{:S(2)}) collective-permute-start(bf16[128,1024]{1,0:T(8,128)(2,1)S(1)} %collective-permute-done.21), channel_id=1, source_target_pairs={{0,8},{8,16},{16,24},{24,28},{28,20},{20,12},{12,4},{4,0},{1,9},{9... | collective-permute-start | bytes 786440 | tf_op jit(solution)/shard_map/ppermute | solution.py:108
  127.6 12.1 %collective-permute-start.26 = (bf16[128,1024]{1,0:T(8,128)(2,1)S(1)}, bf16[128,1024]{1,0:T(8,128)(2,1)S(1)}, u32[]{:S(2)}, u32[]{:S(2)}) collective-permute-start(bf16[128,1024]{1,0:T(8,128)(2,1)S(1)} %collective-permute-done.22), channel_id=1, source_target_pairs={{8,0},{16,8},{24,16},{28,24},{20,28},{12,20},{4,12},{0,4},{9,1},{1... | collective-permute-start | bytes 786440 | tf_op jit(solution)/shard_map/ppermute | solution.py:109
  127.6 11.9 %collective-permute-start.24 = (bf16[130,768]{1,0:T(8,128)(2,1)S(1)}, bf16[130,768]{1,0:T(8,128)(2,1)S(1)}, u32[]{:S(2)}, u32[]{:S(2)}) collective-permute-start(bf16[130,768]{1,0:T(8,128)(2,1)S(1)} %add_convert_fusion.6), channel_id=1, source_target_pairs={{8,0},{16,8},{24,16},{28,24},{20,28},{12,20},{4,12},{0,4},{9,1},{1... | collective-permute-start | bytes 599048 | tf_op jit(solution)/shard_map/ppermute | solution.py:109
  128.9 10.7 %collective-permute-start.23 = (bf16[130,768]{1,0:T(8,128)(2,1)S(1)}, bf16[130,768]{1,0:T(8,128)(2,1)S(1)}, u32[]{:S(2)}, u32[]{:S(2)}) collective-permute-start(bf16[130,768]{1,0:T(8,128)(2,1)S(1)} %add_convert_fusion.7), channel_id=1, source_target_pairs={{0,8},{8,16},{16,24},{24,28},{28,20},{20,12},{12,4},{4,0},{1,9},{9... | collective-permute-start | bytes 599048 | tf_op jit(solution)/shard_map/ppermute | solution.py:108
  139.6 19.4 %copy-start = (f32[16,512]{1,0:T(8,128)S(1)}, f32[16,512]{1,0:T(8,128)}, u32[]{:S(2)}) copy-start(f32[16,512]{1,0:T(8,128)} %param.20) | copy-start | bytes 98308
  139.7 11.9 %collective-permute-start.29 = (bf16[128,1024]{1,0:T(8,128)(2,1)S(1)}, bf16[128,1024]{1,0:T(8,128)(2,1)S(1)}, u32[]{:S(2)}, u32[]{:S(2)}) collective-permute-start(bf16[128,1024]{1,0:T(8,128)(2,1)S(1)} %collective-permute-done.25), channel_id=1, source_target_pairs={{0,8},{8,16},{16,24},{24,28},{28,20},{20,12},{12,4},{4,0},{1,9},{9... | collective-permute-start | bytes 786440 | tf_op jit(solution)/shard_map/ppermute | solution.py:108
  140.6 11.0 %collective-permute-start.30 = (bf16[128,1024]{1,0:T(8,128)(2,1)S(1)}, bf16[128,1024]{1,0:T(8,128)(2,1)S(1)}, u32[]{:S(2)}, u32[]{:S(2)}) collective-permute-start(bf16[128,1024]{1,0:T(8,128)(2,1)S(1)} %collective-permute-done.26), channel_id=1, source_target_pairs={{8,0},{16,8},{24,16},{28,24},{20,28},{12,20},{4,12},{0,4},{9,1},{1... | collective-permute-start | bytes 786440 | tf_op jit(solution)/shard_map/ppermute | solution.py:109
  141.8 9.7 %collective-permute-start.28 = (bf16[130,768]{1,0:T(8,128)(2,1)S(1)}, bf16[130,768]{1,0:T(8,128)(2,1)S(1)}, u32[]{:S(2)}, u32[]{:S(2)}) collective-permute-start(bf16[130,768]{1,0:T(8,128)(2,1)S(1)} %add_convert_fusion.4), channel_id=1, source_target_pairs={{8,0},{16,8},{24,16},{28,24},{20,28},{12,20},{4,12},{0,4},{9,1},{1... | collective-permute-start | bytes 599048 | tf_op jit(solution)/shard_map/ppermute | solution.py:109
  141.8 9.7 %collective-permute-start.27 = (bf16[130,768]{1,0:T(8,128)(2,1)S(1)}, bf16[130,768]{1,0:T(8,128)(2,1)S(1)}, u32[]{:S(2)}, u32[]{:S(2)}) collective-permute-start(bf16[130,768]{1,0:T(8,128)(2,1)S(1)} %add_convert_fusion.5), channel_id=1, source_target_pairs={{0,8},{8,16},{16,24},{24,28},{28,20},{20,12},{12,4},{4,0},{1,9},{9... | collective-permute-start | bytes 599048 | tf_op jit(solution)/shard_map/ppermute | solution.py:108
  151.6 5.9 %collective-permute-start.31 = (bf16[130,768]{1,0:T(8,128)(2,1)S(1)}, bf16[130,768]{1,0:T(8,128)(2,1)S(1)}, u32[]{:S(2)}, u32[]{:S(2)}) collective-permute-start(bf16[130,768]{1,0:T(8,128)(2,1)S(1)} %add_convert_fusion.3), channel_id=1, source_target_pairs={{0,8},{8,16},{16,24},{24,28},{28,20},{20,12},{12,4},{4,0},{1,9},{9... | collective-permute-start | bytes 599048 | tf_op jit(solution)/shard_map/ppermute | solution.py:108
  152.6 6.0 %collective-permute-start.32 = (bf16[130,768]{1,0:T(8,128)(2,1)S(1)}, bf16[130,768]{1,0:T(8,128)(2,1)S(1)}, u32[]{:S(2)}, u32[]{:S(2)}) collective-permute-start(bf16[130,768]{1,0:T(8,128)(2,1)S(1)} %add_convert_fusion.2), channel_id=1, source_target_pairs={{8,0},{16,8},{24,16},{28,24},{20,28},{12,20},{4,12},{0,4},{9,1},{1... | collective-permute-start | bytes 599048 | tf_op jit(solution)/shard_map/ppermute | solution.py:109
  158.7 22.7 %copy-start.1 = (f32[16,512]{1,0:T(8,128)S(1)}, f32[16,512]{1,0:T(8,128)}, u32[]{:S(2)}) copy-start(f32[16,512]{1,0:T(8,128)} %param.21) | copy-start | bytes 98308
  163.4 19.1 %copy-start.2 = (f32[512]{0:T(512)S(1)}, f32[512]{0:T(512)}, u32[]{:S(2)}) copy-start(f32[512]{0:T(512)} %param.22) | copy-start | bytes 6148
  163.4 13.2 %collective-permute-start.33 = (f32[16,512]{1,0:T(8,128)S(1)}, f32[16,512]{1,0:T(8,128)S(1)}, u32[]{:S(2)}, u32[]{:S(2)}) collective-permute-start(f32[16,512]{1,0:T(8,128)S(1)} %bitcast_multiply_fusion), channel_id=1, source_target_pairs={{0,4},{4,8},{8,12},{12,16},{16,20},{20,24},{24,28},{1,5},{5,9},{9,... | collective-permute-start | bytes 98312 | tf_op jit(solution)/shard_map/ppermute | solution.py:33
  166.4 11.5 %collective-permute-start.34 = (f32[16,512]{1,0:T(8,128)S(1)}, f32[16,512]{1,0:T(8,128)S(1)}, u32[]{:S(2)}, u32[]{:S(2)}) collective-permute-start(f32[16,512]{1,0:T(8,128)S(1)} %bitcast_multiply_fusion), channel_id=1, source_target_pairs={{0,8},{4,12},{8,16},{12,20},{16,24},{20,28},{1,9},{5,13},{9,17},{1... | collective-permute-start | bytes 98312 | tf_op jit(solution)/shard_map/ppermute | solution.py:33
  169.6 9.7 %collective-permute-start.35 = (f32[16,512]{1,0:T(8,128)S(1)}, f32[16,512]{1,0:T(8,128)S(1)}, u32[]{:S(2)}, u32[]{:S(2)}) collective-permute-start(f32[16,512]{1,0:T(8,128)S(1)} %bitcast_multiply_fusion), channel_id=1, source_target_pairs={{0,12},{4,16},{8,20},{12,24},{16,28},{1,13},{5,17},{9,21},{13,25},... | collective-permute-start | bytes 98312 | tf_op jit(solution)/shard_map/ppermute | solution.py:33
  174.0 5.3 %collective-permute-start.36 = (f32[16,512]{1,0:T(8,128)S(1)}, f32[16,512]{1,0:T(8,128)S(1)}, u32[]{:S(2)}, u32[]{:S(2)}) collective-permute-start(f32[16,512]{1,0:T(8,128)S(1)} %bitcast_multiply_fusion), channel_id=1, source_target_pairs={{0,16},{4,20},{8,24},{12,28},{1,17},{5,21},{9,25},{13,29},{2,18},{... | collective-permute-start | bytes 98312 | tf_op jit(solution)/shard_map/ppermute | solution.py:33
  175.3 6.0 %collective-permute-start.37 = (f32[16,512]{1,0:T(8,128)S(1)}, f32[16,512]{1,0:T(8,128)S(1)}, u32[]{:S(2)}, u32[]{:S(2)}) collective-permute-start(f32[16,512]{1,0:T(8,128)S(1)} %bitcast_multiply_fusion), channel_id=1, source_target_pairs={{0,20},{4,24},{8,28},{1,21},{5,25},{9,29},{2,22},{6,26},{10,30},{3... | collective-permute-start | bytes 98312 | tf_op jit(solution)/shard_map/ppermute | solution.py:33
  176.6 4.7 %collective-permute-start.38 = (f32[16,512]{1,0:T(8,128)S(1)}, f32[16,512]{1,0:T(8,128)S(1)}, u32[]{:S(2)}, u32[]{:S(2)}) collective-permute-start(f32[16,512]{1,0:T(8,128)S(1)} %bitcast_multiply_fusion), channel_id=1, source_target_pairs={{0,24},{4,28},{1,25},{5,29},{2,26},{6,30},{3,27},{7,31}} | collective-permute-start | bytes 98312 | tf_op jit(solution)/shard_map/ppermute | solution.py:33
  177.9 3.4 %collective-permute-start.39 = (f32[16,512]{1,0:T(8,128)S(1)}, f32[16,512]{1,0:T(8,128)S(1)}, u32[]{:S(2)}, u32[]{:S(2)}) collective-permute-start(f32[16,512]{1,0:T(8,128)S(1)} %bitcast_multiply_fusion), channel_id=1, source_target_pairs={{0,28},{1,29},{2,30},{3,31}} | collective-permute-start | bytes 98312 | tf_op jit(solution)/shard_map/ppermute | solution.py:33
  179.3 10.7 %collective-permute-start.40 = (bf16[128,1024]{1,0:T(8,128)(2,1)S(1)}, bf16[128,1024]{1,0:T(8,128)(2,1)S(1)}, u32[]{:S(2)}, u32[]{:S(2)}) collective-permute-start(bf16[128,1024]{1,0:T(8,128)(2,1)S(1)} %collective-permute-done.29), channel_id=1, source_target_pairs={{0,8},{8,16},{16,24},{24,28},{28,20},{20,12},{12,4},{4,0},{1,9},{9... | collective-permute-start | bytes 786440 | tf_op jit(solution)/shard_map/ppermute | solution.py:108
  179.3 10.7 %collective-permute-start.41 = (bf16[128,1024]{1,0:T(8,128)(2,1)S(1)}, bf16[128,1024]{1,0:T(8,128)(2,1)S(1)}, u32[]{:S(2)}, u32[]{:S(2)}) collective-permute-start(bf16[128,1024]{1,0:T(8,128)(2,1)S(1)} %collective-permute-done.30), channel_id=1, source_target_pairs={{8,0},{16,8},{24,16},{28,24},{20,28},{12,20},{4,12},{0,4},{9,1},{1... | collective-permute-start | bytes 786440 | tf_op jit(solution)/shard_map/ppermute | solution.py:109

commit v11 on v9

--- a/solution.py
+++ b/solution.py
@@ -62,7 +62,9 @@
     ctx_count = lax.axis_size("ctx")
     length = tokens.shape[0]
     width = w_query.shape[1]
-    columns = lax.all_to_all(tokens, "ctx", split_axis=1, concat_axis=0, tiled=True)
+    by_dest = tokens.reshape(length, ctx_count, -1).transpose(1, 0, 2)
+    columns = lax.all_to_all(by_dest, "ctx", split_axis=0, concat_axis=0, tiled=True)
+    columns = columns.reshape(ctx_count * length, -1)
     columns = jnp.concatenate([jnp.zeros((2, columns.shape[1]), columns.dtype), columns], axis=0)
     w_cat = jnp.concatenate([w_query, w_key, w_value], axis=1)
     split = w_cat.shape[1] // 2
@@ -83,7 +85,7 @@
     ring_arr = jnp.array(ring, jnp.int32)
     c_chunk = w_out.shape[0]
     c_half = c_chunk // 2
-    w_up, w_low = w_out[:c_half], w_out[c_half:]
+    w_up, w_low, columns = lax.optimization_barrier((w_out[:c_half], w_out[c_half:], columns))
     w_rows = jnp.zeros((2 * ctx_count, c_half, w_out.shape[1]), w_out.dtype)
     w_rows = lax.dynamic_update_slice_in_dim(w_rows, w_up[None], me * 2, 0)
     w_rows = lax.dynamic_update_slice_in_dim(w_rows, w_low[None], me * 2 + 1, 0)
@@ -94,28 +96,26 @@
         w_rows = lax.dynamic_update_slice_in_dim(w_rows, w_up[None], src_up * 2, 0)
         return lax.dynamic_update_slice_in_dim(w_rows, w_low[None], src_low * 2 + 1, 0)
 
-    early = min(3, ctx_count - 1)
-    for step in range(1, early + 1):
-        w_up = lax.ppermute(w_up, "ctx", perm=fwd)
-        w_low = lax.ppermute(w_low, "ctx", perm=bwd)
-        w_rows = w_step(step, w_up, w_low, w_rows)
-    w_up, w_low, columns = lax.optimization_barrier((w_up, w_low, columns))
     up = piece(ring_arr[(my_pos - 1) % ctx_count], 0)
     down = piece(ring_arr[(my_pos + 1) % ctx_count], 1)
+    tied = max(ctx_count - 3, 0)
     for step in range(1, ctx_count):
-        w_more = early + step < ctx_count
-        if w_more:
+        if step <= tied:
             sent = lax.optimization_barrier(
                 (up.astype(jnp.bfloat16), down.astype(jnp.bfloat16), w_up, w_low)
             )
             up, w_up = lax.ppermute((sent[0], sent[2]), "ctx", perm=fwd)
             down, w_low = lax.ppermute((sent[1], sent[3]), "ctx", perm=bwd)
-            w_rows = w_step(early + step, w_up, w_low, w_rows)
+            w_rows = w_step(step, w_up, w_low, w_rows)
         else:
             up = lax.ppermute(up.astype(jnp.bfloat16), "ctx", perm=fwd)
             down = lax.ppermute(down.astype(jnp.bfloat16), "ctx", perm=bwd)
         up = up.astype(jnp.float32) + piece(ring_arr[(my_pos - step - 1) % ctx_count], 0)
         down = down.astype(jnp.float32) + piece(ring_arr[(my_pos + step + 1) % ctx_count], 1)
+    for step in range(tied + 1, ctx_count):
+        w_up = lax.ppermute(w_up, "ctx", perm=fwd)
+        w_low = lax.ppermute(w_low, "ctx", perm=bwd)
+        w_rows = w_step(step, w_up, w_low, w_rows)
 
     projected = jnp.concatenate([up, down], axis=1).astype(jnp.bfloat16).astype(jnp.float32)
     queries = projected[:, :width]

time: 178 us -> 153 us (0.86)
  local copies, waits for them, and re-layouts: 24.4 us -> 6.51 us
  starting transfers between devices: 53.7 us -> 50.4 us
  waiting for transfers between devices: 46.4 us -> 43.8 us
  matrix products: 12.5 us -> 10.3 us
    ppermute x3 -> x2, waiting for transfers between devices: 10.4 us -> 0.01 us  [body(): up = lax.ppermute(up.astype(jnp.bfloat16), 'ctx', perm=fwd)]
    ppermute x8 -> x10, waiting for transfers between devices: 10.1 us -> 19.9 us  [body(): up, w_up = lax.ppermute((sent[0], sent[2]), 'ctx', perm=fwd)]
    ppermute x8 -> x10, starting transfers between devices: 6.71 us -> 16.3 us  [body(): up, w_up = lax.ppermute((sent[0], sent[2]), 'ctx', perm=fwd)]
    dynamic_update_slice x7, local copies, waits for them, and re-layouts: 6.05 us -> 0.15 us  [w_step(): w_rows = lax.dynamic_update_slice_in_dim(w_rows, w_up[None], src_up * 2, 0)]
    dynamic_update_slice x7, local copies, waits for them, and re-layouts: 5.98 us -> 0.18 us  [w_step(): lax.dynamic_update_slice_in_dim(w_rows, w_low[None], src_low * 2 + 1, 0)]
    ppermute x8 -> x10, starting transfers between devices: 9.73 us -> 4.06 us  [body(): down, w_low = lax.ppermute((sent[1], sent[3]), 'ctx', perm=bwd)]
    ppermute x3 -> x2, starting transfers between devices: 6.79 us -> 1.53 us  [body(): w_up = lax.ppermute(w_up, 'ctx', perm=fwd)]
    ppermute x3 -> x2, waiting for transfers between devices: 4.87 us -> 0.01 us  [body(): w_up = lax.ppermute(w_up, 'ctx', perm=fwd)]
  transfers between devices with their start and end apart: 36 -> 36, of which waited for: 12 -> 20; matrix products, arithmetic and copies ran while one was open for 18% -> 8% of each run, Pallas kernels for 0% -> 0%
where the time goes in v11:
time: 153 us; the launch traced here: 152 us
  starting transfers between devices  50.4 us (33%)
  waiting for transfers between devices  43.8 us (29%)
  between operations  30.2 us (20%)
  matrix products  10.3 us (7%)
  blocking collectives  7.17 us (5%)
  local copies, waits for them, and re-layouts  6.51 us (4%)
  other arithmetic  3.36 us (2%)
    ppermute x10, waiting for transfers between devices, body(): up, w_up = lax.ppermute((sent[0], sent[2]), 'ctx', perm=fwd)  19.9 us
    ppermute x10, waiting for transfers between devices, body(): down, w_low = lax.ppermute((sent[1], sent[3]), 'ctx', perm=bwd)  18.3 us
    ppermute x10, starting transfers between devices, body(): up, w_up = lax.ppermute((sent[0], sent[2]), 'ctx', perm=fwd)  16.3 us
    ppermute x7, starting transfers between devices, modal_long_conv(): lax.ppermute(end_state, 'ctx', perm=[(i, i + shift) for i in range(ctx_co...  14.3 us
    all_to_all x1, starting transfers between devices, body(): lax.all_to_all(by_dest, 'ctx', split_axis=0, concat_axis=0, tiled=True)  7.29 us
    all_gather x1, blocking collectives, body(): features = lax.all_gather(gated, 'tp', axis=1, tiled=True)  7.17 us
    ppermute x2, waiting for transfers between devices, body(): down = lax.ppermute(down.astype(jnp.bfloat16), 'ctx', perm=bwd)  5.56 us
    dot_general x16, matrix products, piece(): return jnp.dot(rows, halves[side], preferred_element_type=jnp.float32)  4.47 us
  transfers between devices with their start and end apart: 36, of which 20 were waited for; matrix products, arithmetic and copies ran while one was open for 8% of the time, Pallas kernels for 0%

profile of v11, /device:TPU:0, one launch (start us, length us, event | category | flops | bytes accessed | tf_op | source)
XLA Modules:
  0.0 151.9 jit_solution(10915144192129652065)
XLA Ops:
  0.0 2.4 %copy.14 = bf16[128,4096]{0,1:T(8,128)(2,1)} copy(bf16[128,4096]{1,0:T(8,128)(2,1)} %param.13) | data formatting | bytes 2097152 | tf_op args[0]
  2.4 7.3 %all-to-all-start = ((bf16[8,128,512]{1,2,0:T(8,128)(2,1)}), bf16[8,128,512]{1,2,0:T(8,128)(2,1)}, u32[]{:S(2)}, u32[]{:S(2)}) async-start(bf16[8,128,512]{1,2,0:T(8,128)(2,1)} %bitcast.2), calls=%async_computation | async-start | bytes 2097152 | tf_op jit(solution)/shard_map/all_to_all | solution.py:66
  40.7 1.1 pad_maximum_fusion.1
  42.0 1.5 copy.15
  46.0 2.1 %collective-permute-start = (bf16[130,768]{1,0:T(8,128)(2,1)S(1)}, bf16[130,768]{1,0:T(8,128)(2,1)S(1)}, u32[]{:S(2)}, u32[]{:S(2)}) collective-permute-start(bf16[130,768]{1,0:T(8,128)(2,1)S(1)} %convolution_convert_fusion.2), channel_id=1, source_target_pairs={{0,8},{8,16},{16,24},{24,28},{28,20},{20,12},{12,4},{4,0},{1,9},{9... | collective-permute-start | bytes 599048 | tf_op jit(solution)/shard_map/ppermute | solution.py:107
  48.1 2.0 %collective-permute-start.2 = (bf16[128,1024]{1,0:T(8,128)(2,1)S(1)}, bf16[128,1024]{1,0:T(8,128)(2,1)S(1)}, u32[]{:S(2)}, u32[]{:S(2)}) collective-permute-start(bf16[128,1024]{1,0:T(8,128)(2,1)S(1)} %get-tuple-element.33), channel_id=1, source_target_pairs={{0,8},{8,16},{16,24},{24,28},{28,20},{20,12},{12,4},{4,0},{1,9},{9... | collective-permute-start | bytes 786440 | tf_op jit(solution)/shard_map/ppermute | solution.py:107
  52.5 1.7 %collective-permute-done = bf16[130,768]{1,0:T(8,128)(2,1)S(1)} collective-permute-done((bf16[130,768]{1,0:T(8,128)(2,1)S(1)}, bf16[130,768]{1,0:T(8,128)(2,1)S(1)}, u32[]{:S(2)}, u32[]{:S(2)}) %collective-permute-start) | collective-permute-done | bytes 199712 | tf_op jit(solution)/shard_map/ppermute | solution.py:107
  54.4 1.7 %collective-permute-done.1 = bf16[130,768]{1,0:T(8,128)(2,1)S(1)} collective-permute-done((bf16[130,768]{1,0:T(8,128)(2,1)S(1)}, bf16[130,768]{1,0:T(8,128)(2,1)S(1)}, u32[]{:S(2)}, u32[]{:S(2)}) %collective-permute-start.1) | collective-permute-done | bytes 199712 | tf_op jit(solution)/shard_map/ppermute | solution.py:108
  56.5 1.8 %collective-permute-done.2 = bf16[128,1024]{1,0:T(8,128)(2,1)S(1)} collective-permute-done((bf16[128,1024]{1,0:T(8,128)(2,1)S(1)}, bf16[128,1024]{1,0:T(8,128)(2,1)S(1)}, u32[]{:S(2)}, u32[]{:S(2)}) %collective-permute-start.2) | collective-permute-done | bytes 262176 | tf_op jit(solution)/shard_map/ppermute | solution.py:107
  58.3 1.4 collective-permute-done.3
  59.8 1.5 collective-permute-start.4
  61.8 1.5 collective-permute-start.6
  63.9 3.8 %collective-permute-done.4 = bf16[130,768]{1,0:T(8,128)(2,1)S(1)} collective-permute-done((bf16[130,768]{1,0:T(8,128)(2,1)S(1)}, bf16[130,768]{1,0:T(8,128)(2,1)S(1)}, u32[]{:S(2)}, u32[]{:S(2)}) %collective-permute-start.4) | collective-permute-done | bytes 199712 | tf_op jit(solution)/shard_map/ppermute | solution.py:107
  67.7 1.1 collective-permute-done.5
  68.9 1.6 %collective-permute-done.6 = bf16[128,1024]{1,0:T(8,128)(2,1)S(1)} collective-permute-done((bf16[128,1024]{1,0:T(8,128)(2,1)S(1)}, bf16[128,1024]{1,0:T(8,128)(2,1)S(1)}, u32[]{:S(2)}, u32[]{:S(2)}) %collective-permute-start.6) | collective-permute-done | bytes 262176 | tf_op jit(solution)/shard_map/ppermute | solution.py:107
  70.5 1.2 collective-permute-done.7
  71.7 1.5 collective-permute-start.8
  73.7 1.5 collective-permute-start.10
  75.8 2.6 %collective-permute-done.8 = bf16[130,768]{1,0:T(8,128)(2,1)S(1)} collective-permute-done((bf16[130,768]{1,0:T(8,128)(2,1)S(1)}, bf16[130,768]{1,0:T(8,128)(2,1)S(1)}, u32[]{:S(2)}, u32[]{:S(2)}) %collective-permute-start.8) | collective-permute-done | bytes 199712 | tf_op jit(solution)/shard_map/ppermute | solution.py:107
  78.5 1.1 collective-permute-done.9
  79.7 2.1 %collective-permute-done.10 = bf16[128,1024]{1,0:T(8,128)(2,1)S(1)} collective-permute-done((bf16[128,1024]{1,0:T(8,128)(2,1)S(1)}, bf16[128,1024]{1,0:T(8,128)(2,1)S(1)}, u32[]{:S(2)}, u32[]{:S(2)}) %collective-permute-start.10) | collective-permute-done | bytes 262176 | tf_op jit(solution)/shard_map/ppermute | solution.py:107
  81.8 1.3 collective-permute-done.11
  83.1 1.9 %collective-permute-start.12 = (bf16[130,768]{1,0:T(8,128)(2,1)S(1)}, bf16[130,768]{1,0:T(8,128)(2,1)S(1)}, u32[]{:S(2)}, u32[]{:S(2)}) collective-permute-start(bf16[130,768]{1,0:T(8,128)(2,1)S(1)} %add_convert_fusion.9), channel_id=1, source_target_pairs={{0,8},{8,16},{16,24},{24,28},{28,20},{20,12},{12,4},{4,0},{1,9},{9... | collective-permute-start | bytes 599048 | tf_op jit(solution)/shard_map/ppermute | solution.py:107
  85.1 1.9 %collective-permute-start.14 = (bf16[128,1024]{1,0:T(8,128)(2,1)S(1)}, bf16[128,1024]{1,0:T(8,128)(2,1)S(1)}, u32[]{:S(2)}, u32[]{:S(2)}) collective-permute-start(bf16[128,1024]{1,0:T(8,128)(2,1)S(1)} %collective-permute-done.10), channel_id=1, source_target_pairs={{0,8},{8,16},{16,24},{24,28},{28,20},{20,12},{12,4},{4,0},{1,9},{9... | collective-permute-start | bytes 786440 | tf_op jit(solution)/shard_map/ppermute | solution.py:107
  87.2 1.7 %collective-permute-done.12 = bf16[130,768]{1,0:T(8,128)(2,1)S(1)} collective-permute-done((bf16[130,768]{1,0:T(8,128)(2,1)S(1)}, bf16[130,768]{1,0:T(8,128)(2,1)S(1)}, u32[]{:S(2)}, u32[]{:S(2)}) %collective-permute-start.12) | collective-permute-done | bytes 199712 | tf_op jit(solution)/shard_map/ppermute | solution.py:107
  89.0 2.3 %collective-permute-done.13 = bf16[130,768]{1,0:T(8,128)(2,1)S(1)} collective-permute-done((bf16[130,768]{1,0:T(8,128)(2,1)S(1)}, bf16[130,768]{1,0:T(8,128)(2,1)S(1)}, u32[]{:S(2)}, u32[]{:S(2)}) %collective-permute-start.13) | collective-permute-done | bytes 199712 | tf_op jit(solution)/shard_map/ppermute | solution.py:108
  91.3 1.6 %collective-permute-done.14 = bf16[128,1024]{1,0:T(8,128)(2,1)S(1)} collective-permute-done((bf16[128,1024]{1,0:T(8,128)(2,1)S(1)}, bf16[128,1024]{1,0:T(8,128)(2,1)S(1)}, u32[]{:S(2)}, u32[]{:S(2)}) %collective-permute-start.14) | collective-permute-done | bytes 262176 | tf_op jit(solution)/shard_map/ppermute | solution.py:107
  92.9 4.0 %collective-permute-done.15 = bf16[128,1024]{1,0:T(8,128)(2,1)S(1)} collective-permute-done((bf16[128,1024]{1,0:T(8,128)(2,1)S(1)}, bf16[128,1024]{1,0:T(8,128)(2,1)S(1)}, u32[]{:S(2)}, u32[]{:S(2)}) %collective-permute-start.15) | collective-permute-done | bytes 262176 | tf_op jit(solution)/shard_map/ppermute | solution.py:108
  96.9 2.0 %collective-permute-start.16 = (bf16[130,768]{1,0:T(8,128)(2,1)S(1)}, bf16[130,768]{1,0:T(8,128)(2,1)S(1)}, u32[]{:S(2)}, u32[]{:S(2)}) collective-permute-start(bf16[130,768]{1,0:T(8,128)(2,1)S(1)} %add_convert_fusion.7), channel_id=1, source_target_pairs={{0,8},{8,16},{16,24},{24,28},{28,20},{20,12},{12,4},{4,0},{1,9},{9... | collective-permute-start | bytes 599048 | tf_op jit(solution)/shard_map/ppermute | solution.py:107
  99.6 1.4 collective-permute-start.30
  101.0 4.0 %collective-permute-done.19 = bf16[130,768]{1,0:T(8,128)(2,1)S(1)} collective-permute-done((bf16[130,768]{1,0:T(8,128)(2,1)S(1)}, bf16[130,768]{1,0:T(8,128)(2,1)S(1)}, u32[]{:S(2)}, u32[]{:S(2)}) %collective-permute-start.19) | collective-permute-done | bytes 199712 | tf_op jit(solution)/shard_map/ppermute | solution.py:108
  105.2 2.1 %collective-permute-start.17 = (bf16[130,768]{1,0:T(8,128)(2,1)S(1)}, bf16[130,768]{1,0:T(8,128)(2,1)S(1)}, u32[]{:S(2)}, u32[]{:S(2)}) collective-permute-start(bf16[130,768]{1,0:T(8,128)(2,1)S(1)} %add_convert_fusion.5), channel_id=1, source_target_pairs={{0,8},{8,16},{16,24},{24,28},{28,20},{20,12},{12,4},{4,0},{1,9},{9... | collective-permute-start | bytes 599048 | tf_op jit(solution)/shard_map/ppermute | solution.py:111
  107.2 3.0 %collective-permute-done.29 = bf16[128,1024]{1,0:T(8,128)(2,1)S(1)} collective-permute-done((bf16[128,1024]{1,0:T(8,128)(2,1)S(1)}, bf16[128,1024]{1,0:T(8,128)(2,1)S(1)}, u32[]{:S(2)}, u32[]{:S(2)}) %collective-permute-start.29) | collective-permute-done | bytes 262176 | tf_op jit(solution)/shard_map/ppermute | solution.py:107
  110.3 1.5 collective-permute-start.31
  113.5 2.1 %collective-permute-start.18 = (bf16[130,768]{1,0:T(8,128)(2,1)S(1)}, bf16[130,768]{1,0:T(8,128)(2,1)S(1)}, u32[]{:S(2)}, u32[]{:S(2)}) collective-permute-start(bf16[130,768]{1,0:T(8,128)(2,1)S(1)} %add_convert_fusion.4), channel_id=1, source_target_pairs={{0,8},{8,16},{16,24},{24,28},{28,20},{20,12},{12,4},{4,0},{1,9},{9... | collective-permute-start | bytes 599048 | tf_op jit(solution)/shard_map/ppermute | solution.py:111
  115.6 4.7 %collective-permute-done.21 = bf16[130,768]{1,0:T(8,128)(2,1)S(1)} collective-permute-done((bf16[130,768]{1,0:T(8,128)(2,1)S(1)}, bf16[130,768]{1,0:T(8,128)(2,1)S(1)}, u32[]{:S(2)}, u32[]{:S(2)}) %collective-permute-start.21) | collective-permute-done | bytes 199712 | tf_op jit(solution)/shard_map/ppermute | solution.py:112
  120.8 4.4 %fusion = f32[16,128,512]{2,1,0:T(8,128)S(1)} fusion(f32[128,512]{1,0:T(8,128)S(1)} %fusion.51, f32[16,512]{1,0:T(8,128)S(1)} %copy-done.3, f32[128,128]{1,0:T(8,128)S(1)} %fusion.52), kind=kOutput, calls=%fused_computation.1 | convolution fusion | flops 1612709888 | bytes 4554752 | tf_op jit(solution)/shard_map/dot_general | solution.py:23
  125.2 3.4 %collective-permute-start.28 = (f32[16,512]{1,0:T(8,128)S(1)}, f32[16,512]{1,0:T(8,128)S(1)}, u32[]{:S(2)}, u32[]{:S(2)}) collective-permute-start(f32[16,512]{1,0:T(8,128)S(1)} %bitcast_multiply_fusion), channel_id=1, source_target_pairs={{0,28},{1,29},{2,30},{3,31}} | collective-permute-start | bytes 98312 | tf_op jit(solution)/shard_map/ppermute | solution.py:33
  128.7 1.3 collective-permute-start.27
  130.0 1.3 collective-permute-start.26
  131.3 1.3 collective-permute-start.25
  132.6 2.5 %collective-permute-start.24 = (f32[16,512]{1,0:T(8,128)S(1)}, f32[16,512]{1,0:T(8,128)S(1)}, u32[]{:S(2)}, u32[]{:S(2)}) collective-permute-start(f32[16,512]{1,0:T(8,128)S(1)} %bitcast_multiply_fusion), channel_id=1, source_target_pairs={{0,12},{4,16},{8,20},{12,24},{16,28},{1,13},{5,17},{9,21},{13,25},... | collective-permute-start | bytes 98312 | tf_op jit(solution)/shard_map/ppermute | solution.py:33
  135.1 1.3 collective-permute-start.23
  136.4 3.2 %collective-permute-start.22 = (f32[16,512]{1,0:T(8,128)S(1)}, f32[16,512]{1,0:T(8,128)S(1)}, u32[]{:S(2)}, u32[]{:S(2)}) collective-permute-start(f32[16,512]{1,0:T(8,128)S(1)} %bitcast_multiply_fusion), channel_id=1, source_target_pairs={{0,4},{4,8},{8,12},{12,16},{16,20},{20,24},{24,28},{1,5},{5,9},{9,... | collective-permute-start | bytes 98312 | tf_op jit(solution)/shard_map/ppermute | solution.py:33
  139.7 2.0 %collective-permute-start.34 = (bf16[128,1024]{1,0:T(8,128)(2,1)S(1)}, bf16[128,1024]{1,0:T(8,128)(2,1)S(1)}, u32[]{:S(2)}, u32[]{:S(2)}) collective-permute-start(bf16[128,1024]{1,0:T(8,128)(2,1)S(1)} %collective-permute-done.32), channel_id=1, source_target_pairs={{8,0},{16,8},{24,16},{28,24},{20,28},{12,20},{4,12},{0,4},{9,1},{1... | collective-permute-start | bytes 786440 | tf_op jit(solution)/shard_map/ppermute | solution.py:117
  141.8 1.0 multiply_reduce_fusion
  143.2 7.2 %all_gather.3 = bf16[128,2048]{1,0:T(8,128)(2,1)S(1)} all-gather(bf16[128,512]{1,0:T(8,128)(2,1)S(1)} %multiply_convert_fusion), channel_id=1, replica_groups=mesh['ctx'=8,'tp'=4] {'tp'}, dimensions={1}, use_global_device_ids=true | all-gather | bytes 655360 | tf_op jit(solution)/shard_map/all_gather | solution.py:131
  150.4 1.4 convolution_convert_fusion
  (112 shorter events, 13.4 us)
Async XLA Ops:
  0.0 9.7 %copy-start.10 = (s32[8]{0:T(128)S(1)}, s32[8]{0:T(128)}, u32[]{:S(2)}) copy-start(s32[8]{0:T(128)} %constant.275.clone) | copy-start | bytes 100
  0.0 21.0 %copy-start.4 = (s32[8]{0:T(128)S(1)}, s32[8]{0:T(128)}, u32[]{:S(2)}) copy-start(s32[8]{0:T(128)} %constant.276.clone) | copy-start | bytes 100
  0.0 40.7 %copy-start.1 = (bf16[512,512]{1,0:T(8,128)(2,1)S(1)}, bf16[512,512]{1,0:T(8,128)(2,1)}, u32[]{:S(2)}) copy-start(bf16[512,512]{1,0:T(8,128)(2,1)} %param.15) | copy-start | bytes 1572868
  0.0 40.7 %copy-start.2 = (bf16[512,512]{1,0:T(8,128)(2,1)S(1)}, bf16[512,512]{1,0:T(8,128)(2,1)}, u32[]{:S(2)}) copy-start(bf16[512,512]{1,0:T(8,128)(2,1)} %param.14) | copy-start | bytes 1572868
  0.0 41.8 %copy-start.6 = (f32[3,512]{1,0:T(4,128)S(1)}, f32[3,512]{1,0:T(4,128)}, u32[]{:S(2)}) copy-start(f32[3,512]{1,0:T(4,128)} %param.19) | copy-start | bytes 18436
  0.0 41.8 %copy-start.7 = (f32[3,512]{1,0:T(4,128)S(1)}, f32[3,512]{1,0:T(4,128)}, u32[]{:S(2)}) copy-start(f32[3,512]{1,0:T(4,128)} %param.18) | copy-start | bytes 18436
  0.0 41.9 %copy-start.8 = (f32[3,512]{1,0:T(4,128)S(1)}, f32[3,512]{1,0:T(4,128)}, u32[]{:S(2)}) copy-start(f32[3,512]{1,0:T(4,128)} %param.17) | copy-start | bytes 18436
  0.0 41.9 %copy-start = (bf16[256,1024]{1,0:T(8,128)(2,1)S(1)}, bf16[256,1024]{1,0:T(8,128)(2,1)}, u32[]{:S(2)}) copy-start(bf16[256,1024]{1,0:T(8,128)(2,1)} %param.23) | copy-start | bytes 1572868
  2.4 39.5 %all-to-all-start = ((bf16[8,128,512]{1,2,0:T(8,128)(2,1)}), bf16[8,128,512]{1,2,0:T(8,128)(2,1)}, u32[]{:S(2)}, u32[]{:S(2)}) async-start(bf16[8,128,512]{1,2,0:T(8,128)(2,1)} %bitcast.2), calls=%async_computation | async-start | bytes 2097152 | tf_op jit(solution)/shard_map/all_to_all | solution.py:66
  46.0 8.1 %collective-permute-start = (bf16[130,768]{1,0:T(8,128)(2,1)S(1)}, bf16[130,768]{1,0:T(8,128)(2,1)S(1)}, u32[]{:S(2)}, u32[]{:S(2)}) collective-permute-start(bf16[130,768]{1,0:T(8,128)(2,1)S(1)} %convolution_convert_fusion.2), channel_id=1, source_target_pairs={{0,8},{8,16},{16,24},{24,28},{28,20},{20,12},{12,4},{4,0},{1,9},{9... | collective-permute-start | bytes 599048 | tf_op jit(solution)/shard_map/ppermute | solution.py:107
  48.1 8.1 %collective-permute-start.1 = (bf16[130,768]{1,0:T(8,128)(2,1)S(1)}, bf16[130,768]{1,0:T(8,128)(2,1)S(1)}, u32[]{:S(2)}, u32[]{:S(2)}) collective-permute-start(bf16[130,768]{1,0:T(8,128)(2,1)S(1)} %convolution_convert_fusion.1), channel_id=1, source_target_pairs={{8,0},{16,8},{24,16},{28,24},{20,28},{12,20},{4,12},{0,4},{9,1},{1... | collective-permute-start | bytes 599048 | tf_op jit(solution)/shard_map/ppermute | solution.py:108
  48.1 10.2 %collective-permute-start.2 = (bf16[128,1024]{1,0:T(8,128)(2,1)S(1)}, bf16[128,1024]{1,0:T(8,128)(2,1)S(1)}, u32[]{:S(2)}, u32[]{:S(2)}) collective-permute-start(bf16[128,1024]{1,0:T(8,128)(2,1)S(1)} %get-tuple-element.33), channel_id=1, source_target_pairs={{0,8},{8,16},{16,24},{24,28},{28,20},{20,12},{12,4},{4,0},{1,9},{9... | collective-permute-start | bytes 786440 | tf_op jit(solution)/shard_map/ppermute | solution.py:107
  50.1 9.7 %collective-permute-start.3 = (bf16[128,1024]{1,0:T(8,128)(2,1)S(1)}, bf16[128,1024]{1,0:T(8,128)(2,1)S(1)}, u32[]{:S(2)}, u32[]{:S(2)}) collective-permute-start(bf16[128,1024]{1,0:T(8,128)(2,1)S(1)} %get-tuple-element.34), channel_id=1, source_target_pairs={{8,0},{16,8},{24,16},{28,24},{20,28},{12,20},{4,12},{0,4},{9,1},{1... | collective-permute-start | bytes 786440 | tf_op jit(solution)/shard_map/ppermute | solution.py:108
  59.8 7.9 %collective-permute-start.4 = (bf16[130,768]{1,0:T(8,128)(2,1)S(1)}, bf16[130,768]{1,0:T(8,128)(2,1)S(1)}, u32[]{:S(2)}, u32[]{:S(2)}) collective-permute-start(bf16[130,768]{1,0:T(8,128)(2,1)S(1)} %add_convert_fusion.13), channel_id=1, source_target_pairs={{0,8},{8,16},{16,24},{24,28},{28,20},{20,12},{12,4},{4,0},{1,9},{9... | collective-permute-start | bytes 599048 | tf_op jit(solution)/shard_map/ppermute | solution.py:107
  61.2 7.7 %collective-permute-start.5 = (bf16[130,768]{1,0:T(8,128)(2,1)S(1)}, bf16[130,768]{1,0:T(8,128)(2,1)S(1)}, u32[]{:S(2)}, u32[]{:S(2)}) collective-permute-start(bf16[130,768]{1,0:T(8,128)(2,1)S(1)} %add_convert_fusion.12), channel_id=1, source_target_pairs={{8,0},{16,8},{24,16},{28,24},{20,28},{12,20},{4,12},{0,4},{9,1},{1... | collective-permute-start | bytes 599048 | tf_op jit(solution)/shard_map/ppermute | solution.py:108
  61.8 8.7 %collective-permute-start.6 = (bf16[128,1024]{1,0:T(8,128)(2,1)S(1)}, bf16[128,1024]{1,0:T(8,128)(2,1)S(1)}, u32[]{:S(2)}, u32[]{:S(2)}) collective-permute-start(bf16[128,1024]{1,0:T(8,128)(2,1)S(1)} %collective-permute-done.2), channel_id=1, source_target_pairs={{0,8},{8,16},{16,24},{24,28},{28,20},{20,12},{12,4},{4,0},{1,9},{9... | collective-permute-start | bytes 786440 | tf_op jit(solution)/shard_map/ppermute | solution.py:107
  63.2 8.4 %collective-permute-start.7 = (bf16[128,1024]{1,0:T(8,128)(2,1)S(1)}, bf16[128,1024]{1,0:T(8,128)(2,1)S(1)}, u32[]{:S(2)}, u32[]{:S(2)}) collective-permute-start(bf16[128,1024]{1,0:T(8,128)(2,1)S(1)} %collective-permute-done.3), channel_id=1, source_target_pairs={{8,0},{16,8},{24,16},{28,24},{20,28},{12,20},{4,12},{0,4},{9,1},{1... | collective-permute-start | bytes 786440 | tf_op jit(solution)/shard_map/ppermute | solution.py:108
  71.7 6.7 %collective-permute-start.8 = (bf16[130,768]{1,0:T(8,128)(2,1)S(1)}, bf16[130,768]{1,0:T(8,128)(2,1)S(1)}, u32[]{:S(2)}, u32[]{:S(2)}) collective-permute-start(bf16[130,768]{1,0:T(8,128)(2,1)S(1)} %add_convert_fusion.11), channel_id=1, source_target_pairs={{0,8},{8,16},{16,24},{24,28},{28,20},{20,12},{12,4},{4,0},{1,9},{9... | collective-permute-start | bytes 599048 | tf_op jit(solution)/shard_map/ppermute | solution.py:107
  73.2 6.5 %collective-permute-start.9 = (bf16[130,768]{1,0:T(8,128)(2,1)S(1)}, bf16[130,768]{1,0:T(8,128)(2,1)S(1)}, u32[]{:S(2)}, u32[]{:S(2)}) collective-permute-start(bf16[130,768]{1,0:T(8,128)(2,1)S(1)} %add_convert_fusion.10), channel_id=1, source_target_pairs={{8,0},{16,8},{24,16},{28,24},{20,28},{12,20},{4,12},{0,4},{9,1},{1... | collective-permute-start | bytes 599048 | tf_op jit(solution)/shard_map/ppermute | solution.py:108
  73.7 8.0 %collective-permute-start.10 = (bf16[128,1024]{1,0:T(8,128)(2,1)S(1)}, bf16[128,1024]{1,0:T(8,128)(2,1)S(1)}, u32[]{:S(2)}, u32[]{:S(2)}) collective-permute-start(bf16[128,1024]{1,0:T(8,128)(2,1)S(1)} %collective-permute-done.6), channel_id=1, source_target_pairs={{0,8},{8,16},{16,24},{24,28},{28,20},{20,12},{12,4},{4,0},{1,9},{9... | collective-permute-start | bytes 786440 | tf_op jit(solution)/shard_map/ppermute | solution.py:107
  75.2 7.9 %collective-permute-start.11 = (bf16[128,1024]{1,0:T(8,128)(2,1)S(1)}, bf16[128,1024]{1,0:T(8,128)(2,1)S(1)}, u32[]{:S(2)}, u32[]{:S(2)}) collective-permute-start(bf16[128,1024]{1,0:T(8,128)(2,1)S(1)} %collective-permute-done.7), channel_id=1, source_target_pairs={{8,0},{16,8},{24,16},{28,24},{20,28},{12,20},{4,12},{0,4},{9,1},{1... | collective-permute-start | bytes 786440 | tf_op jit(solution)/shard_map/ppermute | solution.py:108
  83.1 5.8 %collective-permute-start.12 = (bf16[130,768]{1,0:T(8,128)(2,1)S(1)}, bf16[130,768]{1,0:T(8,128)(2,1)S(1)}, u32[]{:S(2)}, u32[]{:S(2)}) collective-permute-start(bf16[130,768]{1,0:T(8,128)(2,1)S(1)} %add_convert_fusion.9), channel_id=1, source_target_pairs={{0,8},{8,16},{16,24},{24,28},{28,20},{20,12},{12,4},{4,0},{1,9},{9... | collective-permute-start | bytes 599048 | tf_op jit(solution)/shard_map/ppermute | solution.py:107
  85.0 6.3 %collective-permute-start.13 = (bf16[130,768]{1,0:T(8,128)(2,1)S(1)}, bf16[130,768]{1,0:T(8,128)(2,1)S(1)}, u32[]{:S(2)}, u32[]{:S(2)}) collective-permute-start(bf16[130,768]{1,0:T(8,128)(2,1)S(1)} %add_convert_fusion.8), channel_id=1, source_target_pairs={{8,0},{16,8},{24,16},{28,24},{20,28},{12,20},{4,12},{0,4},{9,1},{1... | collective-permute-start | bytes 599048 | tf_op jit(solution)/shard_map/ppermute | solution.py:108
  85.1 7.7 %collective-permute-start.14 = (bf16[128,1024]{1,0:T(8,128)(2,1)S(1)}, bf16[128,1024]{1,0:T(8,128)(2,1)S(1)}, u32[]{:S(2)}, u32[]{:S(2)}) collective-permute-start(bf16[128,1024]{1,0:T(8,128)(2,1)S(1)} %collective-permute-done.10), channel_id=1, source_target_pairs={{0,8},{8,16},{16,24},{24,28},{28,20},{20,12},{12,4},{4,0},{1,9},{9... | collective-permute-start | bytes 786440 | tf_op jit(solution)/shard_map/ppermute | solution.py:107
  87.0 9.9 %collective-permute-start.15 = (bf16[128,1024]{1,0:T(8,128)(2,1)S(1)}, bf16[128,1024]{1,0:T(8,128)(2,1)S(1)}, u32[]{:S(2)}, u32[]{:S(2)}) collective-permute-start(bf16[128,1024]{1,0:T(8,128)(2,1)S(1)} %collective-permute-done.11), channel_id=1, source_target_pairs={{8,0},{16,8},{24,16},{28,24},{20,28},{12,20},{4,12},{0,4},{9,1},{1... | collective-permute-start | bytes 786440 | tf_op jit(solution)/shard_map/ppermute | solution.py:108
  96.9 8.1 %collective-permute-start.19 = (bf16[130,768]{1,0:T(8,128)(2,1)S(1)}, bf16[130,768]{1,0:T(8,128)(2,1)S(1)}, u32[]{:S(2)}, u32[]{:S(2)}) collective-permute-start(bf16[130,768]{1,0:T(8,128)(2,1)S(1)} %add_convert_fusion.6), channel_id=1, source_target_pairs={{8,0},{16,8},{24,16},{28,24},{20,28},{12,20},{4,12},{0,4},{9,1},{1... | collective-permute-start | bytes 599048 | tf_op jit(solution)/shard_map/ppermute | solution.py:108
  96.9 8.2 %collective-permute-start.16 = (bf16[130,768]{1,0:T(8,128)(2,1)S(1)}, bf16[130,768]{1,0:T(8,128)(2,1)S(1)}, u32[]{:S(2)}, u32[]{:S(2)}) collective-permute-start(bf16[130,768]{1,0:T(8,128)(2,1)S(1)} %add_convert_fusion.7), channel_id=1, source_target_pairs={{0,8},{8,16},{16,24},{24,28},{28,20},{20,12},{12,4},{4,0},{1,9},{9... | collective-permute-start | bytes 599048 | tf_op jit(solution)/shard_map/ppermute | solution.py:107
  98.9 11.4 %collective-permute-start.29 = (bf16[128,1024]{1,0:T(8,128)(2,1)S(1)}, bf16[128,1024]{1,0:T(8,128)(2,1)S(1)}, u32[]{:S(2)}, u32[]{:S(2)}) collective-permute-start(bf16[128,1024]{1,0:T(8,128)(2,1)S(1)} %collective-permute-done.14), channel_id=1, source_target_pairs={{0,8},{8,16},{16,24},{24,28},{28,20},{20,12},{12,4},{4,0},{1,9},{9... | collective-permute-start | bytes 786440 | tf_op jit(solution)/shard_map/ppermute | solution.py:107
  99.6 12.1 %collective-permute-start.30 = (bf16[128,1024]{1,0:T(8,128)(2,1)S(1)}, bf16[128,1024]{1,0:T(8,128)(2,1)S(1)}, u32[]{:S(2)}, u32[]{:S(2)}) collective-permute-start(bf16[128,1024]{1,0:T(8,128)(2,1)S(1)} %collective-permute-done.15), channel_id=1, source_target_pairs={{8,0},{16,8},{24,16},{28,24},{20,28},{12,20},{4,12},{0,4},{9,1},{1... | collective-permute-start | bytes 786440 | tf_op jit(solution)/shard_map/ppermute | solution.py:108
  105.0 15.7 %copy-start.3 = (f32[16,512]{1,0:T(8,128)S(1)}, f32[16,512]{1,0:T(8,128)}, u32[]{:S(2)}) copy-start(f32[16,512]{1,0:T(8,128)} %param.20) | copy-start | bytes 98308
  105.1 8.1 %collective-permute-start.20 = (bf16[130,768]{1,0:T(8,128)(2,1)S(1)}, bf16[130,768]{1,0:T(8,128)(2,1)S(1)}, u32[]{:S(2)}, u32[]{:S(2)}) collective-permute-start(bf16[130,768]{1,0:T(8,128)(2,1)S(1)} %add_convert_fusion.2), channel_id=1, source_target_pairs={{8,0},{16,8},{24,16},{28,24},{20,28},{12,20},{4,12},{0,4},{9,1},{1... | collective-permute-start | bytes 599048 | tf_op jit(solution)/shard_map/ppermute | solution.py:112
  105.2 8.3 %collective-permute-start.17 = (bf16[130,768]{1,0:T(8,128)(2,1)S(1)}, bf16[130,768]{1,0:T(8,128)(2,1)S(1)}, u32[]{:S(2)}, u32[]{:S(2)}) collective-permute-start(bf16[130,768]{1,0:T(8,128)(2,1)S(1)} %add_convert_fusion.5), channel_id=1, source_target_pairs={{0,8},{8,16},{16,24},{24,28},{28,20},{20,12},{12,4},{4,0},{1,9},{9... | collective-permute-start | bytes 599048 | tf_op jit(solution)/shard_map/ppermute | solution.py:111
  110.3 19.7 %collective-permute-start.31 = (bf16[128,1024]{1,0:T(8,128)(2,1)S(1)}, bf16[128,1024]{1,0:T(8,128)(2,1)S(1)}, u32[]{:S(2)}, u32[]{:S(2)}) collective-permute-start(bf16[128,1024]{1,0:T(8,128)(2,1)S(1)} %collective-permute-done.29), channel_id=1, source_target_pairs={{0,8},{8,16},{16,24},{24,28},{28,20},{20,12},{12,4},{4,0},{1,9},{9... | collective-permute-start | bytes 786440 | tf_op jit(solution)/shard_map/ppermute | solution.py:116
  111.7 20.9 %collective-permute-start.32 = (bf16[128,1024]{1,0:T(8,128)(2,1)S(1)}, bf16[128,1024]{1,0:T(8,128)(2,1)S(1)}, u32[]{:S(2)}, u32[]{:S(2)}) collective-permute-start(bf16[128,1024]{1,0:T(8,128)(2,1)S(1)} %collective-permute-done.30), channel_id=1, source_target_pairs={{8,0},{16,8},{24,16},{28,24},{20,28},{12,20},{4,12},{0,4},{9,1},{1... | collective-permute-start | bytes 786440 | tf_op jit(solution)/shard_map/ppermute | solution.py:117
  113.2 7.1 %collective-permute-start.21 = (bf16[130,768]{1,0:T(8,128)(2,1)S(1)}, bf16[130,768]{1,0:T(8,128)(2,1)S(1)}, u32[]{:S(2)}, u32[]{:S(2)}) collective-permute-start(bf16[130,768]{1,0:T(8,128)(2,1)S(1)} %add_convert_fusion.1), channel_id=1, source_target_pairs={{8,0},{16,8},{24,16},{28,24},{20,28},{12,20},{4,12},{0,4},{9,1},{1... | collective-permute-start | bytes 599048 | tf_op jit(solution)/shard_map/ppermute | solution.py:112
  113.5 6.9 %collective-permute-start.18 = (bf16[130,768]{1,0:T(8,128)(2,1)S(1)}, bf16[130,768]{1,0:T(8,128)(2,1)S(1)}, u32[]{:S(2)}, u32[]{:S(2)}) collective-permute-start(bf16[130,768]{1,0:T(8,128)(2,1)S(1)} %add_convert_fusion.4), channel_id=1, source_target_pairs={{0,8},{8,16},{16,24},{24,28},{28,20},{20,12},{12,4},{4,0},{1,9},{9... | collective-permute-start | bytes 599048 | tf_op jit(solution)/shard_map/ppermute | solution.py:111
  120.5 21.3 %copy-start.5 = (f32[16,512]{1,0:T(8,128)S(1)}, f32[16,512]{1,0:T(8,128)}, u32[]{:S(2)}) copy-start(f32[16,512]{1,0:T(8,128)} %param.21) | copy-start | bytes 98308
  125.2 17.7 %copy-start.9 = (f32[512]{0:T(512)S(1)}, f32[512]{0:T(512)}, u32[]{:S(2)}) copy-start(f32[512]{0:T(512)} %param.22) | copy-start | bytes 6148
  125.2 9.9 %collective-permute-start.28 = (f32[16,512]{1,0:T(8,128)S(1)}, f32[16,512]{1,0:T(8,128)S(1)}, u32[]{:S(2)}, u32[]{:S(2)}) collective-permute-start(f32[16,512]{1,0:T(8,128)S(1)} %bitcast_multiply_fusion), channel_id=1, source_target_pairs={{0,28},{1,29},{2,30},{3,31}} | collective-permute-start | bytes 98312 | tf_op jit(solution)/shard_map/ppermute | solution.py:33
  128.7 7.7 %collective-permute-start.27 = (f32[16,512]{1,0:T(8,128)S(1)}, f32[16,512]{1,0:T(8,128)S(1)}, u32[]{:S(2)}, u32[]{:S(2)}) collective-permute-start(f32[16,512]{1,0:T(8,128)S(1)} %bitcast_multiply_fusion), channel_id=1, source_target_pairs={{0,24},{4,28},{1,25},{5,29},{2,26},{6,30},{3,27},{7,31}} | collective-permute-start | bytes 98312 | tf_op jit(solution)/shard_map/ppermute | solution.py:33
  130.0 9.7 %collective-permute-start.26 = (f32[16,512]{1,0:T(8,128)S(1)}, f32[16,512]{1,0:T(8,128)S(1)}, u32[]{:S(2)}, u32[]{:S(2)}) collective-permute-start(f32[16,512]{1,0:T(8,128)S(1)} %bitcast_multiply_fusion), channel_id=1, source_target_pairs={{0,20},{4,24},{8,28},{1,21},{5,25},{9,29},{2,22},{6,26},{10,30},{3... | collective-permute-start | bytes 98312 | tf_op jit(solution)/shard_map/ppermute | solution.py:33
  131.3 8.4 %collective-permute-start.25 = (f32[16,512]{1,0:T(8,128)S(1)}, f32[16,512]{1,0:T(8,128)S(1)}, u32[]{:S(2)}, u32[]{:S(2)}) collective-permute-start(f32[16,512]{1,0:T(8,128)S(1)} %bitcast_multiply_fusion), channel_id=1, source_target_pairs={{0,16},{4,20},{8,24},{12,28},{1,17},{5,21},{9,25},{13,29},{2,18},{... | collective-permute-start | bytes 98312 | tf_op jit(solution)/shard_map/ppermute | solution.py:33
  132.6 9.1 %collective-permute-start.24 = (f32[16,512]{1,0:T(8,128)S(1)}, f32[16,512]{1,0:T(8,128)S(1)}, u32[]{:S(2)}, u32[]{:S(2)}) collective-permute-start(f32[16,512]{1,0:T(8,128)S(1)} %bitcast_multiply_fusion), channel_id=1, source_target_pairs={{0,12},{4,16},{8,20},{12,24},{16,28},{1,13},{5,17},{9,21},{13,25},... | collective-permute-start | bytes 98312 | tf_op jit(solution)/shard_map/ppermute | solution.py:33
  135.1 6.7 %collective-permute-start.23 = (f32[16,512]{1,0:T(8,128)S(1)}, f32[16,512]{1,0:T(8,128)S(1)}, u32[]{:S(2)}, u32[]{:S(2)}) collective-permute-start(f32[16,512]{1,0:T(8,128)S(1)} %bitcast_multiply_fusion), channel_id=1, source_target_pairs={{0,8},{4,12},{8,16},{12,20},{16,24},{20,28},{1,9},{5,13},{9,17},{1... | collective-permute-start | bytes 98312 | tf_op jit(solution)/shard_map/ppermute | solution.py:33
  136.4 5.3 %collective-permute-start.22 = (f32[16,512]{1,0:T(8,128)S(1)}, f32[16,512]{1,0:T(8,128)S(1)}, u32[]{:S(2)}, u32[]{:S(2)}) collective-permute-start(f32[16,512]{1,0:T(8,128)S(1)} %bitcast_multiply_fusion), channel_id=1, source_target_pairs={{0,4},{4,8},{8,12},{12,16},{16,20},{20,24},{24,28},{1,5},{5,9},{9,... | collective-permute-start | bytes 98312 | tf_op jit(solution)/shard_map/ppermute | solution.py:33
  139.7 10.7 %collective-permute-start.33 = (bf16[128,1024]{1,0:T(8,128)(2,1)S(1)}, bf16[128,1024]{1,0:T(8,128)(2,1)S(1)}, u32[]{:S(2)}, u32[]{:S(2)}) collective-permute-start(bf16[128,1024]{1,0:T(8,128)(2,1)S(1)} %collective-permute-done.31), channel_id=1, source_target_pairs={{0,8},{8,16},{16,24},{24,28},{28,20},{20,12},{12,4},{4,0},{1,9},{9... | collective-permute-start | bytes 786440 | tf_op jit(solution)/shard_map/ppermute | solution.py:116
  139.7 10.6 %collective-permute-start.34 = (bf16[128,1024]{1,0:T(8,128)(2,1)S(1)}, bf16[128,1024]{1,0:T(8,128)(2,1)S(1)}, u32[]{:S(2)}, u32[]{:S(2)}) collective-permute-start(bf16[128,1024]{1,0:T(8,128)(2,1)S(1)} %collective-permute-done.32), channel_id=1, source_target_pairs={{8,0},{16,8},{24,16},{28,24},{20,28},{12,20},{4,12},{0,4},{9,1},{1... | collective-permute-start | bytes 786440 | tf_op jit(solution)/shard_map/ppermute | solution.py:117

commit v12 on v11

--- a/solution.py
+++ b/solution.py
@@ -98,7 +98,7 @@
 
     up = piece(ring_arr[(my_pos - 1) % ctx_count], 0)
     down = piece(ring_arr[(my_pos + 1) % ctx_count], 1)
-    tied = max(ctx_count - 3, 0)
+    tied = max(ctx_count - 4, 0)
     for step in range(1, ctx_count):
         if step <= tied:
             sent = lax.optimization_barrier(

time: 153 us -> 152 us (level)
  waiting for transfers between devices: 43.8 us -> 42.2 us
    ppermute x10 -> x8, waiting for transfers between devices: 18.3 us -> 13.3 us  [body(): down, w_low = lax.ppermute((sent[1], sent[3]), 'ctx', perm=bwd)]
    ppermute x2 -> x3, waiting for transfers between devices: 0.01 us -> 3.84 us  [body(): w_up = lax.ppermute(w_up, 'ctx', perm=fwd)]
    ppermute x10 -> x8, starting transfers between devices: 16.3 us -> 13 us  [body(): up, w_up = lax.ppermute((sent[0], sent[2]), 'ctx', perm=fwd)]
    ppermute x10 -> x8, waiting for transfers between devices: 19.9 us -> 17.2 us  [body(): up, w_up = lax.ppermute((sent[0], sent[2]), 'ctx', perm=fwd)]
    ppermute x2 -> x3, waiting for transfers between devices: 5.56 us -> 7.5 us  [body(): down = lax.ppermute(down.astype(jnp.bfloat16), 'ctx', perm=bwd)]
    ppermute x2 -> x3, starting transfers between devices: 0.27 us -> 1.88 us  [body(): down = lax.ppermute(down.astype(jnp.bfloat16), 'ctx', perm=bwd)]
    ppermute x10 -> x8, starting transfers between devices: 4.06 us -> 3.33 us  [body(): down, w_low = lax.ppermute((sent[1], sent[3]), 'ctx', perm=bwd)]
    ppermute x2 -> x3, starting transfers between devices: 2.58 us -> 3.14 us  [body(): w_low = lax.ppermute(w_low, 'ctx', perm=bwd)]
  transfers between devices with their start and end apart: 36 -> 36, of which waited for: 20 -> 19; matrix products, arithmetic and copies ran while one was open for 8% -> 8% of each run, Pallas kernels for 0% -> 0%
where the time goes in v12:
time: 152 us; the launch traced here: 151 us
  starting transfers between devices  51.6 us (34%)
  waiting for transfers between devices  42.2 us (28%)
  between operations  30.3 us (20%)
  matrix products  10.3 us (7%)
  blocking collectives  7.17 us (5%)
  local copies, waits for them, and re-layouts  6.51 us (4%)
  other arithmetic  3.36 us (2%)
    ppermute x8, waiting for transfers between devices, body(): up, w_up = lax.ppermute((sent[0], sent[2]), 'ctx', perm=fwd)  17.2 us
    ppermute x7, starting transfers between devices, modal_long_conv(): lax.ppermute(end_state, 'ctx', perm=[(i, i + shift) for i in range(ctx_co...  15.3 us
    ppermute x8, waiting for transfers between devices, body(): down, w_low = lax.ppermute((sent[1], sent[3]), 'ctx', perm=bwd)  13.3 us
    ppermute x8, starting transfers between devices, body(): up, w_up = lax.ppermute((sent[0], sent[2]), 'ctx', perm=fwd)  13 us
    ppermute x3, waiting for transfers between devices, body(): down = lax.ppermute(down.astype(jnp.bfloat16), 'ctx', perm=bwd)  7.5 us
    all_to_all x1, starting transfers between devices, body(): lax.all_to_all(by_dest, 'ctx', split_axis=0, concat_axis=0, tiled=True)  7.29 us
    all_gather x1, blocking collectives, body(): features = lax.all_gather(gated, 'tp', axis=1, tiled=True)  7.17 us
    ppermute x3, starting transfers between devices, body(): up = lax.ppermute(up.astype(jnp.bfloat16), 'ctx', perm=fwd)  4.69 us
  transfers between devices with their start and end apart: 36, of which 19 were waited for; matrix products, arithmetic and copies ran while one was open for 8% of the time, Pallas kernels for 0%

profile of v12, /device:TPU:0, one launch (start us, length us, event | category | flops | bytes accessed | tf_op | source)
XLA Modules:
  0.0 151.4 jit_solution(9025675268912961126)
XLA Ops:
  0.0 2.4 %copy.14 = bf16[128,4096]{0,1:T(8,128)(2,1)} copy(bf16[128,4096]{1,0:T(8,128)(2,1)} %param.13) | data formatting | bytes 2097152 | tf_op args[0]
  2.4 7.3 %all-to-all-start = ((bf16[8,128,512]{1,2,0:T(8,128)(2,1)}), bf16[8,128,512]{1,2,0:T(8,128)(2,1)}, u32[]{:S(2)}, u32[]{:S(2)}) async-start(bf16[8,128,512]{1,2,0:T(8,128)(2,1)} %bitcast.2), calls=%async_computation | async-start | bytes 2097152 | tf_op jit(solution)/shard_map/all_to_all | solution.py:66
  21.0 0.8 fusion.73
  40.8 1.1 pad_maximum_fusion.1
  42.0 1.5 copy.15
  46.1 2.1 %collective-permute-start = (bf16[130,768]{1,0:T(8,128)(2,1)S(1)}, bf16[130,768]{1,0:T(8,128)(2,1)S(1)}, u32[]{:S(2)}, u32[]{:S(2)}) collective-permute-start(bf16[130,768]{1,0:T(8,128)(2,1)S(1)} %convolution_convert_fusion.2), channel_id=1, source_target_pairs={{0,8},{8,16},{16,24},{24,28},{28,20},{20,12},{12,4},{4,0},{1,9},{9... | collective-permute-start | bytes 599048 | tf_op jit(solution)/shard_map/ppermute | solution.py:107
  48.2 2.0 %collective-permute-start.2 = (bf16[128,1024]{1,0:T(8,128)(2,1)S(1)}, bf16[128,1024]{1,0:T(8,128)(2,1)S(1)}, u32[]{:S(2)}, u32[]{:S(2)}) collective-permute-start(bf16[128,1024]{1,0:T(8,128)(2,1)S(1)} %get-tuple-element.29), channel_id=1, source_target_pairs={{0,8},{8,16},{16,24},{24,28},{28,20},{20,12},{12,4},{4,0},{1,9},{9... | collective-permute-start | bytes 786440 | tf_op jit(solution)/shard_map/ppermute | solution.py:107
  52.6 1.7 %collective-permute-done = bf16[130,768]{1,0:T(8,128)(2,1)S(1)} collective-permute-done((bf16[130,768]{1,0:T(8,128)(2,1)S(1)}, bf16[130,768]{1,0:T(8,128)(2,1)S(1)}, u32[]{:S(2)}, u32[]{:S(2)}) %collective-permute-start) | collective-permute-done | bytes 199712 | tf_op jit(solution)/shard_map/ppermute | solution.py:107
  54.5 1.7 %collective-permute-done.1 = bf16[130,768]{1,0:T(8,128)(2,1)S(1)} collective-permute-done((bf16[130,768]{1,0:T(8,128)(2,1)S(1)}, bf16[130,768]{1,0:T(8,128)(2,1)S(1)}, u32[]{:S(2)}, u32[]{:S(2)}) %collective-permute-start.1) | collective-permute-done | bytes 199712 | tf_op jit(solution)/shard_map/ppermute | solution.py:108
  56.5 1.8 %collective-permute-done.2 = bf16[128,1024]{1,0:T(8,128)(2,1)S(1)} collective-permute-done((bf16[128,1024]{1,0:T(8,128)(2,1)S(1)}, bf16[128,1024]{1,0:T(8,128)(2,1)S(1)}, u32[]{:S(2)}, u32[]{:S(2)}) %collective-permute-start.2) | collective-permute-done | bytes 262176 | tf_op jit(solution)/shard_map/ppermute | solution.py:107
  58.4 1.5 collective-permute-done.3
  59.8 1.5 collective-permute-start.4
  61.9 1.5 collective-permute-start.6
  64.0 3.8 %collective-permute-done.4 = bf16[130,768]{1,0:T(8,128)(2,1)S(1)} collective-permute-done((bf16[130,768]{1,0:T(8,128)(2,1)S(1)}, bf16[130,768]{1,0:T(8,128)(2,1)S(1)}, u32[]{:S(2)}, u32[]{:S(2)}) %collective-permute-start.4) | collective-permute-done | bytes 199712 | tf_op jit(solution)/shard_map/ppermute | solution.py:107
  67.8 1.1 collective-permute-done.5
  69.0 1.6 %collective-permute-done.6 = bf16[128,1024]{1,0:T(8,128)(2,1)S(1)} collective-permute-done((bf16[128,1024]{1,0:T(8,128)(2,1)S(1)}, bf16[128,1024]{1,0:T(8,128)(2,1)S(1)}, u32[]{:S(2)}, u32[]{:S(2)}) %collective-permute-start.6) | collective-permute-done | bytes 262176 | tf_op jit(solution)/shard_map/ppermute | solution.py:107
  70.6 1.2 collective-permute-done.7
  71.8 1.5 collective-permute-start.8
  73.8 1.5 collective-permute-start.10
  75.9 2.6 %collective-permute-done.8 = bf16[130,768]{1,0:T(8,128)(2,1)S(1)} collective-permute-done((bf16[130,768]{1,0:T(8,128)(2,1)S(1)}, bf16[130,768]{1,0:T(8,128)(2,1)S(1)}, u32[]{:S(2)}, u32[]{:S(2)}) %collective-permute-start.8) | collective-permute-done | bytes 199712 | tf_op jit(solution)/shard_map/ppermute | solution.py:107
  78.6 1.1 collective-permute-done.9
  79.8 1.8 %collective-permute-done.10 = bf16[128,1024]{1,0:T(8,128)(2,1)S(1)} collective-permute-done((bf16[128,1024]{1,0:T(8,128)(2,1)S(1)}, bf16[128,1024]{1,0:T(8,128)(2,1)S(1)}, u32[]{:S(2)}, u32[]{:S(2)}) %collective-permute-start.10) | collective-permute-done | bytes 262176 | tf_op jit(solution)/shard_map/ppermute | solution.py:107
  81.5 2.6 %collective-permute-done.11 = bf16[128,1024]{1,0:T(8,128)(2,1)S(1)} collective-permute-done((bf16[128,1024]{1,0:T(8,128)(2,1)S(1)}, bf16[128,1024]{1,0:T(8,128)(2,1)S(1)}, u32[]{:S(2)}, u32[]{:S(2)}) %collective-permute-start.11) | collective-permute-done | bytes 262176 | tf_op jit(solution)/shard_map/ppermute | solution.py:108
  84.8 1.5 collective-permute-start.12
  86.2 1.6 %collective-permute-start.27 = (bf16[128,1024]{1,0:T(8,128)(2,1)S(1)}, bf16[128,1024]{1,0:T(8,128)(2,1)S(1)}, u32[]{:S(2)}, u32[]{:S(2)}) collective-permute-start(bf16[128,1024]{1,0:T(8,128)(2,1)S(1)} %collective-permute-done.10), channel_id=1, source_target_pairs={{0,8},{8,16},{16,24},{24,28},{28,20},{20,12},{12,4},{4,0},{1,9},{9... | collective-permute-start | bytes 786440 | tf_op jit(solution)/shard_map/ppermute | solution.py:107
  88.3 4.0 %collective-permute-done.16 = bf16[130,768]{1,0:T(8,128)(2,1)S(1)} collective-permute-done((bf16[130,768]{1,0:T(8,128)(2,1)S(1)}, bf16[130,768]{1,0:T(8,128)(2,1)S(1)}, u32[]{:S(2)}, u32[]{:S(2)}) %collective-permute-start.16) | collective-permute-done | bytes 199712 | tf_op jit(solution)/shard_map/ppermute | solution.py:108
  93.0 1.5 collective-permute-start.13
  94.5 3.8 %collective-permute-done.27 = bf16[128,1024]{1,0:T(8,128)(2,1)S(1)} collective-permute-done((bf16[128,1024]{1,0:T(8,128)(2,1)S(1)}, bf16[128,1024]{1,0:T(8,128)(2,1)S(1)}, u32[]{:S(2)}, u32[]{:S(2)}) %collective-permute-start.27) | collective-permute-done | bytes 262176 | tf_op jit(solution)/shard_map/ppermute | solution.py:107
  98.4 1.5 collective-permute-start.29
  100.5 1.9 %collective-permute-done.17 = bf16[130,768]{1,0:T(8,128)(2,1)S(1)} collective-permute-done((bf16[130,768]{1,0:T(8,128)(2,1)S(1)}, bf16[130,768]{1,0:T(8,128)(2,1)S(1)}, u32[]{:S(2)}, u32[]{:S(2)}) %collective-permute-start.17) | collective-permute-done | bytes 199712 | tf_op jit(solution)/shard_map/ppermute | solution.py:112
  103.1 1.5 collective-permute-start.14
  104.6 3.8 %collective-permute-done.29 = bf16[128,1024]{1,0:T(8,128)(2,1)S(1)} collective-permute-done((bf16[128,1024]{1,0:T(8,128)(2,1)S(1)}, bf16[128,1024]{1,0:T(8,128)(2,1)S(1)}, u32[]{:S(2)}, u32[]{:S(2)}) %collective-permute-start.29) | collective-permute-done | bytes 262176 | tf_op jit(solution)/shard_map/ppermute | solution.py:116
  108.5 1.5 collective-permute-start.31
  110.6 1.7 %collective-permute-done.18 = bf16[130,768]{1,0:T(8,128)(2,1)S(1)} collective-permute-done((bf16[130,768]{1,0:T(8,128)(2,1)S(1)}, bf16[130,768]{1,0:T(8,128)(2,1)S(1)}, u32[]{:S(2)}, u32[]{:S(2)}) %collective-permute-start.18) | collective-permute-done | bytes 199712 | tf_op jit(solution)/shard_map/ppermute | solution.py:112
  113.0 1.7 %collective-permute-start.15 = (bf16[130,768]{1,0:T(8,128)(2,1)S(1)}, bf16[130,768]{1,0:T(8,128)(2,1)S(1)}, u32[]{:S(2)}, u32[]{:S(2)}) collective-permute-start(bf16[130,768]{1,0:T(8,128)(2,1)S(1)} %add_convert_fusion.5), channel_id=1, source_target_pairs={{0,8},{8,16},{16,24},{24,28},{28,20},{20,12},{12,4},{4,0},{1,9},{9... | collective-permute-start | bytes 599048 | tf_op jit(solution)/shard_map/ppermute | solution.py:111
  114.6 3.9 %collective-permute-done.19 = bf16[130,768]{1,0:T(8,128)(2,1)S(1)} collective-permute-done((bf16[130,768]{1,0:T(8,128)(2,1)S(1)}, bf16[130,768]{1,0:T(8,128)(2,1)S(1)}, u32[]{:S(2)}, u32[]{:S(2)}) %collective-permute-start.19) | collective-permute-done | bytes 199712 | tf_op jit(solution)/shard_map/ppermute | solution.py:112
  119.3 4.4 %fusion = f32[16,128,512]{2,1,0:T(8,128)S(1)} fusion(f32[128,512]{1,0:T(8,128)S(1)} %fusion.51, f32[16,512]{1,0:T(8,128)S(1)} %copy-done.3, f32[128,128]{1,0:T(8,128)S(1)} %fusion.52), kind=kOutput, calls=%fused_computation.1 | convolution fusion | flops 1612709888 | bytes 4554752 | tf_op jit(solution)/shard_map/dot_general | solution.py:23
  123.8 4.5 %collective-permute-start.26 = (f32[16,512]{1,0:T(8,128)S(1)}, f32[16,512]{1,0:T(8,128)S(1)}, u32[]{:S(2)}, u32[]{:S(2)}) collective-permute-start(f32[16,512]{1,0:T(8,128)S(1)} %bitcast_multiply_fusion), channel_id=1, source_target_pairs={{0,28},{1,29},{2,30},{3,31}} | collective-permute-start | bytes 98312 | tf_op jit(solution)/shard_map/ppermute | solution.py:33
  128.3 1.3 collective-permute-start.25
  129.7 1.3 collective-permute-start.24
  131.0 1.3 collective-permute-start.23
  132.3 2.5 %collective-permute-start.22 = (f32[16,512]{1,0:T(8,128)S(1)}, f32[16,512]{1,0:T(8,128)S(1)}, u32[]{:S(2)}, u32[]{:S(2)}) collective-permute-start(f32[16,512]{1,0:T(8,128)S(1)} %bitcast_multiply_fusion), channel_id=1, source_target_pairs={{0,12},{4,16},{8,20},{12,24},{16,28},{1,13},{5,17},{9,21},{13,25},... | collective-permute-start | bytes 98312 | tf_op jit(solution)/shard_map/ppermute | solution.py:33
  134.8 1.3 collective-permute-start.21
  136.1 3.1 %collective-permute-start.20 = (f32[16,512]{1,0:T(8,128)S(1)}, f32[16,512]{1,0:T(8,128)S(1)}, u32[]{:S(2)}, u32[]{:S(2)}) collective-permute-start(f32[16,512]{1,0:T(8,128)S(1)} %bitcast_multiply_fusion), channel_id=1, source_target_pairs={{0,4},{4,8},{8,12},{12,16},{16,20},{20,24},{24,28},{1,5},{5,9},{9,... | collective-permute-start | bytes 98312 | tf_op jit(solution)/shard_map/ppermute | solution.py:33
  139.3 2.0 %collective-permute-start.34 = (bf16[128,1024]{1,0:T(8,128)(2,1)S(1)}, bf16[128,1024]{1,0:T(8,128)(2,1)S(1)}, u32[]{:S(2)}, u32[]{:S(2)}) collective-permute-start(bf16[128,1024]{1,0:T(8,128)(2,1)S(1)} %collective-permute-done.32), channel_id=1, source_target_pairs={{8,0},{16,8},{24,16},{28,24},{20,28},{12,20},{4,12},{0,4},{9,1},{1... | collective-permute-start | bytes 786440 | tf_op jit(solution)/shard_map/ppermute | solution.py:117
  141.4 1.0 multiply_reduce_fusion
  142.8 7.2 %all_gather.3 = bf16[128,2048]{1,0:T(8,128)(2,1)S(1)} all-gather(bf16[128,512]{1,0:T(8,128)(2,1)S(1)} %multiply_convert_fusion), channel_id=1, replica_groups=mesh['ctx'=8,'tp'=4] {'tp'}, dimensions={1}, use_global_device_ids=true | all-gather | bytes 655360 | tf_op jit(solution)/shard_map/all_gather | solution.py:131
  150.0 1.4 convolution_convert_fusion
  (112 shorter events, 14.4 us)
Async XLA Ops:
  0.0 9.7 %copy-start.10 = (s32[8]{0:T(128)S(1)}, s32[8]{0:T(128)}, u32[]{:S(2)}) copy-start(s32[8]{0:T(128)} %constant.275.clone) | copy-start | bytes 100
  0.0 21.0 %copy-start.4 = (s32[8]{0:T(128)S(1)}, s32[8]{0:T(128)}, u32[]{:S(2)}) copy-start(s32[8]{0:T(128)} %constant.276.clone) | copy-start | bytes 100
  0.0 40.7 %copy-start.1 = (bf16[512,512]{1,0:T(8,128)(2,1)S(1)}, bf16[512,512]{1,0:T(8,128)(2,1)}, u32[]{:S(2)}) copy-start(bf16[512,512]{1,0:T(8,128)(2,1)} %param.15) | copy-start | bytes 1572868
  0.0 40.7 %copy-start.2 = (bf16[512,512]{1,0:T(8,128)(2,1)S(1)}, bf16[512,512]{1,0:T(8,128)(2,1)}, u32[]{:S(2)}) copy-start(bf16[512,512]{1,0:T(8,128)(2,1)} %param.14) | copy-start | bytes 1572868
  0.0 41.9 %copy-start.6 = (f32[3,512]{1,0:T(4,128)S(1)}, f32[3,512]{1,0:T(4,128)}, u32[]{:S(2)}) copy-start(f32[3,512]{1,0:T(4,128)} %param.19) | copy-start | bytes 18436
  0.0 41.9 %copy-start.7 = (f32[3,512]{1,0:T(4,128)S(1)}, f32[3,512]{1,0:T(4,128)}, u32[]{:S(2)}) copy-start(f32[3,512]{1,0:T(4,128)} %param.18) | copy-start | bytes 18436
  0.0 41.9 %copy-start.8 = (f32[3,512]{1,0:T(4,128)S(1)}, f32[3,512]{1,0:T(4,128)}, u32[]{:S(2)}) copy-start(f32[3,512]{1,0:T(4,128)} %param.17) | copy-start | bytes 18436
  0.0 42.0 %copy-start = (bf16[256,1024]{1,0:T(8,128)(2,1)S(1)}, bf16[256,1024]{1,0:T(8,128)(2,1)}, u32[]{:S(2)}) copy-start(bf16[256,1024]{1,0:T(8,128)(2,1)} %param.23) | copy-start | bytes 1572868
  2.4 39.6 %all-to-all-start = ((bf16[8,128,512]{1,2,0:T(8,128)(2,1)}), bf16[8,128,512]{1,2,0:T(8,128)(2,1)}, u32[]{:S(2)}, u32[]{:S(2)}) async-start(bf16[8,128,512]{1,2,0:T(8,128)(2,1)} %bitcast.2), calls=%async_computation | async-start | bytes 2097152 | tf_op jit(solution)/shard_map/all_to_all | solution.py:66
  46.1 8.1 %collective-permute-start = (bf16[130,768]{1,0:T(8,128)(2,1)S(1)}, bf16[130,768]{1,0:T(8,128)(2,1)S(1)}, u32[]{:S(2)}, u32[]{:S(2)}) collective-permute-start(bf16[130,768]{1,0:T(8,128)(2,1)S(1)} %convolution_convert_fusion.2), channel_id=1, source_target_pairs={{0,8},{8,16},{16,24},{24,28},{28,20},{20,12},{12,4},{4,0},{1,9},{9... | collective-permute-start | bytes 599048 | tf_op jit(solution)/shard_map/ppermute | solution.py:107
  48.2 8.1 %collective-permute-start.1 = (bf16[130,768]{1,0:T(8,128)(2,1)S(1)}, bf16[130,768]{1,0:T(8,128)(2,1)S(1)}, u32[]{:S(2)}, u32[]{:S(2)}) collective-permute-start(bf16[130,768]{1,0:T(8,128)(2,1)S(1)} %convolution_convert_fusion.1), channel_id=1, source_target_pairs={{8,0},{16,8},{24,16},{28,24},{20,28},{12,20},{4,12},{0,4},{9,1},{1... | collective-permute-start | bytes 599048 | tf_op jit(solution)/shard_map/ppermute | solution.py:108
  48.2 10.2 %collective-permute-start.2 = (bf16[128,1024]{1,0:T(8,128)(2,1)S(1)}, bf16[128,1024]{1,0:T(8,128)(2,1)S(1)}, u32[]{:S(2)}, u32[]{:S(2)}) collective-permute-start(bf16[128,1024]{1,0:T(8,128)(2,1)S(1)} %get-tuple-element.29), channel_id=1, source_target_pairs={{0,8},{8,16},{16,24},{24,28},{28,20},{20,12},{12,4},{4,0},{1,9},{9... | collective-permute-start | bytes 786440 | tf_op jit(solution)/shard_map/ppermute | solution.py:107
  50.2 9.7 %collective-permute-start.3 = (bf16[128,1024]{1,0:T(8,128)(2,1)S(1)}, bf16[128,1024]{1,0:T(8,128)(2,1)S(1)}, u32[]{:S(2)}, u32[]{:S(2)}) collective-permute-start(bf16[128,1024]{1,0:T(8,128)(2,1)S(1)} %get-tuple-element.30), channel_id=1, source_target_pairs={{8,0},{16,8},{24,16},{28,24},{20,28},{12,20},{4,12},{0,4},{9,1},{1... | collective-permute-start | bytes 786440 | tf_op jit(solution)/shard_map/ppermute | solution.py:108
  59.8 7.9 %collective-permute-start.4 = (bf16[130,768]{1,0:T(8,128)(2,1)S(1)}, bf16[130,768]{1,0:T(8,128)(2,1)S(1)}, u32[]{:S(2)}, u32[]{:S(2)}) collective-permute-start(bf16[130,768]{1,0:T(8,128)(2,1)S(1)} %add_convert_fusion.13), channel_id=1, source_target_pairs={{0,8},{8,16},{16,24},{24,28},{28,20},{20,12},{12,4},{4,0},{1,9},{9... | collective-permute-start | bytes 599048 | tf_op jit(solution)/shard_map/ppermute | solution.py:107
  61.3 7.7 %collective-permute-start.5 = (bf16[130,768]{1,0:T(8,128)(2,1)S(1)}, bf16[130,768]{1,0:T(8,128)(2,1)S(1)}, u32[]{:S(2)}, u32[]{:S(2)}) collective-permute-start(bf16[130,768]{1,0:T(8,128)(2,1)S(1)} %add_convert_fusion.12), channel_id=1, source_target_pairs={{8,0},{16,8},{24,16},{28,24},{20,28},{12,20},{4,12},{0,4},{9,1},{1... | collective-permute-start | bytes 599048 | tf_op jit(solution)/shard_map/ppermute | solution.py:108
  61.9 8.7 %collective-permute-start.6 = (bf16[128,1024]{1,0:T(8,128)(2,1)S(1)}, bf16[128,1024]{1,0:T(8,128)(2,1)S(1)}, u32[]{:S(2)}, u32[]{:S(2)}) collective-permute-start(bf16[128,1024]{1,0:T(8,128)(2,1)S(1)} %collective-permute-done.2), channel_id=1, source_target_pairs={{0,8},{8,16},{16,24},{24,28},{28,20},{20,12},{12,4},{4,0},{1,9},{9... | collective-permute-start | bytes 786440 | tf_op jit(solution)/shard_map/ppermute | solution.py:107
  63.3 8.5 %collective-permute-start.7 = (bf16[128,1024]{1,0:T(8,128)(2,1)S(1)}, bf16[128,1024]{1,0:T(8,128)(2,1)S(1)}, u32[]{:S(2)}, u32[]{:S(2)}) collective-permute-start(bf16[128,1024]{1,0:T(8,128)(2,1)S(1)} %collective-permute-done.3), channel_id=1, source_target_pairs={{8,0},{16,8},{24,16},{28,24},{20,28},{12,20},{4,12},{0,4},{9,1},{1... | collective-permute-start | bytes 786440 | tf_op jit(solution)/shard_map/ppermute | solution.py:108
  71.8 6.8 %collective-permute-start.8 = (bf16[130,768]{1,0:T(8,128)(2,1)S(1)}, bf16[130,768]{1,0:T(8,128)(2,1)S(1)}, u32[]{:S(2)}, u32[]{:S(2)}) collective-permute-start(bf16[130,768]{1,0:T(8,128)(2,1)S(1)} %add_convert_fusion.11), channel_id=1, source_target_pairs={{0,8},{8,16},{16,24},{24,28},{28,20},{20,12},{12,4},{4,0},{1,9},{9... | collective-permute-start | bytes 599048 | tf_op jit(solution)/shard_map/ppermute | solution.py:107
  73.2 6.5 %collective-permute-start.9 = (bf16[130,768]{1,0:T(8,128)(2,1)S(1)}, bf16[130,768]{1,0:T(8,128)(2,1)S(1)}, u32[]{:S(2)}, u32[]{:S(2)}) collective-permute-start(bf16[130,768]{1,0:T(8,128)(2,1)S(1)} %add_convert_fusion.10), channel_id=1, source_target_pairs={{8,0},{16,8},{24,16},{28,24},{20,28},{12,20},{4,12},{0,4},{9,1},{1... | collective-permute-start | bytes 599048 | tf_op jit(solution)/shard_map/ppermute | solution.py:108
  73.8 7.7 %collective-permute-start.10 = (bf16[128,1024]{1,0:T(8,128)(2,1)S(1)}, bf16[128,1024]{1,0:T(8,128)(2,1)S(1)}, u32[]{:S(2)}, u32[]{:S(2)}) collective-permute-start(bf16[128,1024]{1,0:T(8,128)(2,1)S(1)} %collective-permute-done.6), channel_id=1, source_target_pairs={{0,8},{8,16},{16,24},{24,28},{28,20},{20,12},{12,4},{4,0},{1,9},{9... | collective-permute-start | bytes 786440 | tf_op jit(solution)/shard_map/ppermute | solution.py:107
  75.3 8.9 %collective-permute-start.11 = (bf16[128,1024]{1,0:T(8,128)(2,1)S(1)}, bf16[128,1024]{1,0:T(8,128)(2,1)S(1)}, u32[]{:S(2)}, u32[]{:S(2)}) collective-permute-start(bf16[128,1024]{1,0:T(8,128)(2,1)S(1)} %collective-permute-done.7), channel_id=1, source_target_pairs={{8,0},{16,8},{24,16},{28,24},{20,28},{12,20},{4,12},{0,4},{9,1},{1... | collective-permute-start | bytes 786440 | tf_op jit(solution)/shard_map/ppermute | solution.py:108
  84.2 8.1 %collective-permute-start.16 = (bf16[130,768]{1,0:T(8,128)(2,1)S(1)}, bf16[130,768]{1,0:T(8,128)(2,1)S(1)}, u32[]{:S(2)}, u32[]{:S(2)}) collective-permute-start(bf16[130,768]{1,0:T(8,128)(2,1)S(1)} %add_convert_fusion.8), channel_id=1, source_target_pairs={{8,0},{16,8},{24,16},{28,24},{20,28},{12,20},{4,12},{0,4},{9,1},{1... | collective-permute-start | bytes 599048 | tf_op jit(solution)/shard_map/ppermute | solution.py:108
  84.8 8.2 %collective-permute-start.12 = (bf16[130,768]{1,0:T(8,128)(2,1)S(1)}, bf16[130,768]{1,0:T(8,128)(2,1)S(1)}, u32[]{:S(2)}, u32[]{:S(2)}) collective-permute-start(bf16[130,768]{1,0:T(8,128)(2,1)S(1)} %add_convert_fusion.9), channel_id=1, source_target_pairs={{0,8},{8,16},{16,24},{24,28},{28,20},{20,12},{12,4},{4,0},{1,9},{9... | collective-permute-start | bytes 599048 | tf_op jit(solution)/shard_map/ppermute | solution.py:107
  86.2 12.1 %collective-permute-start.27 = (bf16[128,1024]{1,0:T(8,128)(2,1)S(1)}, bf16[128,1024]{1,0:T(8,128)(2,1)S(1)}, u32[]{:S(2)}, u32[]{:S(2)}) collective-permute-start(bf16[128,1024]{1,0:T(8,128)(2,1)S(1)} %collective-permute-done.10), channel_id=1, source_target_pairs={{0,8},{8,16},{16,24},{24,28},{28,20},{20,12},{12,4},{4,0},{1,9},{9... | collective-permute-start | bytes 786440 | tf_op jit(solution)/shard_map/ppermute | solution.py:107
  87.9 12.0 %collective-permute-start.28 = (bf16[128,1024]{1,0:T(8,128)(2,1)S(1)}, bf16[128,1024]{1,0:T(8,128)(2,1)S(1)}, u32[]{:S(2)}, u32[]{:S(2)}) collective-permute-start(bf16[128,1024]{1,0:T(8,128)(2,1)S(1)} %collective-permute-done.11), channel_id=1, source_target_pairs={{8,0},{16,8},{24,16},{28,24},{20,28},{12,20},{4,12},{0,4},{9,1},{1... | collective-permute-start | bytes 786440 | tf_op jit(solution)/shard_map/ppermute | solution.py:108
  92.3 10.0 %collective-permute-start.17 = (bf16[130,768]{1,0:T(8,128)(2,1)S(1)}, bf16[130,768]{1,0:T(8,128)(2,1)S(1)}, u32[]{:S(2)}, u32[]{:S(2)}) collective-permute-start(bf16[130,768]{1,0:T(8,128)(2,1)S(1)} %add_convert_fusion.3), channel_id=1, source_target_pairs={{8,0},{16,8},{24,16},{28,24},{20,28},{12,20},{4,12},{0,4},{9,1},{1... | collective-permute-start | bytes 599048 | tf_op jit(solution)/shard_map/ppermute | solution.py:112
  93.0 10.0 %collective-permute-start.13 = (bf16[130,768]{1,0:T(8,128)(2,1)S(1)}, bf16[130,768]{1,0:T(8,128)(2,1)S(1)}, u32[]{:S(2)}, u32[]{:S(2)}) collective-permute-start(bf16[130,768]{1,0:T(8,128)(2,1)S(1)} %add_convert_fusion.7), channel_id=1, source_target_pairs={{0,8},{8,16},{16,24},{24,28},{28,20},{20,12},{12,4},{4,0},{1,9},{9... | collective-permute-start | bytes 599048 | tf_op jit(solution)/shard_map/ppermute | solution.py:111
  98.4 10.1 %collective-permute-start.29 = (bf16[128,1024]{1,0:T(8,128)(2,1)S(1)}, bf16[128,1024]{1,0:T(8,128)(2,1)S(1)}, u32[]{:S(2)}, u32[]{:S(2)}) collective-permute-start(bf16[128,1024]{1,0:T(8,128)(2,1)S(1)} %collective-permute-done.27), channel_id=1, source_target_pairs={{0,8},{8,16},{16,24},{24,28},{28,20},{20,12},{12,4},{4,0},{1,9},{9... | collective-permute-start | bytes 786440 | tf_op jit(solution)/shard_map/ppermute | solution.py:116
  99.8 10.1 %collective-permute-start.30 = (bf16[128,1024]{1,0:T(8,128)(2,1)S(1)}, bf16[128,1024]{1,0:T(8,128)(2,1)S(1)}, u32[]{:S(2)}, u32[]{:S(2)}) collective-permute-start(bf16[128,1024]{1,0:T(8,128)(2,1)S(1)} %collective-permute-done.28), channel_id=1, source_target_pairs={{8,0},{16,8},{24,16},{28,24},{20,28},{12,20},{4,12},{0,4},{9,1},{1... | collective-permute-start | bytes 786440 | tf_op jit(solution)/shard_map/ppermute | solution.py:117
  102.4 16.9 %copy-start.3 = (f32[16,512]{1,0:T(8,128)S(1)}, f32[16,512]{1,0:T(8,128)}, u32[]{:S(2)}) copy-start(f32[16,512]{1,0:T(8,128)} %param.20) | copy-start | bytes 98308
  102.4 9.8 %collective-permute-start.18 = (bf16[130,768]{1,0:T(8,128)(2,1)S(1)}, bf16[130,768]{1,0:T(8,128)(2,1)S(1)}, u32[]{:S(2)}, u32[]{:S(2)}) collective-permute-start(bf16[130,768]{1,0:T(8,128)(2,1)S(1)} %add_convert_fusion.2), channel_id=1, source_target_pairs={{8,0},{16,8},{24,16},{28,24},{20,28},{12,20},{4,12},{0,4},{9,1},{1... | collective-permute-start | bytes 599048 | tf_op jit(solution)/shard_map/ppermute | solution.py:112
  103.1 9.8 %collective-permute-start.14 = (bf16[130,768]{1,0:T(8,128)(2,1)S(1)}, bf16[130,768]{1,0:T(8,128)(2,1)S(1)}, u32[]{:S(2)}, u32[]{:S(2)}) collective-permute-start(bf16[130,768]{1,0:T(8,128)(2,1)S(1)} %add_convert_fusion.6), channel_id=1, source_target_pairs={{0,8},{8,16},{16,24},{24,28},{28,20},{20,12},{12,4},{4,0},{1,9},{9... | collective-permute-start | bytes 599048 | tf_op jit(solution)/shard_map/ppermute | solution.py:111
  108.5 21.2 %collective-permute-start.31 = (bf16[128,1024]{1,0:T(8,128)(2,1)S(1)}, bf16[128,1024]{1,0:T(8,128)(2,1)S(1)}, u32[]{:S(2)}, u32[]{:S(2)}) collective-permute-start(bf16[128,1024]{1,0:T(8,128)(2,1)S(1)} %collective-permute-done.29), channel_id=1, source_target_pairs={{0,8},{8,16},{16,24},{24,28},{28,20},{20,12},{12,4},{4,0},{1,9},{9... | collective-permute-start | bytes 786440 | tf_op jit(solution)/shard_map/ppermute | solution.py:116
  109.9 22.4 %collective-permute-start.32 = (bf16[128,1024]{1,0:T(8,128)(2,1)S(1)}, bf16[128,1024]{1,0:T(8,128)(2,1)S(1)}, u32[]{:S(2)}, u32[]{:S(2)}) collective-permute-start(bf16[128,1024]{1,0:T(8,128)(2,1)S(1)} %collective-permute-done.30), channel_id=1, source_target_pairs={{8,0},{16,8},{24,16},{28,24},{20,28},{12,20},{4,12},{0,4},{9,1},{1... | collective-permute-start | bytes 786440 | tf_op jit(solution)/shard_map/ppermute | solution.py:117
  112.3 6.3 %collective-permute-start.19 = (bf16[130,768]{1,0:T(8,128)(2,1)S(1)}, bf16[130,768]{1,0:T(8,128)(2,1)S(1)}, u32[]{:S(2)}, u32[]{:S(2)}) collective-permute-start(bf16[130,768]{1,0:T(8,128)(2,1)S(1)} %add_convert_fusion.1), channel_id=1, source_target_pairs={{8,0},{16,8},{24,16},{28,24},{20,28},{12,20},{4,12},{0,4},{9,1},{1... | collective-permute-start | bytes 599048 | tf_op jit(solution)/shard_map/ppermute | solution.py:112
  113.0 6.0 %collective-permute-start.15 = (bf16[130,768]{1,0:T(8,128)(2,1)S(1)}, bf16[130,768]{1,0:T(8,128)(2,1)S(1)}, u32[]{:S(2)}, u32[]{:S(2)}) collective-permute-start(bf16[130,768]{1,0:T(8,128)(2,1)S(1)} %add_convert_fusion.5), channel_id=1, source_target_pairs={{0,8},{8,16},{16,24},{24,28},{28,20},{20,12},{12,4},{4,0},{1,9},{9... | collective-permute-start | bytes 599048 | tf_op jit(solution)/shard_map/ppermute | solution.py:111
  119.0 22.3 %copy-start.5 = (f32[16,512]{1,0:T(8,128)S(1)}, f32[16,512]{1,0:T(8,128)}, u32[]{:S(2)}) copy-start(f32[16,512]{1,0:T(8,128)} %param.21) | copy-start | bytes 98308
  123.7 18.7 %copy-start.9 = (f32[512]{0:T(512)S(1)}, f32[512]{0:T(512)}, u32[]{:S(2)}) copy-start(f32[512]{0:T(512)} %param.22) | copy-start | bytes 6148
  123.8 11.0 %collective-permute-start.26 = (f32[16,512]{1,0:T(8,128)S(1)}, f32[16,512]{1,0:T(8,128)S(1)}, u32[]{:S(2)}, u32[]{:S(2)}) collective-permute-start(f32[16,512]{1,0:T(8,128)S(1)} %bitcast_multiply_fusion), channel_id=1, source_target_pairs={{0,28},{1,29},{2,30},{3,31}} | collective-permute-start | bytes 98312 | tf_op jit(solution)/shard_map/ppermute | solution.py:33
  128.3 7.7 %collective-permute-start.25 = (f32[16,512]{1,0:T(8,128)S(1)}, f32[16,512]{1,0:T(8,128)S(1)}, u32[]{:S(2)}, u32[]{:S(2)}) collective-permute-start(f32[16,512]{1,0:T(8,128)S(1)} %bitcast_multiply_fusion), channel_id=1, source_target_pairs={{0,24},{4,28},{1,25},{5,29},{2,26},{6,30},{3,27},{7,31}} | collective-permute-start | bytes 98312 | tf_op jit(solution)/shard_map/ppermute | solution.py:33
  129.7 9.6 %collective-permute-start.24 = (f32[16,512]{1,0:T(8,128)S(1)}, f32[16,512]{1,0:T(8,128)S(1)}, u32[]{:S(2)}, u32[]{:S(2)}) collective-permute-start(f32[16,512]{1,0:T(8,128)S(1)} %bitcast_multiply_fusion), channel_id=1, source_target_pairs={{0,20},{4,24},{8,28},{1,21},{5,25},{9,29},{2,22},{6,26},{10,30},{3... | collective-permute-start | bytes 98312 | tf_op jit(solution)/shard_map/ppermute | solution.py:33
  131.0 8.3 %collective-permute-start.23 = (f32[16,512]{1,0:T(8,128)S(1)}, f32[16,512]{1,0:T(8,128)S(1)}, u32[]{:S(2)}, u32[]{:S(2)}) collective-permute-start(f32[16,512]{1,0:T(8,128)S(1)} %bitcast_multiply_fusion), channel_id=1, source_target_pairs={{0,16},{4,20},{8,24},{12,28},{1,17},{5,21},{9,25},{13,29},{2,18},{... | collective-permute-start | bytes 98312 | tf_op jit(solution)/shard_map/ppermute | solution.py:33
  132.3 9.0 %collective-permute-start.22 = (f32[16,512]{1,0:T(8,128)S(1)}, f32[16,512]{1,0:T(8,128)S(1)}, u32[]{:S(2)}, u32[]{:S(2)}) collective-permute-start(f32[16,512]{1,0:T(8,128)S(1)} %bitcast_multiply_fusion), channel_id=1, source_target_pairs={{0,12},{4,16},{8,20},{12,24},{16,28},{1,13},{5,17},{9,21},{13,25},... | collective-permute-start | bytes 98312 | tf_op jit(solution)/shard_map/ppermute | solution.py:33
  134.8 6.5 %collective-permute-start.21 = (f32[16,512]{1,0:T(8,128)S(1)}, f32[16,512]{1,0:T(8,128)S(1)}, u32[]{:S(2)}, u32[]{:S(2)}) collective-permute-start(f32[16,512]{1,0:T(8,128)S(1)} %bitcast_multiply_fusion), channel_id=1, source_target_pairs={{0,8},{4,12},{8,16},{12,20},{16,24},{20,28},{1,9},{5,13},{9,17},{1... | collective-permute-start | bytes 98312 | tf_op jit(solution)/shard_map/ppermute | solution.py:33
  136.1 5.2 %collective-permute-start.20 = (f32[16,512]{1,0:T(8,128)S(1)}, f32[16,512]{1,0:T(8,128)S(1)}, u32[]{:S(2)}, u32[]{:S(2)}) collective-permute-start(f32[16,512]{1,0:T(8,128)S(1)} %bitcast_multiply_fusion), channel_id=1, source_target_pairs={{0,4},{4,8},{8,12},{12,16},{16,20},{20,24},{24,28},{1,5},{5,9},{9,... | collective-permute-start | bytes 98312 | tf_op jit(solution)/shard_map/ppermute | solution.py:33
  139.2 10.7 %collective-permute-start.33 = (bf16[128,1024]{1,0:T(8,128)(2,1)S(1)}, bf16[128,1024]{1,0:T(8,128)(2,1)S(1)}, u32[]{:S(2)}, u32[]{:S(2)}) collective-permute-start(bf16[128,1024]{1,0:T(8,128)(2,1)S(1)} %collective-permute-done.31), channel_id=1, source_target_pairs={{0,8},{8,16},{16,24},{24,28},{28,20},{20,12},{12,4},{4,0},{1,9},{9... | collective-permute-start | bytes 786440 | tf_op jit(solution)/shard_map/ppermute | solution.py:116
  139.3 10.6 %collective-permute-start.34 = (bf16[128,1024]{1,0:T(8,128)(2,1)S(1)}, bf16[128,1024]{1,0:T(8,128)(2,1)S(1)}, u32[]{:S(2)}, u32[]{:S(2)}) collective-permute-start(bf16[128,1024]{1,0:T(8,128)(2,1)S(1)} %collective-permute-done.32), channel_id=1, source_target_pairs={{8,0},{16,8},{24,16},{28,24},{20,28},{12,20},{4,12},{0,4},{9,1},{1... | collective-permute-start | bytes 786440 | tf_op jit(solution)/shard_map/ppermute | solution.py:117

commit v13 on v12

--- a/solution.py
+++ b/solution.py
@@ -28,12 +28,16 @@
         preferred_element_type=jnp.float32,
     )
     end_state = running[:, length - 1] * jnp.exp(-rates * (length - 1))
-    carried = jnp.zeros_like(end_state)
-    for shift in range(1, ctx_count):
-        earlier = lax.ppermute(
-            end_state, "ctx", perm=[(i, i + shift) for i in range(ctx_count - shift)]
-        )
-        carried = carried + jnp.exp(-rates * (length * (shift - 1))) * earlier
+    me = lax.axis_index("ctx")
+    later = jnp.arange(ctx_count, dtype=jnp.int32)
+    gap = jnp.maximum(later - 1 - me, 0).astype(jnp.float32)
+    sendable = jnp.where(
+        (later > me)[:, None, None],
+        jnp.exp(-rates[None] * (gap[:, None, None] * length)) * end_state[None],
+        0.0,
+    )
+    received = lax.all_to_all(sendable, "ctx", split_axis=0, concat_axis=0, tiled=True)
+    carried = jnp.sum(received, axis=0)
     carried = carried * jnp.exp(-rates)
     total = running + carried[:, None, :]
     mixed = jnp.sum((coefs[:, None, :] * decay) * total, axis=0)

time: 152 us -> 153 us (level)
  starting transfers between devices: 51.6 us -> 40 us
  waiting for transfers between devices: 42.2 us -> 48.3 us
  local copies, waits for them, and re-layouts: 6.51 us -> 9.91 us
  other arithmetic: 3.36 us -> 6.48 us
    ppermute x7 -> x0, starting transfers between devices: 15.3 us -> none  [modal_long_conv(): lax.ppermute(end_state, 'ctx', perm=[(i, i + shift) for i in range(ctx_co...]
    all_to_all x0 -> x1, waiting for transfers between devices: none -> 6.75 us  [modal_long_conv(): lax.all_to_all(sendable, 'ctx', split_axis=0, concat_axis=0, tiled=True)]
    all_to_all x0 -> x1, starting transfers between devices: none -> 3.89 us  [modal_long_conv(): lax.all_to_all(sendable, 'ctx', split_axis=0, concat_axis=0, tiled=True)]
    ppermute x3, waiting for transfers between devices: 7.5 us -> 4.68 us  [body(): down = lax.ppermute(down.astype(jnp.bfloat16), 'ctx', perm=bwd)]
    ppermute x3, waiting for transfers between devices: 3.84 us -> 6.3 us  [body(): w_up = lax.ppermute(w_up, 'ctx', perm=fwd)]
    reduce_sum x1, other arithmetic: 1.04 us -> 3.38 us  [modal_long_conv(): mixed = jnp.sum(coefs[:, None, :] * decay * total, axis=0)]
    unnamed x23 -> x29, local copies, waits for them, and re-layouts: 2.43 us -> 4.41 us
  transfers between devices with their start and end apart: 36 -> 30, of which waited for: 19 -> 20; matrix products, arithmetic and copies ran while one was open for 8% -> 9% of each run, Pallas kernels for 0% -> 0%
where the time goes in v13:
time: 153 us; the launch traced here: 152 us
  waiting for transfers between devices  48.3 us (32%)
  starting transfers between devices  40 us (26%)
  between operations  30 us (20%)
  matrix products  10.3 us (7%)
  local copies, waits for them, and re-layouts  9.91 us (6%)
  blocking collectives  7.22 us (5%)
  other arithmetic  6.48 us (4%)
    ppermute x8, waiting for transfers between devices, body(): up, w_up = lax.ppermute((sent[0], sent[2]), 'ctx', perm=fwd)  17.2 us
    ppermute x8, waiting for transfers between devices, body(): down, w_low = lax.ppermute((sent[1], sent[3]), 'ctx', perm=bwd)  13.3 us
    ppermute x8, starting transfers between devices, body(): up, w_up = lax.ppermute((sent[0], sent[2]), 'ctx', perm=fwd)  13 us
    all_to_all x1, starting transfers between devices, body(): lax.all_to_all(by_dest, 'ctx', split_axis=0, concat_axis=0, tiled=True)  7.29 us
    all_gather x1, blocking collectives, body(): features = lax.all_gather(gated, 'tp', axis=1, tiled=True)  7.22 us
    all_to_all x1, waiting for transfers between devices, modal_long_conv(): lax.all_to_all(sendable, 'ctx', split_axis=0, concat_axis=0, tiled=True)  6.75 us
    ppermute x3, waiting for transfers between devices, body(): w_up = lax.ppermute(w_up, 'ctx', perm=fwd)  6.3 us
    ppermute x3, waiting for transfers between devices, body(): down = lax.ppermute(down.astype(jnp.bfloat16), 'ctx', perm=bwd)  4.68 us
  transfers between devices with their start and end apart: 30, of which 20 were waited for; matrix products, arithmetic and copies ran while one was open for 9% of the time, Pallas kernels for 0%

profile of v13, /device:TPU:0, one launch (start us, length us, event | category | flops | bytes accessed | tf_op | source)
XLA Modules:
  0.0 152.1 jit_solution(7547062746911637737)
XLA Ops:
  0.0 2.4 %copy.16 = bf16[128,4096]{0,1:T(8,128)(2,1)} copy(bf16[128,4096]{1,0:T(8,128)(2,1)} %param.13) | data formatting | bytes 2097152 | tf_op args[0]
  2.4 7.3 %all-to-all-start = ((bf16[8,128,512]{1,2,0:T(8,128)(2,1)}), bf16[8,128,512]{1,2,0:T(8,128)(2,1)}, u32[]{:S(2)}, u32[]{:S(2)}) async-start(bf16[8,128,512]{1,2,0:T(8,128)(2,1)} %bitcast.2), calls=%async_computation | async-start | bytes 2097152 | tf_op jit(solution)/shard_map/all_to_all | solution.py:70
  21.0 0.8 fusion.73
  40.6 1.1 pad_maximum_fusion.1
  41.9 1.5 copy.17
  45.9 2.1 %collective-permute-start = (bf16[130,768]{1,0:T(8,128)(2,1)S(1)}, bf16[130,768]{1,0:T(8,128)(2,1)S(1)}, u32[]{:S(2)}, u32[]{:S(2)}) collective-permute-start(bf16[130,768]{1,0:T(8,128)(2,1)S(1)} %convolution_convert_fusion.2), channel_id=1, source_target_pairs={{0,8},{8,16},{16,24},{24,28},{28,20},{20,12},{12,4},{4,0},{1,9},{9... | collective-permute-start | bytes 599048 | tf_op jit(solution)/shard_map/ppermute | solution.py:111
  48.0 2.0 %collective-permute-start.2 = (bf16[128,1024]{1,0:T(8,128)(2,1)S(1)}, bf16[128,1024]{1,0:T(8,128)(2,1)S(1)}, u32[]{:S(2)}, u32[]{:S(2)}) collective-permute-start(bf16[128,1024]{1,0:T(8,128)(2,1)S(1)} %get-tuple-element.29), channel_id=1, source_target_pairs={{0,8},{8,16},{16,24},{24,28},{28,20},{20,12},{12,4},{4,0},{1,9},{9... | collective-permute-start | bytes 786440 | tf_op jit(solution)/shard_map/ppermute | solution.py:111
  52.4 1.7 %collective-permute-done = bf16[130,768]{1,0:T(8,128)(2,1)S(1)} collective-permute-done((bf16[130,768]{1,0:T(8,128)(2,1)S(1)}, bf16[130,768]{1,0:T(8,128)(2,1)S(1)}, u32[]{:S(2)}, u32[]{:S(2)}) %collective-permute-start) | collective-permute-done | bytes 199712 | tf_op jit(solution)/shard_map/ppermute | solution.py:111
  54.3 1.7 %collective-permute-done.1 = bf16[130,768]{1,0:T(8,128)(2,1)S(1)} collective-permute-done((bf16[130,768]{1,0:T(8,128)(2,1)S(1)}, bf16[130,768]{1,0:T(8,128)(2,1)S(1)}, u32[]{:S(2)}, u32[]{:S(2)}) %collective-permute-start.1) | collective-permute-done | bytes 199712 | tf_op jit(solution)/shard_map/ppermute | solution.py:112
  56.4 1.8 %collective-permute-done.2 = bf16[128,1024]{1,0:T(8,128)(2,1)S(1)} collective-permute-done((bf16[128,1024]{1,0:T(8,128)(2,1)S(1)}, bf16[128,1024]{1,0:T(8,128)(2,1)S(1)}, u32[]{:S(2)}, u32[]{:S(2)}) %collective-permute-start.2) | collective-permute-done | bytes 262176 | tf_op jit(solution)/shard_map/ppermute | solution.py:111
  58.2 1.4 collective-permute-done.3
  59.6 1.5 collective-permute-start.4
  61.7 1.5 collective-permute-start.6
  63.8 3.8 %collective-permute-done.4 = bf16[130,768]{1,0:T(8,128)(2,1)S(1)} collective-permute-done((bf16[130,768]{1,0:T(8,128)(2,1)S(1)}, bf16[130,768]{1,0:T(8,128)(2,1)S(1)}, u32[]{:S(2)}, u32[]{:S(2)}) %collective-permute-start.4) | collective-permute-done | bytes 199712 | tf_op jit(solution)/shard_map/ppermute | solution.py:111
  67.6 1.1 collective-permute-done.5
  68.8 1.6 %collective-permute-done.6 = bf16[128,1024]{1,0:T(8,128)(2,1)S(1)} collective-permute-done((bf16[128,1024]{1,0:T(8,128)(2,1)S(1)}, bf16[128,1024]{1,0:T(8,128)(2,1)S(1)}, u32[]{:S(2)}, u32[]{:S(2)}) %collective-permute-start.6) | collective-permute-done | bytes 262176 | tf_op jit(solution)/shard_map/ppermute | solution.py:111
  70.4 1.2 collective-permute-done.7
  71.6 1.5 collective-permute-start.8
  73.6 1.5 collective-permute-start.10
  75.7 2.6 %collective-permute-done.8 = bf16[130,768]{1,0:T(8,128)(2,1)S(1)} collective-permute-done((bf16[130,768]{1,0:T(8,128)(2,1)S(1)}, bf16[130,768]{1,0:T(8,128)(2,1)S(1)}, u32[]{:S(2)}, u32[]{:S(2)}) %collective-permute-start.8) | collective-permute-done | bytes 199712 | tf_op jit(solution)/shard_map/ppermute | solution.py:111
  78.4 1.1 collective-permute-done.9
  79.6 1.8 %collective-permute-done.10 = bf16[128,1024]{1,0:T(8,128)(2,1)S(1)} collective-permute-done((bf16[128,1024]{1,0:T(8,128)(2,1)S(1)}, bf16[128,1024]{1,0:T(8,128)(2,1)S(1)}, u32[]{:S(2)}, u32[]{:S(2)}) %collective-permute-start.10) | collective-permute-done | bytes 262176 | tf_op jit(solution)/shard_map/ppermute | solution.py:111
  81.4 2.6 %collective-permute-done.11 = bf16[128,1024]{1,0:T(8,128)(2,1)S(1)} collective-permute-done((bf16[128,1024]{1,0:T(8,128)(2,1)S(1)}, bf16[128,1024]{1,0:T(8,128)(2,1)S(1)}, u32[]{:S(2)}, u32[]{:S(2)}) %collective-permute-start.11) | collective-permute-done | bytes 262176 | tf_op jit(solution)/shard_map/ppermute | solution.py:112
  84.6 1.5 collective-permute-start.12
  86.0 1.6 %collective-permute-start.20 = (bf16[128,1024]{1,0:T(8,128)(2,1)S(1)}, bf16[128,1024]{1,0:T(8,128)(2,1)S(1)}, u32[]{:S(2)}, u32[]{:S(2)}) collective-permute-start(bf16[128,1024]{1,0:T(8,128)(2,1)S(1)} %collective-permute-done.10), channel_id=1, source_target_pairs={{0,8},{8,16},{16,24},{24,28},{28,20},{20,12},{12,4},{4,0},{1,9},{9... | collective-permute-start | bytes 786440 | tf_op jit(solution)/shard_map/ppermute | solution.py:111
  88.1 4.0 %collective-permute-done.16 = bf16[130,768]{1,0:T(8,128)(2,1)S(1)} collective-permute-done((bf16[130,768]{1,0:T(8,128)(2,1)S(1)}, bf16[130,768]{1,0:T(8,128)(2,1)S(1)}, u32[]{:S(2)}, u32[]{:S(2)}) %collective-permute-start.16) | collective-permute-done | bytes 199712 | tf_op jit(solution)/shard_map/ppermute | solution.py:112
  92.2 0.6 collective-permute-start.17
  92.8 1.5 collective-permute-start.13
  94.3 3.8 %collective-permute-done.20 = bf16[128,1024]{1,0:T(8,128)(2,1)S(1)} collective-permute-done((bf16[128,1024]{1,0:T(8,128)(2,1)S(1)}, bf16[128,1024]{1,0:T(8,128)(2,1)S(1)}, u32[]{:S(2)}, u32[]{:S(2)}) %collective-permute-start.20) | collective-permute-done | bytes 262176 | tf_op jit(solution)/shard_map/ppermute | solution.py:111
  98.2 1.5 collective-permute-start.22
  100.3 1.9 %collective-permute-done.17 = bf16[130,768]{1,0:T(8,128)(2,1)S(1)} collective-permute-done((bf16[130,768]{1,0:T(8,128)(2,1)S(1)}, bf16[130,768]{1,0:T(8,128)(2,1)S(1)}, u32[]{:S(2)}, u32[]{:S(2)}) %collective-permute-start.17) | collective-permute-done | bytes 199712 | tf_op jit(solution)/shard_map/ppermute | solution.py:116
  102.9 1.5 collective-permute-start.14
  104.4 3.8 %collective-permute-done.22 = bf16[128,1024]{1,0:T(8,128)(2,1)S(1)} collective-permute-done((bf16[128,1024]{1,0:T(8,128)(2,1)S(1)}, bf16[128,1024]{1,0:T(8,128)(2,1)S(1)}, u32[]{:S(2)}, u32[]{:S(2)}) %collective-permute-start.22) | collective-permute-done | bytes 262176 | tf_op jit(solution)/shard_map/ppermute | solution.py:120
  108.3 1.5 collective-permute-start.24
  110.4 2.7 %collective-permute-done.18 = bf16[130,768]{1,0:T(8,128)(2,1)S(1)} collective-permute-done((bf16[130,768]{1,0:T(8,128)(2,1)S(1)}, bf16[130,768]{1,0:T(8,128)(2,1)S(1)}, u32[]{:S(2)}, u32[]{:S(2)}) %collective-permute-start.18) | collective-permute-done | bytes 199712 | tf_op jit(solution)/shard_map/ppermute | solution.py:116
  113.8 1.5 collective-permute-start.15
  115.3 2.5 %collective-permute-done.24 = bf16[128,1024]{1,0:T(8,128)(2,1)S(1)} collective-permute-done((bf16[128,1024]{1,0:T(8,128)(2,1)S(1)}, bf16[128,1024]{1,0:T(8,128)(2,1)S(1)}, u32[]{:S(2)}, u32[]{:S(2)}) %collective-permute-start.24) | collective-permute-done | bytes 262176 | tf_op jit(solution)/shard_map/ppermute | solution.py:120
  117.8 1.5 collective-permute-start.26
  120.3 4.4 %fusion = f32[16,128,512]{2,1,0:T(8,128)S(1)} fusion(f32[128,512]{1,0:T(8,128)S(1)} %fusion.51, f32[16,512]{1,0:T(8,128)S(1)} %copy-done.6, f32[128,128]{1,0:T(8,128)S(1)} %fusion.52), kind=kOutput, calls=%fused_computation.1 | convolution fusion | flops 1612709888 | bytes 4554752 | tf_op jit(solution)/shard_map/dot_general | solution.py:23
  124.8 2.0 %copy-done = f32[16,128,512]{2,1,0:T(8,128)} copy-done((f32[16,128,512]{2,1,0:T(8,128)}, f32[16,128,512]{2,1,0:T(8,128)S(1)}, u32[]{:S(2)}) %copy-start) | copy-done | bytes 4194328
  126.8 0.8 multiply_select_fusion
  127.6 3.9 %all-to-all-start.1 = ((f32[8,16,512]{2,1,0:T(8,128)}), f32[8,16,512]{2,1,0:T(8,128)S(1)}, u32[]{:S(2)}, u32[]{:S(2)}) async-start(f32[8,16,512]{2,1,0:T(8,128)} %multiply_select_fusion), calls=%async_computation.1 | async-start | bytes 524288 | tf_op jit(solution)/shard_map/all_to_all | solution.py:39
  131.5 0.7 bitcast_dynamic-update-slice_fusion.1
  132.2 0.7 bitcast_dynamic-update-slice_fusion
  133.0 6.8 %all-to-all-done.1 = f32[8,16,512]{2,1,0:T(8,128)S(1)} async-done(((f32[8,16,512]{2,1,0:T(8,128)}), f32[8,16,512]{2,1,0:T(8,128)S(1)}, u32[]{:S(2)}, u32[]{:S(2)}) %all-to-all-start.1) | async-done | bytes 262176 | tf_op jit(solution)/shard_map/all_to_all | solution.py:39
  139.8 3.4 %multiply_reduce_fusion = f32[128,512]{1,0:T(8,128)S(1)} fusion(f32[16,128,512]{2,1,0:T(8,128)} %copy-done, f32[16,512]{1,0:T(8,128)S(1)} %exponential_multiply_fusion, f32[16,512]{1,0:T(8,128)S(1)} %get-tuple-element.49, f32[16,512]{1,0:T(8,128)S(1)} %get-tuple-element.47), kind=kLoop, calls=%fused_computation | loop fusion | flops 5177344 | bytes 4554752 | tf_op jit(solution)/shard_map/reduce_sum | solution.py:43
  143.5 7.2 %all_gather.3 = bf16[128,2048]{1,0:T(8,128)(2,1)S(1)} all-gather(bf16[128,512]{1,0:T(8,128)(2,1)S(1)} %multiply_convert_fusion), channel_id=1, replica_groups=mesh['ctx'=8,'tp'=4] {'tp'}, dimensions={1}, use_global_device_ids=true | all-gather | bytes 655360 | tf_op jit(solution)/shard_map/all_gather | solution.py:135
  150.7 1.4 convolution_convert_fusion
  (110 shorter events, 13.8 us)
Async XLA Ops:
  0.0 9.7 %copy-start.13 = (s32[8]{0:T(128)S(1)}, s32[8]{0:T(128)}, u32[]{:S(2)}) copy-start(s32[8]{0:T(128)} %constant.268.clone) | copy-start | bytes 100
  0.0 21.0 %copy-start.7 = (s32[8]{0:T(128)S(1)}, s32[8]{0:T(128)}, u32[]{:S(2)}) copy-start(s32[8]{0:T(128)} %constant.269.clone) | copy-start | bytes 100
  0.0 40.5 %copy-start.4 = (bf16[512,512]{1,0:T(8,128)(2,1)S(1)}, bf16[512,512]{1,0:T(8,128)(2,1)}, u32[]{:S(2)}) copy-start(bf16[512,512]{1,0:T(8,128)(2,1)} %param.15) | copy-start | bytes 1572868
  0.0 40.6 %copy-start.5 = (bf16[512,512]{1,0:T(8,128)(2,1)S(1)}, bf16[512,512]{1,0:T(8,128)(2,1)}, u32[]{:S(2)}) copy-start(bf16[512,512]{1,0:T(8,128)(2,1)} %param.14) | copy-start | bytes 1572868
  0.0 41.7 %copy-start.9 = (f32[3,512]{1,0:T(4,128)S(1)}, f32[3,512]{1,0:T(4,128)}, u32[]{:S(2)}) copy-start(f32[3,512]{1,0:T(4,128)} %param.19) | copy-start | bytes 18436
  0.0 41.7 %copy-start.10 = (f32[3,512]{1,0:T(4,128)S(1)}, f32[3,512]{1,0:T(4,128)}, u32[]{:S(2)}) copy-start(f32[3,512]{1,0:T(4,128)} %param.18) | copy-start | bytes 18436
  0.0 41.7 %copy-start.11 = (f32[3,512]{1,0:T(4,128)S(1)}, f32[3,512]{1,0:T(4,128)}, u32[]{:S(2)}) copy-start(f32[3,512]{1,0:T(4,128)} %param.17) | copy-start | bytes 18436
  0.0 41.8 %copy-start.3 = (bf16[256,1024]{1,0:T(8,128)(2,1)S(1)}, bf16[256,1024]{1,0:T(8,128)(2,1)}, u32[]{:S(2)}) copy-start(bf16[256,1024]{1,0:T(8,128)(2,1)} %param.23) | copy-start | bytes 1572868
  2.4 39.4 %all-to-all-start = ((bf16[8,128,512]{1,2,0:T(8,128)(2,1)}), bf16[8,128,512]{1,2,0:T(8,128)(2,1)}, u32[]{:S(2)}, u32[]{:S(2)}) async-start(bf16[8,128,512]{1,2,0:T(8,128)(2,1)} %bitcast.2), calls=%async_computation | async-start | bytes 2097152 | tf_op jit(solution)/shard_map/all_to_all | solution.py:70
  45.9 8.1 %collective-permute-start = (bf16[130,768]{1,0:T(8,128)(2,1)S(1)}, bf16[130,768]{1,0:T(8,128)(2,1)S(1)}, u32[]{:S(2)}, u32[]{:S(2)}) collective-permute-start(bf16[130,768]{1,0:T(8,128)(2,1)S(1)} %convolution_convert_fusion.2), channel_id=1, source_target_pairs={{0,8},{8,16},{16,24},{24,28},{28,20},{20,12},{12,4},{4,0},{1,9},{9... | collective-permute-start | bytes 599048 | tf_op jit(solution)/shard_map/ppermute | solution.py:111
  48.0 8.1 %collective-permute-start.1 = (bf16[130,768]{1,0:T(8,128)(2,1)S(1)}, bf16[130,768]{1,0:T(8,128)(2,1)S(1)}, u32[]{:S(2)}, u32[]{:S(2)}) collective-permute-start(bf16[130,768]{1,0:T(8,128)(2,1)S(1)} %convolution_convert_fusion.1), channel_id=1, source_target_pairs={{8,0},{16,8},{24,16},{28,24},{20,28},{12,20},{4,12},{0,4},{9,1},{1... | collective-permute-start | bytes 599048 | tf_op jit(solution)/shard_map/ppermute | solution.py:112
  48.0 10.2 %collective-permute-start.2 = (bf16[128,1024]{1,0:T(8,128)(2,1)S(1)}, bf16[128,1024]{1,0:T(8,128)(2,1)S(1)}, u32[]{:S(2)}, u32[]{:S(2)}) collective-permute-start(bf16[128,1024]{1,0:T(8,128)(2,1)S(1)} %get-tuple-element.29), channel_id=1, source_target_pairs={{0,8},{8,16},{16,24},{24,28},{28,20},{20,12},{12,4},{4,0},{1,9},{9... | collective-permute-start | bytes 786440 | tf_op jit(solution)/shard_map/ppermute | solution.py:111
  50.0 9.7 %collective-permute-start.3 = (bf16[128,1024]{1,0:T(8,128)(2,1)S(1)}, bf16[128,1024]{1,0:T(8,128)(2,1)S(1)}, u32[]{:S(2)}, u32[]{:S(2)}) collective-permute-start(bf16[128,1024]{1,0:T(8,128)(2,1)S(1)} %get-tuple-element.30), channel_id=1, source_target_pairs={{8,0},{16,8},{24,16},{28,24},{20,28},{12,20},{4,12},{0,4},{9,1},{1... | collective-permute-start | bytes 786440 | tf_op jit(solution)/shard_map/ppermute | solution.py:112
  59.6 7.9 %collective-permute-start.4 = (bf16[130,768]{1,0:T(8,128)(2,1)S(1)}, bf16[130,768]{1,0:T(8,128)(2,1)S(1)}, u32[]{:S(2)}, u32[]{:S(2)}) collective-permute-start(bf16[130,768]{1,0:T(8,128)(2,1)S(1)} %add_convert_fusion.13), channel_id=1, source_target_pairs={{0,8},{8,16},{16,24},{24,28},{28,20},{20,12},{12,4},{4,0},{1,9},{9... | collective-permute-start | bytes 599048 | tf_op jit(solution)/shard_map/ppermute | solution.py:111
  61.1 7.7 %collective-permute-start.5 = (bf16[130,768]{1,0:T(8,128)(2,1)S(1)}, bf16[130,768]{1,0:T(8,128)(2,1)S(1)}, u32[]{:S(2)}, u32[]{:S(2)}) collective-permute-start(bf16[130,768]{1,0:T(8,128)(2,1)S(1)} %add_convert_fusion.12), channel_id=1, source_target_pairs={{8,0},{16,8},{24,16},{28,24},{20,28},{12,20},{4,12},{0,4},{9,1},{1... | collective-permute-start | bytes 599048 | tf_op jit(solution)/shard_map/ppermute | solution.py:112
  61.7 8.7 %collective-permute-start.6 = (bf16[128,1024]{1,0:T(8,128)(2,1)S(1)}, bf16[128,1024]{1,0:T(8,128)(2,1)S(1)}, u32[]{:S(2)}, u32[]{:S(2)}) collective-permute-start(bf16[128,1024]{1,0:T(8,128)(2,1)S(1)} %collective-permute-done.2), channel_id=1, source_target_pairs={{0,8},{8,16},{16,24},{24,28},{28,20},{20,12},{12,4},{4,0},{1,9},{9... | collective-permute-start | bytes 786440 | tf_op jit(solution)/shard_map/ppermute | solution.py:111
  63.1 8.5 %collective-permute-start.7 = (bf16[128,1024]{1,0:T(8,128)(2,1)S(1)}, bf16[128,1024]{1,0:T(8,128)(2,1)S(1)}, u32[]{:S(2)}, u32[]{:S(2)}) collective-permute-start(bf16[128,1024]{1,0:T(8,128)(2,1)S(1)} %collective-permute-done.3), channel_id=1, source_target_pairs={{8,0},{16,8},{24,16},{28,24},{20,28},{12,20},{4,12},{0,4},{9,1},{1... | collective-permute-start | bytes 786440 | tf_op jit(solution)/shard_map/ppermute | solution.py:112
  71.6 6.8 %collective-permute-start.8 = (bf16[130,768]{1,0:T(8,128)(2,1)S(1)}, bf16[130,768]{1,0:T(8,128)(2,1)S(1)}, u32[]{:S(2)}, u32[]{:S(2)}) collective-permute-start(bf16[130,768]{1,0:T(8,128)(2,1)S(1)} %add_convert_fusion.11), channel_id=1, source_target_pairs={{0,8},{8,16},{16,24},{24,28},{28,20},{20,12},{12,4},{4,0},{1,9},{9... | collective-permute-start | bytes 599048 | tf_op jit(solution)/shard_map/ppermute | solution.py:111
  73.1 6.5 %collective-permute-start.9 = (bf16[130,768]{1,0:T(8,128)(2,1)S(1)}, bf16[130,768]{1,0:T(8,128)(2,1)S(1)}, u32[]{:S(2)}, u32[]{:S(2)}) collective-permute-start(bf16[130,768]{1,0:T(8,128)(2,1)S(1)} %add_convert_fusion.10), channel_id=1, source_target_pairs={{8,0},{16,8},{24,16},{28,24},{20,28},{12,20},{4,12},{0,4},{9,1},{1... | collective-permute-start | bytes 599048 | tf_op jit(solution)/shard_map/ppermute | solution.py:112
  73.6 7.7 %collective-permute-start.10 = (bf16[128,1024]{1,0:T(8,128)(2,1)S(1)}, bf16[128,1024]{1,0:T(8,128)(2,1)S(1)}, u32[]{:S(2)}, u32[]{:S(2)}) collective-permute-start(bf16[128,1024]{1,0:T(8,128)(2,1)S(1)} %collective-permute-done.6), channel_id=1, source_target_pairs={{0,8},{8,16},{16,24},{24,28},{28,20},{20,12},{12,4},{4,0},{1,9},{9... | collective-permute-start | bytes 786440 | tf_op jit(solution)/shard_map/ppermute | solution.py:111
  75.1 8.9 %collective-permute-start.11 = (bf16[128,1024]{1,0:T(8,128)(2,1)S(1)}, bf16[128,1024]{1,0:T(8,128)(2,1)S(1)}, u32[]{:S(2)}, u32[]{:S(2)}) collective-permute-start(bf16[128,1024]{1,0:T(8,128)(2,1)S(1)} %collective-permute-done.7), channel_id=1, source_target_pairs={{8,0},{16,8},{24,16},{28,24},{20,28},{12,20},{4,12},{0,4},{9,1},{1... | collective-permute-start | bytes 786440 | tf_op jit(solution)/shard_map/ppermute | solution.py:112
  84.0 8.1 %collective-permute-start.16 = (bf16[130,768]{1,0:T(8,128)(2,1)S(1)}, bf16[130,768]{1,0:T(8,128)(2,1)S(1)}, u32[]{:S(2)}, u32[]{:S(2)}) collective-permute-start(bf16[130,768]{1,0:T(8,128)(2,1)S(1)} %add_convert_fusion.8), channel_id=1, source_target_pairs={{8,0},{16,8},{24,16},{28,24},{20,28},{12,20},{4,12},{0,4},{9,1},{1... | collective-permute-start | bytes 599048 | tf_op jit(solution)/shard_map/ppermute | solution.py:112
  84.6 8.2 %collective-permute-start.12 = (bf16[130,768]{1,0:T(8,128)(2,1)S(1)}, bf16[130,768]{1,0:T(8,128)(2,1)S(1)}, u32[]{:S(2)}, u32[]{:S(2)}) collective-permute-start(bf16[130,768]{1,0:T(8,128)(2,1)S(1)} %add_convert_fusion.9), channel_id=1, source_target_pairs={{0,8},{8,16},{16,24},{24,28},{28,20},{20,12},{12,4},{4,0},{1,9},{9... | collective-permute-start | bytes 599048 | tf_op jit(solution)/shard_map/ppermute | solution.py:111
  86.0 12.1 %collective-permute-start.20 = (bf16[128,1024]{1,0:T(8,128)(2,1)S(1)}, bf16[128,1024]{1,0:T(8,128)(2,1)S(1)}, u32[]{:S(2)}, u32[]{:S(2)}) collective-permute-start(bf16[128,1024]{1,0:T(8,128)(2,1)S(1)} %collective-permute-done.10), channel_id=1, source_target_pairs={{0,8},{8,16},{16,24},{24,28},{28,20},{20,12},{12,4},{4,0},{1,9},{9... | collective-permute-start | bytes 786440 | tf_op jit(solution)/shard_map/ppermute | solution.py:111
  87.7 12.0 %collective-permute-start.21 = (bf16[128,1024]{1,0:T(8,128)(2,1)S(1)}, bf16[128,1024]{1,0:T(8,128)(2,1)S(1)}, u32[]{:S(2)}, u32[]{:S(2)}) collective-permute-start(bf16[128,1024]{1,0:T(8,128)(2,1)S(1)} %collective-permute-done.11), channel_id=1, source_target_pairs={{8,0},{16,8},{24,16},{28,24},{20,28},{12,20},{4,12},{0,4},{9,1},{1... | collective-permute-start | bytes 786440 | tf_op jit(solution)/shard_map/ppermute | solution.py:112
  92.2 10.0 %collective-permute-start.17 = (bf16[130,768]{1,0:T(8,128)(2,1)S(1)}, bf16[130,768]{1,0:T(8,128)(2,1)S(1)}, u32[]{:S(2)}, u32[]{:S(2)}) collective-permute-start(bf16[130,768]{1,0:T(8,128)(2,1)S(1)} %add_convert_fusion.3), channel_id=1, source_target_pairs={{8,0},{16,8},{24,16},{28,24},{20,28},{12,20},{4,12},{0,4},{9,1},{1... | collective-permute-start | bytes 599048 | tf_op jit(solution)/shard_map/ppermute | solution.py:116
  92.8 10.0 %collective-permute-start.13 = (bf16[130,768]{1,0:T(8,128)(2,1)S(1)}, bf16[130,768]{1,0:T(8,128)(2,1)S(1)}, u32[]{:S(2)}, u32[]{:S(2)}) collective-permute-start(bf16[130,768]{1,0:T(8,128)(2,1)S(1)} %add_convert_fusion.7), channel_id=1, source_target_pairs={{0,8},{8,16},{16,24},{24,28},{28,20},{20,12},{12,4},{4,0},{1,9},{9... | collective-permute-start | bytes 599048 | tf_op jit(solution)/shard_map/ppermute | solution.py:115
  98.2 10.1 %collective-permute-start.22 = (bf16[128,1024]{1,0:T(8,128)(2,1)S(1)}, bf16[128,1024]{1,0:T(8,128)(2,1)S(1)}, u32[]{:S(2)}, u32[]{:S(2)}) collective-permute-start(bf16[128,1024]{1,0:T(8,128)(2,1)S(1)} %collective-permute-done.20), channel_id=1, source_target_pairs={{0,8},{8,16},{16,24},{24,28},{28,20},{20,12},{12,4},{4,0},{1,9},{9... | collective-permute-start | bytes 786440 | tf_op jit(solution)/shard_map/ppermute | solution.py:120
  99.6 10.1 %collective-permute-start.23 = (bf16[128,1024]{1,0:T(8,128)(2,1)S(1)}, bf16[128,1024]{1,0:T(8,128)(2,1)S(1)}, u32[]{:S(2)}, u32[]{:S(2)}) collective-permute-start(bf16[128,1024]{1,0:T(8,128)(2,1)S(1)} %collective-permute-done.21), channel_id=1, source_target_pairs={{8,0},{16,8},{24,16},{28,24},{20,28},{12,20},{4,12},{0,4},{9,1},{1... | collective-permute-start | bytes 786440 | tf_op jit(solution)/shard_map/ppermute | solution.py:121
  102.2 10.8 %collective-permute-start.18 = (bf16[130,768]{1,0:T(8,128)(2,1)S(1)}, bf16[130,768]{1,0:T(8,128)(2,1)S(1)}, u32[]{:S(2)}, u32[]{:S(2)}) collective-permute-start(bf16[130,768]{1,0:T(8,128)(2,1)S(1)} %add_convert_fusion.2), channel_id=1, source_target_pairs={{8,0},{16,8},{24,16},{28,24},{20,28},{12,20},{4,12},{0,4},{9,1},{1... | collective-permute-start | bytes 599048 | tf_op jit(solution)/shard_map/ppermute | solution.py:116
  102.9 17.4 %copy-start.6 = (f32[16,512]{1,0:T(8,128)S(1)}, f32[16,512]{1,0:T(8,128)}, u32[]{:S(2)}) copy-start(f32[16,512]{1,0:T(8,128)} %param.20) | copy-start | bytes 98308
  102.9 10.8 %collective-permute-start.14 = (bf16[130,768]{1,0:T(8,128)(2,1)S(1)}, bf16[130,768]{1,0:T(8,128)(2,1)S(1)}, u32[]{:S(2)}, u32[]{:S(2)}) collective-permute-start(bf16[130,768]{1,0:T(8,128)(2,1)S(1)} %add_convert_fusion.6), channel_id=1, source_target_pairs={{0,8},{8,16},{16,24},{24,28},{28,20},{20,12},{12,4},{4,0},{1,9},{9... | collective-permute-start | bytes 599048 | tf_op jit(solution)/shard_map/ppermute | solution.py:115
  108.3 9.5 %collective-permute-start.24 = (bf16[128,1024]{1,0:T(8,128)(2,1)S(1)}, bf16[128,1024]{1,0:T(8,128)(2,1)S(1)}, u32[]{:S(2)}, u32[]{:S(2)}) collective-permute-start(bf16[128,1024]{1,0:T(8,128)(2,1)S(1)} %collective-permute-done.22), channel_id=1, source_target_pairs={{0,8},{8,16},{16,24},{24,28},{28,20},{20,12},{12,4},{4,0},{1,9},{9... | collective-permute-start | bytes 786440 | tf_op jit(solution)/shard_map/ppermute | solution.py:120
  109.7 9.5 %collective-permute-start.25 = (bf16[128,1024]{1,0:T(8,128)(2,1)S(1)}, bf16[128,1024]{1,0:T(8,128)(2,1)S(1)}, u32[]{:S(2)}, u32[]{:S(2)}) collective-permute-start(bf16[128,1024]{1,0:T(8,128)(2,1)S(1)} %collective-permute-done.23), channel_id=1, source_target_pairs={{8,0},{16,8},{24,16},{28,24},{20,28},{12,20},{4,12},{0,4},{9,1},{1... | collective-permute-start | bytes 786440 | tf_op jit(solution)/shard_map/ppermute | solution.py:121
  113.1 6.8 %collective-permute-start.19 = (bf16[130,768]{1,0:T(8,128)(2,1)S(1)}, bf16[130,768]{1,0:T(8,128)(2,1)S(1)}, u32[]{:S(2)}, u32[]{:S(2)}) collective-permute-start(bf16[130,768]{1,0:T(8,128)(2,1)S(1)} %add_convert_fusion.1), channel_id=1, source_target_pairs={{8,0},{16,8},{24,16},{28,24},{20,28},{12,20},{4,12},{0,4},{9,1},{1... | collective-permute-start | bytes 599048 | tf_op jit(solution)/shard_map/ppermute | solution.py:116
  113.8 6.2 %collective-permute-start.15 = (bf16[130,768]{1,0:T(8,128)(2,1)S(1)}, bf16[130,768]{1,0:T(8,128)(2,1)S(1)}, u32[]{:S(2)}, u32[]{:S(2)}) collective-permute-start(bf16[130,768]{1,0:T(8,128)(2,1)S(1)} %add_convert_fusion.5), channel_id=1, source_target_pairs={{0,8},{8,16},{16,24},{24,28},{28,20},{20,12},{12,4},{4,0},{1,9},{9... | collective-permute-start | bytes 599048 | tf_op jit(solution)/shard_map/ppermute | solution.py:115
  117.8 13.7 %collective-permute-start.26 = (bf16[128,1024]{1,0:T(8,128)(2,1)S(1)}, bf16[128,1024]{1,0:T(8,128)(2,1)S(1)}, u32[]{:S(2)}, u32[]{:S(2)}) collective-permute-start(bf16[128,1024]{1,0:T(8,128)(2,1)S(1)} %collective-permute-done.24), channel_id=1, source_target_pairs={{0,8},{8,16},{16,24},{24,28},{28,20},{20,12},{12,4},{4,0},{1,9},{9... | collective-permute-start | bytes 786440 | tf_op jit(solution)/shard_map/ppermute | solution.py:120
  119.2 13.0 %collective-permute-start.27 = (bf16[128,1024]{1,0:T(8,128)(2,1)S(1)}, bf16[128,1024]{1,0:T(8,128)(2,1)S(1)}, u32[]{:S(2)}, u32[]{:S(2)}) collective-permute-start(bf16[128,1024]{1,0:T(8,128)(2,1)S(1)} %collective-permute-done.25), channel_id=1, source_target_pairs={{8,0},{16,8},{24,16},{28,24},{20,28},{12,20},{4,12},{0,4},{9,1},{1... | collective-permute-start | bytes 786440 | tf_op jit(solution)/shard_map/ppermute | solution.py:121
  119.9 4.9 %copy-start.1 = (bf16[16,128,1024]{2,1,0:T(8,128)(2,1)}, bf16[16,128,1024]{2,1,0:T(8,128)(2,1)S(1)}, u32[]{:S(2)}) copy-start(bf16[16,128,1024]{2,1,0:T(8,128)(2,1)S(1)} %bitcast_dynamic-update-slice_fusion.2) | copy-start | bytes 12582916
  119.9 6.8 %copy-start.8 = (f32[16,512]{1,0:T(8,128)S(1)}, f32[16,512]{1,0:T(8,128)}, u32[]{:S(2)}) copy-start(f32[16,512]{1,0:T(8,128)} %param.21) | copy-start | bytes 98308
  124.7 2.0 %copy-start = (f32[16,128,512]{2,1,0:T(8,128)}, f32[16,128,512]{2,1,0:T(8,128)S(1)}, u32[]{:S(2)}) copy-start(f32[16,128,512]{2,1,0:T(8,128)S(1)} %fusion) | copy-start | bytes 12582916
  126.7 16.4 %copy-start.12 = (f32[512]{0:T(512)S(1)}, f32[512]{0:T(512)}, u32[]{:S(2)}) copy-start(f32[512]{0:T(512)} %param.22) | copy-start | bytes 6148
  127.6 12.1 %all-to-all-start.1 = ((f32[8,16,512]{2,1,0:T(8,128)}), f32[8,16,512]{2,1,0:T(8,128)S(1)}, u32[]{:S(2)}, u32[]{:S(2)}) async-start(f32[8,16,512]{2,1,0:T(8,128)} %multiply_select_fusion), calls=%async_computation.1 | async-start | bytes 524288 | tf_op jit(solution)/shard_map/all_to_all | solution.py:39
  139.7 10.9 %copy-start.2 = (bf16[16,128,1024]{2,1,0:T(8,128)(2,1)S(1)}, bf16[16,128,1024]{2,1,0:T(8,128)(2,1)}, u32[]{:S(2)}) copy-start(bf16[16,128,1024]{2,1,0:T(8,128)(2,1)} %bitcast_dynamic-update-slice_fusion) | copy-start | bytes 12582916

commit v14 on v12

--- a/solution.py
+++ b/solution.py
@@ -27,7 +27,7 @@
         precision=lax.Precision.HIGHEST,
         preferred_element_type=jnp.float32,
     )
-    end_state = running[:, length - 1] * jnp.exp(-rates * (length - 1))
+    end_state = jnp.sum(lifted, axis=1) * jnp.exp(-rates * (length - 1))
     carried = jnp.zeros_like(end_state)
     for shift in range(1, ctx_count):
         earlier = lax.ppermute(

time: 152 us -> 152 us (level)
  no operation moved by 1% of the time
where the time goes in v14:
time: 152 us
  starting transfers between devices  51.4 us (34%)
  waiting for transfers between devices  42.3 us (28%)
  between operations  30.3 us (20%)
  matrix products  10.9 us (7%)
  blocking collectives  7.16 us (5%)
  local copies, waits for them, and re-layouts  6.49 us (4%)
  other arithmetic  3.05 us (2%)
    ppermute x8, waiting for transfers between devices, body(): up, w_up = lax.ppermute((sent[0], sent[2]), 'ctx', perm=fwd)  17.2 us
    ppermute x7, starting transfers between devices, modal_long_conv(): lax.ppermute(end_state, 'ctx', perm=[(i, i + shift) for i in range(ctx_co...  15.3 us
    ppermute x8, waiting for transfers between devices, body(): down, w_low = lax.ppermute((sent[1], sent[3]), 'ctx', perm=bwd)  13.3 us
    ppermute x8, starting transfers between devices, body(): up, w_up = lax.ppermute((sent[0], sent[2]), 'ctx', perm=fwd)  13 us
    ppermute x3, waiting for transfers between devices, body(): down = lax.ppermute(down.astype(jnp.bfloat16), 'ctx', perm=bwd)  7.66 us
    all_to_all x1, starting transfers between devices, body(): lax.all_to_all(by_dest, 'ctx', split_axis=0, concat_axis=0, tiled=True)  7.29 us
    all_gather x1, blocking collectives, body(): features = lax.all_gather(gated, 'tp', axis=1, tiled=True)  7.16 us
    dot_general x1, matrix products, modal_long_conv(): lax.dot_general(lower, lifted, (((2,), (1,)), ((0,), (0,))), precision=la...  4.98 us
  transfers between devices with their start and end apart: 36, of which 19 were waited for; matrix products, arithmetic and copies ran while one was open for 8% of the time, Pallas kernels for 0%

profile of v14, /device:TPU:0, one launch (start us, length us, event | category | flops | bytes accessed | tf_op | source)
XLA Modules:
  0.0 151.6 jit_solution(10313208525959034509)
XLA Ops:
  0.0 2.4 %copy.14 = bf16[128,4096]{0,1:T(8,128)(2,1)} copy(bf16[128,4096]{1,0:T(8,128)(2,1)} %param.13) | data formatting | bytes 2097152 | tf_op args[0]
  2.4 7.3 %all-to-all-start = ((bf16[8,128,512]{1,2,0:T(8,128)(2,1)}), bf16[8,128,512]{1,2,0:T(8,128)(2,1)}, u32[]{:S(2)}, u32[]{:S(2)}) async-start(bf16[8,128,512]{1,2,0:T(8,128)(2,1)} %bitcast.2), calls=%async_computation | async-start | bytes 2097152 | tf_op jit(solution)/shard_map/all_to_all | solution.py:66
  21.0 0.8 fusion.70
  40.8 1.1 pad_maximum_fusion.1
  42.1 1.5 copy.15
  46.1 2.1 %collective-permute-start = (bf16[130,768]{1,0:T(8,128)(2,1)S(1)}, bf16[130,768]{1,0:T(8,128)(2,1)S(1)}, u32[]{:S(2)}, u32[]{:S(2)}) collective-permute-start(bf16[130,768]{1,0:T(8,128)(2,1)S(1)} %convolution_convert_fusion.2), channel_id=1, source_target_pairs={{0,8},{8,16},{16,24},{24,28},{28,20},{20,12},{12,4},{4,0},{1,9},{9... | collective-permute-start | bytes 599048 | tf_op jit(solution)/shard_map/ppermute | solution.py:107
  48.3 2.0 %collective-permute-start.2 = (bf16[128,1024]{1,0:T(8,128)(2,1)S(1)}, bf16[128,1024]{1,0:T(8,128)(2,1)S(1)}, u32[]{:S(2)}, u32[]{:S(2)}) collective-permute-start(bf16[128,1024]{1,0:T(8,128)(2,1)S(1)} %get-tuple-element.29), channel_id=1, source_target_pairs={{0,8},{8,16},{16,24},{24,28},{28,20},{20,12},{12,4},{4,0},{1,9},{9... | collective-permute-start | bytes 786440 | tf_op jit(solution)/shard_map/ppermute | solution.py:107
  52.6 1.7 %collective-permute-done = bf16[130,768]{1,0:T(8,128)(2,1)S(1)} collective-permute-done((bf16[130,768]{1,0:T(8,128)(2,1)S(1)}, bf16[130,768]{1,0:T(8,128)(2,1)S(1)}, u32[]{:S(2)}, u32[]{:S(2)}) %collective-permute-start) | collective-permute-done | bytes 199712 | tf_op jit(solution)/shard_map/ppermute | solution.py:107
  54.6 1.7 %collective-permute-done.1 = bf16[130,768]{1,0:T(8,128)(2,1)S(1)} collective-permute-done((bf16[130,768]{1,0:T(8,128)(2,1)S(1)}, bf16[130,768]{1,0:T(8,128)(2,1)S(1)}, u32[]{:S(2)}, u32[]{:S(2)}) %collective-permute-start.1) | collective-permute-done | bytes 199712 | tf_op jit(solution)/shard_map/ppermute | solution.py:108
  56.6 1.8 %collective-permute-done.2 = bf16[128,1024]{1,0:T(8,128)(2,1)S(1)} collective-permute-done((bf16[128,1024]{1,0:T(8,128)(2,1)S(1)}, bf16[128,1024]{1,0:T(8,128)(2,1)S(1)}, u32[]{:S(2)}, u32[]{:S(2)}) %collective-permute-start.2) | collective-permute-done | bytes 262176 | tf_op jit(solution)/shard_map/ppermute | solution.py:107
  58.4 1.5 collective-permute-done.3
  59.9 1.5 collective-permute-start.4
  61.9 1.5 collective-permute-start.6
  64.0 3.8 %collective-permute-done.4 = bf16[130,768]{1,0:T(8,128)(2,1)S(1)} collective-permute-done((bf16[130,768]{1,0:T(8,128)(2,1)S(1)}, bf16[130,768]{1,0:T(8,128)(2,1)S(1)}, u32[]{:S(2)}, u32[]{:S(2)}) %collective-permute-start.4) | collective-permute-done | bytes 199712 | tf_op jit(solution)/shard_map/ppermute | solution.py:107
  67.9 1.1 collective-permute-done.5
  69.1 1.6 %collective-permute-done.6 = bf16[128,1024]{1,0:T(8,128)(2,1)S(1)} collective-permute-done((bf16[128,1024]{1,0:T(8,128)(2,1)S(1)}, bf16[128,1024]{1,0:T(8,128)(2,1)S(1)}, u32[]{:S(2)}, u32[]{:S(2)}) %collective-permute-start.6) | collective-permute-done | bytes 262176 | tf_op jit(solution)/shard_map/ppermute | solution.py:107
  70.6 1.2 collective-permute-done.7
  71.8 1.5 collective-permute-start.8
  73.9 1.5 collective-permute-start.10
  75.9 2.6 %collective-permute-done.8 = bf16[130,768]{1,0:T(8,128)(2,1)S(1)} collective-permute-done((bf16[130,768]{1,0:T(8,128)(2,1)S(1)}, bf16[130,768]{1,0:T(8,128)(2,1)S(1)}, u32[]{:S(2)}, u32[]{:S(2)}) %collective-permute-start.8) | collective-permute-done | bytes 199712 | tf_op jit(solution)/shard_map/ppermute | solution.py:107
  78.6 1.1 collective-permute-done.9
  79.8 1.8 %collective-permute-done.10 = bf16[128,1024]{1,0:T(8,128)(2,1)S(1)} collective-permute-done((bf16[128,1024]{1,0:T(8,128)(2,1)S(1)}, bf16[128,1024]{1,0:T(8,128)(2,1)S(1)}, u32[]{:S(2)}, u32[]{:S(2)}) %collective-permute-start.10) | collective-permute-done | bytes 262176 | tf_op jit(solution)/shard_map/ppermute | solution.py:107
  81.6 2.6 %collective-permute-done.11 = bf16[128,1024]{1,0:T(8,128)(2,1)S(1)} collective-permute-done((bf16[128,1024]{1,0:T(8,128)(2,1)S(1)}, bf16[128,1024]{1,0:T(8,128)(2,1)S(1)}, u32[]{:S(2)}, u32[]{:S(2)}) %collective-permute-start.11) | collective-permute-done | bytes 262176 | tf_op jit(solution)/shard_map/ppermute | solution.py:108
  84.8 1.5 collective-permute-start.12
  86.3 1.6 %collective-permute-start.27 = (bf16[128,1024]{1,0:T(8,128)(2,1)S(1)}, bf16[128,1024]{1,0:T(8,128)(2,1)S(1)}, u32[]{:S(2)}, u32[]{:S(2)}) collective-permute-start(bf16[128,1024]{1,0:T(8,128)(2,1)S(1)} %collective-permute-done.10), channel_id=1, source_target_pairs={{0,8},{8,16},{16,24},{24,28},{28,20},{20,12},{12,4},{4,0},{1,9},{9... | collective-permute-start | bytes 786440 | tf_op jit(solution)/shard_map/ppermute | solution.py:107
  88.3 4.0 %collective-permute-done.16 = bf16[130,768]{1,0:T(8,128)(2,1)S(1)} collective-permute-done((bf16[130,768]{1,0:T(8,128)(2,1)S(1)}, bf16[130,768]{1,0:T(8,128)(2,1)S(1)}, u32[]{:S(2)}, u32[]{:S(2)}) %collective-permute-start.16) | collective-permute-done | bytes 199712 | tf_op jit(solution)/shard_map/ppermute | solution.py:108
  93.1 1.5 collective-permute-start.13
  94.6 3.9 %collective-permute-done.27 = bf16[128,1024]{1,0:T(8,128)(2,1)S(1)} collective-permute-done((bf16[128,1024]{1,0:T(8,128)(2,1)S(1)}, bf16[128,1024]{1,0:T(8,128)(2,1)S(1)}, u32[]{:S(2)}, u32[]{:S(2)}) %collective-permute-start.27) | collective-permute-done | bytes 262176 | tf_op jit(solution)/shard_map/ppermute | solution.py:107
  98.4 1.5 collective-permute-start.29
  100.5 1.9 %collective-permute-done.17 = bf16[130,768]{1,0:T(8,128)(2,1)S(1)} collective-permute-done((bf16[130,768]{1,0:T(8,128)(2,1)S(1)}, bf16[130,768]{1,0:T(8,128)(2,1)S(1)}, u32[]{:S(2)}, u32[]{:S(2)}) %collective-permute-start.17) | collective-permute-done | bytes 199712 | tf_op jit(solution)/shard_map/ppermute | solution.py:112
  103.2 1.5 collective-permute-start.14
  104.7 3.8 %collective-permute-done.29 = bf16[128,1024]{1,0:T(8,128)(2,1)S(1)} collective-permute-done((bf16[128,1024]{1,0:T(8,128)(2,1)S(1)}, bf16[128,1024]{1,0:T(8,128)(2,1)S(1)}, u32[]{:S(2)}, u32[]{:S(2)}) %collective-permute-start.29) | collective-permute-done | bytes 262176 | tf_op jit(solution)/shard_map/ppermute | solution.py:116
  108.5 1.5 collective-permute-start.31
  110.6 1.7 %collective-permute-done.18 = bf16[130,768]{1,0:T(8,128)(2,1)S(1)} collective-permute-done((bf16[130,768]{1,0:T(8,128)(2,1)S(1)}, bf16[130,768]{1,0:T(8,128)(2,1)S(1)}, u32[]{:S(2)}, u32[]{:S(2)}) %collective-permute-start.18) | collective-permute-done | bytes 199712 | tf_op jit(solution)/shard_map/ppermute | solution.py:112
  113.0 1.5 collective-permute-start.15
  114.5 4.1 %collective-permute-done.19 = bf16[130,768]{1,0:T(8,128)(2,1)S(1)} collective-permute-done((bf16[130,768]{1,0:T(8,128)(2,1)S(1)}, bf16[130,768]{1,0:T(8,128)(2,1)S(1)}, u32[]{:S(2)}, u32[]{:S(2)}) %collective-permute-start.19) | collective-permute-done | bytes 199712 | tf_op jit(solution)/shard_map/ppermute | solution.py:112
  119.2 0.8 fusion
  120.0 4.5 %collective-permute-start.26 = (f32[16,512]{1,0:T(8,128)S(1)}, f32[16,512]{1,0:T(8,128)S(1)}, u32[]{:S(2)}, u32[]{:S(2)}) collective-permute-start(f32[16,512]{1,0:T(8,128)S(1)} %exponential_multiply_fusion.5), channel_id=1, source_target_pairs={{0,28},{1,29},{2,30},{3,31}} | collective-permute-start | bytes 98312 | tf_op jit(solution)/shard_map/ppermute | solution.py:33
  124.5 1.3 collective-permute-start.25
  125.9 1.3 collective-permute-start.24
  127.2 1.3 collective-permute-start.23
  128.5 2.5 %collective-permute-start.22 = (f32[16,512]{1,0:T(8,128)S(1)}, f32[16,512]{1,0:T(8,128)S(1)}, u32[]{:S(2)}, u32[]{:S(2)}) collective-permute-start(f32[16,512]{1,0:T(8,128)S(1)} %exponential_multiply_fusion.5), channel_id=1, source_target_pairs={{0,12},{4,16},{8,20},{12,24},{16,28},{1,13},{5,17},{9,21},{13,25},... | collective-permute-start | bytes 98312 | tf_op jit(solution)/shard_map/ppermute | solution.py:33
  131.0 1.3 collective-permute-start.21
  132.3 3.1 %collective-permute-start.20 = (f32[16,512]{1,0:T(8,128)S(1)}, f32[16,512]{1,0:T(8,128)S(1)}, u32[]{:S(2)}, u32[]{:S(2)}) collective-permute-start(f32[16,512]{1,0:T(8,128)S(1)} %exponential_multiply_fusion.5), channel_id=1, source_target_pairs={{0,4},{4,8},{8,12},{12,16},{16,20},{20,24},{24,28},{1,5},{5,9},{9,... | collective-permute-start | bytes 98312 | tf_op jit(solution)/shard_map/ppermute | solution.py:33
  135.5 2.0 %collective-permute-start.34 = (bf16[128,1024]{1,0:T(8,128)(2,1)S(1)}, bf16[128,1024]{1,0:T(8,128)(2,1)S(1)}, u32[]{:S(2)}, u32[]{:S(2)}) collective-permute-start(bf16[128,1024]{1,0:T(8,128)(2,1)S(1)} %collective-permute-done.32), channel_id=1, source_target_pairs={{8,0},{16,8},{24,16},{28,24},{20,28},{12,20},{4,12},{0,4},{9,1},{1... | collective-permute-start | bytes 786440 | tf_op jit(solution)/shard_map/ppermute | solution.py:117
  137.6 5.0 %multiply_reduce_fusion = f32[128,512]{1,0:T(8,128)S(1)} fusion(f32[16,512]{1,0:T(8,128)S(1)} %get-tuple-element.48, f32[16,512]{1,0:T(8,128)S(1)} %get-tuple-element.49, f32[16,512]{1,0:T(8,128)S(1)} %get-tuple-element.47, f32[128,512]{1,0:T(8,128)S(1)} %fusion.48, f32[16,512]{1,0:T(8,128)S(1)} %copy-done.3, f32[128,128]{1,0:T(8,128)S(1)} %fusion.49), kind=kOutput, calls=%fused_computation | convolution fusion | flops 1617887232 | bytes 720896 | tf_op jit(solution)/shard_map/dot_general | solution.py:23
  142.9 7.2 %all_gather.3 = bf16[128,2048]{1,0:T(8,128)(2,1)S(1)} all-gather(bf16[128,512]{1,0:T(8,128)(2,1)S(1)} %multiply_convert_fusion), channel_id=1, replica_groups=mesh['ctx'=8,'tp'=4] {'tp'}, dimensions={1}, use_global_device_ids=true | all-gather | bytes 655360 | tf_op jit(solution)/shard_map/all_gather | solution.py:131
  150.1 1.4 convolution_convert_fusion
  (111 shorter events, 14.2 us)
Async XLA Ops:
  0.0 9.7 %copy-start.10 = (s32[8]{0:T(128)S(1)}, s32[8]{0:T(128)}, u32[]{:S(2)}) copy-start(s32[8]{0:T(128)} %constant.275.clone) | copy-start | bytes 100
  0.0 21.0 %copy-start.4 = (s32[8]{0:T(128)S(1)}, s32[8]{0:T(128)}, u32[]{:S(2)}) copy-start(s32[8]{0:T(128)} %constant.276.clone) | copy-start | bytes 100
  0.0 40.8 %copy-start.1 = (bf16[512,512]{1,0:T(8,128)(2,1)S(1)}, bf16[512,512]{1,0:T(8,128)(2,1)}, u32[]{:S(2)}) copy-start(bf16[512,512]{1,0:T(8,128)(2,1)} %param.15) | copy-start | bytes 1572868
  0.0 40.8 %copy-start.2 = (bf16[512,512]{1,0:T(8,128)(2,1)S(1)}, bf16[512,512]{1,0:T(8,128)(2,1)}, u32[]{:S(2)}) copy-start(bf16[512,512]{1,0:T(8,128)(2,1)} %param.14) | copy-start | bytes 1572868
  0.0 41.9 %copy-start.6 = (f32[3,512]{1,0:T(4,128)S(1)}, f32[3,512]{1,0:T(4,128)}, u32[]{:S(2)}) copy-start(f32[3,512]{1,0:T(4,128)} %param.19) | copy-start | bytes 18436
  0.0 42.0 %copy-start.7 = (f32[3,512]{1,0:T(4,128)S(1)}, f32[3,512]{1,0:T(4,128)}, u32[]{:S(2)}) copy-start(f32[3,512]{1,0:T(4,128)} %param.18) | copy-start | bytes 18436
  0.0 42.0 %copy-start.8 = (f32[3,512]{1,0:T(4,128)S(1)}, f32[3,512]{1,0:T(4,128)}, u32[]{:S(2)}) copy-start(f32[3,512]{1,0:T(4,128)} %param.17) | copy-start | bytes 18436
  0.0 42.0 %copy-start = (bf16[256,1024]{1,0:T(8,128)(2,1)S(1)}, bf16[256,1024]{1,0:T(8,128)(2,1)}, u32[]{:S(2)}) copy-start(bf16[256,1024]{1,0:T(8,128)(2,1)} %param.23) | copy-start | bytes 1572868
  2.4 39.6 %all-to-all-start = ((bf16[8,128,512]{1,2,0:T(8,128)(2,1)}), bf16[8,128,512]{1,2,0:T(8,128)(2,1)}, u32[]{:S(2)}, u32[]{:S(2)}) async-start(bf16[8,128,512]{1,2,0:T(8,128)(2,1)} %bitcast.2), calls=%async_computation | async-start | bytes 2097152 | tf_op jit(solution)/shard_map/all_to_all | solution.py:66
  46.1 8.1 %collective-permute-start = (bf16[130,768]{1,0:T(8,128)(2,1)S(1)}, bf16[130,768]{1,0:T(8,128)(2,1)S(1)}, u32[]{:S(2)}, u32[]{:S(2)}) collective-permute-start(bf16[130,768]{1,0:T(8,128)(2,1)S(1)} %convolution_convert_fusion.2), channel_id=1, source_target_pairs={{0,8},{8,16},{16,24},{24,28},{28,20},{20,12},{12,4},{4,0},{1,9},{9... | collective-permute-start | bytes 599048 | tf_op jit(solution)/shard_map/ppermute | solution.py:107
  48.2 8.1 %collective-permute-start.1 = (bf16[130,768]{1,0:T(8,128)(2,1)S(1)}, bf16[130,768]{1,0:T(8,128)(2,1)S(1)}, u32[]{:S(2)}, u32[]{:S(2)}) collective-permute-start(bf16[130,768]{1,0:T(8,128)(2,1)S(1)} %convolution_convert_fusion.1), channel_id=1, source_target_pairs={{8,0},{16,8},{24,16},{28,24},{20,28},{12,20},{4,12},{0,4},{9,1},{1... | collective-permute-start | bytes 599048 | tf_op jit(solution)/shard_map/ppermute | solution.py:108
  48.3 10.2 %collective-permute-start.2 = (bf16[128,1024]{1,0:T(8,128)(2,1)S(1)}, bf16[128,1024]{1,0:T(8,128)(2,1)S(1)}, u32[]{:S(2)}, u32[]{:S(2)}) collective-permute-start(bf16[128,1024]{1,0:T(8,128)(2,1)S(1)} %get-tuple-element.29), channel_id=1, source_target_pairs={{0,8},{8,16},{16,24},{24,28},{28,20},{20,12},{12,4},{4,0},{1,9},{9... | collective-permute-start | bytes 786440 | tf_op jit(solution)/shard_map/ppermute | solution.py:107
  50.2 9.7 %collective-permute-start.3 = (bf16[128,1024]{1,0:T(8,128)(2,1)S(1)}, bf16[128,1024]{1,0:T(8,128)(2,1)S(1)}, u32[]{:S(2)}, u32[]{:S(2)}) collective-permute-start(bf16[128,1024]{1,0:T(8,128)(2,1)S(1)} %get-tuple-element.30), channel_id=1, source_target_pairs={{8,0},{16,8},{24,16},{28,24},{20,28},{12,20},{4,12},{0,4},{9,1},{1... | collective-permute-start | bytes 786440 | tf_op jit(solution)/shard_map/ppermute | solution.py:108
  59.9 7.9 %collective-permute-start.4 = (bf16[130,768]{1,0:T(8,128)(2,1)S(1)}, bf16[130,768]{1,0:T(8,128)(2,1)S(1)}, u32[]{:S(2)}, u32[]{:S(2)}) collective-permute-start(bf16[130,768]{1,0:T(8,128)(2,1)S(1)} %add_convert_fusion.13), channel_id=1, source_target_pairs={{0,8},{8,16},{16,24},{24,28},{28,20},{20,12},{12,4},{4,0},{1,9},{9... | collective-permute-start | bytes 599048 | tf_op jit(solution)/shard_map/ppermute | solution.py:107
  61.3 7.7 %collective-permute-start.5 = (bf16[130,768]{1,0:T(8,128)(2,1)S(1)}, bf16[130,768]{1,0:T(8,128)(2,1)S(1)}, u32[]{:S(2)}, u32[]{:S(2)}) collective-permute-start(bf16[130,768]{1,0:T(8,128)(2,1)S(1)} %add_convert_fusion.12), channel_id=1, source_target_pairs={{8,0},{16,8},{24,16},{28,24},{20,28},{12,20},{4,12},{0,4},{9,1},{1... | collective-permute-start | bytes 599048 | tf_op jit(solution)/shard_map/ppermute | solution.py:108
  61.9 8.7 %collective-permute-start.6 = (bf16[128,1024]{1,0:T(8,128)(2,1)S(1)}, bf16[128,1024]{1,0:T(8,128)(2,1)S(1)}, u32[]{:S(2)}, u32[]{:S(2)}) collective-permute-start(bf16[128,1024]{1,0:T(8,128)(2,1)S(1)} %collective-permute-done.2), channel_id=1, source_target_pairs={{0,8},{8,16},{16,24},{24,28},{28,20},{20,12},{12,4},{4,0},{1,9},{9... | collective-permute-start | bytes 786440 | tf_op jit(solution)/shard_map/ppermute | solution.py:107
  63.4 8.5 %collective-permute-start.7 = (bf16[128,1024]{1,0:T(8,128)(2,1)S(1)}, bf16[128,1024]{1,0:T(8,128)(2,1)S(1)}, u32[]{:S(2)}, u32[]{:S(2)}) collective-permute-start(bf16[128,1024]{1,0:T(8,128)(2,1)S(1)} %collective-permute-done.3), channel_id=1, source_target_pairs={{8,0},{16,8},{24,16},{28,24},{20,28},{12,20},{4,12},{0,4},{9,1},{1... | collective-permute-start | bytes 786440 | tf_op jit(solution)/shard_map/ppermute | solution.py:108
  71.8 6.8 %collective-permute-start.8 = (bf16[130,768]{1,0:T(8,128)(2,1)S(1)}, bf16[130,768]{1,0:T(8,128)(2,1)S(1)}, u32[]{:S(2)}, u32[]{:S(2)}) collective-permute-start(bf16[130,768]{1,0:T(8,128)(2,1)S(1)} %add_convert_fusion.11), channel_id=1, source_target_pairs={{0,8},{8,16},{16,24},{24,28},{28,20},{20,12},{12,4},{4,0},{1,9},{9... | collective-permute-start | bytes 599048 | tf_op jit(solution)/shard_map/ppermute | solution.py:107
  73.3 6.5 %collective-permute-start.9 = (bf16[130,768]{1,0:T(8,128)(2,1)S(1)}, bf16[130,768]{1,0:T(8,128)(2,1)S(1)}, u32[]{:S(2)}, u32[]{:S(2)}) collective-permute-start(bf16[130,768]{1,0:T(8,128)(2,1)S(1)} %add_convert_fusion.10), channel_id=1, source_target_pairs={{8,0},{16,8},{24,16},{28,24},{20,28},{12,20},{4,12},{0,4},{9,1},{1... | collective-permute-start | bytes 599048 | tf_op jit(solution)/shard_map/ppermute | solution.py:108
  73.9 7.7 %collective-permute-start.10 = (bf16[128,1024]{1,0:T(8,128)(2,1)S(1)}, bf16[128,1024]{1,0:T(8,128)(2,1)S(1)}, u32[]{:S(2)}, u32[]{:S(2)}) collective-permute-start(bf16[128,1024]{1,0:T(8,128)(2,1)S(1)} %collective-permute-done.6), channel_id=1, source_target_pairs={{0,8},{8,16},{16,24},{24,28},{28,20},{20,12},{12,4},{4,0},{1,9},{9... | collective-permute-start | bytes 786440 | tf_op jit(solution)/shard_map/ppermute | solution.py:107
  75.3 8.9 %collective-permute-start.11 = (bf16[128,1024]{1,0:T(8,128)(2,1)S(1)}, bf16[128,1024]{1,0:T(8,128)(2,1)S(1)}, u32[]{:S(2)}, u32[]{:S(2)}) collective-permute-start(bf16[128,1024]{1,0:T(8,128)(2,1)S(1)} %collective-permute-done.7), channel_id=1, source_target_pairs={{8,0},{16,8},{24,16},{28,24},{20,28},{12,20},{4,12},{0,4},{9,1},{1... | collective-permute-start | bytes 786440 | tf_op jit(solution)/shard_map/ppermute | solution.py:108
  84.2 8.1 %collective-permute-start.16 = (bf16[130,768]{1,0:T(8,128)(2,1)S(1)}, bf16[130,768]{1,0:T(8,128)(2,1)S(1)}, u32[]{:S(2)}, u32[]{:S(2)}) collective-permute-start(bf16[130,768]{1,0:T(8,128)(2,1)S(1)} %add_convert_fusion.8), channel_id=1, source_target_pairs={{8,0},{16,8},{24,16},{28,24},{20,28},{12,20},{4,12},{0,4},{9,1},{1... | collective-permute-start | bytes 599048 | tf_op jit(solution)/shard_map/ppermute | solution.py:108
  84.8 8.2 %collective-permute-start.12 = (bf16[130,768]{1,0:T(8,128)(2,1)S(1)}, bf16[130,768]{1,0:T(8,128)(2,1)S(1)}, u32[]{:S(2)}, u32[]{:S(2)}) collective-permute-start(bf16[130,768]{1,0:T(8,128)(2,1)S(1)} %add_convert_fusion.9), channel_id=1, source_target_pairs={{0,8},{8,16},{16,24},{24,28},{28,20},{20,12},{12,4},{4,0},{1,9},{9... | collective-permute-start | bytes 599048 | tf_op jit(solution)/shard_map/ppermute | solution.py:107
  86.3 12.1 %collective-permute-start.27 = (bf16[128,1024]{1,0:T(8,128)(2,1)S(1)}, bf16[128,1024]{1,0:T(8,128)(2,1)S(1)}, u32[]{:S(2)}, u32[]{:S(2)}) collective-permute-start(bf16[128,1024]{1,0:T(8,128)(2,1)S(1)} %collective-permute-done.10), channel_id=1, source_target_pairs={{0,8},{8,16},{16,24},{24,28},{28,20},{20,12},{12,4},{4,0},{1,9},{9... | collective-permute-start | bytes 786440 | tf_op jit(solution)/shard_map/ppermute | solution.py:107
  87.9 12.0 %collective-permute-start.28 = (bf16[128,1024]{1,0:T(8,128)(2,1)S(1)}, bf16[128,1024]{1,0:T(8,128)(2,1)S(1)}, u32[]{:S(2)}, u32[]{:S(2)}) collective-permute-start(bf16[128,1024]{1,0:T(8,128)(2,1)S(1)} %collective-permute-done.11), channel_id=1, source_target_pairs={{8,0},{16,8},{24,16},{28,24},{20,28},{12,20},{4,12},{0,4},{9,1},{1... | collective-permute-start | bytes 786440 | tf_op jit(solution)/shard_map/ppermute | solution.py:108
  92.4 10.0 %collective-permute-start.17 = (bf16[130,768]{1,0:T(8,128)(2,1)S(1)}, bf16[130,768]{1,0:T(8,128)(2,1)S(1)}, u32[]{:S(2)}, u32[]{:S(2)}) collective-permute-start(bf16[130,768]{1,0:T(8,128)(2,1)S(1)} %add_convert_fusion.3), channel_id=1, source_target_pairs={{8,0},{16,8},{24,16},{28,24},{20,28},{12,20},{4,12},{0,4},{9,1},{1... | collective-permute-start | bytes 599048 | tf_op jit(solution)/shard_map/ppermute | solution.py:112
  93.1 10.1 %collective-permute-start.13 = (bf16[130,768]{1,0:T(8,128)(2,1)S(1)}, bf16[130,768]{1,0:T(8,128)(2,1)S(1)}, u32[]{:S(2)}, u32[]{:S(2)}) collective-permute-start(bf16[130,768]{1,0:T(8,128)(2,1)S(1)} %add_convert_fusion.7), channel_id=1, source_target_pairs={{0,8},{8,16},{16,24},{24,28},{28,20},{20,12},{12,4},{4,0},{1,9},{9... | collective-permute-start | bytes 599048 | tf_op jit(solution)/shard_map/ppermute | solution.py:111
  98.4 10.1 %collective-permute-start.29 = (bf16[128,1024]{1,0:T(8,128)(2,1)S(1)}, bf16[128,1024]{1,0:T(8,128)(2,1)S(1)}, u32[]{:S(2)}, u32[]{:S(2)}) collective-permute-start(bf16[128,1024]{1,0:T(8,128)(2,1)S(1)} %collective-permute-done.27), channel_id=1, source_target_pairs={{0,8},{8,16},{16,24},{24,28},{28,20},{20,12},{12,4},{4,0},{1,9},{9... | collective-permute-start | bytes 786440 | tf_op jit(solution)/shard_map/ppermute | solution.py:116
  99.9 10.1 %collective-permute-start.30 = (bf16[128,1024]{1,0:T(8,128)(2,1)S(1)}, bf16[128,1024]{1,0:T(8,128)(2,1)S(1)}, u32[]{:S(2)}, u32[]{:S(2)}) collective-permute-start(bf16[128,1024]{1,0:T(8,128)(2,1)S(1)} %collective-permute-done.28), channel_id=1, source_target_pairs={{8,0},{16,8},{24,16},{28,24},{20,28},{12,20},{4,12},{0,4},{9,1},{1... | collective-permute-start | bytes 786440 | tf_op jit(solution)/shard_map/ppermute | solution.py:117
  102.5 16.7 %copy-start.3 = (f32[16,512]{1,0:T(8,128)S(1)}, f32[16,512]{1,0:T(8,128)}, u32[]{:S(2)}) copy-start(f32[16,512]{1,0:T(8,128)} %param.20) | copy-start | bytes 98308
  102.5 9.8 %collective-permute-start.18 = (bf16[130,768]{1,0:T(8,128)(2,1)S(1)}, bf16[130,768]{1,0:T(8,128)(2,1)S(1)}, u32[]{:S(2)}, u32[]{:S(2)}) collective-permute-start(bf16[130,768]{1,0:T(8,128)(2,1)S(1)} %add_convert_fusion.2), channel_id=1, source_target_pairs={{8,0},{16,8},{24,16},{28,24},{20,28},{12,20},{4,12},{0,4},{9,1},{1... | collective-permute-start | bytes 599048 | tf_op jit(solution)/shard_map/ppermute | solution.py:112
  103.2 9.8 %collective-permute-start.14 = (bf16[130,768]{1,0:T(8,128)(2,1)S(1)}, bf16[130,768]{1,0:T(8,128)(2,1)S(1)}, u32[]{:S(2)}, u32[]{:S(2)}) collective-permute-start(bf16[130,768]{1,0:T(8,128)(2,1)S(1)} %add_convert_fusion.6), channel_id=1, source_target_pairs={{0,8},{8,16},{16,24},{24,28},{28,20},{20,12},{12,4},{4,0},{1,9},{9... | collective-permute-start | bytes 599048 | tf_op jit(solution)/shard_map/ppermute | solution.py:111
  108.5 17.3 %collective-permute-start.31 = (bf16[128,1024]{1,0:T(8,128)(2,1)S(1)}, bf16[128,1024]{1,0:T(8,128)(2,1)S(1)}, u32[]{:S(2)}, u32[]{:S(2)}) collective-permute-start(bf16[128,1024]{1,0:T(8,128)(2,1)S(1)} %collective-permute-done.29), channel_id=1, source_target_pairs={{0,8},{8,16},{16,24},{24,28},{28,20},{20,12},{12,4},{4,0},{1,9},{9... | collective-permute-start | bytes 786440 | tf_op jit(solution)/shard_map/ppermute | solution.py:116
  110.0 18.5 %collective-permute-start.32 = (bf16[128,1024]{1,0:T(8,128)(2,1)S(1)}, bf16[128,1024]{1,0:T(8,128)(2,1)S(1)}, u32[]{:S(2)}, u32[]{:S(2)}) collective-permute-start(bf16[128,1024]{1,0:T(8,128)(2,1)S(1)} %collective-permute-done.30), channel_id=1, source_target_pairs={{8,0},{16,8},{24,16},{28,24},{20,28},{12,20},{4,12},{0,4},{9,1},{1... | collective-permute-start | bytes 786440 | tf_op jit(solution)/shard_map/ppermute | solution.py:117
  112.3 25.2 %copy-start.5 = (f32[16,512]{1,0:T(8,128)S(1)}, f32[16,512]{1,0:T(8,128)}, u32[]{:S(2)}) copy-start(f32[16,512]{1,0:T(8,128)} %param.21) | copy-start | bytes 98308
  112.3 6.2 %collective-permute-start.19 = (bf16[130,768]{1,0:T(8,128)(2,1)S(1)}, bf16[130,768]{1,0:T(8,128)(2,1)S(1)}, u32[]{:S(2)}, u32[]{:S(2)}) collective-permute-start(bf16[130,768]{1,0:T(8,128)(2,1)S(1)} %add_convert_fusion.1), channel_id=1, source_target_pairs={{8,0},{16,8},{24,16},{28,24},{20,28},{12,20},{4,12},{0,4},{9,1},{1... | collective-permute-start | bytes 599048 | tf_op jit(solution)/shard_map/ppermute | solution.py:112
  113.0 5.9 %collective-permute-start.15 = (bf16[130,768]{1,0:T(8,128)(2,1)S(1)}, bf16[130,768]{1,0:T(8,128)(2,1)S(1)}, u32[]{:S(2)}, u32[]{:S(2)}) collective-permute-start(bf16[130,768]{1,0:T(8,128)(2,1)S(1)} %add_convert_fusion.5), channel_id=1, source_target_pairs={{0,8},{8,16},{16,24},{24,28},{28,20},{20,12},{12,4},{4,0},{1,9},{9... | collective-permute-start | bytes 599048 | tf_op jit(solution)/shard_map/ppermute | solution.py:111
  120.0 11.0 %collective-permute-start.26 = (f32[16,512]{1,0:T(8,128)S(1)}, f32[16,512]{1,0:T(8,128)S(1)}, u32[]{:S(2)}, u32[]{:S(2)}) collective-permute-start(f32[16,512]{1,0:T(8,128)S(1)} %exponential_multiply_fusion.5), channel_id=1, source_target_pairs={{0,28},{1,29},{2,30},{3,31}} | collective-permute-start | bytes 98312 | tf_op jit(solution)/shard_map/ppermute | solution.py:33
  124.5 7.7 %collective-permute-start.25 = (f32[16,512]{1,0:T(8,128)S(1)}, f32[16,512]{1,0:T(8,128)S(1)}, u32[]{:S(2)}, u32[]{:S(2)}) collective-permute-start(f32[16,512]{1,0:T(8,128)S(1)} %exponential_multiply_fusion.5), channel_id=1, source_target_pairs={{0,24},{4,28},{1,25},{5,29},{2,26},{6,30},{3,27},{7,31}} | collective-permute-start | bytes 98312 | tf_op jit(solution)/shard_map/ppermute | solution.py:33
  125.9 9.6 %collective-permute-start.24 = (f32[16,512]{1,0:T(8,128)S(1)}, f32[16,512]{1,0:T(8,128)S(1)}, u32[]{:S(2)}, u32[]{:S(2)}) collective-permute-start(f32[16,512]{1,0:T(8,128)S(1)} %exponential_multiply_fusion.5), channel_id=1, source_target_pairs={{0,20},{4,24},{8,28},{1,21},{5,25},{9,29},{2,22},{6,26},{10,30},{3... | collective-permute-start | bytes 98312 | tf_op jit(solution)/shard_map/ppermute | solution.py:33
  127.2 8.3 %collective-permute-start.23 = (f32[16,512]{1,0:T(8,128)S(1)}, f32[16,512]{1,0:T(8,128)S(1)}, u32[]{:S(2)}, u32[]{:S(2)}) collective-permute-start(f32[16,512]{1,0:T(8,128)S(1)} %exponential_multiply_fusion.5), channel_id=1, source_target_pairs={{0,16},{4,20},{8,24},{12,28},{1,17},{5,21},{9,25},{13,29},{2,18},{... | collective-permute-start | bytes 98312 | tf_op jit(solution)/shard_map/ppermute | solution.py:33
  128.5 9.0 %collective-permute-start.22 = (f32[16,512]{1,0:T(8,128)S(1)}, f32[16,512]{1,0:T(8,128)S(1)}, u32[]{:S(2)}, u32[]{:S(2)}) collective-permute-start(f32[16,512]{1,0:T(8,128)S(1)} %exponential_multiply_fusion.5), channel_id=1, source_target_pairs={{0,12},{4,16},{8,20},{12,24},{16,28},{1,13},{5,17},{9,21},{13,25},... | collective-permute-start | bytes 98312 | tf_op jit(solution)/shard_map/ppermute | solution.py:33
  131.0 6.5 %collective-permute-start.21 = (f32[16,512]{1,0:T(8,128)S(1)}, f32[16,512]{1,0:T(8,128)S(1)}, u32[]{:S(2)}, u32[]{:S(2)}) collective-permute-start(f32[16,512]{1,0:T(8,128)S(1)} %exponential_multiply_fusion.5), channel_id=1, source_target_pairs={{0,8},{4,12},{8,16},{12,20},{16,24},{20,28},{1,9},{5,13},{9,17},{1... | collective-permute-start | bytes 98312 | tf_op jit(solution)/shard_map/ppermute | solution.py:33
  132.3 5.2 %collective-permute-start.20 = (f32[16,512]{1,0:T(8,128)S(1)}, f32[16,512]{1,0:T(8,128)S(1)}, u32[]{:S(2)}, u32[]{:S(2)}) collective-permute-start(f32[16,512]{1,0:T(8,128)S(1)} %exponential_multiply_fusion.5), channel_id=1, source_target_pairs={{0,4},{4,8},{8,12},{12,16},{16,20},{20,24},{24,28},{1,5},{5,9},{9,... | collective-permute-start | bytes 98312 | tf_op jit(solution)/shard_map/ppermute | solution.py:33
  135.4 14.6 %collective-permute-start.33 = (bf16[128,1024]{1,0:T(8,128)(2,1)S(1)}, bf16[128,1024]{1,0:T(8,128)(2,1)S(1)}, u32[]{:S(2)}, u32[]{:S(2)}) collective-permute-start(bf16[128,1024]{1,0:T(8,128)(2,1)S(1)} %collective-permute-done.31), channel_id=1, source_target_pairs={{0,8},{8,16},{16,24},{24,28},{28,20},{20,12},{12,4},{4,0},{1,9},{9... | collective-permute-start | bytes 786440 | tf_op jit(solution)/shard_map/ppermute | solution.py:116
  135.5 14.6 %collective-permute-start.34 = (bf16[128,1024]{1,0:T(8,128)(2,1)S(1)}, bf16[128,1024]{1,0:T(8,128)(2,1)S(1)}, u32[]{:S(2)}, u32[]{:S(2)}) collective-permute-start(bf16[128,1024]{1,0:T(8,128)(2,1)S(1)} %collective-permute-done.32), channel_id=1, source_target_pairs={{8,0},{16,8},{24,16},{28,24},{20,28},{12,20},{4,12},{0,4},{9,1},{1... | collective-permute-start | bytes 786440 | tf_op jit(solution)/shard_map/ppermute | solution.py:117
  137.6 5.0 %copy-start.9 = (f32[512]{0:T(512)S(1)}, f32[512]{0:T(512)}, u32[]{:S(2)}) copy-start(f32[512]{0:T(512)} %param.22) | copy-start | bytes 6148

commit v15 on v14

--- a/solution.py
+++ b/solution.py
@@ -24,7 +24,7 @@
         lower,
         lifted,
         (((2,), (1,)), ((0,), (0,))),
-        precision=lax.Precision.HIGHEST,
+        precision=lax.Precision.HIGH,
         preferred_element_type=jnp.float32,
     )
     end_state = jnp.sum(lifted, axis=1) * jnp.exp(-rates * (length - 1))

time: 152 us -> 150 us (0.987)
  matrix products: 10.9 us -> 9.02 us
    dot_general x1, matrix products: 4.98 us -> 3.1 us  [modal_long_conv(): lax.dot_general(lower, lifted, (((2,), (1,)), ((0,), (0,))), precision=la...]
  transfers between devices with their start and end apart: 36 -> 36, of which waited for: 19 -> 19; matrix products, arithmetic and copies ran while one was open for 8% -> 7% of each run, Pallas kernels for 0% -> 0%
where the time goes in v15:
time: 150 us
  starting transfers between devices  51.4 us (34%)
  waiting for transfers between devices  42.3 us (28%)
  between operations  30.3 us (20%)
  matrix products  9.02 us (6%)
  blocking collectives  7.17 us (5%)
  local copies, waits for them, and re-layouts  6.49 us (4%)
  other arithmetic  3.05 us (2%)
    ppermute x8, waiting for transfers between devices, body(): up, w_up = lax.ppermute((sent[0], sent[2]), 'ctx', perm=fwd)  17.2 us
    ppermute x7, starting transfers between devices, modal_long_conv(): lax.ppermute(end_state, 'ctx', perm=[(i, i + shift) for i in range(ctx_co...  15.3 us
    ppermute x8, waiting for transfers between devices, body(): down, w_low = lax.ppermute((sent[1], sent[3]), 'ctx', perm=bwd)  13.3 us
    ppermute x8, starting transfers between devices, body(): up, w_up = lax.ppermute((sent[0], sent[2]), 'ctx', perm=fwd)  13 us
    ppermute x3, waiting for transfers between devices, body(): down = lax.ppermute(down.astype(jnp.bfloat16), 'ctx', perm=bwd)  7.66 us
    all_to_all x1, starting transfers between devices, body(): lax.all_to_all(by_dest, 'ctx', split_axis=0, concat_axis=0, tiled=True)  7.29 us
    all_gather x1, blocking collectives, body(): features = lax.all_gather(gated, 'tp', axis=1, tiled=True)  7.17 us
    ppermute x3, starting transfers between devices, body(): up = lax.ppermute(up.astype(jnp.bfloat16), 'ctx', perm=fwd)  4.51 us
  transfers between devices with their start and end apart: 36, of which 19 were waited for; matrix products, arithmetic and copies ran while one was open for 7% of the time, Pallas kernels for 0%

profile of v15, /device:TPU:0, one launch (start us, length us, event | category | flops | bytes accessed | tf_op | source)
XLA Modules:
  0.0 149.7 jit_solution(16104379873698696471)
XLA Ops:
  0.0 2.4 %copy.14 = bf16[128,4096]{0,1:T(8,128)(2,1)} copy(bf16[128,4096]{1,0:T(8,128)(2,1)} %param.13) | data formatting | bytes 2097152 | tf_op args[0]
  2.4 7.3 %all-to-all-start = ((bf16[8,128,512]{1,2,0:T(8,128)(2,1)}), bf16[8,128,512]{1,2,0:T(8,128)(2,1)}, u32[]{:S(2)}, u32[]{:S(2)}) async-start(bf16[8,128,512]{1,2,0:T(8,128)(2,1)} %bitcast.2), calls=%async_computation | async-start | bytes 2097152 | tf_op jit(solution)/shard_map/all_to_all | solution.py:66
  21.0 0.8 fusion.70
  40.8 1.1 pad_maximum_fusion.1
  42.1 1.5 copy.15
  46.1 2.1 %collective-permute-start = (bf16[130,768]{1,0:T(8,128)(2,1)S(1)}, bf16[130,768]{1,0:T(8,128)(2,1)S(1)}, u32[]{:S(2)}, u32[]{:S(2)}) collective-permute-start(bf16[130,768]{1,0:T(8,128)(2,1)S(1)} %convolution_convert_fusion.2), channel_id=1, source_target_pairs={{0,8},{8,16},{16,24},{24,28},{28,20},{20,12},{12,4},{4,0},{1,9},{9... | collective-permute-start | bytes 599048 | tf_op jit(solution)/shard_map/ppermute | solution.py:107
  48.3 2.0 %collective-permute-start.2 = (bf16[128,1024]{1,0:T(8,128)(2,1)S(1)}, bf16[128,1024]{1,0:T(8,128)(2,1)S(1)}, u32[]{:S(2)}, u32[]{:S(2)}) collective-permute-start(bf16[128,1024]{1,0:T(8,128)(2,1)S(1)} %get-tuple-element.29), channel_id=1, source_target_pairs={{0,8},{8,16},{16,24},{24,28},{28,20},{20,12},{12,4},{4,0},{1,9},{9... | collective-permute-start | bytes 786440 | tf_op jit(solution)/shard_map/ppermute | solution.py:107
  52.6 1.7 %collective-permute-done = bf16[130,768]{1,0:T(8,128)(2,1)S(1)} collective-permute-done((bf16[130,768]{1,0:T(8,128)(2,1)S(1)}, bf16[130,768]{1,0:T(8,128)(2,1)S(1)}, u32[]{:S(2)}, u32[]{:S(2)}) %collective-permute-start) | collective-permute-done | bytes 199712 | tf_op jit(solution)/shard_map/ppermute | solution.py:107
  54.6 1.7 %collective-permute-done.1 = bf16[130,768]{1,0:T(8,128)(2,1)S(1)} collective-permute-done((bf16[130,768]{1,0:T(8,128)(2,1)S(1)}, bf16[130,768]{1,0:T(8,128)(2,1)S(1)}, u32[]{:S(2)}, u32[]{:S(2)}) %collective-permute-start.1) | collective-permute-done | bytes 199712 | tf_op jit(solution)/shard_map/ppermute | solution.py:108
  56.6 1.8 %collective-permute-done.2 = bf16[128,1024]{1,0:T(8,128)(2,1)S(1)} collective-permute-done((bf16[128,1024]{1,0:T(8,128)(2,1)S(1)}, bf16[128,1024]{1,0:T(8,128)(2,1)S(1)}, u32[]{:S(2)}, u32[]{:S(2)}) %collective-permute-start.2) | collective-permute-done | bytes 262176 | tf_op jit(solution)/shard_map/ppermute | solution.py:107
  58.4 1.5 collective-permute-done.3
  59.9 1.5 collective-permute-start.4
  61.9 1.5 collective-permute-start.6
  64.0 3.8 %collective-permute-done.4 = bf16[130,768]{1,0:T(8,128)(2,1)S(1)} collective-permute-done((bf16[130,768]{1,0:T(8,128)(2,1)S(1)}, bf16[130,768]{1,0:T(8,128)(2,1)S(1)}, u32[]{:S(2)}, u32[]{:S(2)}) %collective-permute-start.4) | collective-permute-done | bytes 199712 | tf_op jit(solution)/shard_map/ppermute | solution.py:107
  67.9 1.1 collective-permute-done.5
  69.1 1.6 %collective-permute-done.6 = bf16[128,1024]{1,0:T(8,128)(2,1)S(1)} collective-permute-done((bf16[128,1024]{1,0:T(8,128)(2,1)S(1)}, bf16[128,1024]{1,0:T(8,128)(2,1)S(1)}, u32[]{:S(2)}, u32[]{:S(2)}) %collective-permute-start.6) | collective-permute-done | bytes 262176 | tf_op jit(solution)/shard_map/ppermute | solution.py:107
  70.6 1.2 collective-permute-done.7
  71.8 1.5 collective-permute-start.8
  73.9 1.5 collective-permute-start.10
  75.9 2.6 %collective-permute-done.8 = bf16[130,768]{1,0:T(8,128)(2,1)S(1)} collective-permute-done((bf16[130,768]{1,0:T(8,128)(2,1)S(1)}, bf16[130,768]{1,0:T(8,128)(2,1)S(1)}, u32[]{:S(2)}, u32[]{:S(2)}) %collective-permute-start.8) | collective-permute-done | bytes 199712 | tf_op jit(solution)/shard_map/ppermute | solution.py:107
  78.6 1.1 collective-permute-done.9
  79.8 1.8 %collective-permute-done.10 = bf16[128,1024]{1,0:T(8,128)(2,1)S(1)} collective-permute-done((bf16[128,1024]{1,0:T(8,128)(2,1)S(1)}, bf16[128,1024]{1,0:T(8,128)(2,1)S(1)}, u32[]{:S(2)}, u32[]{:S(2)}) %collective-permute-start.10) | collective-permute-done | bytes 262176 | tf_op jit(solution)/shard_map/ppermute | solution.py:107
  81.6 2.6 %collective-permute-done.11 = bf16[128,1024]{1,0:T(8,128)(2,1)S(1)} collective-permute-done((bf16[128,1024]{1,0:T(8,128)(2,1)S(1)}, bf16[128,1024]{1,0:T(8,128)(2,1)S(1)}, u32[]{:S(2)}, u32[]{:S(2)}) %collective-permute-start.11) | collective-permute-done | bytes 262176 | tf_op jit(solution)/shard_map/ppermute | solution.py:108
  84.8 1.5 collective-permute-start.12
  86.3 1.6 %collective-permute-start.27 = (bf16[128,1024]{1,0:T(8,128)(2,1)S(1)}, bf16[128,1024]{1,0:T(8,128)(2,1)S(1)}, u32[]{:S(2)}, u32[]{:S(2)}) collective-permute-start(bf16[128,1024]{1,0:T(8,128)(2,1)S(1)} %collective-permute-done.10), channel_id=1, source_target_pairs={{0,8},{8,16},{16,24},{24,28},{28,20},{20,12},{12,4},{4,0},{1,9},{9... | collective-permute-start | bytes 786440 | tf_op jit(solution)/shard_map/ppermute | solution.py:107
  88.3 4.0 %collective-permute-done.16 = bf16[130,768]{1,0:T(8,128)(2,1)S(1)} collective-permute-done((bf16[130,768]{1,0:T(8,128)(2,1)S(1)}, bf16[130,768]{1,0:T(8,128)(2,1)S(1)}, u32[]{:S(2)}, u32[]{:S(2)}) %collective-permute-start.16) | collective-permute-done | bytes 199712 | tf_op jit(solution)/shard_map/ppermute | solution.py:108
  93.1 1.5 %collective-permute-start.13 = (bf16[130,768]{1,0:T(8,128)(2,1)S(1)}, bf16[130,768]{1,0:T(8,128)(2,1)S(1)}, u32[]{:S(2)}, u32[]{:S(2)}) collective-permute-start(bf16[130,768]{1,0:T(8,128)(2,1)S(1)} %add_convert_fusion.7), channel_id=1, source_target_pairs={{0,8},{8,16},{16,24},{24,28},{28,20},{20,12},{12,4},{4,0},{1,9},{9... | collective-permute-start | bytes 599048 | tf_op jit(solution)/shard_map/ppermute | solution.py:111
  94.6 3.9 %collective-permute-done.27 = bf16[128,1024]{1,0:T(8,128)(2,1)S(1)} collective-permute-done((bf16[128,1024]{1,0:T(8,128)(2,1)S(1)}, bf16[128,1024]{1,0:T(8,128)(2,1)S(1)}, u32[]{:S(2)}, u32[]{:S(2)}) %collective-permute-start.27) | collective-permute-done | bytes 262176 | tf_op jit(solution)/shard_map/ppermute | solution.py:107
  98.4 1.5 collective-permute-start.29
  100.5 1.9 %collective-permute-done.17 = bf16[130,768]{1,0:T(8,128)(2,1)S(1)} collective-permute-done((bf16[130,768]{1,0:T(8,128)(2,1)S(1)}, bf16[130,768]{1,0:T(8,128)(2,1)S(1)}, u32[]{:S(2)}, u32[]{:S(2)}) %collective-permute-start.17) | collective-permute-done | bytes 199712 | tf_op jit(solution)/shard_map/ppermute | solution.py:112
  103.2 1.5 %collective-permute-start.14 = (bf16[130,768]{1,0:T(8,128)(2,1)S(1)}, bf16[130,768]{1,0:T(8,128)(2,1)S(1)}, u32[]{:S(2)}, u32[]{:S(2)}) collective-permute-start(bf16[130,768]{1,0:T(8,128)(2,1)S(1)} %add_convert_fusion.6), channel_id=1, source_target_pairs={{0,8},{8,16},{16,24},{24,28},{28,20},{20,12},{12,4},{4,0},{1,9},{9... | collective-permute-start | bytes 599048 | tf_op jit(solution)/shard_map/ppermute | solution.py:111
  104.7 3.8 %collective-permute-done.29 = bf16[128,1024]{1,0:T(8,128)(2,1)S(1)} collective-permute-done((bf16[128,1024]{1,0:T(8,128)(2,1)S(1)}, bf16[128,1024]{1,0:T(8,128)(2,1)S(1)}, u32[]{:S(2)}, u32[]{:S(2)}) %collective-permute-start.29) | collective-permute-done | bytes 262176 | tf_op jit(solution)/shard_map/ppermute | solution.py:116
  108.5 1.5 collective-permute-start.31
  110.6 1.7 %collective-permute-done.18 = bf16[130,768]{1,0:T(8,128)(2,1)S(1)} collective-permute-done((bf16[130,768]{1,0:T(8,128)(2,1)S(1)}, bf16[130,768]{1,0:T(8,128)(2,1)S(1)}, u32[]{:S(2)}, u32[]{:S(2)}) %collective-permute-start.18) | collective-permute-done | bytes 199712 | tf_op jit(solution)/shard_map/ppermute | solution.py:112
  113.0 1.5 %collective-permute-start.15 = (bf16[130,768]{1,0:T(8,128)(2,1)S(1)}, bf16[130,768]{1,0:T(8,128)(2,1)S(1)}, u32[]{:S(2)}, u32[]{:S(2)}) collective-permute-start(bf16[130,768]{1,0:T(8,128)(2,1)S(1)} %add_convert_fusion.5), channel_id=1, source_target_pairs={{0,8},{8,16},{16,24},{24,28},{28,20},{20,12},{12,4},{4,0},{1,9},{9... | collective-permute-start | bytes 599048 | tf_op jit(solution)/shard_map/ppermute | solution.py:111
  114.5 4.1 %collective-permute-done.19 = bf16[130,768]{1,0:T(8,128)(2,1)S(1)} collective-permute-done((bf16[130,768]{1,0:T(8,128)(2,1)S(1)}, bf16[130,768]{1,0:T(8,128)(2,1)S(1)}, u32[]{:S(2)}, u32[]{:S(2)}) %collective-permute-start.19) | collective-permute-done | bytes 199712 | tf_op jit(solution)/shard_map/ppermute | solution.py:112
  119.2 0.8 fusion
  120.0 4.5 %collective-permute-start.26 = (f32[16,512]{1,0:T(8,128)S(1)}, f32[16,512]{1,0:T(8,128)S(1)}, u32[]{:S(2)}, u32[]{:S(2)}) collective-permute-start(f32[16,512]{1,0:T(8,128)S(1)} %exponential_multiply_fusion.5), channel_id=1, source_target_pairs={{0,28},{1,29},{2,30},{3,31}} | collective-permute-start | bytes 98312 | tf_op jit(solution)/shard_map/ppermute | solution.py:33
  124.5 1.3 collective-permute-start.25
  125.9 1.3 collective-permute-start.24
  127.2 1.3 collective-permute-start.23
  128.5 2.5 %collective-permute-start.22 = (f32[16,512]{1,0:T(8,128)S(1)}, f32[16,512]{1,0:T(8,128)S(1)}, u32[]{:S(2)}, u32[]{:S(2)}) collective-permute-start(f32[16,512]{1,0:T(8,128)S(1)} %exponential_multiply_fusion.5), channel_id=1, source_target_pairs={{0,12},{4,16},{8,20},{12,24},{16,28},{1,13},{5,17},{9,21},{13,25},... | collective-permute-start | bytes 98312 | tf_op jit(solution)/shard_map/ppermute | solution.py:33
  131.0 1.3 collective-permute-start.21
  132.3 3.1 %collective-permute-start.20 = (f32[16,512]{1,0:T(8,128)S(1)}, f32[16,512]{1,0:T(8,128)S(1)}, u32[]{:S(2)}, u32[]{:S(2)}) collective-permute-start(f32[16,512]{1,0:T(8,128)S(1)} %exponential_multiply_fusion.5), channel_id=1, source_target_pairs={{0,4},{4,8},{8,12},{12,16},{16,20},{20,24},{24,28},{1,5},{5,9},{9,... | collective-permute-start | bytes 98312 | tf_op jit(solution)/shard_map/ppermute | solution.py:33
  135.5 2.0 %collective-permute-start.34 = (bf16[128,1024]{1,0:T(8,128)(2,1)S(1)}, bf16[128,1024]{1,0:T(8,128)(2,1)S(1)}, u32[]{:S(2)}, u32[]{:S(2)}) collective-permute-start(bf16[128,1024]{1,0:T(8,128)(2,1)S(1)} %collective-permute-done.32), channel_id=1, source_target_pairs={{8,0},{16,8},{24,16},{28,24},{20,28},{12,20},{4,12},{0,4},{9,1},{1... | collective-permute-start | bytes 786440 | tf_op jit(solution)/shard_map/ppermute | solution.py:117
  137.6 3.1 %multiply_reduce_fusion = f32[128,512]{1,0:T(8,128)S(1)} fusion(f32[16,512]{1,0:T(8,128)S(1)} %get-tuple-element.48, f32[16,512]{1,0:T(8,128)S(1)} %get-tuple-element.49, f32[16,512]{1,0:T(8,128)S(1)} %get-tuple-element.47, f32[128,512]{1,0:T(8,128)S(1)} %fusion.48, f32[16,512]{1,0:T(8,128)S(1)} %copy-done.3, f32[128,128]{1,0:T(8,128)S(1)} %fusion.49), kind=kOutput, calls=%fused_computation | convolution fusion | flops 812580864 | bytes 720896 | tf_op jit(solution)/shard_map/dot_general | solution.py:23
  141.0 7.2 %all_gather.3 = bf16[128,2048]{1,0:T(8,128)(2,1)S(1)} all-gather(bf16[128,512]{1,0:T(8,128)(2,1)S(1)} %multiply_convert_fusion), channel_id=1, replica_groups=mesh['ctx'=8,'tp'=4] {'tp'}, dimensions={1}, use_global_device_ids=true | all-gather | bytes 655360 | tf_op jit(solution)/shard_map/all_gather | solution.py:131
  148.3 1.4 convolution_convert_fusion
  (111 shorter events, 14.2 us)
Async XLA Ops:
  0.0 9.7 %copy-start.10 = (s32[8]{0:T(128)S(1)}, s32[8]{0:T(128)}, u32[]{:S(2)}) copy-start(s32[8]{0:T(128)} %constant.275.clone) | copy-start | bytes 100
  0.0 21.0 %copy-start.4 = (s32[8]{0:T(128)S(1)}, s32[8]{0:T(128)}, u32[]{:S(2)}) copy-start(s32[8]{0:T(128)} %constant.276.clone) | copy-start | bytes 100
  0.0 40.8 %copy-start.1 = (bf16[512,512]{1,0:T(8,128)(2,1)S(1)}, bf16[512,512]{1,0:T(8,128)(2,1)}, u32[]{:S(2)}) copy-start(bf16[512,512]{1,0:T(8,128)(2,1)} %param.15) | copy-start | bytes 1572868
  0.0 40.8 %copy-start.2 = (bf16[512,512]{1,0:T(8,128)(2,1)S(1)}, bf16[512,512]{1,0:T(8,128)(2,1)}, u32[]{:S(2)}) copy-start(bf16[512,512]{1,0:T(8,128)(2,1)} %param.14) | copy-start | bytes 1572868
  0.0 41.9 %copy-start.6 = (f32[3,512]{1,0:T(4,128)S(1)}, f32[3,512]{1,0:T(4,128)}, u32[]{:S(2)}) copy-start(f32[3,512]{1,0:T(4,128)} %param.19) | copy-start | bytes 18436
  0.0 42.0 %copy-start.7 = (f32[3,512]{1,0:T(4,128)S(1)}, f32[3,512]{1,0:T(4,128)}, u32[]{:S(2)}) copy-start(f32[3,512]{1,0:T(4,128)} %param.18) | copy-start | bytes 18436
  0.0 42.0 %copy-start.8 = (f32[3,512]{1,0:T(4,128)S(1)}, f32[3,512]{1,0:T(4,128)}, u32[]{:S(2)}) copy-start(f32[3,512]{1,0:T(4,128)} %param.17) | copy-start | bytes 18436
  0.0 42.0 %copy-start = (bf16[256,1024]{1,0:T(8,128)(2,1)S(1)}, bf16[256,1024]{1,0:T(8,128)(2,1)}, u32[]{:S(2)}) copy-start(bf16[256,1024]{1,0:T(8,128)(2,1)} %param.23) | copy-start | bytes 1572868
  2.4 39.6 %all-to-all-start = ((bf16[8,128,512]{1,2,0:T(8,128)(2,1)}), bf16[8,128,512]{1,2,0:T(8,128)(2,1)}, u32[]{:S(2)}, u32[]{:S(2)}) async-start(bf16[8,128,512]{1,2,0:T(8,128)(2,1)} %bitcast.2), calls=%async_computation | async-start | bytes 2097152 | tf_op jit(solution)/shard_map/all_to_all | solution.py:66
  46.1 8.1 %collective-permute-start = (bf16[130,768]{1,0:T(8,128)(2,1)S(1)}, bf16[130,768]{1,0:T(8,128)(2,1)S(1)}, u32[]{:S(2)}, u32[]{:S(2)}) collective-permute-start(bf16[130,768]{1,0:T(8,128)(2,1)S(1)} %convolution_convert_fusion.2), channel_id=1, source_target_pairs={{0,8},{8,16},{16,24},{24,28},{28,20},{20,12},{12,4},{4,0},{1,9},{9... | collective-permute-start | bytes 599048 | tf_op jit(solution)/shard_map/ppermute | solution.py:107
  48.2 8.1 %collective-permute-start.1 = (bf16[130,768]{1,0:T(8,128)(2,1)S(1)}, bf16[130,768]{1,0:T(8,128)(2,1)S(1)}, u32[]{:S(2)}, u32[]{:S(2)}) collective-permute-start(bf16[130,768]{1,0:T(8,128)(2,1)S(1)} %convolution_convert_fusion.1), channel_id=1, source_target_pairs={{8,0},{16,8},{24,16},{28,24},{20,28},{12,20},{4,12},{0,4},{9,1},{1... | collective-permute-start | bytes 599048 | tf_op jit(solution)/shard_map/ppermute | solution.py:108
  48.3 10.2 %collective-permute-start.2 = (bf16[128,1024]{1,0:T(8,128)(2,1)S(1)}, bf16[128,1024]{1,0:T(8,128)(2,1)S(1)}, u32[]{:S(2)}, u32[]{:S(2)}) collective-permute-start(bf16[128,1024]{1,0:T(8,128)(2,1)S(1)} %get-tuple-element.29), channel_id=1, source_target_pairs={{0,8},{8,16},{16,24},{24,28},{28,20},{20,12},{12,4},{4,0},{1,9},{9... | collective-permute-start | bytes 786440 | tf_op jit(solution)/shard_map/ppermute | solution.py:107
  50.2 9.7 %collective-permute-start.3 = (bf16[128,1024]{1,0:T(8,128)(2,1)S(1)}, bf16[128,1024]{1,0:T(8,128)(2,1)S(1)}, u32[]{:S(2)}, u32[]{:S(2)}) collective-permute-start(bf16[128,1024]{1,0:T(8,128)(2,1)S(1)} %get-tuple-element.30), channel_id=1, source_target_pairs={{8,0},{16,8},{24,16},{28,24},{20,28},{12,20},{4,12},{0,4},{9,1},{1... | collective-permute-start | bytes 786440 | tf_op jit(solution)/shard_map/ppermute | solution.py:108
  59.9 7.9 %collective-permute-start.4 = (bf16[130,768]{1,0:T(8,128)(2,1)S(1)}, bf16[130,768]{1,0:T(8,128)(2,1)S(1)}, u32[]{:S(2)}, u32[]{:S(2)}) collective-permute-start(bf16[130,768]{1,0:T(8,128)(2,1)S(1)} %add_convert_fusion.13), channel_id=1, source_target_pairs={{0,8},{8,16},{16,24},{24,28},{28,20},{20,12},{12,4},{4,0},{1,9},{9... | collective-permute-start | bytes 599048 | tf_op jit(solution)/shard_map/ppermute | solution.py:107
  61.3 7.7 %collective-permute-start.5 = (bf16[130,768]{1,0:T(8,128)(2,1)S(1)}, bf16[130,768]{1,0:T(8,128)(2,1)S(1)}, u32[]{:S(2)}, u32[]{:S(2)}) collective-permute-start(bf16[130,768]{1,0:T(8,128)(2,1)S(1)} %add_convert_fusion.12), channel_id=1, source_target_pairs={{8,0},{16,8},{24,16},{28,24},{20,28},{12,20},{4,12},{0,4},{9,1},{1... | collective-permute-start | bytes 599048 | tf_op jit(solution)/shard_map/ppermute | solution.py:108
  61.9 8.7 %collective-permute-start.6 = (bf16[128,1024]{1,0:T(8,128)(2,1)S(1)}, bf16[128,1024]{1,0:T(8,128)(2,1)S(1)}, u32[]{:S(2)}, u32[]{:S(2)}) collective-permute-start(bf16[128,1024]{1,0:T(8,128)(2,1)S(1)} %collective-permute-done.2), channel_id=1, source_target_pairs={{0,8},{8,16},{16,24},{24,28},{28,20},{20,12},{12,4},{4,0},{1,9},{9... | collective-permute-start | bytes 786440 | tf_op jit(solution)/shard_map/ppermute | solution.py:107
  63.4 8.5 %collective-permute-start.7 = (bf16[128,1024]{1,0:T(8,128)(2,1)S(1)}, bf16[128,1024]{1,0:T(8,128)(2,1)S(1)}, u32[]{:S(2)}, u32[]{:S(2)}) collective-permute-start(bf16[128,1024]{1,0:T(8,128)(2,1)S(1)} %collective-permute-done.3), channel_id=1, source_target_pairs={{8,0},{16,8},{24,16},{28,24},{20,28},{12,20},{4,12},{0,4},{9,1},{1... | collective-permute-start | bytes 786440 | tf_op jit(solution)/shard_map/ppermute | solution.py:108
  71.8 6.8 %collective-permute-start.8 = (bf16[130,768]{1,0:T(8,128)(2,1)S(1)}, bf16[130,768]{1,0:T(8,128)(2,1)S(1)}, u32[]{:S(2)}, u32[]{:S(2)}) collective-permute-start(bf16[130,768]{1,0:T(8,128)(2,1)S(1)} %add_convert_fusion.11), channel_id=1, source_target_pairs={{0,8},{8,16},{16,24},{24,28},{28,20},{20,12},{12,4},{4,0},{1,9},{9... | collective-permute-start | bytes 599048 | tf_op jit(solution)/shard_map/ppermute | solution.py:107
  73.3 6.5 %collective-permute-start.9 = (bf16[130,768]{1,0:T(8,128)(2,1)S(1)}, bf16[130,768]{1,0:T(8,128)(2,1)S(1)}, u32[]{:S(2)}, u32[]{:S(2)}) collective-permute-start(bf16[130,768]{1,0:T(8,128)(2,1)S(1)} %add_convert_fusion.10), channel_id=1, source_target_pairs={{8,0},{16,8},{24,16},{28,24},{20,28},{12,20},{4,12},{0,4},{9,1},{1... | collective-permute-start | bytes 599048 | tf_op jit(solution)/shard_map/ppermute | solution.py:108
  73.9 7.7 %collective-permute-start.10 = (bf16[128,1024]{1,0:T(8,128)(2,1)S(1)}, bf16[128,1024]{1,0:T(8,128)(2,1)S(1)}, u32[]{:S(2)}, u32[]{:S(2)}) collective-permute-start(bf16[128,1024]{1,0:T(8,128)(2,1)S(1)} %collective-permute-done.6), channel_id=1, source_target_pairs={{0,8},{8,16},{16,24},{24,28},{28,20},{20,12},{12,4},{4,0},{1,9},{9... | collective-permute-start | bytes 786440 | tf_op jit(solution)/shard_map/ppermute | solution.py:107
  75.3 8.9 %collective-permute-start.11 = (bf16[128,1024]{1,0:T(8,128)(2,1)S(1)}, bf16[128,1024]{1,0:T(8,128)(2,1)S(1)}, u32[]{:S(2)}, u32[]{:S(2)}) collective-permute-start(bf16[128,1024]{1,0:T(8,128)(2,1)S(1)} %collective-permute-done.7), channel_id=1, source_target_pairs={{8,0},{16,8},{24,16},{28,24},{20,28},{12,20},{4,12},{0,4},{9,1},{1... | collective-permute-start | bytes 786440 | tf_op jit(solution)/shard_map/ppermute | solution.py:108
  84.2 8.1 %collective-permute-start.16 = (bf16[130,768]{1,0:T(8,128)(2,1)S(1)}, bf16[130,768]{1,0:T(8,128)(2,1)S(1)}, u32[]{:S(2)}, u32[]{:S(2)}) collective-permute-start(bf16[130,768]{1,0:T(8,128)(2,1)S(1)} %add_convert_fusion.8), channel_id=1, source_target_pairs={{8,0},{16,8},{24,16},{28,24},{20,28},{12,20},{4,12},{0,4},{9,1},{1... | collective-permute-start | bytes 599048 | tf_op jit(solution)/shard_map/ppermute | solution.py:108
  84.8 8.2 %collective-permute-start.12 = (bf16[130,768]{1,0:T(8,128)(2,1)S(1)}, bf16[130,768]{1,0:T(8,128)(2,1)S(1)}, u32[]{:S(2)}, u32[]{:S(2)}) collective-permute-start(bf16[130,768]{1,0:T(8,128)(2,1)S(1)} %add_convert_fusion.9), channel_id=1, source_target_pairs={{0,8},{8,16},{16,24},{24,28},{28,20},{20,12},{12,4},{4,0},{1,9},{9... | collective-permute-start | bytes 599048 | tf_op jit(solution)/shard_map/ppermute | solution.py:107
  86.3 12.1 %collective-permute-start.27 = (bf16[128,1024]{1,0:T(8,128)(2,1)S(1)}, bf16[128,1024]{1,0:T(8,128)(2,1)S(1)}, u32[]{:S(2)}, u32[]{:S(2)}) collective-permute-start(bf16[128,1024]{1,0:T(8,128)(2,1)S(1)} %collective-permute-done.10), channel_id=1, source_target_pairs={{0,8},{8,16},{16,24},{24,28},{28,20},{20,12},{12,4},{4,0},{1,9},{9... | collective-permute-start | bytes 786440 | tf_op jit(solution)/shard_map/ppermute | solution.py:107
  87.9 12.0 %collective-permute-start.28 = (bf16[128,1024]{1,0:T(8,128)(2,1)S(1)}, bf16[128,1024]{1,0:T(8,128)(2,1)S(1)}, u32[]{:S(2)}, u32[]{:S(2)}) collective-permute-start(bf16[128,1024]{1,0:T(8,128)(2,1)S(1)} %collective-permute-done.11), channel_id=1, source_target_pairs={{8,0},{16,8},{24,16},{28,24},{20,28},{12,20},{4,12},{0,4},{9,1},{1... | collective-permute-start | bytes 786440 | tf_op jit(solution)/shard_map/ppermute | solution.py:108
  92.4 10.0 %collective-permute-start.17 = (bf16[130,768]{1,0:T(8,128)(2,1)S(1)}, bf16[130,768]{1,0:T(8,128)(2,1)S(1)}, u32[]{:S(2)}, u32[]{:S(2)}) collective-permute-start(bf16[130,768]{1,0:T(8,128)(2,1)S(1)} %add_convert_fusion.3), channel_id=1, source_target_pairs={{8,0},{16,8},{24,16},{28,24},{20,28},{12,20},{4,12},{0,4},{9,1},{1... | collective-permute-start | bytes 599048 | tf_op jit(solution)/shard_map/ppermute | solution.py:112
  93.1 10.1 %collective-permute-start.13 = (bf16[130,768]{1,0:T(8,128)(2,1)S(1)}, bf16[130,768]{1,0:T(8,128)(2,1)S(1)}, u32[]{:S(2)}, u32[]{:S(2)}) collective-permute-start(bf16[130,768]{1,0:T(8,128)(2,1)S(1)} %add_convert_fusion.7), channel_id=1, source_target_pairs={{0,8},{8,16},{16,24},{24,28},{28,20},{20,12},{12,4},{4,0},{1,9},{9... | collective-permute-start | bytes 599048 | tf_op jit(solution)/shard_map/ppermute | solution.py:111
  98.4 10.1 %collective-permute-start.29 = (bf16[128,1024]{1,0:T(8,128)(2,1)S(1)}, bf16[128,1024]{1,0:T(8,128)(2,1)S(1)}, u32[]{:S(2)}, u32[]{:S(2)}) collective-permute-start(bf16[128,1024]{1,0:T(8,128)(2,1)S(1)} %collective-permute-done.27), channel_id=1, source_target_pairs={{0,8},{8,16},{16,24},{24,28},{28,20},{20,12},{12,4},{4,0},{1,9},{9... | collective-permute-start | bytes 786440 | tf_op jit(solution)/shard_map/ppermute | solution.py:116
  99.9 10.1 %collective-permute-start.30 = (bf16[128,1024]{1,0:T(8,128)(2,1)S(1)}, bf16[128,1024]{1,0:T(8,128)(2,1)S(1)}, u32[]{:S(2)}, u32[]{:S(2)}) collective-permute-start(bf16[128,1024]{1,0:T(8,128)(2,1)S(1)} %collective-permute-done.28), channel_id=1, source_target_pairs={{8,0},{16,8},{24,16},{28,24},{20,28},{12,20},{4,12},{0,4},{9,1},{1... | collective-permute-start | bytes 786440 | tf_op jit(solution)/shard_map/ppermute | solution.py:117
  102.5 16.7 %copy-start.3 = (f32[16,512]{1,0:T(8,128)S(1)}, f32[16,512]{1,0:T(8,128)}, u32[]{:S(2)}) copy-start(f32[16,512]{1,0:T(8,128)} %param.20) | copy-start | bytes 98308
  102.5 9.8 %collective-permute-start.18 = (bf16[130,768]{1,0:T(8,128)(2,1)S(1)}, bf16[130,768]{1,0:T(8,128)(2,1)S(1)}, u32[]{:S(2)}, u32[]{:S(2)}) collective-permute-start(bf16[130,768]{1,0:T(8,128)(2,1)S(1)} %add_convert_fusion.2), channel_id=1, source_target_pairs={{8,0},{16,8},{24,16},{28,24},{20,28},{12,20},{4,12},{0,4},{9,1},{1... | collective-permute-start | bytes 599048 | tf_op jit(solution)/shard_map/ppermute | solution.py:112
  103.2 9.8 %collective-permute-start.14 = (bf16[130,768]{1,0:T(8,128)(2,1)S(1)}, bf16[130,768]{1,0:T(8,128)(2,1)S(1)}, u32[]{:S(2)}, u32[]{:S(2)}) collective-permute-start(bf16[130,768]{1,0:T(8,128)(2,1)S(1)} %add_convert_fusion.6), channel_id=1, source_target_pairs={{0,8},{8,16},{16,24},{24,28},{28,20},{20,12},{12,4},{4,0},{1,9},{9... | collective-permute-start | bytes 599048 | tf_op jit(solution)/shard_map/ppermute | solution.py:111
  108.5 17.3 %collective-permute-start.31 = (bf16[128,1024]{1,0:T(8,128)(2,1)S(1)}, bf16[128,1024]{1,0:T(8,128)(2,1)S(1)}, u32[]{:S(2)}, u32[]{:S(2)}) collective-permute-start(bf16[128,1024]{1,0:T(8,128)(2,1)S(1)} %collective-permute-done.29), channel_id=1, source_target_pairs={{0,8},{8,16},{16,24},{24,28},{28,20},{20,12},{12,4},{4,0},{1,9},{9... | collective-permute-start | bytes 786440 | tf_op jit(solution)/shard_map/ppermute | solution.py:116
  110.0 18.5 %collective-permute-start.32 = (bf16[128,1024]{1,0:T(8,128)(2,1)S(1)}, bf16[128,1024]{1,0:T(8,128)(2,1)S(1)}, u32[]{:S(2)}, u32[]{:S(2)}) collective-permute-start(bf16[128,1024]{1,0:T(8,128)(2,1)S(1)} %collective-permute-done.30), channel_id=1, source_target_pairs={{8,0},{16,8},{24,16},{28,24},{20,28},{12,20},{4,12},{0,4},{9,1},{1... | collective-permute-start | bytes 786440 | tf_op jit(solution)/shard_map/ppermute | solution.py:117
  112.3 25.2 %copy-start.5 = (f32[16,512]{1,0:T(8,128)S(1)}, f32[16,512]{1,0:T(8,128)}, u32[]{:S(2)}) copy-start(f32[16,512]{1,0:T(8,128)} %param.21) | copy-start | bytes 98308
  112.3 6.2 %collective-permute-start.19 = (bf16[130,768]{1,0:T(8,128)(2,1)S(1)}, bf16[130,768]{1,0:T(8,128)(2,1)S(1)}, u32[]{:S(2)}, u32[]{:S(2)}) collective-permute-start(bf16[130,768]{1,0:T(8,128)(2,1)S(1)} %add_convert_fusion.1), channel_id=1, source_target_pairs={{8,0},{16,8},{24,16},{28,24},{20,28},{12,20},{4,12},{0,4},{9,1},{1... | collective-permute-start | bytes 599048 | tf_op jit(solution)/shard_map/ppermute | solution.py:112
  113.0 5.9 %collective-permute-start.15 = (bf16[130,768]{1,0:T(8,128)(2,1)S(1)}, bf16[130,768]{1,0:T(8,128)(2,1)S(1)}, u32[]{:S(2)}, u32[]{:S(2)}) collective-permute-start(bf16[130,768]{1,0:T(8,128)(2,1)S(1)} %add_convert_fusion.5), channel_id=1, source_target_pairs={{0,8},{8,16},{16,24},{24,28},{28,20},{20,12},{12,4},{4,0},{1,9},{9... | collective-permute-start | bytes 599048 | tf_op jit(solution)/shard_map/ppermute | solution.py:111
  120.0 11.0 %collective-permute-start.26 = (f32[16,512]{1,0:T(8,128)S(1)}, f32[16,512]{1,0:T(8,128)S(1)}, u32[]{:S(2)}, u32[]{:S(2)}) collective-permute-start(f32[16,512]{1,0:T(8,128)S(1)} %exponential_multiply_fusion.5), channel_id=1, source_target_pairs={{0,28},{1,29},{2,30},{3,31}} | collective-permute-start | bytes 98312 | tf_op jit(solution)/shard_map/ppermute | solution.py:33
  124.5 7.7 %collective-permute-start.25 = (f32[16,512]{1,0:T(8,128)S(1)}, f32[16,512]{1,0:T(8,128)S(1)}, u32[]{:S(2)}, u32[]{:S(2)}) collective-permute-start(f32[16,512]{1,0:T(8,128)S(1)} %exponential_multiply_fusion.5), channel_id=1, source_target_pairs={{0,24},{4,28},{1,25},{5,29},{2,26},{6,30},{3,27},{7,31}} | collective-permute-start | bytes 98312 | tf_op jit(solution)/shard_map/ppermute | solution.py:33
  125.9 9.6 %collective-permute-start.24 = (f32[16,512]{1,0:T(8,128)S(1)}, f32[16,512]{1,0:T(8,128)S(1)}, u32[]{:S(2)}, u32[]{:S(2)}) collective-permute-start(f32[16,512]{1,0:T(8,128)S(1)} %exponential_multiply_fusion.5), channel_id=1, source_target_pairs={{0,20},{4,24},{8,28},{1,21},{5,25},{9,29},{2,22},{6,26},{10,30},{3... | collective-permute-start | bytes 98312 | tf_op jit(solution)/shard_map/ppermute | solution.py:33
  127.2 8.3 %collective-permute-start.23 = (f32[16,512]{1,0:T(8,128)S(1)}, f32[16,512]{1,0:T(8,128)S(1)}, u32[]{:S(2)}, u32[]{:S(2)}) collective-permute-start(f32[16,512]{1,0:T(8,128)S(1)} %exponential_multiply_fusion.5), channel_id=1, source_target_pairs={{0,16},{4,20},{8,24},{12,28},{1,17},{5,21},{9,25},{13,29},{2,18},{... | collective-permute-start | bytes 98312 | tf_op jit(solution)/shard_map/ppermute | solution.py:33
  128.5 9.0 %collective-permute-start.22 = (f32[16,512]{1,0:T(8,128)S(1)}, f32[16,512]{1,0:T(8,128)S(1)}, u32[]{:S(2)}, u32[]{:S(2)}) collective-permute-start(f32[16,512]{1,0:T(8,128)S(1)} %exponential_multiply_fusion.5), channel_id=1, source_target_pairs={{0,12},{4,16},{8,20},{12,24},{16,28},{1,13},{5,17},{9,21},{13,25},... | collective-permute-start | bytes 98312 | tf_op jit(solution)/shard_map/ppermute | solution.py:33
  131.0 6.5 %collective-permute-start.21 = (f32[16,512]{1,0:T(8,128)S(1)}, f32[16,512]{1,0:T(8,128)S(1)}, u32[]{:S(2)}, u32[]{:S(2)}) collective-permute-start(f32[16,512]{1,0:T(8,128)S(1)} %exponential_multiply_fusion.5), channel_id=1, source_target_pairs={{0,8},{4,12},{8,16},{12,20},{16,24},{20,28},{1,9},{5,13},{9,17},{1... | collective-permute-start | bytes 98312 | tf_op jit(solution)/shard_map/ppermute | solution.py:33
  132.3 5.2 %collective-permute-start.20 = (f32[16,512]{1,0:T(8,128)S(1)}, f32[16,512]{1,0:T(8,128)S(1)}, u32[]{:S(2)}, u32[]{:S(2)}) collective-permute-start(f32[16,512]{1,0:T(8,128)S(1)} %exponential_multiply_fusion.5), channel_id=1, source_target_pairs={{0,4},{4,8},{8,12},{12,16},{16,20},{20,24},{24,28},{1,5},{5,9},{9,... | collective-permute-start | bytes 98312 | tf_op jit(solution)/shard_map/ppermute | solution.py:33
  135.4 12.8 %collective-permute-start.33 = (bf16[128,1024]{1,0:T(8,128)(2,1)S(1)}, bf16[128,1024]{1,0:T(8,128)(2,1)S(1)}, u32[]{:S(2)}, u32[]{:S(2)}) collective-permute-start(bf16[128,1024]{1,0:T(8,128)(2,1)S(1)} %collective-permute-done.31), channel_id=1, source_target_pairs={{0,8},{8,16},{16,24},{24,28},{28,20},{20,12},{12,4},{4,0},{1,9},{9... | collective-permute-start | bytes 786440 | tf_op jit(solution)/shard_map/ppermute | solution.py:116
  135.5 12.7 %collective-permute-start.34 = (bf16[128,1024]{1,0:T(8,128)(2,1)S(1)}, bf16[128,1024]{1,0:T(8,128)(2,1)S(1)}, u32[]{:S(2)}, u32[]{:S(2)}) collective-permute-start(bf16[128,1024]{1,0:T(8,128)(2,1)S(1)} %collective-permute-done.32), channel_id=1, source_target_pairs={{8,0},{16,8},{24,16},{28,24},{20,28},{12,20},{4,12},{0,4},{9,1},{1... | collective-permute-start | bytes 786440 | tf_op jit(solution)/shard_map/ppermute | solution.py:117
  137.6 3.1 %copy-start.9 = (f32[512]{0:T(512)S(1)}, f32[512]{0:T(512)}, u32[]{:S(2)}) copy-start(f32[512]{0:T(512)} %param.22) | copy-start | bytes 6148

commit v16 on v15

--- a/solution.py
+++ b/solution.py
@@ -18,15 +18,14 @@
     decay = jnp.exp(-rates[:, None, :] * times)
     lifted = grow * signal[None]
     rows = jnp.arange(length, dtype=jnp.int32)
-    lower = (rows[:, None] >= rows[None, :]).astype(jnp.float32)
+    lower = (rows[:, None] >= rows[None, :]).astype(jnp.bfloat16)
     lower = jnp.broadcast_to(lower[None], (order, length, length))
+    lifted_hi = lifted.astype(jnp.bfloat16)
+    lifted_lo = (lifted - lifted_hi.astype(jnp.float32)).astype(jnp.bfloat16)
+    dims = (((2,), (1,)), ((0,), (0,)))
     running = lax.dot_general(
-        lower,
-        lifted,
-        (((2,), (1,)), ((0,), (0,))),
-        precision=lax.Precision.HIGH,
-        preferred_element_type=jnp.float32,
-    )
+        lower, lifted_hi, dims, preferred_element_type=jnp.float32
+    ) + lax.dot_general(lower, lifted_lo, dims, preferred_element_type=jnp.float32)
     end_state = jnp.sum(lifted, axis=1) * jnp.exp(-rates * (length - 1))
     carried = jnp.zeros_like(end_state)
     for shift in range(1, ctx_count):

time: 150 us -> 151 us (level)
    dot_general x1 -> x2, matrix products: 3.1 us -> 3.26 us  [the longest x1 2.13 us: modal_long_conv(): lax.dot_general(lower, lifted_hi, dims, preferred_element_type=jnp.float32)]
  transfers between devices with their start and end apart: 36 -> 36, of which waited for: 19 -> 20; matrix products, arithmetic and copies ran while one was open for 7% -> 7% of each run, Pallas kernels for 0% -> 0%
where the time goes in v16:
time: 151 us; the launch traced here: 150 us
  starting transfers between devices  51.4 us (34%)
  waiting for transfers between devices  42.2 us (28%)
  between operations  30.3 us (20%)
  matrix products  9.17 us (6%)
  blocking collectives  7.18 us (5%)
  local copies, waits for them, and re-layouts  6.49 us (4%)
  other arithmetic  3.03 us (2%)
    ppermute x8, waiting for transfers between devices, body(): up, w_up = lax.ppermute((sent[0], sent[2]), 'ctx', perm=fwd)  17.2 us
    ppermute x7, starting transfers between devices, modal_long_conv(): lax.ppermute(end_state, 'ctx', perm=[(i, i + shift) for i in range(ctx_co...  15.3 us
    ppermute x8, waiting for transfers between devices, body(): down, w_low = lax.ppermute((sent[1], sent[3]), 'ctx', perm=bwd)  13.3 us
    ppermute x8, starting transfers between devices, body(): up, w_up = lax.ppermute((sent[0], sent[2]), 'ctx', perm=fwd)  13 us
    all_to_all x1, starting transfers between devices, body(): lax.all_to_all(by_dest, 'ctx', split_axis=0, concat_axis=0, tiled=True)  7.29 us
    all_gather x1, blocking collectives, body(): features = lax.all_gather(gated, 'tp', axis=1, tiled=True)  7.18 us
    ppermute x3, waiting for transfers between devices, body(): down = lax.ppermute(down.astype(jnp.bfloat16), 'ctx', perm=bwd)  6.99 us
    ppermute x3, starting transfers between devices, body(): up = lax.ppermute(up.astype(jnp.bfloat16), 'ctx', perm=fwd)  4.53 us
  transfers between devices with their start and end apart: 36, of which 20 were waited for; matrix products, arithmetic and copies ran while one was open for 7% of the time, Pallas kernels for 0%

profile of v16, /device:TPU:0, one launch (start us, length us, event | category | flops | bytes accessed | tf_op | source)
XLA Modules:
  0.0 149.8 jit_solution(3050106105826572851)
XLA Ops:
  0.0 2.4 %copy.14 = bf16[128,4096]{0,1:T(8,128)(2,1)} copy(bf16[128,4096]{1,0:T(8,128)(2,1)} %param.13) | data formatting | bytes 2097152 | tf_op args[0]
  2.4 7.3 %all-to-all-start = ((bf16[8,128,512]{1,2,0:T(8,128)(2,1)}), bf16[8,128,512]{1,2,0:T(8,128)(2,1)}, u32[]{:S(2)}, u32[]{:S(2)}) async-start(bf16[8,128,512]{1,2,0:T(8,128)(2,1)} %bitcast.2), calls=%async_computation | async-start | bytes 2097152 | tf_op jit(solution)/shard_map/all_to_all | solution.py:65
  21.0 0.8 fusion.78
  40.8 1.1 pad_maximum_fusion.1
  42.1 1.5 copy.15
  46.1 2.1 %collective-permute-start = (bf16[130,768]{1,0:T(8,128)(2,1)S(1)}, bf16[130,768]{1,0:T(8,128)(2,1)S(1)}, u32[]{:S(2)}, u32[]{:S(2)}) collective-permute-start(bf16[130,768]{1,0:T(8,128)(2,1)S(1)} %convolution_convert_fusion.2), channel_id=1, source_target_pairs={{0,8},{8,16},{16,24},{24,28},{28,20},{20,12},{12,4},{4,0},{1,9},{9... | collective-permute-start | bytes 599048 | tf_op jit(solution)/shard_map/ppermute | solution.py:106
  48.3 2.0 %collective-permute-start.2 = (bf16[128,1024]{1,0:T(8,128)(2,1)S(1)}, bf16[128,1024]{1,0:T(8,128)(2,1)S(1)}, u32[]{:S(2)}, u32[]{:S(2)}) collective-permute-start(bf16[128,1024]{1,0:T(8,128)(2,1)S(1)} %get-tuple-element.29), channel_id=1, source_target_pairs={{0,8},{8,16},{16,24},{24,28},{28,20},{20,12},{12,4},{4,0},{1,9},{9... | collective-permute-start | bytes 786440 | tf_op jit(solution)/shard_map/ppermute | solution.py:106
  52.6 1.7 %collective-permute-done = bf16[130,768]{1,0:T(8,128)(2,1)S(1)} collective-permute-done((bf16[130,768]{1,0:T(8,128)(2,1)S(1)}, bf16[130,768]{1,0:T(8,128)(2,1)S(1)}, u32[]{:S(2)}, u32[]{:S(2)}) %collective-permute-start) | collective-permute-done | bytes 199712 | tf_op jit(solution)/shard_map/ppermute | solution.py:106
  54.6 1.7 %collective-permute-done.1 = bf16[130,768]{1,0:T(8,128)(2,1)S(1)} collective-permute-done((bf16[130,768]{1,0:T(8,128)(2,1)S(1)}, bf16[130,768]{1,0:T(8,128)(2,1)S(1)}, u32[]{:S(2)}, u32[]{:S(2)}) %collective-permute-start.1) | collective-permute-done | bytes 199712 | tf_op jit(solution)/shard_map/ppermute | solution.py:107
  56.6 1.8 %collective-permute-done.2 = bf16[128,1024]{1,0:T(8,128)(2,1)S(1)} collective-permute-done((bf16[128,1024]{1,0:T(8,128)(2,1)S(1)}, bf16[128,1024]{1,0:T(8,128)(2,1)S(1)}, u32[]{:S(2)}, u32[]{:S(2)}) %collective-permute-start.2) | collective-permute-done | bytes 262176 | tf_op jit(solution)/shard_map/ppermute | solution.py:106
  58.4 1.4 collective-permute-done.3
  59.9 1.5 collective-permute-start.4
  61.9 1.5 collective-permute-start.6
  64.0 3.8 %collective-permute-done.4 = bf16[130,768]{1,0:T(8,128)(2,1)S(1)} collective-permute-done((bf16[130,768]{1,0:T(8,128)(2,1)S(1)}, bf16[130,768]{1,0:T(8,128)(2,1)S(1)}, u32[]{:S(2)}, u32[]{:S(2)}) %collective-permute-start.4) | collective-permute-done | bytes 199712 | tf_op jit(solution)/shard_map/ppermute | solution.py:106
  67.9 1.1 collective-permute-done.5
  69.1 1.6 %collective-permute-done.6 = bf16[128,1024]{1,0:T(8,128)(2,1)S(1)} collective-permute-done((bf16[128,1024]{1,0:T(8,128)(2,1)S(1)}, bf16[128,1024]{1,0:T(8,128)(2,1)S(1)}, u32[]{:S(2)}, u32[]{:S(2)}) %collective-permute-start.6) | collective-permute-done | bytes 262176 | tf_op jit(solution)/shard_map/ppermute | solution.py:106
  70.6 1.2 collective-permute-done.7
  71.8 1.5 collective-permute-start.8
  73.9 1.5 collective-permute-start.10
  75.9 2.6 %collective-permute-done.8 = bf16[130,768]{1,0:T(8,128)(2,1)S(1)} collective-permute-done((bf16[130,768]{1,0:T(8,128)(2,1)S(1)}, bf16[130,768]{1,0:T(8,128)(2,1)S(1)}, u32[]{:S(2)}, u32[]{:S(2)}) %collective-permute-start.8) | collective-permute-done | bytes 199712 | tf_op jit(solution)/shard_map/ppermute | solution.py:106
  78.6 1.1 collective-permute-done.9
  79.8 1.8 %collective-permute-done.10 = bf16[128,1024]{1,0:T(8,128)(2,1)S(1)} collective-permute-done((bf16[128,1024]{1,0:T(8,128)(2,1)S(1)}, bf16[128,1024]{1,0:T(8,128)(2,1)S(1)}, u32[]{:S(2)}, u32[]{:S(2)}) %collective-permute-start.10) | collective-permute-done | bytes 262176 | tf_op jit(solution)/shard_map/ppermute | solution.py:106
  81.6 2.6 %collective-permute-done.11 = bf16[128,1024]{1,0:T(8,128)(2,1)S(1)} collective-permute-done((bf16[128,1024]{1,0:T(8,128)(2,1)S(1)}, bf16[128,1024]{1,0:T(8,128)(2,1)S(1)}, u32[]{:S(2)}, u32[]{:S(2)}) %collective-permute-start.11) | collective-permute-done | bytes 262176 | tf_op jit(solution)/shard_map/ppermute | solution.py:107
  84.8 1.5 collective-permute-start.12
  86.3 1.6 %collective-permute-start.27 = (bf16[128,1024]{1,0:T(8,128)(2,1)S(1)}, bf16[128,1024]{1,0:T(8,128)(2,1)S(1)}, u32[]{:S(2)}, u32[]{:S(2)}) collective-permute-start(bf16[128,1024]{1,0:T(8,128)(2,1)S(1)} %collective-permute-done.10), channel_id=1, source_target_pairs={{0,8},{8,16},{16,24},{24,28},{28,20},{20,12},{12,4},{4,0},{1,9},{9... | collective-permute-start | bytes 786440 | tf_op jit(solution)/shard_map/ppermute | solution.py:106
  88.3 4.0 %collective-permute-done.16 = bf16[130,768]{1,0:T(8,128)(2,1)S(1)} collective-permute-done((bf16[130,768]{1,0:T(8,128)(2,1)S(1)}, bf16[130,768]{1,0:T(8,128)(2,1)S(1)}, u32[]{:S(2)}, u32[]{:S(2)}) %collective-permute-start.16) | collective-permute-done | bytes 199712 | tf_op jit(solution)/shard_map/ppermute | solution.py:107
  93.1 1.5 %collective-permute-start.13 = (bf16[130,768]{1,0:T(8,128)(2,1)S(1)}, bf16[130,768]{1,0:T(8,128)(2,1)S(1)}, u32[]{:S(2)}, u32[]{:S(2)}) collective-permute-start(bf16[130,768]{1,0:T(8,128)(2,1)S(1)} %add_convert_fusion.7), channel_id=1, source_target_pairs={{0,8},{8,16},{16,24},{24,28},{28,20},{20,12},{12,4},{4,0},{1,9},{9... | collective-permute-start | bytes 599048 | tf_op jit(solution)/shard_map/ppermute | solution.py:110
  94.6 3.8 %collective-permute-done.27 = bf16[128,1024]{1,0:T(8,128)(2,1)S(1)} collective-permute-done((bf16[128,1024]{1,0:T(8,128)(2,1)S(1)}, bf16[128,1024]{1,0:T(8,128)(2,1)S(1)}, u32[]{:S(2)}, u32[]{:S(2)}) %collective-permute-start.27) | collective-permute-done | bytes 262176 | tf_op jit(solution)/shard_map/ppermute | solution.py:106
  98.4 1.5 collective-permute-start.29
  100.5 1.9 %collective-permute-done.17 = bf16[130,768]{1,0:T(8,128)(2,1)S(1)} collective-permute-done((bf16[130,768]{1,0:T(8,128)(2,1)S(1)}, bf16[130,768]{1,0:T(8,128)(2,1)S(1)}, u32[]{:S(2)}, u32[]{:S(2)}) %collective-permute-start.17) | collective-permute-done | bytes 199712 | tf_op jit(solution)/shard_map/ppermute | solution.py:111
  103.2 1.5 %collective-permute-start.14 = (bf16[130,768]{1,0:T(8,128)(2,1)S(1)}, bf16[130,768]{1,0:T(8,128)(2,1)S(1)}, u32[]{:S(2)}, u32[]{:S(2)}) collective-permute-start(bf16[130,768]{1,0:T(8,128)(2,1)S(1)} %add_convert_fusion.6), channel_id=1, source_target_pairs={{0,8},{8,16},{16,24},{24,28},{28,20},{20,12},{12,4},{4,0},{1,9},{9... | collective-permute-start | bytes 599048 | tf_op jit(solution)/shard_map/ppermute | solution.py:110
  104.7 3.8 %collective-permute-done.29 = bf16[128,1024]{1,0:T(8,128)(2,1)S(1)} collective-permute-done((bf16[128,1024]{1,0:T(8,128)(2,1)S(1)}, bf16[128,1024]{1,0:T(8,128)(2,1)S(1)}, u32[]{:S(2)}, u32[]{:S(2)}) %collective-permute-start.29) | collective-permute-done | bytes 262176 | tf_op jit(solution)/shard_map/ppermute | solution.py:115
  108.5 1.5 collective-permute-start.31
  110.6 1.7 %collective-permute-done.18 = bf16[130,768]{1,0:T(8,128)(2,1)S(1)} collective-permute-done((bf16[130,768]{1,0:T(8,128)(2,1)S(1)}, bf16[130,768]{1,0:T(8,128)(2,1)S(1)}, u32[]{:S(2)}, u32[]{:S(2)}) %collective-permute-start.18) | collective-permute-done | bytes 199712 | tf_op jit(solution)/shard_map/ppermute | solution.py:111
  113.0 1.5 %collective-permute-start.15 = (bf16[130,768]{1,0:T(8,128)(2,1)S(1)}, bf16[130,768]{1,0:T(8,128)(2,1)S(1)}, u32[]{:S(2)}, u32[]{:S(2)}) collective-permute-start(bf16[130,768]{1,0:T(8,128)(2,1)S(1)} %add_convert_fusion.5), channel_id=1, source_target_pairs={{0,8},{8,16},{16,24},{24,28},{28,20},{20,12},{12,4},{4,0},{1,9},{9... | collective-permute-start | bytes 599048 | tf_op jit(solution)/shard_map/ppermute | solution.py:110
  115.2 3.4 %collective-permute-done.19 = bf16[130,768]{1,0:T(8,128)(2,1)S(1)} collective-permute-done((bf16[130,768]{1,0:T(8,128)(2,1)S(1)}, bf16[130,768]{1,0:T(8,128)(2,1)S(1)}, u32[]{:S(2)}, u32[]{:S(2)}) %collective-permute-start.19) | collective-permute-done | bytes 199712 | tf_op jit(solution)/shard_map/ppermute | solution.py:111
  120.0 4.5 %collective-permute-start.26 = (f32[16,512]{1,0:T(8,128)S(1)}, f32[16,512]{1,0:T(8,128)S(1)}, u32[]{:S(2)}, u32[]{:S(2)}) collective-permute-start(f32[16,512]{1,0:T(8,128)S(1)} %exponential_multiply_fusion.2), channel_id=1, source_target_pairs={{0,28},{1,29},{2,30},{3,31}} | collective-permute-start | bytes 98312 | tf_op jit(solution)/shard_map/ppermute | solution.py:32
  124.5 1.3 collective-permute-start.25
  125.8 1.3 collective-permute-start.24
  127.1 1.3 collective-permute-start.23
  128.4 2.5 %collective-permute-start.22 = (f32[16,512]{1,0:T(8,128)S(1)}, f32[16,512]{1,0:T(8,128)S(1)}, u32[]{:S(2)}, u32[]{:S(2)}) collective-permute-start(f32[16,512]{1,0:T(8,128)S(1)} %exponential_multiply_fusion.2), channel_id=1, source_target_pairs={{0,12},{4,16},{8,20},{12,24},{16,28},{1,13},{5,17},{9,21},{13,25},... | collective-permute-start | bytes 98312 | tf_op jit(solution)/shard_map/ppermute | solution.py:32
  130.9 1.3 collective-permute-start.21
  132.2 3.1 %collective-permute-start.20 = (f32[16,512]{1,0:T(8,128)S(1)}, f32[16,512]{1,0:T(8,128)S(1)}, u32[]{:S(2)}, u32[]{:S(2)}) collective-permute-start(f32[16,512]{1,0:T(8,128)S(1)} %exponential_multiply_fusion.2), channel_id=1, source_target_pairs={{0,4},{4,8},{8,12},{12,16},{16,20},{20,24},{24,28},{1,5},{5,9},{9,... | collective-permute-start | bytes 98312 | tf_op jit(solution)/shard_map/ppermute | solution.py:32
  135.3 1.1 fusion.4
  136.6 2.0 %collective-permute-start.34 = (bf16[128,1024]{1,0:T(8,128)(2,1)S(1)}, bf16[128,1024]{1,0:T(8,128)(2,1)S(1)}, u32[]{:S(2)}, u32[]{:S(2)}) collective-permute-start(bf16[128,1024]{1,0:T(8,128)(2,1)S(1)} %collective-permute-done.32), channel_id=1, source_target_pairs={{8,0},{16,8},{24,16},{28,24},{20,28},{12,20},{4,12},{0,4},{9,1},{1... | collective-permute-start | bytes 786440 | tf_op jit(solution)/shard_map/ppermute | solution.py:116
  138.7 2.1 %multiply_reduce_fusion = f32[128,512]{1,0:T(8,128)S(1)} fusion(f32[16,128,512]{2,1,0:T(8,128)S(1)} %fusion.4, f32[16,512]{1,0:T(8,128)S(1)} %get-tuple-element.48, f32[16,512]{1,0:T(8,128)S(1)} %get-tuple-element.49, f32[16,512]{1,0:T(8,128)S(1)} %get-tuple-element.47, f32[128,512]{1,0:T(8,128)S(1)} %fusion.56, f32[16,512]{1,0:T(8,128)S(1)} %copy-done.3, ...), kind=kOutput, calls=%fused_computation | convolution fusion | flops 277807104 | bytes 4882432 | tf_op jit(solution)/shard_map/dot_general | solution.py:26
  141.1 7.2 %all_gather.3 = bf16[128,2048]{1,0:T(8,128)(2,1)S(1)} all-gather(bf16[128,512]{1,0:T(8,128)(2,1)S(1)} %multiply_convert_fusion), channel_id=1, replica_groups=mesh['ctx'=8,'tp'=4] {'tp'}, dimensions={1}, use_global_device_ids=true | all-gather | bytes 655360 | tf_op jit(solution)/shard_map/all_gather | solution.py:130
  148.4 1.4 convolution_convert_fusion
  (112 shorter events, 15.5 us)
Async XLA Ops:
  0.0 9.7 %copy-start.10 = (s32[8]{0:T(128)S(1)}, s32[8]{0:T(128)}, u32[]{:S(2)}) copy-start(s32[8]{0:T(128)} %constant.275.clone) | copy-start | bytes 100
  0.0 21.0 %copy-start.4 = (s32[8]{0:T(128)S(1)}, s32[8]{0:T(128)}, u32[]{:S(2)}) copy-start(s32[8]{0:T(128)} %constant.276.clone) | copy-start | bytes 100
  0.0 40.8 %copy-start.1 = (bf16[512,512]{1,0:T(8,128)(2,1)S(1)}, bf16[512,512]{1,0:T(8,128)(2,1)}, u32[]{:S(2)}) copy-start(bf16[512,512]{1,0:T(8,128)(2,1)} %param.15) | copy-start | bytes 1572868
  0.0 40.8 %copy-start.2 = (bf16[512,512]{1,0:T(8,128)(2,1)S(1)}, bf16[512,512]{1,0:T(8,128)(2,1)}, u32[]{:S(2)}) copy-start(bf16[512,512]{1,0:T(8,128)(2,1)} %param.14) | copy-start | bytes 1572868
  0.0 41.9 %copy-start.6 = (f32[3,512]{1,0:T(4,128)S(1)}, f32[3,512]{1,0:T(4,128)}, u32[]{:S(2)}) copy-start(f32[3,512]{1,0:T(4,128)} %param.19) | copy-start | bytes 18436
  0.0 42.0 %copy-start.7 = (f32[3,512]{1,0:T(4,128)S(1)}, f32[3,512]{1,0:T(4,128)}, u32[]{:S(2)}) copy-start(f32[3,512]{1,0:T(4,128)} %param.18) | copy-start | bytes 18436
  0.0 42.0 %copy-start.8 = (f32[3,512]{1,0:T(4,128)S(1)}, f32[3,512]{1,0:T(4,128)}, u32[]{:S(2)}) copy-start(f32[3,512]{1,0:T(4,128)} %param.17) | copy-start | bytes 18436
  0.0 42.0 %copy-start = (bf16[256,1024]{1,0:T(8,128)(2,1)S(1)}, bf16[256,1024]{1,0:T(8,128)(2,1)}, u32[]{:S(2)}) copy-start(bf16[256,1024]{1,0:T(8,128)(2,1)} %param.23) | copy-start | bytes 1572868
  2.4 39.6 %all-to-all-start = ((bf16[8,128,512]{1,2,0:T(8,128)(2,1)}), bf16[8,128,512]{1,2,0:T(8,128)(2,1)}, u32[]{:S(2)}, u32[]{:S(2)}) async-start(bf16[8,128,512]{1,2,0:T(8,128)(2,1)} %bitcast.2), calls=%async_computation | async-start | bytes 2097152 | tf_op jit(solution)/shard_map/all_to_all | solution.py:65
  46.1 8.1 %collective-permute-start = (bf16[130,768]{1,0:T(8,128)(2,1)S(1)}, bf16[130,768]{1,0:T(8,128)(2,1)S(1)}, u32[]{:S(2)}, u32[]{:S(2)}) collective-permute-start(bf16[130,768]{1,0:T(8,128)(2,1)S(1)} %convolution_convert_fusion.2), channel_id=1, source_target_pairs={{0,8},{8,16},{16,24},{24,28},{28,20},{20,12},{12,4},{4,0},{1,9},{9... | collective-permute-start | bytes 599048 | tf_op jit(solution)/shard_map/ppermute | solution.py:106
  48.2 8.1 %collective-permute-start.1 = (bf16[130,768]{1,0:T(8,128)(2,1)S(1)}, bf16[130,768]{1,0:T(8,128)(2,1)S(1)}, u32[]{:S(2)}, u32[]{:S(2)}) collective-permute-start(bf16[130,768]{1,0:T(8,128)(2,1)S(1)} %convolution_convert_fusion.1), channel_id=1, source_target_pairs={{8,0},{16,8},{24,16},{28,24},{20,28},{12,20},{4,12},{0,4},{9,1},{1... | collective-permute-start | bytes 599048 | tf_op jit(solution)/shard_map/ppermute | solution.py:107
  48.3 10.2 %collective-permute-start.2 = (bf16[128,1024]{1,0:T(8,128)(2,1)S(1)}, bf16[128,1024]{1,0:T(8,128)(2,1)S(1)}, u32[]{:S(2)}, u32[]{:S(2)}) collective-permute-start(bf16[128,1024]{1,0:T(8,128)(2,1)S(1)} %get-tuple-element.29), channel_id=1, source_target_pairs={{0,8},{8,16},{16,24},{24,28},{28,20},{20,12},{12,4},{4,0},{1,9},{9... | collective-permute-start | bytes 786440 | tf_op jit(solution)/shard_map/ppermute | solution.py:106
  50.2 9.7 %collective-permute-start.3 = (bf16[128,1024]{1,0:T(8,128)(2,1)S(1)}, bf16[128,1024]{1,0:T(8,128)(2,1)S(1)}, u32[]{:S(2)}, u32[]{:S(2)}) collective-permute-start(bf16[128,1024]{1,0:T(8,128)(2,1)S(1)} %get-tuple-element.30), channel_id=1, source_target_pairs={{8,0},{16,8},{24,16},{28,24},{20,28},{12,20},{4,12},{0,4},{9,1},{1... | collective-permute-start | bytes 786440 | tf_op jit(solution)/shard_map/ppermute | solution.py:107
  59.9 7.9 %collective-permute-start.4 = (bf16[130,768]{1,0:T(8,128)(2,1)S(1)}, bf16[130,768]{1,0:T(8,128)(2,1)S(1)}, u32[]{:S(2)}, u32[]{:S(2)}) collective-permute-start(bf16[130,768]{1,0:T(8,128)(2,1)S(1)} %add_convert_fusion.13), channel_id=1, source_target_pairs={{0,8},{8,16},{16,24},{24,28},{28,20},{20,12},{12,4},{4,0},{1,9},{9... | collective-permute-start | bytes 599048 | tf_op jit(solution)/shard_map/ppermute | solution.py:106
  61.3 7.7 %collective-permute-start.5 = (bf16[130,768]{1,0:T(8,128)(2,1)S(1)}, bf16[130,768]{1,0:T(8,128)(2,1)S(1)}, u32[]{:S(2)}, u32[]{:S(2)}) collective-permute-start(bf16[130,768]{1,0:T(8,128)(2,1)S(1)} %add_convert_fusion.12), channel_id=1, source_target_pairs={{8,0},{16,8},{24,16},{28,24},{20,28},{12,20},{4,12},{0,4},{9,1},{1... | collective-permute-start | bytes 599048 | tf_op jit(solution)/shard_map/ppermute | solution.py:107
  61.9 8.7 %collective-permute-start.6 = (bf16[128,1024]{1,0:T(8,128)(2,1)S(1)}, bf16[128,1024]{1,0:T(8,128)(2,1)S(1)}, u32[]{:S(2)}, u32[]{:S(2)}) collective-permute-start(bf16[128,1024]{1,0:T(8,128)(2,1)S(1)} %collective-permute-done.2), channel_id=1, source_target_pairs={{0,8},{8,16},{16,24},{24,28},{28,20},{20,12},{12,4},{4,0},{1,9},{9... | collective-permute-start | bytes 786440 | tf_op jit(solution)/shard_map/ppermute | solution.py:106
  63.4 8.4 %collective-permute-start.7 = (bf16[128,1024]{1,0:T(8,128)(2,1)S(1)}, bf16[128,1024]{1,0:T(8,128)(2,1)S(1)}, u32[]{:S(2)}, u32[]{:S(2)}) collective-permute-start(bf16[128,1024]{1,0:T(8,128)(2,1)S(1)} %collective-permute-done.3), channel_id=1, source_target_pairs={{8,0},{16,8},{24,16},{28,24},{20,28},{12,20},{4,12},{0,4},{9,1},{1... | collective-permute-start | bytes 786440 | tf_op jit(solution)/shard_map/ppermute | solution.py:107
  71.8 6.7 %collective-permute-start.8 = (bf16[130,768]{1,0:T(8,128)(2,1)S(1)}, bf16[130,768]{1,0:T(8,128)(2,1)S(1)}, u32[]{:S(2)}, u32[]{:S(2)}) collective-permute-start(bf16[130,768]{1,0:T(8,128)(2,1)S(1)} %add_convert_fusion.11), channel_id=1, source_target_pairs={{0,8},{8,16},{16,24},{24,28},{28,20},{20,12},{12,4},{4,0},{1,9},{9... | collective-permute-start | bytes 599048 | tf_op jit(solution)/shard_map/ppermute | solution.py:106
  73.3 6.5 %collective-permute-start.9 = (bf16[130,768]{1,0:T(8,128)(2,1)S(1)}, bf16[130,768]{1,0:T(8,128)(2,1)S(1)}, u32[]{:S(2)}, u32[]{:S(2)}) collective-permute-start(bf16[130,768]{1,0:T(8,128)(2,1)S(1)} %add_convert_fusion.10), channel_id=1, source_target_pairs={{8,0},{16,8},{24,16},{28,24},{20,28},{12,20},{4,12},{0,4},{9,1},{1... | collective-permute-start | bytes 599048 | tf_op jit(solution)/shard_map/ppermute | solution.py:107
  73.9 7.7 %collective-permute-start.10 = (bf16[128,1024]{1,0:T(8,128)(2,1)S(1)}, bf16[128,1024]{1,0:T(8,128)(2,1)S(1)}, u32[]{:S(2)}, u32[]{:S(2)}) collective-permute-start(bf16[128,1024]{1,0:T(8,128)(2,1)S(1)} %collective-permute-done.6), channel_id=1, source_target_pairs={{0,8},{8,16},{16,24},{24,28},{28,20},{20,12},{12,4},{4,0},{1,9},{9... | collective-permute-start | bytes 786440 | tf_op jit(solution)/shard_map/ppermute | solution.py:106
  75.3 8.9 %collective-permute-start.11 = (bf16[128,1024]{1,0:T(8,128)(2,1)S(1)}, bf16[128,1024]{1,0:T(8,128)(2,1)S(1)}, u32[]{:S(2)}, u32[]{:S(2)}) collective-permute-start(bf16[128,1024]{1,0:T(8,128)(2,1)S(1)} %collective-permute-done.7), channel_id=1, source_target_pairs={{8,0},{16,8},{24,16},{28,24},{20,28},{12,20},{4,12},{0,4},{9,1},{1... | collective-permute-start | bytes 786440 | tf_op jit(solution)/shard_map/ppermute | solution.py:107
  84.2 8.1 %collective-permute-start.16 = (bf16[130,768]{1,0:T(8,128)(2,1)S(1)}, bf16[130,768]{1,0:T(8,128)(2,1)S(1)}, u32[]{:S(2)}, u32[]{:S(2)}) collective-permute-start(bf16[130,768]{1,0:T(8,128)(2,1)S(1)} %add_convert_fusion.8), channel_id=1, source_target_pairs={{8,0},{16,8},{24,16},{28,24},{20,28},{12,20},{4,12},{0,4},{9,1},{1... | collective-permute-start | bytes 599048 | tf_op jit(solution)/shard_map/ppermute | solution.py:107
  84.8 8.2 %collective-permute-start.12 = (bf16[130,768]{1,0:T(8,128)(2,1)S(1)}, bf16[130,768]{1,0:T(8,128)(2,1)S(1)}, u32[]{:S(2)}, u32[]{:S(2)}) collective-permute-start(bf16[130,768]{1,0:T(8,128)(2,1)S(1)} %add_convert_fusion.9), channel_id=1, source_target_pairs={{0,8},{8,16},{16,24},{24,28},{28,20},{20,12},{12,4},{4,0},{1,9},{9... | collective-permute-start | bytes 599048 | tf_op jit(solution)/shard_map/ppermute | solution.py:106
  86.3 12.1 %collective-permute-start.27 = (bf16[128,1024]{1,0:T(8,128)(2,1)S(1)}, bf16[128,1024]{1,0:T(8,128)(2,1)S(1)}, u32[]{:S(2)}, u32[]{:S(2)}) collective-permute-start(bf16[128,1024]{1,0:T(8,128)(2,1)S(1)} %collective-permute-done.10), channel_id=1, source_target_pairs={{0,8},{8,16},{16,24},{24,28},{28,20},{20,12},{12,4},{4,0},{1,9},{9... | collective-permute-start | bytes 786440 | tf_op jit(solution)/shard_map/ppermute | solution.py:106
  87.9 12.0 %collective-permute-start.28 = (bf16[128,1024]{1,0:T(8,128)(2,1)S(1)}, bf16[128,1024]{1,0:T(8,128)(2,1)S(1)}, u32[]{:S(2)}, u32[]{:S(2)}) collective-permute-start(bf16[128,1024]{1,0:T(8,128)(2,1)S(1)} %collective-permute-done.11), channel_id=1, source_target_pairs={{8,0},{16,8},{24,16},{28,24},{20,28},{12,20},{4,12},{0,4},{9,1},{1... | collective-permute-start | bytes 786440 | tf_op jit(solution)/shard_map/ppermute | solution.py:107
  92.4 10.0 %collective-permute-start.17 = (bf16[130,768]{1,0:T(8,128)(2,1)S(1)}, bf16[130,768]{1,0:T(8,128)(2,1)S(1)}, u32[]{:S(2)}, u32[]{:S(2)}) collective-permute-start(bf16[130,768]{1,0:T(8,128)(2,1)S(1)} %add_convert_fusion.3), channel_id=1, source_target_pairs={{8,0},{16,8},{24,16},{28,24},{20,28},{12,20},{4,12},{0,4},{9,1},{1... | collective-permute-start | bytes 599048 | tf_op jit(solution)/shard_map/ppermute | solution.py:111
  93.1 10.0 %collective-permute-start.13 = (bf16[130,768]{1,0:T(8,128)(2,1)S(1)}, bf16[130,768]{1,0:T(8,128)(2,1)S(1)}, u32[]{:S(2)}, u32[]{:S(2)}) collective-permute-start(bf16[130,768]{1,0:T(8,128)(2,1)S(1)} %add_convert_fusion.7), channel_id=1, source_target_pairs={{0,8},{8,16},{16,24},{24,28},{28,20},{20,12},{12,4},{4,0},{1,9},{9... | collective-permute-start | bytes 599048 | tf_op jit(solution)/shard_map/ppermute | solution.py:110
  98.4 10.1 %collective-permute-start.29 = (bf16[128,1024]{1,0:T(8,128)(2,1)S(1)}, bf16[128,1024]{1,0:T(8,128)(2,1)S(1)}, u32[]{:S(2)}, u32[]{:S(2)}) collective-permute-start(bf16[128,1024]{1,0:T(8,128)(2,1)S(1)} %collective-permute-done.27), channel_id=1, source_target_pairs={{0,8},{8,16},{16,24},{24,28},{28,20},{20,12},{12,4},{4,0},{1,9},{9... | collective-permute-start | bytes 786440 | tf_op jit(solution)/shard_map/ppermute | solution.py:115
  99.9 10.1 %collective-permute-start.30 = (bf16[128,1024]{1,0:T(8,128)(2,1)S(1)}, bf16[128,1024]{1,0:T(8,128)(2,1)S(1)}, u32[]{:S(2)}, u32[]{:S(2)}) collective-permute-start(bf16[128,1024]{1,0:T(8,128)(2,1)S(1)} %collective-permute-done.28), channel_id=1, source_target_pairs={{8,0},{16,8},{24,16},{28,24},{20,28},{12,20},{4,12},{0,4},{9,1},{1... | collective-permute-start | bytes 786440 | tf_op jit(solution)/shard_map/ppermute | solution.py:116
  102.5 9.8 %collective-permute-start.18 = (bf16[130,768]{1,0:T(8,128)(2,1)S(1)}, bf16[130,768]{1,0:T(8,128)(2,1)S(1)}, u32[]{:S(2)}, u32[]{:S(2)}) collective-permute-start(bf16[130,768]{1,0:T(8,128)(2,1)S(1)} %add_convert_fusion.2), channel_id=1, source_target_pairs={{8,0},{16,8},{24,16},{28,24},{20,28},{12,20},{4,12},{0,4},{9,1},{1... | collective-permute-start | bytes 599048 | tf_op jit(solution)/shard_map/ppermute | solution.py:111
  103.1 16.0 %copy-start.3 = (f32[16,512]{1,0:T(8,128)S(1)}, f32[16,512]{1,0:T(8,128)}, u32[]{:S(2)}) copy-start(f32[16,512]{1,0:T(8,128)} %param.20) | copy-start | bytes 98308
  103.2 9.8 %collective-permute-start.14 = (bf16[130,768]{1,0:T(8,128)(2,1)S(1)}, bf16[130,768]{1,0:T(8,128)(2,1)S(1)}, u32[]{:S(2)}, u32[]{:S(2)}) collective-permute-start(bf16[130,768]{1,0:T(8,128)(2,1)S(1)} %add_convert_fusion.6), channel_id=1, source_target_pairs={{0,8},{8,16},{16,24},{24,28},{28,20},{20,12},{12,4},{4,0},{1,9},{9... | collective-permute-start | bytes 599048 | tf_op jit(solution)/shard_map/ppermute | solution.py:110
  108.5 6.7 %collective-permute-start.31 = (bf16[128,1024]{1,0:T(8,128)(2,1)S(1)}, bf16[128,1024]{1,0:T(8,128)(2,1)S(1)}, u32[]{:S(2)}, u32[]{:S(2)}) collective-permute-start(bf16[128,1024]{1,0:T(8,128)(2,1)S(1)} %collective-permute-done.29), channel_id=1, source_target_pairs={{0,8},{8,16},{16,24},{24,28},{28,20},{20,12},{12,4},{4,0},{1,9},{9... | collective-permute-start | bytes 786440 | tf_op jit(solution)/shard_map/ppermute | solution.py:115
  110.0 15.8 %collective-permute-start.32 = (bf16[128,1024]{1,0:T(8,128)(2,1)S(1)}, bf16[128,1024]{1,0:T(8,128)(2,1)S(1)}, u32[]{:S(2)}, u32[]{:S(2)}) collective-permute-start(bf16[128,1024]{1,0:T(8,128)(2,1)S(1)} %collective-permute-done.30), channel_id=1, source_target_pairs={{8,0},{16,8},{24,16},{28,24},{20,28},{12,20},{4,12},{0,4},{9,1},{1... | collective-permute-start | bytes 786440 | tf_op jit(solution)/shard_map/ppermute | solution.py:116
  112.3 6.3 %collective-permute-start.19 = (bf16[130,768]{1,0:T(8,128)(2,1)S(1)}, bf16[130,768]{1,0:T(8,128)(2,1)S(1)}, u32[]{:S(2)}, u32[]{:S(2)}) collective-permute-start(bf16[130,768]{1,0:T(8,128)(2,1)S(1)} %add_convert_fusion.1), channel_id=1, source_target_pairs={{8,0},{16,8},{24,16},{28,24},{20,28},{12,20},{4,12},{0,4},{9,1},{1... | collective-permute-start | bytes 599048 | tf_op jit(solution)/shard_map/ppermute | solution.py:111
  113.0 5.9 %collective-permute-start.15 = (bf16[130,768]{1,0:T(8,128)(2,1)S(1)}, bf16[130,768]{1,0:T(8,128)(2,1)S(1)}, u32[]{:S(2)}, u32[]{:S(2)}) collective-permute-start(bf16[130,768]{1,0:T(8,128)(2,1)S(1)} %add_convert_fusion.5), channel_id=1, source_target_pairs={{0,8},{8,16},{16,24},{24,28},{28,20},{20,12},{12,4},{4,0},{1,9},{9... | collective-permute-start | bytes 599048 | tf_op jit(solution)/shard_map/ppermute | solution.py:110
  119.0 19.6 %copy-start.5 = (f32[16,512]{1,0:T(8,128)S(1)}, f32[16,512]{1,0:T(8,128)}, u32[]{:S(2)}) copy-start(f32[16,512]{1,0:T(8,128)} %param.21) | copy-start | bytes 98308
  120.0 11.0 %collective-permute-start.26 = (f32[16,512]{1,0:T(8,128)S(1)}, f32[16,512]{1,0:T(8,128)S(1)}, u32[]{:S(2)}, u32[]{:S(2)}) collective-permute-start(f32[16,512]{1,0:T(8,128)S(1)} %exponential_multiply_fusion.2), channel_id=1, source_target_pairs={{0,28},{1,29},{2,30},{3,31}} | collective-permute-start | bytes 98312 | tf_op jit(solution)/shard_map/ppermute | solution.py:32
  124.5 7.7 %collective-permute-start.25 = (f32[16,512]{1,0:T(8,128)S(1)}, f32[16,512]{1,0:T(8,128)S(1)}, u32[]{:S(2)}, u32[]{:S(2)}) collective-permute-start(f32[16,512]{1,0:T(8,128)S(1)} %exponential_multiply_fusion.2), channel_id=1, source_target_pairs={{0,24},{4,28},{1,25},{5,29},{2,26},{6,30},{3,27},{7,31}} | collective-permute-start | bytes 98312 | tf_op jit(solution)/shard_map/ppermute | solution.py:32
  125.8 10.6 %collective-permute-start.24 = (f32[16,512]{1,0:T(8,128)S(1)}, f32[16,512]{1,0:T(8,128)S(1)}, u32[]{:S(2)}, u32[]{:S(2)}) collective-permute-start(f32[16,512]{1,0:T(8,128)S(1)} %exponential_multiply_fusion.2), channel_id=1, source_target_pairs={{0,20},{4,24},{8,28},{1,21},{5,25},{9,29},{2,22},{6,26},{10,30},{3... | collective-permute-start | bytes 98312 | tf_op jit(solution)/shard_map/ppermute | solution.py:32
  127.1 9.4 %collective-permute-start.23 = (f32[16,512]{1,0:T(8,128)S(1)}, f32[16,512]{1,0:T(8,128)S(1)}, u32[]{:S(2)}, u32[]{:S(2)}) collective-permute-start(f32[16,512]{1,0:T(8,128)S(1)} %exponential_multiply_fusion.2), channel_id=1, source_target_pairs={{0,16},{4,20},{8,24},{12,28},{1,17},{5,21},{9,25},{13,29},{2,18},{... | collective-permute-start | bytes 98312 | tf_op jit(solution)/shard_map/ppermute | solution.py:32
  128.4 10.1 %collective-permute-start.22 = (f32[16,512]{1,0:T(8,128)S(1)}, f32[16,512]{1,0:T(8,128)S(1)}, u32[]{:S(2)}, u32[]{:S(2)}) collective-permute-start(f32[16,512]{1,0:T(8,128)S(1)} %exponential_multiply_fusion.2), channel_id=1, source_target_pairs={{0,12},{4,16},{8,20},{12,24},{16,28},{1,13},{5,17},{9,21},{13,25},... | collective-permute-start | bytes 98312 | tf_op jit(solution)/shard_map/ppermute | solution.py:32
  130.9 7.7 %collective-permute-start.21 = (f32[16,512]{1,0:T(8,128)S(1)}, f32[16,512]{1,0:T(8,128)S(1)}, u32[]{:S(2)}, u32[]{:S(2)}) collective-permute-start(f32[16,512]{1,0:T(8,128)S(1)} %exponential_multiply_fusion.2), channel_id=1, source_target_pairs={{0,8},{4,12},{8,16},{12,20},{16,24},{20,28},{1,9},{5,13},{9,17},{1... | collective-permute-start | bytes 98312 | tf_op jit(solution)/shard_map/ppermute | solution.py:32
  132.2 6.3 %collective-permute-start.20 = (f32[16,512]{1,0:T(8,128)S(1)}, f32[16,512]{1,0:T(8,128)S(1)}, u32[]{:S(2)}, u32[]{:S(2)}) collective-permute-start(f32[16,512]{1,0:T(8,128)S(1)} %exponential_multiply_fusion.2), channel_id=1, source_target_pairs={{0,4},{4,8},{8,12},{12,16},{16,20},{20,24},{24,28},{1,5},{5,9},{9,... | collective-permute-start | bytes 98312 | tf_op jit(solution)/shard_map/ppermute | solution.py:32
  136.5 11.8 %collective-permute-start.33 = (bf16[128,1024]{1,0:T(8,128)(2,1)S(1)}, bf16[128,1024]{1,0:T(8,128)(2,1)S(1)}, u32[]{:S(2)}, u32[]{:S(2)}) collective-permute-start(bf16[128,1024]{1,0:T(8,128)(2,1)S(1)} %collective-permute-done.31), channel_id=1, source_target_pairs={{0,8},{8,16},{16,24},{24,28},{28,20},{20,12},{12,4},{4,0},{1,9},{9... | collective-permute-start | bytes 786440 | tf_op jit(solution)/shard_map/ppermute | solution.py:115
  136.6 11.8 %collective-permute-start.34 = (bf16[128,1024]{1,0:T(8,128)(2,1)S(1)}, bf16[128,1024]{1,0:T(8,128)(2,1)S(1)}, u32[]{:S(2)}, u32[]{:S(2)}) collective-permute-start(bf16[128,1024]{1,0:T(8,128)(2,1)S(1)} %collective-permute-done.32), channel_id=1, source_target_pairs={{8,0},{16,8},{24,16},{28,24},{20,28},{12,20},{4,12},{0,4},{9,1},{1... | collective-permute-start | bytes 786440 | tf_op jit(solution)/shard_map/ppermute | solution.py:116
  138.7 2.2 %copy-start.9 = (f32[512]{0:T(512)S(1)}, f32[512]{0:T(512)}, u32[]{:S(2)}) copy-start(f32[512]{0:T(512)} %param.22) | copy-start | bytes 6148

commit v17 on v15

--- a/solution.py
+++ b/solution.py
@@ -15,7 +15,7 @@
     coefs = residues * jnp.sqrt(2.0 * rates)
     times = jnp.arange(length, dtype=jnp.float32)[None, :, None]
     grow = jnp.exp(rates[:, None, :] * times)
-    decay = jnp.exp(-rates[:, None, :] * times)
+    decay = 1.0 / grow
     lifted = grow * signal[None]
     rows = jnp.arange(length, dtype=jnp.int32)
     lower = (rows[:, None] >= rows[None, :]).astype(jnp.float32)

time: 150 us -> 151 us (level)
  no operation moved by 1% of the time
where the time goes in v17:
time: 151 us; the launch traced here: 150 us
  starting transfers between devices  51.4 us (34%)
  waiting for transfers between devices  42.2 us (28%)
  between operations  30.3 us (20%)
  matrix products  9.21 us (6%)
  blocking collectives  7.16 us (5%)
  local copies, waits for them, and re-layouts  6.49 us (4%)
  other arithmetic  3.07 us (2%)
    ppermute x8, waiting for transfers between devices, body(): up, w_up = lax.ppermute((sent[0], sent[2]), 'ctx', perm=fwd)  17.2 us
    ppermute x7, starting transfers between devices, modal_long_conv(): lax.ppermute(end_state, 'ctx', perm=[(i, i + shift) for i in range(ctx_co...  15.3 us
    ppermute x8, waiting for transfers between devices, body(): down, w_low = lax.ppermute((sent[1], sent[3]), 'ctx', perm=bwd)  13.3 us
    ppermute x8, starting transfers between devices, body(): up, w_up = lax.ppermute((sent[0], sent[2]), 'ctx', perm=fwd)  13 us
    ppermute x3, waiting for transfers between devices, body(): down = lax.ppermute(down.astype(jnp.bfloat16), 'ctx', perm=bwd)  7.67 us
    all_to_all x1, starting transfers between devices, body(): lax.all_to_all(by_dest, 'ctx', split_axis=0, concat_axis=0, tiled=True)  7.29 us
    all_gather x1, blocking collectives, body(): features = lax.all_gather(gated, 'tp', axis=1, tiled=True)  7.16 us
    ppermute x3, starting transfers between devices, body(): up = lax.ppermute(up.astype(jnp.bfloat16), 'ctx', perm=fwd)  4.51 us
  transfers between devices with their start and end apart: 36, of which 19 were waited for; matrix products, arithmetic and copies ran while one was open for 7% of the time, Pallas kernels for 0%

profile of v17, /device:TPU:0, one launch (start us, length us, event | category | flops | bytes accessed | tf_op | source)
XLA Modules:
  0.0 149.9 jit_solution(3630780569035282331)
XLA Ops:
  0.0 2.4 %copy.14 = bf16[128,4096]{0,1:T(8,128)(2,1)} copy(bf16[128,4096]{1,0:T(8,128)(2,1)} %param.13) | data formatting | bytes 2097152 | tf_op args[0]
  2.4 7.3 %all-to-all-start = ((bf16[8,128,512]{1,2,0:T(8,128)(2,1)}), bf16[8,128,512]{1,2,0:T(8,128)(2,1)}, u32[]{:S(2)}, u32[]{:S(2)}) async-start(bf16[8,128,512]{1,2,0:T(8,128)(2,1)} %bitcast.2), calls=%async_computation | async-start | bytes 2097152 | tf_op jit(solution)/shard_map/all_to_all | solution.py:66
  21.0 0.8 fusion.74
  40.8 1.1 pad_maximum_fusion.1
  42.1 1.5 copy.15
  46.1 2.1 %collective-permute-start = (bf16[130,768]{1,0:T(8,128)(2,1)S(1)}, bf16[130,768]{1,0:T(8,128)(2,1)S(1)}, u32[]{:S(2)}, u32[]{:S(2)}) collective-permute-start(bf16[130,768]{1,0:T(8,128)(2,1)S(1)} %convolution_convert_fusion.2), channel_id=1, source_target_pairs={{0,8},{8,16},{16,24},{24,28},{28,20},{20,12},{12,4},{4,0},{1,9},{9... | collective-permute-start | bytes 599048 | tf_op jit(solution)/shard_map/ppermute | solution.py:107
  48.3 2.0 %collective-permute-start.2 = (bf16[128,1024]{1,0:T(8,128)(2,1)S(1)}, bf16[128,1024]{1,0:T(8,128)(2,1)S(1)}, u32[]{:S(2)}, u32[]{:S(2)}) collective-permute-start(bf16[128,1024]{1,0:T(8,128)(2,1)S(1)} %get-tuple-element.29), channel_id=1, source_target_pairs={{0,8},{8,16},{16,24},{24,28},{28,20},{20,12},{12,4},{4,0},{1,9},{9... | collective-permute-start | bytes 786440 | tf_op jit(solution)/shard_map/ppermute | solution.py:107
  52.6 1.7 %collective-permute-done = bf16[130,768]{1,0:T(8,128)(2,1)S(1)} collective-permute-done((bf16[130,768]{1,0:T(8,128)(2,1)S(1)}, bf16[130,768]{1,0:T(8,128)(2,1)S(1)}, u32[]{:S(2)}, u32[]{:S(2)}) %collective-permute-start) | collective-permute-done | bytes 199712 | tf_op jit(solution)/shard_map/ppermute | solution.py:107
  54.6 1.7 %collective-permute-done.1 = bf16[130,768]{1,0:T(8,128)(2,1)S(1)} collective-permute-done((bf16[130,768]{1,0:T(8,128)(2,1)S(1)}, bf16[130,768]{1,0:T(8,128)(2,1)S(1)}, u32[]{:S(2)}, u32[]{:S(2)}) %collective-permute-start.1) | collective-permute-done | bytes 199712 | tf_op jit(solution)/shard_map/ppermute | solution.py:108
  56.6 1.8 %collective-permute-done.2 = bf16[128,1024]{1,0:T(8,128)(2,1)S(1)} collective-permute-done((bf16[128,1024]{1,0:T(8,128)(2,1)S(1)}, bf16[128,1024]{1,0:T(8,128)(2,1)S(1)}, u32[]{:S(2)}, u32[]{:S(2)}) %collective-permute-start.2) | collective-permute-done | bytes 262176 | tf_op jit(solution)/shard_map/ppermute | solution.py:107
  58.4 1.5 collective-permute-done.3
  59.9 1.5 collective-permute-start.4
  61.9 1.5 collective-permute-start.6
  64.0 3.8 %collective-permute-done.4 = bf16[130,768]{1,0:T(8,128)(2,1)S(1)} collective-permute-done((bf16[130,768]{1,0:T(8,128)(2,1)S(1)}, bf16[130,768]{1,0:T(8,128)(2,1)S(1)}, u32[]{:S(2)}, u32[]{:S(2)}) %collective-permute-start.4) | collective-permute-done | bytes 199712 | tf_op jit(solution)/shard_map/ppermute | solution.py:107
  67.9 1.1 collective-permute-done.5
  69.1 1.6 %collective-permute-done.6 = bf16[128,1024]{1,0:T(8,128)(2,1)S(1)} collective-permute-done((bf16[128,1024]{1,0:T(8,128)(2,1)S(1)}, bf16[128,1024]{1,0:T(8,128)(2,1)S(1)}, u32[]{:S(2)}, u32[]{:S(2)}) %collective-permute-start.6) | collective-permute-done | bytes 262176 | tf_op jit(solution)/shard_map/ppermute | solution.py:107
  70.6 1.2 collective-permute-done.7
  71.8 1.5 collective-permute-start.8
  73.9 1.5 collective-permute-start.10
  75.9 2.6 %collective-permute-done.8 = bf16[130,768]{1,0:T(8,128)(2,1)S(1)} collective-permute-done((bf16[130,768]{1,0:T(8,128)(2,1)S(1)}, bf16[130,768]{1,0:T(8,128)(2,1)S(1)}, u32[]{:S(2)}, u32[]{:S(2)}) %collective-permute-start.8) | collective-permute-done | bytes 199712 | tf_op jit(solution)/shard_map/ppermute | solution.py:107
  78.6 1.1 collective-permute-done.9
  79.8 1.8 %collective-permute-done.10 = bf16[128,1024]{1,0:T(8,128)(2,1)S(1)} collective-permute-done((bf16[128,1024]{1,0:T(8,128)(2,1)S(1)}, bf16[128,1024]{1,0:T(8,128)(2,1)S(1)}, u32[]{:S(2)}, u32[]{:S(2)}) %collective-permute-start.10) | collective-permute-done | bytes 262176 | tf_op jit(solution)/shard_map/ppermute | solution.py:107
  81.6 2.6 %collective-permute-done.11 = bf16[128,1024]{1,0:T(8,128)(2,1)S(1)} collective-permute-done((bf16[128,1024]{1,0:T(8,128)(2,1)S(1)}, bf16[128,1024]{1,0:T(8,128)(2,1)S(1)}, u32[]{:S(2)}, u32[]{:S(2)}) %collective-permute-start.11) | collective-permute-done | bytes 262176 | tf_op jit(solution)/shard_map/ppermute | solution.py:108
  84.8 1.5 collective-permute-start.12
  86.3 1.6 %collective-permute-start.27 = (bf16[128,1024]{1,0:T(8,128)(2,1)S(1)}, bf16[128,1024]{1,0:T(8,128)(2,1)S(1)}, u32[]{:S(2)}, u32[]{:S(2)}) collective-permute-start(bf16[128,1024]{1,0:T(8,128)(2,1)S(1)} %collective-permute-done.10), channel_id=1, source_target_pairs={{0,8},{8,16},{16,24},{24,28},{28,20},{20,12},{12,4},{4,0},{1,9},{9... | collective-permute-start | bytes 786440 | tf_op jit(solution)/shard_map/ppermute | solution.py:107
  88.3 4.0 %collective-permute-done.16 = bf16[130,768]{1,0:T(8,128)(2,1)S(1)} collective-permute-done((bf16[130,768]{1,0:T(8,128)(2,1)S(1)}, bf16[130,768]{1,0:T(8,128)(2,1)S(1)}, u32[]{:S(2)}, u32[]{:S(2)}) %collective-permute-start.16) | collective-permute-done | bytes 199712 | tf_op jit(solution)/shard_map/ppermute | solution.py:108
  93.1 1.5 %collective-permute-start.13 = (bf16[130,768]{1,0:T(8,128)(2,1)S(1)}, bf16[130,768]{1,0:T(8,128)(2,1)S(1)}, u32[]{:S(2)}, u32[]{:S(2)}) collective-permute-start(bf16[130,768]{1,0:T(8,128)(2,1)S(1)} %add_convert_fusion.7), channel_id=1, source_target_pairs={{0,8},{8,16},{16,24},{24,28},{28,20},{20,12},{12,4},{4,0},{1,9},{9... | collective-permute-start | bytes 599048 | tf_op jit(solution)/shard_map/ppermute | solution.py:111
  94.6 3.8 %collective-permute-done.27 = bf16[128,1024]{1,0:T(8,128)(2,1)S(1)} collective-permute-done((bf16[128,1024]{1,0:T(8,128)(2,1)S(1)}, bf16[128,1024]{1,0:T(8,128)(2,1)S(1)}, u32[]{:S(2)}, u32[]{:S(2)}) %collective-permute-start.27) | collective-permute-done | bytes 262176 | tf_op jit(solution)/shard_map/ppermute | solution.py:107
  98.4 1.5 collective-permute-start.29
  100.5 1.9 %collective-permute-done.17 = bf16[130,768]{1,0:T(8,128)(2,1)S(1)} collective-permute-done((bf16[130,768]{1,0:T(8,128)(2,1)S(1)}, bf16[130,768]{1,0:T(8,128)(2,1)S(1)}, u32[]{:S(2)}, u32[]{:S(2)}) %collective-permute-start.17) | collective-permute-done | bytes 199712 | tf_op jit(solution)/shard_map/ppermute | solution.py:112
  103.2 1.5 %collective-permute-start.14 = (bf16[130,768]{1,0:T(8,128)(2,1)S(1)}, bf16[130,768]{1,0:T(8,128)(2,1)S(1)}, u32[]{:S(2)}, u32[]{:S(2)}) collective-permute-start(bf16[130,768]{1,0:T(8,128)(2,1)S(1)} %add_convert_fusion.6), channel_id=1, source_target_pairs={{0,8},{8,16},{16,24},{24,28},{28,20},{20,12},{12,4},{4,0},{1,9},{9... | collective-permute-start | bytes 599048 | tf_op jit(solution)/shard_map/ppermute | solution.py:111
  104.7 3.8 %collective-permute-done.29 = bf16[128,1024]{1,0:T(8,128)(2,1)S(1)} collective-permute-done((bf16[128,1024]{1,0:T(8,128)(2,1)S(1)}, bf16[128,1024]{1,0:T(8,128)(2,1)S(1)}, u32[]{:S(2)}, u32[]{:S(2)}) %collective-permute-start.29) | collective-permute-done | bytes 262176 | tf_op jit(solution)/shard_map/ppermute | solution.py:116
  108.5 1.5 collective-permute-start.31
  110.6 1.7 %collective-permute-done.18 = bf16[130,768]{1,0:T(8,128)(2,1)S(1)} collective-permute-done((bf16[130,768]{1,0:T(8,128)(2,1)S(1)}, bf16[130,768]{1,0:T(8,128)(2,1)S(1)}, u32[]{:S(2)}, u32[]{:S(2)}) %collective-permute-start.18) | collective-permute-done | bytes 199712 | tf_op jit(solution)/shard_map/ppermute | solution.py:112
  113.0 1.5 %collective-permute-start.15 = (bf16[130,768]{1,0:T(8,128)(2,1)S(1)}, bf16[130,768]{1,0:T(8,128)(2,1)S(1)}, u32[]{:S(2)}, u32[]{:S(2)}) collective-permute-start(bf16[130,768]{1,0:T(8,128)(2,1)S(1)} %add_convert_fusion.5), channel_id=1, source_target_pairs={{0,8},{8,16},{16,24},{24,28},{28,20},{20,12},{12,4},{4,0},{1,9},{9... | collective-permute-start | bytes 599048 | tf_op jit(solution)/shard_map/ppermute | solution.py:111
  114.5 4.1 %collective-permute-done.19 = bf16[130,768]{1,0:T(8,128)(2,1)S(1)} collective-permute-done((bf16[130,768]{1,0:T(8,128)(2,1)S(1)}, bf16[130,768]{1,0:T(8,128)(2,1)S(1)}, u32[]{:S(2)}, u32[]{:S(2)}) %collective-permute-start.19) | collective-permute-done | bytes 199712 | tf_op jit(solution)/shard_map/ppermute | solution.py:112
  119.2 0.7 fusion.1
  120.0 4.5 %collective-permute-start.26 = (f32[16,512]{1,0:T(8,128)S(1)}, f32[16,512]{1,0:T(8,128)S(1)}, u32[]{:S(2)}, u32[]{:S(2)}) collective-permute-start(f32[16,512]{1,0:T(8,128)S(1)} %get-tuple-element.48), channel_id=1, source_target_pairs={{0,28},{1,29},{2,30},{3,31}} | collective-permute-start | bytes 98312 | tf_op jit(solution)/shard_map/ppermute | solution.py:33
  124.5 1.3 collective-permute-start.25
  125.9 1.3 collective-permute-start.24
  127.2 1.3 collective-permute-start.23
  128.5 2.5 %collective-permute-start.22 = (f32[16,512]{1,0:T(8,128)S(1)}, f32[16,512]{1,0:T(8,128)S(1)}, u32[]{:S(2)}, u32[]{:S(2)}) collective-permute-start(f32[16,512]{1,0:T(8,128)S(1)} %get-tuple-element.48), channel_id=1, source_target_pairs={{0,12},{4,16},{8,20},{12,24},{16,28},{1,13},{5,17},{9,21},{13,25},... | collective-permute-start | bytes 98312 | tf_op jit(solution)/shard_map/ppermute | solution.py:33
  131.0 1.3 collective-permute-start.21
  132.3 3.1 %collective-permute-start.20 = (f32[16,512]{1,0:T(8,128)S(1)}, f32[16,512]{1,0:T(8,128)S(1)}, u32[]{:S(2)}, u32[]{:S(2)}) collective-permute-start(f32[16,512]{1,0:T(8,128)S(1)} %get-tuple-element.48), channel_id=1, source_target_pairs={{0,4},{4,8},{8,12},{12,16},{16,20},{20,24},{24,28},{1,5},{5,9},{9,... | collective-permute-start | bytes 98312 | tf_op jit(solution)/shard_map/ppermute | solution.py:33
  135.5 2.0 %collective-permute-start.34 = (bf16[128,1024]{1,0:T(8,128)(2,1)S(1)}, bf16[128,1024]{1,0:T(8,128)(2,1)S(1)}, u32[]{:S(2)}, u32[]{:S(2)}) collective-permute-start(bf16[128,1024]{1,0:T(8,128)(2,1)S(1)} %collective-permute-done.32), channel_id=1, source_target_pairs={{8,0},{16,8},{24,16},{28,24},{20,28},{12,20},{4,12},{0,4},{9,1},{1... | collective-permute-start | bytes 786440 | tf_op jit(solution)/shard_map/ppermute | solution.py:117
  137.6 3.3 %multiply_reduce_fusion = f32[128,512]{1,0:T(8,128)S(1)} fusion(f32[16,512]{1,0:T(8,128)S(1)} %exponential_multiply_fusion, f32[128,512]{1,0:T(8,128)S(1)} %fusion.52, f32[16,512]{1,0:T(8,128)S(1)} %copy-done.3, f32[16,512]{1,0:T(8,128)S(1)} %get-tuple-element.47, f32[128,128]{1,0:T(8,128)S(1)} %fusion.53), kind=kOutput, calls=%fused_computation | convolution fusion | flops 813629440 | bytes 688128 | tf_op jit(solution)/shard_map/dot_general | solution.py:23
  141.2 7.2 %all_gather.3 = bf16[128,2048]{1,0:T(8,128)(2,1)S(1)} all-gather(bf16[128,512]{1,0:T(8,128)(2,1)S(1)} %multiply_convert_fusion), channel_id=1, replica_groups=mesh['ctx'=8,'tp'=4] {'tp'}, dimensions={1}, use_global_device_ids=true | all-gather | bytes 655360 | tf_op jit(solution)/shard_map/all_gather | solution.py:131
  148.4 1.4 convolution_convert_fusion
  (111 shorter events, 14.2 us)
Async XLA Ops:
  0.0 9.7 %copy-start.10 = (s32[8]{0:T(128)S(1)}, s32[8]{0:T(128)}, u32[]{:S(2)}) copy-start(s32[8]{0:T(128)} %constant.277.clone) | copy-start | bytes 100
  0.0 21.0 %copy-start.4 = (s32[8]{0:T(128)S(1)}, s32[8]{0:T(128)}, u32[]{:S(2)}) copy-start(s32[8]{0:T(128)} %constant.278.clone) | copy-start | bytes 100
  0.0 40.8 %copy-start.1 = (bf16[512,512]{1,0:T(8,128)(2,1)S(1)}, bf16[512,512]{1,0:T(8,128)(2,1)}, u32[]{:S(2)}) copy-start(bf16[512,512]{1,0:T(8,128)(2,1)} %param.15) | copy-start | bytes 1572868
  0.0 40.8 %copy-start.2 = (bf16[512,512]{1,0:T(8,128)(2,1)S(1)}, bf16[512,512]{1,0:T(8,128)(2,1)}, u32[]{:S(2)}) copy-start(bf16[512,512]{1,0:T(8,128)(2,1)} %param.14) | copy-start | bytes 1572868
  0.0 41.9 %copy-start.6 = (f32[3,512]{1,0:T(4,128)S(1)}, f32[3,512]{1,0:T(4,128)}, u32[]{:S(2)}) copy-start(f32[3,512]{1,0:T(4,128)} %param.19) | copy-start | bytes 18436
  0.0 42.0 %copy-start.7 = (f32[3,512]{1,0:T(4,128)S(1)}, f32[3,512]{1,0:T(4,128)}, u32[]{:S(2)}) copy-start(f32[3,512]{1,0:T(4,128)} %param.18) | copy-start | bytes 18436
  0.0 42.0 %copy-start.8 = (f32[3,512]{1,0:T(4,128)S(1)}, f32[3,512]{1,0:T(4,128)}, u32[]{:S(2)}) copy-start(f32[3,512]{1,0:T(4,128)} %param.17) | copy-start | bytes 18436
  0.0 42.0 %copy-start = (bf16[256,1024]{1,0:T(8,128)(2,1)S(1)}, bf16[256,1024]{1,0:T(8,128)(2,1)}, u32[]{:S(2)}) copy-start(bf16[256,1024]{1,0:T(8,128)(2,1)} %param.23) | copy-start | bytes 1572868
  2.4 39.6 %all-to-all-start = ((bf16[8,128,512]{1,2,0:T(8,128)(2,1)}), bf16[8,128,512]{1,2,0:T(8,128)(2,1)}, u32[]{:S(2)}, u32[]{:S(2)}) async-start(bf16[8,128,512]{1,2,0:T(8,128)(2,1)} %bitcast.2), calls=%async_computation | async-start | bytes 2097152 | tf_op jit(solution)/shard_map/all_to_all | solution.py:66
  46.1 8.1 %collective-permute-start = (bf16[130,768]{1,0:T(8,128)(2,1)S(1)}, bf16[130,768]{1,0:T(8,128)(2,1)S(1)}, u32[]{:S(2)}, u32[]{:S(2)}) collective-permute-start(bf16[130,768]{1,0:T(8,128)(2,1)S(1)} %convolution_convert_fusion.2), channel_id=1, source_target_pairs={{0,8},{8,16},{16,24},{24,28},{28,20},{20,12},{12,4},{4,0},{1,9},{9... | collective-permute-start | bytes 599048 | tf_op jit(solution)/shard_map/ppermute | solution.py:107
  48.2 8.1 %collective-permute-start.1 = (bf16[130,768]{1,0:T(8,128)(2,1)S(1)}, bf16[130,768]{1,0:T(8,128)(2,1)S(1)}, u32[]{:S(2)}, u32[]{:S(2)}) collective-permute-start(bf16[130,768]{1,0:T(8,128)(2,1)S(1)} %convolution_convert_fusion.1), channel_id=1, source_target_pairs={{8,0},{16,8},{24,16},{28,24},{20,28},{12,20},{4,12},{0,4},{9,1},{1... | collective-permute-start | bytes 599048 | tf_op jit(solution)/shard_map/ppermute | solution.py:108
  48.3 10.2 %collective-permute-start.2 = (bf16[128,1024]{1,0:T(8,128)(2,1)S(1)}, bf16[128,1024]{1,0:T(8,128)(2,1)S(1)}, u32[]{:S(2)}, u32[]{:S(2)}) collective-permute-start(bf16[128,1024]{1,0:T(8,128)(2,1)S(1)} %get-tuple-element.29), channel_id=1, source_target_pairs={{0,8},{8,16},{16,24},{24,28},{28,20},{20,12},{12,4},{4,0},{1,9},{9... | collective-permute-start | bytes 786440 | tf_op jit(solution)/shard_map/ppermute | solution.py:107
  50.2 9.7 %collective-permute-start.3 = (bf16[128,1024]{1,0:T(8,128)(2,1)S(1)}, bf16[128,1024]{1,0:T(8,128)(2,1)S(1)}, u32[]{:S(2)}, u32[]{:S(2)}) collective-permute-start(bf16[128,1024]{1,0:T(8,128)(2,1)S(1)} %get-tuple-element.30), channel_id=1, source_target_pairs={{8,0},{16,8},{24,16},{28,24},{20,28},{12,20},{4,12},{0,4},{9,1},{1... | collective-permute-start | bytes 786440 | tf_op jit(solution)/shard_map/ppermute | solution.py:108
  59.9 7.9 %collective-permute-start.4 = (bf16[130,768]{1,0:T(8,128)(2,1)S(1)}, bf16[130,768]{1,0:T(8,128)(2,1)S(1)}, u32[]{:S(2)}, u32[]{:S(2)}) collective-permute-start(bf16[130,768]{1,0:T(8,128)(2,1)S(1)} %add_convert_fusion.13), channel_id=1, source_target_pairs={{0,8},{8,16},{16,24},{24,28},{28,20},{20,12},{12,4},{4,0},{1,9},{9... | collective-permute-start | bytes 599048 | tf_op jit(solution)/shard_map/ppermute | solution.py:107
  61.3 7.7 %collective-permute-start.5 = (bf16[130,768]{1,0:T(8,128)(2,1)S(1)}, bf16[130,768]{1,0:T(8,128)(2,1)S(1)}, u32[]{:S(2)}, u32[]{:S(2)}) collective-permute-start(bf16[130,768]{1,0:T(8,128)(2,1)S(1)} %add_convert_fusion.12), channel_id=1, source_target_pairs={{8,0},{16,8},{24,16},{28,24},{20,28},{12,20},{4,12},{0,4},{9,1},{1... | collective-permute-start | bytes 599048 | tf_op jit(solution)/shard_map/ppermute | solution.py:108
  61.9 8.7 %collective-permute-start.6 = (bf16[128,1024]{1,0:T(8,128)(2,1)S(1)}, bf16[128,1024]{1,0:T(8,128)(2,1)S(1)}, u32[]{:S(2)}, u32[]{:S(2)}) collective-permute-start(bf16[128,1024]{1,0:T(8,128)(2,1)S(1)} %collective-permute-done.2), channel_id=1, source_target_pairs={{0,8},{8,16},{16,24},{24,28},{28,20},{20,12},{12,4},{4,0},{1,9},{9... | collective-permute-start | bytes 786440 | tf_op jit(solution)/shard_map/ppermute | solution.py:107
  63.4 8.5 %collective-permute-start.7 = (bf16[128,1024]{1,0:T(8,128)(2,1)S(1)}, bf16[128,1024]{1,0:T(8,128)(2,1)S(1)}, u32[]{:S(2)}, u32[]{:S(2)}) collective-permute-start(bf16[128,1024]{1,0:T(8,128)(2,1)S(1)} %collective-permute-done.3), channel_id=1, source_target_pairs={{8,0},{16,8},{24,16},{28,24},{20,28},{12,20},{4,12},{0,4},{9,1},{1... | collective-permute-start | bytes 786440 | tf_op jit(solution)/shard_map/ppermute | solution.py:108
  71.8 6.8 %collective-permute-start.8 = (bf16[130,768]{1,0:T(8,128)(2,1)S(1)}, bf16[130,768]{1,0:T(8,128)(2,1)S(1)}, u32[]{:S(2)}, u32[]{:S(2)}) collective-permute-start(bf16[130,768]{1,0:T(8,128)(2,1)S(1)} %add_convert_fusion.11), channel_id=1, source_target_pairs={{0,8},{8,16},{16,24},{24,28},{28,20},{20,12},{12,4},{4,0},{1,9},{9... | collective-permute-start | bytes 599048 | tf_op jit(solution)/shard_map/ppermute | solution.py:107
  73.3 6.5 %collective-permute-start.9 = (bf16[130,768]{1,0:T(8,128)(2,1)S(1)}, bf16[130,768]{1,0:T(8,128)(2,1)S(1)}, u32[]{:S(2)}, u32[]{:S(2)}) collective-permute-start(bf16[130,768]{1,0:T(8,128)(2,1)S(1)} %add_convert_fusion.10), channel_id=1, source_target_pairs={{8,0},{16,8},{24,16},{28,24},{20,28},{12,20},{4,12},{0,4},{9,1},{1... | collective-permute-start | bytes 599048 | tf_op jit(solution)/shard_map/ppermute | solution.py:108
  73.9 7.7 %collective-permute-start.10 = (bf16[128,1024]{1,0:T(8,128)(2,1)S(1)}, bf16[128,1024]{1,0:T(8,128)(2,1)S(1)}, u32[]{:S(2)}, u32[]{:S(2)}) collective-permute-start(bf16[128,1024]{1,0:T(8,128)(2,1)S(1)} %collective-permute-done.6), channel_id=1, source_target_pairs={{0,8},{8,16},{16,24},{24,28},{28,20},{20,12},{12,4},{4,0},{1,9},{9... | collective-permute-start | bytes 786440 | tf_op jit(solution)/shard_map/ppermute | solution.py:107
  75.3 8.9 %collective-permute-start.11 = (bf16[128,1024]{1,0:T(8,128)(2,1)S(1)}, bf16[128,1024]{1,0:T(8,128)(2,1)S(1)}, u32[]{:S(2)}, u32[]{:S(2)}) collective-permute-start(bf16[128,1024]{1,0:T(8,128)(2,1)S(1)} %collective-permute-done.7), channel_id=1, source_target_pairs={{8,0},{16,8},{24,16},{28,24},{20,28},{12,20},{4,12},{0,4},{9,1},{1... | collective-permute-start | bytes 786440 | tf_op jit(solution)/shard_map/ppermute | solution.py:108
  84.2 8.1 %collective-permute-start.16 = (bf16[130,768]{1,0:T(8,128)(2,1)S(1)}, bf16[130,768]{1,0:T(8,128)(2,1)S(1)}, u32[]{:S(2)}, u32[]{:S(2)}) collective-permute-start(bf16[130,768]{1,0:T(8,128)(2,1)S(1)} %add_convert_fusion.8), channel_id=1, source_target_pairs={{8,0},{16,8},{24,16},{28,24},{20,28},{12,20},{4,12},{0,4},{9,1},{1... | collective-permute-start | bytes 599048 | tf_op jit(solution)/shard_map/ppermute | solution.py:108
  84.8 8.2 %collective-permute-start.12 = (bf16[130,768]{1,0:T(8,128)(2,1)S(1)}, bf16[130,768]{1,0:T(8,128)(2,1)S(1)}, u32[]{:S(2)}, u32[]{:S(2)}) collective-permute-start(bf16[130,768]{1,0:T(8,128)(2,1)S(1)} %add_convert_fusion.9), channel_id=1, source_target_pairs={{0,8},{8,16},{16,24},{24,28},{28,20},{20,12},{12,4},{4,0},{1,9},{9... | collective-permute-start | bytes 599048 | tf_op jit(solution)/shard_map/ppermute | solution.py:107
  86.3 12.1 %collective-permute-start.27 = (bf16[128,1024]{1,0:T(8,128)(2,1)S(1)}, bf16[128,1024]{1,0:T(8,128)(2,1)S(1)}, u32[]{:S(2)}, u32[]{:S(2)}) collective-permute-start(bf16[128,1024]{1,0:T(8,128)(2,1)S(1)} %collective-permute-done.10), channel_id=1, source_target_pairs={{0,8},{8,16},{16,24},{24,28},{28,20},{20,12},{12,4},{4,0},{1,9},{9... | collective-permute-start | bytes 786440 | tf_op jit(solution)/shard_map/ppermute | solution.py:107
  87.9 12.0 %collective-permute-start.28 = (bf16[128,1024]{1,0:T(8,128)(2,1)S(1)}, bf16[128,1024]{1,0:T(8,128)(2,1)S(1)}, u32[]{:S(2)}, u32[]{:S(2)}) collective-permute-start(bf16[128,1024]{1,0:T(8,128)(2,1)S(1)} %collective-permute-done.11), channel_id=1, source_target_pairs={{8,0},{16,8},{24,16},{28,24},{20,28},{12,20},{4,12},{0,4},{9,1},{1... | collective-permute-start | bytes 786440 | tf_op jit(solution)/shard_map/ppermute | solution.py:108
  92.4 10.0 %collective-permute-start.17 = (bf16[130,768]{1,0:T(8,128)(2,1)S(1)}, bf16[130,768]{1,0:T(8,128)(2,1)S(1)}, u32[]{:S(2)}, u32[]{:S(2)}) collective-permute-start(bf16[130,768]{1,0:T(8,128)(2,1)S(1)} %add_convert_fusion.3), channel_id=1, source_target_pairs={{8,0},{16,8},{24,16},{28,24},{20,28},{12,20},{4,12},{0,4},{9,1},{1... | collective-permute-start | bytes 599048 | tf_op jit(solution)/shard_map/ppermute | solution.py:112
  93.1 10.0 %collective-permute-start.13 = (bf16[130,768]{1,0:T(8,128)(2,1)S(1)}, bf16[130,768]{1,0:T(8,128)(2,1)S(1)}, u32[]{:S(2)}, u32[]{:S(2)}) collective-permute-start(bf16[130,768]{1,0:T(8,128)(2,1)S(1)} %add_convert_fusion.7), channel_id=1, source_target_pairs={{0,8},{8,16},{16,24},{24,28},{28,20},{20,12},{12,4},{4,0},{1,9},{9... | collective-permute-start | bytes 599048 | tf_op jit(solution)/shard_map/ppermute | solution.py:111
  98.4 10.1 %collective-permute-start.29 = (bf16[128,1024]{1,0:T(8,128)(2,1)S(1)}, bf16[128,1024]{1,0:T(8,128)(2,1)S(1)}, u32[]{:S(2)}, u32[]{:S(2)}) collective-permute-start(bf16[128,1024]{1,0:T(8,128)(2,1)S(1)} %collective-permute-done.27), channel_id=1, source_target_pairs={{0,8},{8,16},{16,24},{24,28},{28,20},{20,12},{12,4},{4,0},{1,9},{9... | collective-permute-start | bytes 786440 | tf_op jit(solution)/shard_map/ppermute | solution.py:116
  99.9 10.1 %collective-permute-start.30 = (bf16[128,1024]{1,0:T(8,128)(2,1)S(1)}, bf16[128,1024]{1,0:T(8,128)(2,1)S(1)}, u32[]{:S(2)}, u32[]{:S(2)}) collective-permute-start(bf16[128,1024]{1,0:T(8,128)(2,1)S(1)} %collective-permute-done.28), channel_id=1, source_target_pairs={{8,0},{16,8},{24,16},{28,24},{20,28},{12,20},{4,12},{0,4},{9,1},{1... | collective-permute-start | bytes 786440 | tf_op jit(solution)/shard_map/ppermute | solution.py:117
  102.5 16.7 %copy-start.3 = (f32[16,512]{1,0:T(8,128)S(1)}, f32[16,512]{1,0:T(8,128)}, u32[]{:S(2)}) copy-start(f32[16,512]{1,0:T(8,128)} %param.20) | copy-start | bytes 98308
  102.5 9.8 %collective-permute-start.18 = (bf16[130,768]{1,0:T(8,128)(2,1)S(1)}, bf16[130,768]{1,0:T(8,128)(2,1)S(1)}, u32[]{:S(2)}, u32[]{:S(2)}) collective-permute-start(bf16[130,768]{1,0:T(8,128)(2,1)S(1)} %add_convert_fusion.2), channel_id=1, source_target_pairs={{8,0},{16,8},{24,16},{28,24},{20,28},{12,20},{4,12},{0,4},{9,1},{1... | collective-permute-start | bytes 599048 | tf_op jit(solution)/shard_map/ppermute | solution.py:112
  103.2 9.8 %collective-permute-start.14 = (bf16[130,768]{1,0:T(8,128)(2,1)S(1)}, bf16[130,768]{1,0:T(8,128)(2,1)S(1)}, u32[]{:S(2)}, u32[]{:S(2)}) collective-permute-start(bf16[130,768]{1,0:T(8,128)(2,1)S(1)} %add_convert_fusion.6), channel_id=1, source_target_pairs={{0,8},{8,16},{16,24},{24,28},{28,20},{20,12},{12,4},{4,0},{1,9},{9... | collective-permute-start | bytes 599048 | tf_op jit(solution)/shard_map/ppermute | solution.py:111
  108.5 17.3 %collective-permute-start.31 = (bf16[128,1024]{1,0:T(8,128)(2,1)S(1)}, bf16[128,1024]{1,0:T(8,128)(2,1)S(1)}, u32[]{:S(2)}, u32[]{:S(2)}) collective-permute-start(bf16[128,1024]{1,0:T(8,128)(2,1)S(1)} %collective-permute-done.29), channel_id=1, source_target_pairs={{0,8},{8,16},{16,24},{24,28},{28,20},{20,12},{12,4},{4,0},{1,9},{9... | collective-permute-start | bytes 786440 | tf_op jit(solution)/shard_map/ppermute | solution.py:116
  110.0 18.5 %collective-permute-start.32 = (bf16[128,1024]{1,0:T(8,128)(2,1)S(1)}, bf16[128,1024]{1,0:T(8,128)(2,1)S(1)}, u32[]{:S(2)}, u32[]{:S(2)}) collective-permute-start(bf16[128,1024]{1,0:T(8,128)(2,1)S(1)} %collective-permute-done.30), channel_id=1, source_target_pairs={{8,0},{16,8},{24,16},{28,24},{20,28},{12,20},{4,12},{0,4},{9,1},{1... | collective-permute-start | bytes 786440 | tf_op jit(solution)/shard_map/ppermute | solution.py:117
  110.6 9.3 %copy-start.5 = (f32[16,512]{1,0:T(8,128)S(1)}, f32[16,512]{1,0:T(8,128)}, u32[]{:S(2)}) copy-start(f32[16,512]{1,0:T(8,128)} %param.21) | copy-start | bytes 98308
  112.3 6.3 %collective-permute-start.19 = (bf16[130,768]{1,0:T(8,128)(2,1)S(1)}, bf16[130,768]{1,0:T(8,128)(2,1)S(1)}, u32[]{:S(2)}, u32[]{:S(2)}) collective-permute-start(bf16[130,768]{1,0:T(8,128)(2,1)S(1)} %add_convert_fusion.1), channel_id=1, source_target_pairs={{8,0},{16,8},{24,16},{28,24},{20,28},{12,20},{4,12},{0,4},{9,1},{1... | collective-permute-start | bytes 599048 | tf_op jit(solution)/shard_map/ppermute | solution.py:112
  113.0 5.9 %collective-permute-start.15 = (bf16[130,768]{1,0:T(8,128)(2,1)S(1)}, bf16[130,768]{1,0:T(8,128)(2,1)S(1)}, u32[]{:S(2)}, u32[]{:S(2)}) collective-permute-start(bf16[130,768]{1,0:T(8,128)(2,1)S(1)} %add_convert_fusion.5), channel_id=1, source_target_pairs={{0,8},{8,16},{16,24},{24,28},{28,20},{20,12},{12,4},{4,0},{1,9},{9... | collective-permute-start | bytes 599048 | tf_op jit(solution)/shard_map/ppermute | solution.py:111
  120.0 11.0 %collective-permute-start.26 = (f32[16,512]{1,0:T(8,128)S(1)}, f32[16,512]{1,0:T(8,128)S(1)}, u32[]{:S(2)}, u32[]{:S(2)}) collective-permute-start(f32[16,512]{1,0:T(8,128)S(1)} %get-tuple-element.48), channel_id=1, source_target_pairs={{0,28},{1,29},{2,30},{3,31}} | collective-permute-start | bytes 98312 | tf_op jit(solution)/shard_map/ppermute | solution.py:33
  124.5 7.7 %collective-permute-start.25 = (f32[16,512]{1,0:T(8,128)S(1)}, f32[16,512]{1,0:T(8,128)S(1)}, u32[]{:S(2)}, u32[]{:S(2)}) collective-permute-start(f32[16,512]{1,0:T(8,128)S(1)} %get-tuple-element.48), channel_id=1, source_target_pairs={{0,24},{4,28},{1,25},{5,29},{2,26},{6,30},{3,27},{7,31}} | collective-permute-start | bytes 98312 | tf_op jit(solution)/shard_map/ppermute | solution.py:33
  125.9 9.6 %collective-permute-start.24 = (f32[16,512]{1,0:T(8,128)S(1)}, f32[16,512]{1,0:T(8,128)S(1)}, u32[]{:S(2)}, u32[]{:S(2)}) collective-permute-start(f32[16,512]{1,0:T(8,128)S(1)} %get-tuple-element.48), channel_id=1, source_target_pairs={{0,20},{4,24},{8,28},{1,21},{5,25},{9,29},{2,22},{6,26},{10,30},{3... | collective-permute-start | bytes 98312 | tf_op jit(solution)/shard_map/ppermute | solution.py:33
  127.2 8.3 %collective-permute-start.23 = (f32[16,512]{1,0:T(8,128)S(1)}, f32[16,512]{1,0:T(8,128)S(1)}, u32[]{:S(2)}, u32[]{:S(2)}) collective-permute-start(f32[16,512]{1,0:T(8,128)S(1)} %get-tuple-element.48), channel_id=1, source_target_pairs={{0,16},{4,20},{8,24},{12,28},{1,17},{5,21},{9,25},{13,29},{2,18},{... | collective-permute-start | bytes 98312 | tf_op jit(solution)/shard_map/ppermute | solution.py:33
  128.5 9.0 %collective-permute-start.22 = (f32[16,512]{1,0:T(8,128)S(1)}, f32[16,512]{1,0:T(8,128)S(1)}, u32[]{:S(2)}, u32[]{:S(2)}) collective-permute-start(f32[16,512]{1,0:T(8,128)S(1)} %get-tuple-element.48), channel_id=1, source_target_pairs={{0,12},{4,16},{8,20},{12,24},{16,28},{1,13},{5,17},{9,21},{13,25},... | collective-permute-start | bytes 98312 | tf_op jit(solution)/shard_map/ppermute | solution.py:33
  131.0 6.5 %collective-permute-start.21 = (f32[16,512]{1,0:T(8,128)S(1)}, f32[16,512]{1,0:T(8,128)S(1)}, u32[]{:S(2)}, u32[]{:S(2)}) collective-permute-start(f32[16,512]{1,0:T(8,128)S(1)} %get-tuple-element.48), channel_id=1, source_target_pairs={{0,8},{4,12},{8,16},{12,20},{16,24},{20,28},{1,9},{5,13},{9,17},{1... | collective-permute-start | bytes 98312 | tf_op jit(solution)/shard_map/ppermute | solution.py:33
  132.3 5.2 %collective-permute-start.20 = (f32[16,512]{1,0:T(8,128)S(1)}, f32[16,512]{1,0:T(8,128)S(1)}, u32[]{:S(2)}, u32[]{:S(2)}) collective-permute-start(f32[16,512]{1,0:T(8,128)S(1)} %get-tuple-element.48), channel_id=1, source_target_pairs={{0,4},{4,8},{8,12},{12,16},{16,20},{20,24},{24,28},{1,5},{5,9},{9,... | collective-permute-start | bytes 98312 | tf_op jit(solution)/shard_map/ppermute | solution.py:33
  135.4 12.9 %collective-permute-start.33 = (bf16[128,1024]{1,0:T(8,128)(2,1)S(1)}, bf16[128,1024]{1,0:T(8,128)(2,1)S(1)}, u32[]{:S(2)}, u32[]{:S(2)}) collective-permute-start(bf16[128,1024]{1,0:T(8,128)(2,1)S(1)} %collective-permute-done.31), channel_id=1, source_target_pairs={{0,8},{8,16},{16,24},{24,28},{28,20},{20,12},{12,4},{4,0},{1,9},{9... | collective-permute-start | bytes 786440 | tf_op jit(solution)/shard_map/ppermute | solution.py:116
  135.5 12.9 %collective-permute-start.34 = (bf16[128,1024]{1,0:T(8,128)(2,1)S(1)}, bf16[128,1024]{1,0:T(8,128)(2,1)S(1)}, u32[]{:S(2)}, u32[]{:S(2)}) collective-permute-start(bf16[128,1024]{1,0:T(8,128)(2,1)S(1)} %collective-permute-done.32), channel_id=1, source_target_pairs={{8,0},{16,8},{24,16},{28,24},{20,28},{12,20},{4,12},{0,4},{9,1},{1... | collective-permute-start | bytes 786440 | tf_op jit(solution)/shard_map/ppermute | solution.py:117
  137.6 3.3 %copy-start.9 = (f32[512]{0:T(512)S(1)}, f32[512]{0:T(512)}, u32[]{:S(2)}) copy-start(f32[512]{0:T(512)} %param.22) | copy-start | bytes 6148

commit v18 on v15

--- a/solution.py
+++ b/solution.py
@@ -98,7 +98,7 @@
 
     up = piece(ring_arr[(my_pos - 1) % ctx_count], 0)
     down = piece(ring_arr[(my_pos + 1) % ctx_count], 1)
-    tied = max(ctx_count - 4, 0)
+    tied = max(ctx_count - 5, 0)
     for step in range(1, ctx_count):
         if step <= tied:
             sent = lax.optimization_barrier(

time: 150 us -> 158 us (1.053)
  waiting for transfers between devices: 42.3 us -> 49 us
    ppermute x3 -> x4, waiting for transfers between devices: 3.84 us -> 10.2 us  [body(): w_up = lax.ppermute(w_up, 'ctx', perm=fwd)]
    ppermute x3 -> x4, waiting for transfers between devices: 7.66 us -> 13.7 us  [body(): down = lax.ppermute(down.astype(jnp.bfloat16), 'ctx', perm=bwd)]
    ppermute x8 -> x6, waiting for transfers between devices: 17.2 us -> 12.7 us  [body(): up, w_up = lax.ppermute((sent[0], sent[2]), 'ctx', perm=fwd)]
    ppermute x8 -> x6, waiting for transfers between devices: 13.3 us -> 9.99 us  [body(): down, w_low = lax.ppermute((sent[1], sent[3]), 'ctx', perm=bwd)]
    ppermute x8 -> x6, starting transfers between devices: 13 us -> 9.89 us  [body(): up, w_up = lax.ppermute((sent[0], sent[2]), 'ctx', perm=fwd)]
    ppermute x3 -> x4, starting transfers between devices: 2.98 us -> 5.05 us  [body(): w_up = lax.ppermute(w_up, 'ctx', perm=fwd)]
    ppermute x3 -> x4, waiting for transfers between devices: 0.01 us -> 1.72 us  [body(): w_low = lax.ppermute(w_low, 'ctx', perm=bwd)]
    ppermute x3 -> x4, starting transfers between devices: 4.51 us -> 6.09 us  [body(): up = lax.ppermute(up.astype(jnp.bfloat16), 'ctx', perm=fwd)]
  transfers between devices with their start and end apart: 36 -> 36, of which waited for: 19 -> 18; matrix products, arithmetic and copies ran while one was open for 7% -> 7% of each run, Pallas kernels for 0% -> 0%
where the time goes in v18:
time: 158 us; the launch traced here: 157 us
  starting transfers between devices  52.2 us (33%)
  waiting for transfers between devices  49 us (31%)
  between operations  30.5 us (19%)
  matrix products  9.06 us (6%)
  blocking collectives  7.17 us (5%)
  local copies, waits for them, and re-layouts  6.5 us (4%)
  other arithmetic  3.03 us (2%)
    ppermute x7, starting transfers between devices, modal_long_conv(): lax.ppermute(end_state, 'ctx', perm=[(i, i + shift) for i in range(ctx_co...  15.9 us
    ppermute x4, waiting for transfers between devices, body(): down = lax.ppermute(down.astype(jnp.bfloat16), 'ctx', perm=bwd)  13.7 us
    ppermute x6, waiting for transfers between devices, body(): up, w_up = lax.ppermute((sent[0], sent[2]), 'ctx', perm=fwd)  12.7 us
    ppermute x4, waiting for transfers between devices, body(): w_up = lax.ppermute(w_up, 'ctx', perm=fwd)  10.2 us
    ppermute x6, waiting for transfers between devices, body(): down, w_low = lax.ppermute((sent[1], sent[3]), 'ctx', perm=bwd)  9.99 us
    ppermute x6, starting transfers between devices, body(): up, w_up = lax.ppermute((sent[0], sent[2]), 'ctx', perm=fwd)  9.89 us
    all_to_all x1, starting transfers between devices, body(): lax.all_to_all(by_dest, 'ctx', split_axis=0, concat_axis=0, tiled=True)  7.29 us
    all_gather x1, blocking collectives, body(): features = lax.all_gather(gated, 'tp', axis=1, tiled=True)  7.17 us
  transfers between devices with their start and end apart: 36, of which 18 were waited for; matrix products, arithmetic and copies ran while one was open for 7% of the time, Pallas kernels for 0%

profile of v18, /device:TPU:0, one launch (start us, length us, event | category | flops | bytes accessed | tf_op | source)
XLA Modules:
  0.0 157.3 jit_solution(4799369986152081017)
XLA Ops:
  0.0 2.4 %copy.14 = bf16[128,4096]{0,1:T(8,128)(2,1)} copy(bf16[128,4096]{1,0:T(8,128)(2,1)} %param.13) | data formatting | bytes 2097152 | tf_op args[0]
  2.4 7.3 %all-to-all-start = ((bf16[8,128,512]{1,2,0:T(8,128)(2,1)}), bf16[8,128,512]{1,2,0:T(8,128)(2,1)}, u32[]{:S(2)}, u32[]{:S(2)}) async-start(bf16[8,128,512]{1,2,0:T(8,128)(2,1)} %bitcast.2), calls=%async_computation | async-start | bytes 2097152 | tf_op jit(solution)/shard_map/all_to_all | solution.py:66
  21.0 0.8 fusion.70
  41.0 1.1 pad_maximum_fusion.1
  42.3 1.5 copy.15
  46.3 2.1 %collective-permute-start = (bf16[130,768]{1,0:T(8,128)(2,1)S(1)}, bf16[130,768]{1,0:T(8,128)(2,1)S(1)}, u32[]{:S(2)}, u32[]{:S(2)}) collective-permute-start(bf16[130,768]{1,0:T(8,128)(2,1)S(1)} %convolution_convert_fusion.2), channel_id=1, source_target_pairs={{0,8},{8,16},{16,24},{24,28},{28,20},{20,12},{12,4},{4,0},{1,9},{9... | collective-permute-start | bytes 599048 | tf_op jit(solution)/shard_map/ppermute | solution.py:107
  48.4 2.0 %collective-permute-start.2 = (bf16[128,1024]{1,0:T(8,128)(2,1)S(1)}, bf16[128,1024]{1,0:T(8,128)(2,1)S(1)}, u32[]{:S(2)}, u32[]{:S(2)}) collective-permute-start(bf16[128,1024]{1,0:T(8,128)(2,1)S(1)} %get-tuple-element.25), channel_id=1, source_target_pairs={{0,8},{8,16},{16,24},{24,28},{28,20},{20,12},{12,4},{4,0},{1,9},{9... | collective-permute-start | bytes 786440 | tf_op jit(solution)/shard_map/ppermute | solution.py:107
  52.8 1.7 %collective-permute-done = bf16[130,768]{1,0:T(8,128)(2,1)S(1)} collective-permute-done((bf16[130,768]{1,0:T(8,128)(2,1)S(1)}, bf16[130,768]{1,0:T(8,128)(2,1)S(1)}, u32[]{:S(2)}, u32[]{:S(2)}) %collective-permute-start) | collective-permute-done | bytes 199712 | tf_op jit(solution)/shard_map/ppermute | solution.py:107
  54.7 1.7 %collective-permute-done.1 = bf16[130,768]{1,0:T(8,128)(2,1)S(1)} collective-permute-done((bf16[130,768]{1,0:T(8,128)(2,1)S(1)}, bf16[130,768]{1,0:T(8,128)(2,1)S(1)}, u32[]{:S(2)}, u32[]{:S(2)}) %collective-permute-start.1) | collective-permute-done | bytes 199712 | tf_op jit(solution)/shard_map/ppermute | solution.py:108
  56.8 1.8 %collective-permute-done.2 = bf16[128,1024]{1,0:T(8,128)(2,1)S(1)} collective-permute-done((bf16[128,1024]{1,0:T(8,128)(2,1)S(1)}, bf16[128,1024]{1,0:T(8,128)(2,1)S(1)}, u32[]{:S(2)}, u32[]{:S(2)}) %collective-permute-start.2) | collective-permute-done | bytes 262176 | tf_op jit(solution)/shard_map/ppermute | solution.py:107
  58.6 1.5 collective-permute-done.3
  60.1 1.5 collective-permute-start.4
  62.1 1.5 collective-permute-start.6
  64.2 3.8 %collective-permute-done.4 = bf16[130,768]{1,0:T(8,128)(2,1)S(1)} collective-permute-done((bf16[130,768]{1,0:T(8,128)(2,1)S(1)}, bf16[130,768]{1,0:T(8,128)(2,1)S(1)}, u32[]{:S(2)}, u32[]{:S(2)}) %collective-permute-start.4) | collective-permute-done | bytes 199712 | tf_op jit(solution)/shard_map/ppermute | solution.py:107
  68.1 1.1 collective-permute-done.5
  69.2 1.6 %collective-permute-done.6 = bf16[128,1024]{1,0:T(8,128)(2,1)S(1)} collective-permute-done((bf16[128,1024]{1,0:T(8,128)(2,1)S(1)}, bf16[128,1024]{1,0:T(8,128)(2,1)S(1)}, u32[]{:S(2)}, u32[]{:S(2)}) %collective-permute-start.6) | collective-permute-done | bytes 262176 | tf_op jit(solution)/shard_map/ppermute | solution.py:107
  70.8 1.7 %collective-permute-done.7 = bf16[128,1024]{1,0:T(8,128)(2,1)S(1)} collective-permute-done((bf16[128,1024]{1,0:T(8,128)(2,1)S(1)}, bf16[128,1024]{1,0:T(8,128)(2,1)S(1)}, u32[]{:S(2)}, u32[]{:S(2)}) %collective-permute-start.7) | collective-permute-done | bytes 262176 | tf_op jit(solution)/shard_map/ppermute | solution.py:108
  73.0 1.5 collective-permute-start.8
  74.5 1.5 collective-permute-start.25
  76.6 4.0 %collective-permute-done.13 = bf16[130,768]{1,0:T(8,128)(2,1)S(1)} collective-permute-done((bf16[130,768]{1,0:T(8,128)(2,1)S(1)}, bf16[130,768]{1,0:T(8,128)(2,1)S(1)}, u32[]{:S(2)}, u32[]{:S(2)}) %collective-permute-start.13) | collective-permute-done | bytes 199712 | tf_op jit(solution)/shard_map/ppermute | solution.py:108
  80.6 0.6 collective-permute-start.14
  81.3 1.5 collective-permute-start.9
  82.8 3.7 %collective-permute-done.25 = bf16[128,1024]{1,0:T(8,128)(2,1)S(1)} collective-permute-done((bf16[128,1024]{1,0:T(8,128)(2,1)S(1)}, bf16[128,1024]{1,0:T(8,128)(2,1)S(1)}, u32[]{:S(2)}, u32[]{:S(2)}) %collective-permute-start.25) | collective-permute-done | bytes 262176 | tf_op jit(solution)/shard_map/ppermute | solution.py:107
  86.5 1.5 collective-permute-start.27
  88.6 2.0 %collective-permute-done.14 = bf16[130,768]{1,0:T(8,128)(2,1)S(1)} collective-permute-done((bf16[130,768]{1,0:T(8,128)(2,1)S(1)}, bf16[130,768]{1,0:T(8,128)(2,1)S(1)}, u32[]{:S(2)}, u32[]{:S(2)}) %collective-permute-start.14) | collective-permute-done | bytes 199712 | tf_op jit(solution)/shard_map/ppermute | solution.py:112
  91.4 1.5 collective-permute-start.10
  92.9 3.7 %collective-permute-done.27 = bf16[128,1024]{1,0:T(8,128)(2,1)S(1)} collective-permute-done((bf16[128,1024]{1,0:T(8,128)(2,1)S(1)}, bf16[128,1024]{1,0:T(8,128)(2,1)S(1)}, u32[]{:S(2)}, u32[]{:S(2)}) %collective-permute-start.27) | collective-permute-done | bytes 262176 | tf_op jit(solution)/shard_map/ppermute | solution.py:116
  96.6 1.5 collective-permute-start.29
  98.7 3.0 %collective-permute-done.15 = bf16[130,768]{1,0:T(8,128)(2,1)S(1)} collective-permute-done((bf16[130,768]{1,0:T(8,128)(2,1)S(1)}, bf16[130,768]{1,0:T(8,128)(2,1)S(1)}, u32[]{:S(2)}, u32[]{:S(2)}) %collective-permute-start.15) | collective-permute-done | bytes 199712 | tf_op jit(solution)/shard_map/ppermute | solution.py:112
  102.4 1.5 collective-permute-start.11
  104.0 5.1 %collective-permute-done.16 = bf16[130,768]{1,0:T(8,128)(2,1)S(1)} collective-permute-done((bf16[130,768]{1,0:T(8,128)(2,1)S(1)}, bf16[130,768]{1,0:T(8,128)(2,1)S(1)}, u32[]{:S(2)}, u32[]{:S(2)}) %collective-permute-start.16) | collective-permute-done | bytes 199712 | tf_op jit(solution)/shard_map/ppermute | solution.py:112
  109.7 1.5 collective-permute-start.12
  111.2 3.7 %collective-permute-done.17 = bf16[130,768]{1,0:T(8,128)(2,1)S(1)} collective-permute-done((bf16[130,768]{1,0:T(8,128)(2,1)S(1)}, bf16[130,768]{1,0:T(8,128)(2,1)S(1)}, u32[]{:S(2)}, u32[]{:S(2)}) %collective-permute-start.17) | collective-permute-done | bytes 199712 | tf_op jit(solution)/shard_map/ppermute | solution.py:112
  115.9 0.8 fusion
  116.7 5.2 %collective-permute-start.24 = (f32[16,512]{1,0:T(8,128)S(1)}, f32[16,512]{1,0:T(8,128)S(1)}, u32[]{:S(2)}, u32[]{:S(2)}) collective-permute-start(f32[16,512]{1,0:T(8,128)S(1)} %exponential_multiply_fusion.5), channel_id=1, source_target_pairs={{0,28},{1,29},{2,30},{3,31}} | collective-permute-start | bytes 98312 | tf_op jit(solution)/shard_map/ppermute | solution.py:33
  121.9 1.3 collective-permute-start.23
  123.2 1.3 collective-permute-start.22
  124.5 1.3 collective-permute-start.21
  125.8 2.5 %collective-permute-start.20 = (f32[16,512]{1,0:T(8,128)S(1)}, f32[16,512]{1,0:T(8,128)S(1)}, u32[]{:S(2)}, u32[]{:S(2)}) collective-permute-start(f32[16,512]{1,0:T(8,128)S(1)} %exponential_multiply_fusion.5), channel_id=1, source_target_pairs={{0,12},{4,16},{8,20},{12,24},{16,28},{1,13},{5,17},{9,21},{13,25},... | collective-permute-start | bytes 98312 | tf_op jit(solution)/shard_map/ppermute | solution.py:33
  128.3 1.3 collective-permute-start.19
  129.6 3.1 %collective-permute-start.18 = (f32[16,512]{1,0:T(8,128)S(1)}, f32[16,512]{1,0:T(8,128)S(1)}, u32[]{:S(2)}, u32[]{:S(2)}) collective-permute-start(f32[16,512]{1,0:T(8,128)S(1)} %exponential_multiply_fusion.5), channel_id=1, source_target_pairs={{0,4},{4,8},{8,12},{12,16},{16,20},{20,24},{24,28},{1,5},{5,9},{9,... | collective-permute-start | bytes 98312 | tf_op jit(solution)/shard_map/ppermute | solution.py:33
  132.8 2.0 %collective-permute-start.32 = (bf16[128,1024]{1,0:T(8,128)(2,1)S(1)}, bf16[128,1024]{1,0:T(8,128)(2,1)S(1)}, u32[]{:S(2)}, u32[]{:S(2)}) collective-permute-start(bf16[128,1024]{1,0:T(8,128)(2,1)S(1)} %collective-permute-done.30), channel_id=1, source_target_pairs={{8,0},{16,8},{24,16},{28,24},{20,28},{12,20},{4,12},{0,4},{9,1},{1... | collective-permute-start | bytes 786440 | tf_op jit(solution)/shard_map/ppermute | solution.py:117
  135.0 3.1 %multiply_reduce_fusion = f32[128,512]{1,0:T(8,128)S(1)} fusion(f32[16,512]{1,0:T(8,128)S(1)} %get-tuple-element.40, f32[16,512]{1,0:T(8,128)S(1)} %get-tuple-element.41, f32[16,512]{1,0:T(8,128)S(1)} %get-tuple-element.39, f32[128,512]{1,0:T(8,128)S(1)} %fusion.48, f32[16,512]{1,0:T(8,128)S(1)} %copy-done.3, f32[128,128]{1,0:T(8,128)S(1)} %fusion.49), kind=kOutput, calls=%fused_computation | convolution fusion | flops 812580864 | bytes 720896 | tf_op jit(solution)/shard_map/dot_general | solution.py:23
  138.4 7.2 %all_gather.3 = bf16[128,2048]{1,0:T(8,128)(2,1)S(1)} all-gather(bf16[128,512]{1,0:T(8,128)(2,1)S(1)} %multiply_convert_fusion), channel_id=1, replica_groups=mesh['ctx'=8,'tp'=4] {'tp'}, dimensions={1}, use_global_device_ids=true | all-gather | bytes 655360 | tf_op jit(solution)/shard_map/all_gather | solution.py:131
  145.6 2.0 %collective-permute-start.33 = (bf16[128,1024]{1,0:T(8,128)(2,1)S(1)}, bf16[128,1024]{1,0:T(8,128)(2,1)S(1)}, u32[]{:S(2)}, u32[]{:S(2)}) collective-permute-start(bf16[128,1024]{1,0:T(8,128)(2,1)S(1)} %collective-permute-done.31), channel_id=1, source_target_pairs={{0,8},{8,16},{16,24},{24,28},{28,20},{20,12},{12,4},{4,0},{1,9},{9... | collective-permute-start | bytes 786440 | tf_op jit(solution)/shard_map/ppermute | solution.py:116
  147.7 6.5 %collective-permute-done.33 = bf16[128,1024]{1,0:T(8,128)(2,1)S(1)} collective-permute-done((bf16[128,1024]{1,0:T(8,128)(2,1)S(1)}, bf16[128,1024]{1,0:T(8,128)(2,1)S(1)}, u32[]{:S(2)}, u32[]{:S(2)}) %collective-permute-start.33) | collective-permute-done | bytes 262176 | tf_op jit(solution)/shard_map/ppermute | solution.py:116
  154.2 1.7 %collective-permute-done.34 = bf16[128,1024]{1,0:T(8,128)(2,1)S(1)} collective-permute-done((bf16[128,1024]{1,0:T(8,128)(2,1)S(1)}, bf16[128,1024]{1,0:T(8,128)(2,1)S(1)}, u32[]{:S(2)}, u32[]{:S(2)}) %collective-permute-start.34) | collective-permute-done | bytes 262176 | tf_op jit(solution)/shard_map/ppermute | solution.py:117
  155.9 1.4 convolution_convert_fusion
  (111 shorter events, 13.5 us)
Async XLA Ops:
  0.0 9.7 %copy-start.10 = (s32[8]{0:T(128)S(1)}, s32[8]{0:T(128)}, u32[]{:S(2)}) copy-start(s32[8]{0:T(128)} %constant.275.clone) | copy-start | bytes 100
  0.0 21.0 %copy-start.4 = (s32[8]{0:T(128)S(1)}, s32[8]{0:T(128)}, u32[]{:S(2)}) copy-start(s32[8]{0:T(128)} %constant.276.clone) | copy-start | bytes 100
  0.0 41.0 %copy-start.1 = (bf16[512,512]{1,0:T(8,128)(2,1)S(1)}, bf16[512,512]{1,0:T(8,128)(2,1)}, u32[]{:S(2)}) copy-start(bf16[512,512]{1,0:T(8,128)(2,1)} %param.15) | copy-start | bytes 1572868
  0.0 41.0 %copy-start.2 = (bf16[512,512]{1,0:T(8,128)(2,1)S(1)}, bf16[512,512]{1,0:T(8,128)(2,1)}, u32[]{:S(2)}) copy-start(bf16[512,512]{1,0:T(8,128)(2,1)} %param.14) | copy-start | bytes 1572868
  0.0 42.1 %copy-start.6 = (f32[3,512]{1,0:T(4,128)S(1)}, f32[3,512]{1,0:T(4,128)}, u32[]{:S(2)}) copy-start(f32[3,512]{1,0:T(4,128)} %param.19) | copy-start | bytes 18436
  0.0 42.1 %copy-start.7 = (f32[3,512]{1,0:T(4,128)S(1)}, f32[3,512]{1,0:T(4,128)}, u32[]{:S(2)}) copy-start(f32[3,512]{1,0:T(4,128)} %param.18) | copy-start | bytes 18436
  0.0 42.2 %copy-start.8 = (f32[3,512]{1,0:T(4,128)S(1)}, f32[3,512]{1,0:T(4,128)}, u32[]{:S(2)}) copy-start(f32[3,512]{1,0:T(4,128)} %param.17) | copy-start | bytes 18436
  0.0 42.2 %copy-start = (bf16[256,1024]{1,0:T(8,128)(2,1)S(1)}, bf16[256,1024]{1,0:T(8,128)(2,1)}, u32[]{:S(2)}) copy-start(bf16[256,1024]{1,0:T(8,128)(2,1)} %param.23) | copy-start | bytes 1572868
  2.4 39.8 %all-to-all-start = ((bf16[8,128,512]{1,2,0:T(8,128)(2,1)}), bf16[8,128,512]{1,2,0:T(8,128)(2,1)}, u32[]{:S(2)}, u32[]{:S(2)}) async-start(bf16[8,128,512]{1,2,0:T(8,128)(2,1)} %bitcast.2), calls=%async_computation | async-start | bytes 2097152 | tf_op jit(solution)/shard_map/all_to_all | solution.py:66
  46.3 8.1 %collective-permute-start = (bf16[130,768]{1,0:T(8,128)(2,1)S(1)}, bf16[130,768]{1,0:T(8,128)(2,1)S(1)}, u32[]{:S(2)}, u32[]{:S(2)}) collective-permute-start(bf16[130,768]{1,0:T(8,128)(2,1)S(1)} %convolution_convert_fusion.2), channel_id=1, source_target_pairs={{0,8},{8,16},{16,24},{24,28},{28,20},{20,12},{12,4},{4,0},{1,9},{9... | collective-permute-start | bytes 599048 | tf_op jit(solution)/shard_map/ppermute | solution.py:107
  48.4 8.1 %collective-permute-start.1 = (bf16[130,768]{1,0:T(8,128)(2,1)S(1)}, bf16[130,768]{1,0:T(8,128)(2,1)S(1)}, u32[]{:S(2)}, u32[]{:S(2)}) collective-permute-start(bf16[130,768]{1,0:T(8,128)(2,1)S(1)} %convolution_convert_fusion.1), channel_id=1, source_target_pairs={{8,0},{16,8},{24,16},{28,24},{20,28},{12,20},{4,12},{0,4},{9,1},{1... | collective-permute-start | bytes 599048 | tf_op jit(solution)/shard_map/ppermute | solution.py:108
  48.4 10.2 %collective-permute-start.2 = (bf16[128,1024]{1,0:T(8,128)(2,1)S(1)}, bf16[128,1024]{1,0:T(8,128)(2,1)S(1)}, u32[]{:S(2)}, u32[]{:S(2)}) collective-permute-start(bf16[128,1024]{1,0:T(8,128)(2,1)S(1)} %get-tuple-element.25), channel_id=1, source_target_pairs={{0,8},{8,16},{16,24},{24,28},{28,20},{20,12},{12,4},{4,0},{1,9},{9... | collective-permute-start | bytes 786440 | tf_op jit(solution)/shard_map/ppermute | solution.py:107
  50.4 9.7 %collective-permute-start.3 = (bf16[128,1024]{1,0:T(8,128)(2,1)S(1)}, bf16[128,1024]{1,0:T(8,128)(2,1)S(1)}, u32[]{:S(2)}, u32[]{:S(2)}) collective-permute-start(bf16[128,1024]{1,0:T(8,128)(2,1)S(1)} %get-tuple-element.26), channel_id=1, source_target_pairs={{8,0},{16,8},{24,16},{28,24},{20,28},{12,20},{4,12},{0,4},{9,1},{1... | collective-permute-start | bytes 786440 | tf_op jit(solution)/shard_map/ppermute | solution.py:108
  60.1 7.9 %collective-permute-start.4 = (bf16[130,768]{1,0:T(8,128)(2,1)S(1)}, bf16[130,768]{1,0:T(8,128)(2,1)S(1)}, u32[]{:S(2)}, u32[]{:S(2)}) collective-permute-start(bf16[130,768]{1,0:T(8,128)(2,1)S(1)} %add_convert_fusion.13), channel_id=1, source_target_pairs={{0,8},{8,16},{16,24},{24,28},{28,20},{20,12},{12,4},{4,0},{1,9},{9... | collective-permute-start | bytes 599048 | tf_op jit(solution)/shard_map/ppermute | solution.py:107
  61.5 7.7 %collective-permute-start.5 = (bf16[130,768]{1,0:T(8,128)(2,1)S(1)}, bf16[130,768]{1,0:T(8,128)(2,1)S(1)}, u32[]{:S(2)}, u32[]{:S(2)}) collective-permute-start(bf16[130,768]{1,0:T(8,128)(2,1)S(1)} %add_convert_fusion.12), channel_id=1, source_target_pairs={{8,0},{16,8},{24,16},{28,24},{20,28},{12,20},{4,12},{0,4},{9,1},{1... | collective-permute-start | bytes 599048 | tf_op jit(solution)/shard_map/ppermute | solution.py:108
  62.1 8.7 %collective-permute-start.6 = (bf16[128,1024]{1,0:T(8,128)(2,1)S(1)}, bf16[128,1024]{1,0:T(8,128)(2,1)S(1)}, u32[]{:S(2)}, u32[]{:S(2)}) collective-permute-start(bf16[128,1024]{1,0:T(8,128)(2,1)S(1)} %collective-permute-done.2), channel_id=1, source_target_pairs={{0,8},{8,16},{16,24},{24,28},{28,20},{20,12},{12,4},{4,0},{1,9},{9... | collective-permute-start | bytes 786440 | tf_op jit(solution)/shard_map/ppermute | solution.py:107
  63.6 8.9 %collective-permute-start.7 = (bf16[128,1024]{1,0:T(8,128)(2,1)S(1)}, bf16[128,1024]{1,0:T(8,128)(2,1)S(1)}, u32[]{:S(2)}, u32[]{:S(2)}) collective-permute-start(bf16[128,1024]{1,0:T(8,128)(2,1)S(1)} %collective-permute-done.3), channel_id=1, source_target_pairs={{8,0},{16,8},{24,16},{28,24},{20,28},{12,20},{4,12},{0,4},{9,1},{1... | collective-permute-start | bytes 786440 | tf_op jit(solution)/shard_map/ppermute | solution.py:108
  72.5 8.1 %collective-permute-start.13 = (bf16[130,768]{1,0:T(8,128)(2,1)S(1)}, bf16[130,768]{1,0:T(8,128)(2,1)S(1)}, u32[]{:S(2)}, u32[]{:S(2)}) collective-permute-start(bf16[130,768]{1,0:T(8,128)(2,1)S(1)} %add_convert_fusion.10), channel_id=1, source_target_pairs={{8,0},{16,8},{24,16},{28,24},{20,28},{12,20},{4,12},{0,4},{9,1},{1... | collective-permute-start | bytes 599048 | tf_op jit(solution)/shard_map/ppermute | solution.py:108
  73.0 8.2 %collective-permute-start.8 = (bf16[130,768]{1,0:T(8,128)(2,1)S(1)}, bf16[130,768]{1,0:T(8,128)(2,1)S(1)}, u32[]{:S(2)}, u32[]{:S(2)}) collective-permute-start(bf16[130,768]{1,0:T(8,128)(2,1)S(1)} %add_convert_fusion.11), channel_id=1, source_target_pairs={{0,8},{8,16},{16,24},{24,28},{28,20},{20,12},{12,4},{4,0},{1,9},{9... | collective-permute-start | bytes 599048 | tf_op jit(solution)/shard_map/ppermute | solution.py:107
  74.5 12.0 %collective-permute-start.25 = (bf16[128,1024]{1,0:T(8,128)(2,1)S(1)}, bf16[128,1024]{1,0:T(8,128)(2,1)S(1)}, u32[]{:S(2)}, u32[]{:S(2)}) collective-permute-start(bf16[128,1024]{1,0:T(8,128)(2,1)S(1)} %collective-permute-done.6), channel_id=1, source_target_pairs={{0,8},{8,16},{16,24},{24,28},{28,20},{20,12},{12,4},{4,0},{1,9},{9... | collective-permute-start | bytes 786440 | tf_op jit(solution)/shard_map/ppermute | solution.py:107
  76.0 12.1 %collective-permute-start.26 = (bf16[128,1024]{1,0:T(8,128)(2,1)S(1)}, bf16[128,1024]{1,0:T(8,128)(2,1)S(1)}, u32[]{:S(2)}, u32[]{:S(2)}) collective-permute-start(bf16[128,1024]{1,0:T(8,128)(2,1)S(1)} %collective-permute-done.7), channel_id=1, source_target_pairs={{8,0},{16,8},{24,16},{28,24},{20,28},{12,20},{4,12},{0,4},{9,1},{1... | collective-permute-start | bytes 786440 | tf_op jit(solution)/shard_map/ppermute | solution.py:108
  80.6 10.0 %collective-permute-start.14 = (bf16[130,768]{1,0:T(8,128)(2,1)S(1)}, bf16[130,768]{1,0:T(8,128)(2,1)S(1)}, u32[]{:S(2)}, u32[]{:S(2)}) collective-permute-start(bf16[130,768]{1,0:T(8,128)(2,1)S(1)} %add_convert_fusion.4), channel_id=1, source_target_pairs={{8,0},{16,8},{24,16},{28,24},{20,28},{12,20},{4,12},{0,4},{9,1},{1... | collective-permute-start | bytes 599048 | tf_op jit(solution)/shard_map/ppermute | solution.py:112
  81.3 10.0 %collective-permute-start.9 = (bf16[130,768]{1,0:T(8,128)(2,1)S(1)}, bf16[130,768]{1,0:T(8,128)(2,1)S(1)}, u32[]{:S(2)}, u32[]{:S(2)}) collective-permute-start(bf16[130,768]{1,0:T(8,128)(2,1)S(1)} %add_convert_fusion.9), channel_id=1, source_target_pairs={{0,8},{8,16},{16,24},{24,28},{28,20},{20,12},{12,4},{4,0},{1,9},{9... | collective-permute-start | bytes 599048 | tf_op jit(solution)/shard_map/ppermute | solution.py:111
  86.5 10.1 %collective-permute-start.27 = (bf16[128,1024]{1,0:T(8,128)(2,1)S(1)}, bf16[128,1024]{1,0:T(8,128)(2,1)S(1)}, u32[]{:S(2)}, u32[]{:S(2)}) collective-permute-start(bf16[128,1024]{1,0:T(8,128)(2,1)S(1)} %collective-permute-done.25), channel_id=1, source_target_pairs={{0,8},{8,16},{16,24},{24,28},{28,20},{20,12},{12,4},{4,0},{1,9},{9... | collective-permute-start | bytes 786440 | tf_op jit(solution)/shard_map/ppermute | solution.py:116
  88.0 10.1 %collective-permute-start.28 = (bf16[128,1024]{1,0:T(8,128)(2,1)S(1)}, bf16[128,1024]{1,0:T(8,128)(2,1)S(1)}, u32[]{:S(2)}, u32[]{:S(2)}) collective-permute-start(bf16[128,1024]{1,0:T(8,128)(2,1)S(1)} %collective-permute-done.26), channel_id=1, source_target_pairs={{8,0},{16,8},{24,16},{28,24},{20,28},{12,20},{4,12},{0,4},{9,1},{1... | collective-permute-start | bytes 786440 | tf_op jit(solution)/shard_map/ppermute | solution.py:117
  90.7 11.0 %collective-permute-start.15 = (bf16[130,768]{1,0:T(8,128)(2,1)S(1)}, bf16[130,768]{1,0:T(8,128)(2,1)S(1)}, u32[]{:S(2)}, u32[]{:S(2)}) collective-permute-start(bf16[130,768]{1,0:T(8,128)(2,1)S(1)} %add_convert_fusion.3), channel_id=1, source_target_pairs={{8,0},{16,8},{24,16},{28,24},{20,28},{12,20},{4,12},{0,4},{9,1},{1... | collective-permute-start | bytes 599048 | tf_op jit(solution)/shard_map/ppermute | solution.py:112
  91.4 11.0 %collective-permute-start.10 = (bf16[130,768]{1,0:T(8,128)(2,1)S(1)}, bf16[130,768]{1,0:T(8,128)(2,1)S(1)}, u32[]{:S(2)}, u32[]{:S(2)}) collective-permute-start(bf16[130,768]{1,0:T(8,128)(2,1)S(1)} %add_convert_fusion.8), channel_id=1, source_target_pairs={{0,8},{8,16},{16,24},{24,28},{28,20},{20,12},{12,4},{4,0},{1,9},{9... | collective-permute-start | bytes 599048 | tf_op jit(solution)/shard_map/ppermute | solution.py:111
  96.6 26.5 %collective-permute-start.29 = (bf16[128,1024]{1,0:T(8,128)(2,1)S(1)}, bf16[128,1024]{1,0:T(8,128)(2,1)S(1)}, u32[]{:S(2)}, u32[]{:S(2)}) collective-permute-start(bf16[128,1024]{1,0:T(8,128)(2,1)S(1)} %collective-permute-done.27), channel_id=1, source_target_pairs={{0,8},{8,16},{16,24},{24,28},{28,20},{20,12},{12,4},{4,0},{1,9},{9... | collective-permute-start | bytes 786440 | tf_op jit(solution)/shard_map/ppermute | solution.py:116
  98.1 27.7 %collective-permute-start.30 = (bf16[128,1024]{1,0:T(8,128)(2,1)S(1)}, bf16[128,1024]{1,0:T(8,128)(2,1)S(1)}, u32[]{:S(2)}, u32[]{:S(2)}) collective-permute-start(bf16[128,1024]{1,0:T(8,128)(2,1)S(1)} %collective-permute-done.28), channel_id=1, source_target_pairs={{8,0},{16,8},{24,16},{28,24},{20,28},{12,20},{4,12},{0,4},{9,1},{1... | collective-permute-start | bytes 786440 | tf_op jit(solution)/shard_map/ppermute | solution.py:117
  98.7 17.2 %copy-start.3 = (f32[16,512]{1,0:T(8,128)S(1)}, f32[16,512]{1,0:T(8,128)}, u32[]{:S(2)}) copy-start(f32[16,512]{1,0:T(8,128)} %param.20) | copy-start | bytes 98308
  101.8 7.2 %collective-permute-start.16 = (bf16[130,768]{1,0:T(8,128)(2,1)S(1)}, bf16[130,768]{1,0:T(8,128)(2,1)S(1)}, u32[]{:S(2)}, u32[]{:S(2)}) collective-permute-start(bf16[130,768]{1,0:T(8,128)(2,1)S(1)} %add_convert_fusion.2), channel_id=1, source_target_pairs={{8,0},{16,8},{24,16},{28,24},{20,28},{12,20},{4,12},{0,4},{9,1},{1... | collective-permute-start | bytes 599048 | tf_op jit(solution)/shard_map/ppermute | solution.py:112
  102.4 7.2 %collective-permute-start.11 = (bf16[130,768]{1,0:T(8,128)(2,1)S(1)}, bf16[130,768]{1,0:T(8,128)(2,1)S(1)}, u32[]{:S(2)}, u32[]{:S(2)}) collective-permute-start(bf16[130,768]{1,0:T(8,128)(2,1)S(1)} %add_convert_fusion.7), channel_id=1, source_target_pairs={{0,8},{8,16},{16,24},{24,28},{28,20},{20,12},{12,4},{4,0},{1,9},{9... | collective-permute-start | bytes 599048 | tf_op jit(solution)/shard_map/ppermute | solution.py:111
  109.0 25.8 %copy-start.5 = (f32[16,512]{1,0:T(8,128)S(1)}, f32[16,512]{1,0:T(8,128)}, u32[]{:S(2)}) copy-start(f32[16,512]{1,0:T(8,128)} %param.21) | copy-start | bytes 98308
  109.1 5.9 %collective-permute-start.17 = (bf16[130,768]{1,0:T(8,128)(2,1)S(1)}, bf16[130,768]{1,0:T(8,128)(2,1)S(1)}, u32[]{:S(2)}, u32[]{:S(2)}) collective-permute-start(bf16[130,768]{1,0:T(8,128)(2,1)S(1)} %add_convert_fusion.1), channel_id=1, source_target_pairs={{8,0},{16,8},{24,16},{28,24},{20,28},{12,20},{4,12},{0,4},{9,1},{1... | collective-permute-start | bytes 599048 | tf_op jit(solution)/shard_map/ppermute | solution.py:112
  109.7 5.9 %collective-permute-start.12 = (bf16[130,768]{1,0:T(8,128)(2,1)S(1)}, bf16[130,768]{1,0:T(8,128)(2,1)S(1)}, u32[]{:S(2)}, u32[]{:S(2)}) collective-permute-start(bf16[130,768]{1,0:T(8,128)(2,1)S(1)} %add_convert_fusion.6), channel_id=1, source_target_pairs={{0,8},{8,16},{16,24},{24,28},{28,20},{20,12},{12,4},{4,0},{1,9},{9... | collective-permute-start | bytes 599048 | tf_op jit(solution)/shard_map/ppermute | solution.py:111
  116.7 11.6 %collective-permute-start.24 = (f32[16,512]{1,0:T(8,128)S(1)}, f32[16,512]{1,0:T(8,128)S(1)}, u32[]{:S(2)}, u32[]{:S(2)}) collective-permute-start(f32[16,512]{1,0:T(8,128)S(1)} %exponential_multiply_fusion.5), channel_id=1, source_target_pairs={{0,28},{1,29},{2,30},{3,31}} | collective-permute-start | bytes 98312 | tf_op jit(solution)/shard_map/ppermute | solution.py:33
  121.9 7.7 %collective-permute-start.23 = (f32[16,512]{1,0:T(8,128)S(1)}, f32[16,512]{1,0:T(8,128)S(1)}, u32[]{:S(2)}, u32[]{:S(2)}) collective-permute-start(f32[16,512]{1,0:T(8,128)S(1)} %exponential_multiply_fusion.5), channel_id=1, source_target_pairs={{0,24},{4,28},{1,25},{5,29},{2,26},{6,30},{3,27},{7,31}} | collective-permute-start | bytes 98312 | tf_op jit(solution)/shard_map/ppermute | solution.py:33
  123.2 9.6 %collective-permute-start.22 = (f32[16,512]{1,0:T(8,128)S(1)}, f32[16,512]{1,0:T(8,128)S(1)}, u32[]{:S(2)}, u32[]{:S(2)}) collective-permute-start(f32[16,512]{1,0:T(8,128)S(1)} %exponential_multiply_fusion.5), channel_id=1, source_target_pairs={{0,20},{4,24},{8,28},{1,21},{5,25},{9,29},{2,22},{6,26},{10,30},{3... | collective-permute-start | bytes 98312 | tf_op jit(solution)/shard_map/ppermute | solution.py:33
  124.5 8.3 %collective-permute-start.21 = (f32[16,512]{1,0:T(8,128)S(1)}, f32[16,512]{1,0:T(8,128)S(1)}, u32[]{:S(2)}, u32[]{:S(2)}) collective-permute-start(f32[16,512]{1,0:T(8,128)S(1)} %exponential_multiply_fusion.5), channel_id=1, source_target_pairs={{0,16},{4,20},{8,24},{12,28},{1,17},{5,21},{9,25},{13,29},{2,18},{... | collective-permute-start | bytes 98312 | tf_op jit(solution)/shard_map/ppermute | solution.py:33
  125.8 9.0 %collective-permute-start.20 = (f32[16,512]{1,0:T(8,128)S(1)}, f32[16,512]{1,0:T(8,128)S(1)}, u32[]{:S(2)}, u32[]{:S(2)}) collective-permute-start(f32[16,512]{1,0:T(8,128)S(1)} %exponential_multiply_fusion.5), channel_id=1, source_target_pairs={{0,12},{4,16},{8,20},{12,24},{16,28},{1,13},{5,17},{9,21},{13,25},... | collective-permute-start | bytes 98312 | tf_op jit(solution)/shard_map/ppermute | solution.py:33
  128.3 6.5 %collective-permute-start.19 = (f32[16,512]{1,0:T(8,128)S(1)}, f32[16,512]{1,0:T(8,128)S(1)}, u32[]{:S(2)}, u32[]{:S(2)}) collective-permute-start(f32[16,512]{1,0:T(8,128)S(1)} %exponential_multiply_fusion.5), channel_id=1, source_target_pairs={{0,8},{4,12},{8,16},{12,20},{16,24},{20,28},{1,9},{5,13},{9,17},{1... | collective-permute-start | bytes 98312 | tf_op jit(solution)/shard_map/ppermute | solution.py:33
  129.6 5.2 %collective-permute-start.18 = (f32[16,512]{1,0:T(8,128)S(1)}, f32[16,512]{1,0:T(8,128)S(1)}, u32[]{:S(2)}, u32[]{:S(2)}) collective-permute-start(f32[16,512]{1,0:T(8,128)S(1)} %exponential_multiply_fusion.5), channel_id=1, source_target_pairs={{0,4},{4,8},{8,12},{12,16},{16,20},{20,24},{24,28},{1,5},{5,9},{9,... | collective-permute-start | bytes 98312 | tf_op jit(solution)/shard_map/ppermute | solution.py:33
  132.8 12.8 %collective-permute-start.31 = (bf16[128,1024]{1,0:T(8,128)(2,1)S(1)}, bf16[128,1024]{1,0:T(8,128)(2,1)S(1)}, u32[]{:S(2)}, u32[]{:S(2)}) collective-permute-start(bf16[128,1024]{1,0:T(8,128)(2,1)S(1)} %collective-permute-done.29), channel_id=1, source_target_pairs={{0,8},{8,16},{16,24},{24,28},{28,20},{20,12},{12,4},{4,0},{1,9},{9... | collective-permute-start | bytes 786440 | tf_op jit(solution)/shard_map/ppermute | solution.py:116
  132.8 14.8 %collective-permute-start.32 = (bf16[128,1024]{1,0:T(8,128)(2,1)S(1)}, bf16[128,1024]{1,0:T(8,128)(2,1)S(1)}, u32[]{:S(2)}, u32[]{:S(2)}) collective-permute-start(bf16[128,1024]{1,0:T(8,128)(2,1)S(1)} %collective-permute-done.30), channel_id=1, source_target_pairs={{8,0},{16,8},{24,16},{28,24},{20,28},{12,20},{4,12},{0,4},{9,1},{1... | collective-permute-start | bytes 786440 | tf_op jit(solution)/shard_map/ppermute | solution.py:117
  134.9 3.2 %copy-start.9 = (f32[512]{0:T(512)S(1)}, f32[512]{0:T(512)}, u32[]{:S(2)}) copy-start(f32[512]{0:T(512)} %param.22) | copy-start | bytes 6148
  145.6 8.6 %collective-permute-start.33 = (bf16[128,1024]{1,0:T(8,128)(2,1)S(1)}, bf16[128,1024]{1,0:T(8,128)(2,1)S(1)}, u32[]{:S(2)}, u32[]{:S(2)}) collective-permute-start(bf16[128,1024]{1,0:T(8,128)(2,1)S(1)} %collective-permute-done.31), channel_id=1, source_target_pairs={{0,8},{8,16},{16,24},{24,28},{28,20},{20,12},{12,4},{4,0},{1,9},{9... | collective-permute-start | bytes 786440 | tf_op jit(solution)/shard_map/ppermute | solution.py:116
  147.6 8.3 %collective-permute-start.34 = (bf16[128,1024]{1,0:T(8,128)(2,1)S(1)}, bf16[128,1024]{1,0:T(8,128)(2,1)S(1)}, u32[]{:S(2)}, u32[]{:S(2)}) collective-permute-start(bf16[128,1024]{1,0:T(8,128)(2,1)S(1)} %collective-permute-done.32), channel_id=1, source_target_pairs={{8,0},{16,8},{24,16},{28,24},{20,28},{12,20},{4,12},{0,4},{9,1},{1... | collective-permute-start | bytes 786440 | tf_op jit(solution)/shard_map/ppermute | solution.py:117
